TPU v7x, 32 devices: a whole 2x2x4 slice. The times are simulated.
32 devices in a mesh: dp: 8 (over z, y), tensor: 4 (over x, core).
Axes of the slice: x: 2, y: 2, z: 4, core: 2. Of those that a mesh axis runs over, the one named last changes fastest.
Arguments:
- tokens_in: bfloat16 [4096, 8192], P('dp', 'tensor'), may hold values from -6 to 6
- grad_out: bfloat16 [4096, 2, 1024], P('dp', None, 'tensor'), may hold values from -6 to 6
- base_weight: bfloat16 [2, 8192, 1024], P(None, None, 'tensor'), may hold values from -0.1875 to 0.1875
- a_master: float32 [65536, 128], P(('tensor', 'dp')), may hold values from -0.0625 to 0.0625
- b_master: float32 [4096, 256], P(('tensor', 'dp')), may hold values from -0.1875 to 0.1875
- a_first: float32 [65536, 128], P(('tensor', 'dp')), may hold values from -120 to 120
- a_second: float32 [65536, 128], P(('tensor', 'dp')), may hold values from 20 to 5000
- b_first: float32 [4096, 256], P(('tensor', 'dp')), may hold values from -120 to 120
- b_second: float32 [4096, 256], P(('tensor', 'dp')), may hold values from 20 to 5000
- block_tenant: int32 [32], P('dp'), may hold values from 0 to 7
- tenant_rank: int32 [8], replicated, may hold values from 16 to 64, as said below
- tenant_slot: int32 [8], replicated, may hold values from 0 to 7, each once
Outputs:
- input_gradient_layer: float32 [4096, 8192], P('dp', 'tensor')
- a_grad: float32 [65536, 128], P(('tensor', 'dp'))
- b_grad: float32 [4096, 256], P(('tensor', 'dp'))
- a_step: float32 [65536, 128], P(('tensor', 'dp'))
- b_step: float32 [4096, 256], P(('tensor', 'dp'))
Inputs may be any that keep to these rules, and one draw needn't show every extreme that they name: `tenant_rank`: a whole multiple of 16; some tenant has rank 64 and some has 16. `tenant_slot`: each slot is taken by exactly one tenant.
All inputs are finite; a program needn't handle non-finite values.
Results may differ from a plain program's by a relative error of at most 0.0041.
Values may be sent and summed in bfloat16 or wider, within the bound.
No kernel may reach another device: no remote copies, remote signals or barrier semaphores. Data moves between devices by JAX's collectives and lax.ppermute only.
A program may use at most 128 MiB of HBM per device.

v0:
```python
import jax
import jax.numpy as jnp
from jax import lax
from jax.sharding import PartitionSpec as P

PADDED_RANK = 64
TENANTS = 8
TENANT_BLOCK = 128


adapter_alpha_factor = 32.0
beta_one = 0.9
beta_two = 0.999
adam_eps = 1e-08
corr_one = 1.0 - 0.9**3
corr_two = 1.0 - 0.999**3


def adam_step(grad_value, first_moment, second_moment):
    new_first = beta_one * first_moment + (1.0 - beta_one) * grad_value
    new_second = beta_two * second_moment + (1.0 - beta_two) * grad_value * grad_value
    return new_first / corr_one / (jnp.sqrt(new_second / corr_two) + adam_eps)


def local(
    tokens_in,
    grad_out,
    base_weight,
    a_master,
    b_master,
    a_first,
    a_second,
    b_first,
    b_second,
    block_tenant,
    tenant_rank,
    tenant_slot,
):
    tok_rows, feat_shard = tokens_in.shape
    kv_shard = grad_out.shape[2]
    rank_width = a_master.shape[1]
    block_count = tok_rows // TENANT_BLOCK
    a_all, b_all = (
        lax.all_gather(a_master.astype(jnp.bfloat16), "dp", axis=0, tiled=True),
        lax.all_gather(b_master.astype(jnp.bfloat16), "dp", axis=0, tiled=True),
    )
    a_all = a_all.reshape(TENANTS, feat_shard, rank_width)
    b_all = b_all.reshape(TENANTS, rank_width, kv_shard)
    block_slot = tenant_slot[block_tenant]
    rank_of_block = tenant_rank[block_tenant].astype(jnp.float32)
    column_rank = (jnp.arange(rank_width) % PADDED_RANK).astype(jnp.float32)
    column_rank_mask = (column_rank[None, :] < rank_of_block[:, None]).astype(jnp.float32)
    adapter_scale_factor = adapter_alpha_factor / rank_of_block
    a_blocks = a_all[block_slot]
    b_blocks = b_all[block_slot].reshape(block_count, 2, PADDED_RANK, kv_shard)
    x_blocks = tokens_in.reshape(block_count, TENANT_BLOCK, feat_shard)
    dy_blocks = grad_out.reshape(block_count, TENANT_BLOCK, 2, kv_shard)
    mid_part = jnp.einsum("bnd,bdc->bnc", x_blocks, a_blocks, preferred_element_type=jnp.float32)
    back_part = jnp.einsum(
        "bnpk,bprk->bnpr", dy_blocks, b_blocks, preferred_element_type=jnp.float32
    ).reshape(block_count, TENANT_BLOCK, rank_width)
    mid_sum, backward_gradient_sum = lax.psum((mid_part, back_part), "tensor")
    middle_rank_rows = (mid_sum * column_rank_mask[:, None, :]).astype(jnp.bfloat16)
    backward_token_rows = (
        backward_gradient_sum * (column_rank_mask * adapter_scale_factor[:, None])[:, None, :]
    ).astype(jnp.bfloat16)
    dy_full = lax.all_gather(grad_out, "tensor", axis=2, tiled=True)
    weight_rows = lax.all_to_all(base_weight, "tensor", split_axis=1, concat_axis=2, tiled=True)
    frozen_gradient_share = jnp.einsum(
        "tpk,pdk->td", dy_full, weight_rows, preferred_element_type=jnp.float32
    )
    adapter_gradient_term = jnp.einsum(
        "bnc,bdc->bnd", backward_token_rows, a_blocks, preferred_element_type=jnp.float32
    ).reshape(tok_rows, feat_shard)
    input_gradient_layer = frozen_gradient_share + adapter_gradient_term
    a_terms = jnp.einsum(
        "bnd,bnc->bdc", x_blocks, backward_token_rows, preferred_element_type=jnp.float32
    )
    b_terms = (
        jnp.einsum(
            "bnpr,bnpk->bprk",
            middle_rank_rows.reshape(block_count, TENANT_BLOCK, 2, PADDED_RANK),
            dy_blocks,
            preferred_element_type=jnp.float32,
        )
        * adapter_scale_factor[:, None, None, None]
    )
    one_hot = (block_slot[None, :] == jnp.arange(TENANTS)[:, None]).astype(jnp.float32)
    a_flat = jnp.einsum("sb,bdc->sdc", one_hot, a_terms, precision=lax.Precision.HIGHEST).reshape(
        TENANTS * feat_shard, rank_width
    )
    b_flat = jnp.einsum("sb,bprk->sprk", one_hot, b_terms, precision=lax.Precision.HIGHEST).reshape(
        TENANTS * rank_width, kv_shard
    )
    a_total, b_total = lax.psum((a_flat, b_flat), "dp")
    owner_index = lax.axis_index("dp")
    a_rows = a_flat.shape[0] // lax.axis_size("dp")
    b_rows = b_flat.shape[0] // lax.axis_size("dp")
    a_grad = lax.dynamic_slice_in_dim(a_total, owner_index * a_rows, a_rows, 0)
    b_grad = lax.dynamic_slice_in_dim(b_total, owner_index * b_rows, b_rows, 0)
    return (
        input_gradient_layer,
        a_grad,
        b_grad,
        adam_step(a_grad, a_first, a_second),
        adam_step(b_grad, b_first, b_second),
    )


def solution(mesh):
    in_specs = (
        P("dp", "tensor"),
        P("dp", None, "tensor"),
        P(None, None, "tensor"),
        P(("tensor", "dp"), None),
        P(("tensor", "dp"), None),
        P(("tensor", "dp"), None),
        P(("tensor", "dp"), None),
        P(("tensor", "dp"), None),
        P(("tensor", "dp"), None),
        P("dp"),
        P(),
        P(),
    )
    out_specs = (
        P("dp", "tensor"),
        P(("tensor", "dp"), None),
        P(("tensor", "dp"), None),
        P(("tensor", "dp"), None),
        P(("tensor", "dp"), None),
    )
    return jax.shard_map(local, mesh=mesh, in_specs=in_specs, out_specs=out_specs, check_vma=False)
```

profile of v0, /device:TPU:0, one launch (start us, length us, event | category | flops | bytes accessed | tf_op | source)
XLA Modules:
  0.0 469.5 jit_solution(6542326159169784122)
XLA Ops:
  7.2 2.2 convert_element_type.45
  11.1 1.3 gather_fusion
  12.4 34.8 %all_gather.10 = bf16[1024,256]{1,0:T(8,128)(2,1)S(1)} all-gather(bf16[128,256]{1,0:T(8,128)(2,1)S(1)} %convert_element_type.41), channel_id=1, replica_groups=mesh['dp'=8,'tensor'=4] {'dp'}, dimensions={0}, use_global_device_ids=true | all-gather | bytes 589824 | tf_op jit(solution)/shard_map/all_gather | solution.py:45
  47.8 2.0 fusion.8
  49.8 40.4 %all-gather.5.cloned.1.call-done = bf16[16384,128]{1,0:T(8,128)(2,1)} async-done(((bf16[2048,128]{1,0:T(8,128)(2,1)}), bf16[16384,128]{1,0:T(8,128)(2,1)}) %all-gather.5.cloned.1.call-update) | async-done | bytes 4194320 | tf_op jit(solution)/shard_map/all_gather | solution.py:44
  90.2 4.4 gather_fusion.3
  94.6 3.2 convolution_bitcast_fusion.1
  99.6 29.8 %all-reduce.7.cloned.1.call-done = (f32[4,128,128]{1,2,0:T(8,128)}, f32[4,128,128]{1,2,0:T(8,128)}) async-done(((f32[4,128,128]{1,2,0:T(8,128)}, f32[4,128,128]{1,2,0:T(8,128)}), (f32[4,128,128]{1,2,0:T(8,128)}, f32[4,128,128]{1,2,0:T(8,128)})) %all-reduce.7.cloned.1.call-update) | async-done | bytes 524304 | tf_op jit(solution)/shard_map/psum | solution.py:62
  129.3 3.7 convolution_bitcast_fusion
  133.1 5.2 %copy.34 = f32[4,2048,128]{2,0,1:T(4,128)} copy(f32[4,2048,128]{1,2,0:T(8,128)} %convolution_bitcast_fusion) | data formatting | bytes 8388608 | tf_op jit(solution)/shard_map/bnd,bnc->bdc/dot_general | solution.py:76
  138.3 7.2 %fusion.18 = f32[8,2048,128]{2,0,1:T(8,128)S(1)} fusion(f32[4,2048,128]{2,0,1:T(4,128)} %copy.34, s32[4]{0:T(128)S(1)} %gather_fusion), kind=kOutput, calls=%fused_computation.38 | convolution fusion | flops 100663328 | bytes 12582928 | tf_op jit(solution)/shard_map/sb,bdc->sdc/dot_general | solution.py:89
  145.5 4.8 %copy.35 = f32[8,2048,128]{2,1,0:T(8,128)} copy(f32[8,2048,128]{2,0,1:T(8,128)S(1)} %fusion.18) | data formatting | bytes 16777216 | tf_op jit(solution)/shard_map/sb,bdc->sdc/dot_general | solution.py:89
  150.6 1.0 fusion.5
  151.6 1.3 copy.39
  153.0 16.4 %copy.30 = bf16[2,8192,256]{2,0,1:T(2,128)(2,1)} copy(bf16[2,8192,256]{2,1,0:T(8,128)(2,1)} %param.14) | data formatting | bytes 16777216 | tf_op args[2]
  169.4 5.8 %all-to-all-start = ((bf16[2,8192,256]{2,0,1:T(2,128)(2,1)}), bf16[2,8192,256]{2,0,1:T(2,128)(2,1)}, u32[]{:S(2)}, u32[]{:S(2)}) async-start(bf16[2,8192,256]{2,0,1:T(2,128)(2,1)} %copy.30), calls=%async_computation | async-start | bytes 16777216 | tf_op jit(solution)/shard_map/all_to_all | solution.py:68
  175.2 93.0 %all-to-all-done = bf16[2,8192,256]{2,0,1:T(2,128)(2,1)} async-done(((bf16[2,8192,256]{2,0,1:T(2,128)(2,1)}), bf16[2,8192,256]{2,0,1:T(2,128)(2,1)}, u32[]{:S(2)}, u32[]{:S(2)}) %all-to-all-start) | async-done | bytes 8388640 | tf_op jit(solution)/shard_map/all_to_all | solution.py:68
  268.2 12.2 %copy.50 = bf16[2,4,2048,256]{3,1,2,0:T(4,128)(2,1)} copy(bf16[2,4,2048,256]{3,0,2,1:T(2,128)(2,1)} %bitcast) | data formatting | bytes 16777216 | tf_op jit(solution)/shard_map/all_to_all | solution.py:68
  280.4 14.5 %all_to_all.16 = bf16[2,2048,1024]{2,1,0:T(8,128)(2,1)} reshape(bf16[2,2048,4,256]{3,2,1,0:T(4,128)(2,1)} %bitcast.47) | data formatting | bytes 16777216 | tf_op jit(solution)/shard_map/all_to_all | solution.py:68
  294.9 2.9 fusion.15
  297.8 11.9 %bitcast_add_fusion = f32[512,2048]{1,0:T(8,128)} fusion(f32[4,128,2048]{2,1,0:T(8,128)} %fusion.15, bf16[512,2,1024]{2,0,1:T(8,128)(2,1)} %all-gather.3.cloned.1.call-done, bf16[2,2048,1024]{2,1,0:T(8,128)(2,1)} %all_to_all.16), kind=kOutput, calls=%fused_computation.5 | convolution fusion | flops 4296015872 | bytes 18874368 | tf_op jit(solution)/shard_map/tpk,pdk->td/dot_general | solution.py:69
  309.8 148.1 %all-reduce.5.cloned.1.call-done = (f32[16384,128]{1,0:T(8,128)}, f32[1024,256]{1,0:T(8,128)}) async-done(((f32[16384,128]{1,0:T(8,128)}, f32[1024,256]{1,0:T(8,128)}), (f32[16384,128]{1,0:T(8,128)}, f32[1024,256]{1,0:T(8,128)})) %all-reduce.5.cloned.1.call-update) | async-done | bytes 9437200 | tf_op jit(solution)/shard_map/psum | solution.py:95
  457.9 3.4 fusion.4
  461.3 1.7 fusion.14
  (44 shorter events, 4.4 us)
Async XLA Ops:
  7.2 87.4 %copy-start = (bf16[512,2048]{1,0:T(8,128)(2,1)S(1)}, bf16[512,2048]{1,0:T(8,128)(2,1)}, u32[]{:S(2)}) copy-start(bf16[512,2048]{1,0:T(8,128)(2,1)} %param.12) | copy-start | bytes 6291460
  7.2 83.0 %all-gather.5.cloned.1.call-start = ((), (), s32[]{:S(2)}) async-start(), calls=%async_computation.2 | async-start | bytes 4718592 | tf_op jit(solution)/shard_map/all_gather | solution.py:44
  9.5 119.9 %all-reduce.7.cloned.1.call-start = ((), (), s32[]{:S(2)}) async-start(), calls=%async_computation.4 | async-start | bytes 1048576 | tf_op jit(solution)/shard_map/psum | solution.py:62
  90.2 7.6 %copy-start.4 = (bf16[512,2,256]{2,1,0:T(2,128)(2,1)S(1)}, bf16[512,2,256]{2,1,0:T(2,128)(2,1)}, u32[]{:S(2)}) copy-start(bf16[512,2,256]{2,1,0:T(2,128)(2,1)} %param.13) | copy-start | bytes 1572868
  94.6 4.2 copy-start.2
  97.8 200.1 %all-gather.3.cloned.1.call-start = ((), (), s32[]{:S(2)}) async-start(), calls=%async_computation.1 | async-start | bytes 2621440 | tf_op jit(solution)/shard_map/all_gather | solution.py:67
  98.7 359.2 %all-reduce.5.cloned.1.call-start = ((), (), s32[]{:S(2)}) async-start(), calls=%async_computation.3 | async-start | bytes 18874368 | tf_op jit(solution)/shard_map/psum | solution.py:95
  145.5 4.8 %copy-start.7 = (f32[4,128,128]{1,2,0:T(8,128)S(1)}, f32[4,128,128]{1,2,0:T(8,128)}, u32[]{:S(2)}) copy-start(f32[4,128,128]{1,2,0:T(8,128)} %get-tuple-element.8) | copy-start | bytes 786436
  169.4 98.8 %all-to-all-start = ((bf16[2,8192,256]{2,0,1:T(2,128)(2,1)}), bf16[2,8192,256]{2,0,1:T(2,128)(2,1)}, u32[]{:S(2)}, u32[]{:S(2)}) async-start(bf16[2,8192,256]{2,0,1:T(2,128)(2,1)} %copy.30), calls=%async_computation | async-start | bytes 16777216 | tf_op jit(solution)/shard_map/all_to_all | solution.py:68
  280.4 14.5 %copy-start.3 = (bf16[4,2048,128]{2,1,0:T(8,128)(2,1)S(1)}, bf16[4,2048,128]{2,1,0:T(8,128)(2,1)}, u32[]{:S(2)}) copy-start(bf16[4,2048,128]{2,1,0:T(8,128)(2,1)} %gather_fusion.3) | copy-start | bytes 6291460
  280.4 14.5 %copy-start.5 = (f32[4,128,128]{1,2,0:T(8,128)S(1)}, f32[4,128,128]{1,2,0:T(8,128)}, u32[]{:S(2)}) copy-start(f32[4,128,128]{1,2,0:T(8,128)} %get-tuple-element.7) | copy-start | bytes 786436
  297.8 160.0 %copy-start.6 = (f32[2048,128]{1,0:T(8,128)S(1)}, f32[2048,128]{1,0:T(8,128)}, u32[]{:S(2)}) copy-start(f32[2048,128]{1,0:T(8,128)} %param.18) | copy-start | bytes 3145732
  297.8 165.1 %copy-start.1 = (bf16[512,2048]{1,0:T(8,128)(2,1)S(1)}, bf16[512,2048]{1,0:T(8,128)(2,1)}, u32[]{:S(2)}) copy-start(bf16[512,2048]{1,0:T(8,128)(2,1)} %param.12) | copy-start | bytes 6291460
  309.8 151.5 %copy-start.8 = (f32[128,256]{1,0:T(8,128)S(1)}, f32[128,256]{1,0:T(8,128)}, u32[]{:S(2)}) copy-start(f32[128,256]{1,0:T(8,128)} %param.20) | copy-start | bytes 393220
  309.8 151.5 %copy-start.9 = (f32[128,256]{1,0:T(8,128)S(1)}, f32[128,256]{1,0:T(8,128)}, u32[]{:S(2)}) copy-start(f32[128,256]{1,0:T(8,128)} %param.19) | copy-start | bytes 393220
Sparse Core Ops, SparseCore 0:
  10.7 79.4 all-gather.4
  97.9 31.4 all-reduce.6
  131.5 22.9 all-gather.2
  158.9 298.9 all-reduce.4
where the time goes:
time: 470 us; the launch traced here: 469 us
  waiting for transfers between devices  311 us (66%)
  local copies, waits for them, and re-layouts  62.2 us (13%)
  blocking collectives  34.8 us (7%)
  matrix products  32.2 us (7%)
  between operations  13.9 us (3%)
  other arithmetic  9.17 us (2%)
  starting transfers between devices  5.98 us (1%)
    psum x1, waiting for transfers between devices, local(): a_total, b_total = lax.psum((a_flat, b_flat), 'dp')  148 us
    all_to_all x1, waiting for transfers between devices, local(): lax.all_to_all(base_weight, 'tensor', split_axis=1, concat_axis=2, tiled=...  93 us
    all_gather x1, waiting for transfers between devices, local(): lax.all_gather(a_master.astype(jnp.bfloat16), 'dp', axis=0, tiled=True)  40.4 us
    all_gather x1, blocking collectives, local(): lax.all_gather(b_master.astype(jnp.bfloat16), 'dp', axis=0, tiled=True)  34.8 us
    psum x1, waiting for transfers between devices, local(): mid_sum, backward_gradient_sum = lax.psum((mid_part, back_part), 'tensor')  29.8 us
    all_to_all x2, local copies, waits for them, and re-layouts, local(): lax.all_to_all(base_weight, 'tensor', split_axis=1, concat_axis=2, tiled=...  26.7 us
    unnamed x22, local copies, waits for them, and re-layouts  17.3 us
    dot_general x1, matrix products, local(): jnp.einsum('tpk,pdk->td', dy_full, weight_rows, preferred_element_type=jn...  11.9 us
  transfers between devices with their start and end apart: 5, of which 4 were waited for; matrix products, arithmetic and copies ran while one was open for 16% of the time, Pallas kernels for 0%

commit v1 on v0

--- a/solution.py
+++ b/solution.py
@@ -40,12 +40,16 @@
     kv_shard = grad_out.shape[2]
     rank_width = a_master.shape[1]
     block_count = tok_rows // TENANT_BLOCK
-    a_all, b_all = (
-        lax.all_gather(a_master.astype(jnp.bfloat16), "dp", axis=0, tiled=True),
-        lax.all_gather(b_master.astype(jnp.bfloat16), "dp", axis=0, tiled=True),
+    dp_size = lax.axis_size("dp")
+    a_rows_own = a_master.shape[0]
+    b_rows_own = b_master.shape[0]
+    b_as_a = b_master.astype(jnp.bfloat16).reshape(b_rows_own * kv_shard // rank_width, rank_width)
+    packed = jnp.concatenate([a_master.astype(jnp.bfloat16), b_as_a], axis=0)
+    packed_all = lax.all_gather(packed, "dp", axis=0, tiled=False)
+    a_all = packed_all[:, :a_rows_own].reshape(TENANTS, feat_shard, rank_width)
+    b_all = packed_all[:, a_rows_own:].reshape(dp_size, b_rows_own, kv_shard).reshape(
+        TENANTS, rank_width, kv_shard
     )
-    a_all = a_all.reshape(TENANTS, feat_shard, rank_width)
-    b_all = b_all.reshape(TENANTS, rank_width, kv_shard)
     block_slot = tenant_slot[block_tenant]
     rank_of_block = tenant_rank[block_tenant].astype(jnp.float32)
     column_rank = (jnp.arange(rank_width) % PADDED_RANK).astype(jnp.float32)
@@ -64,10 +68,12 @@
     backward_token_rows = (
         backward_gradient_sum * (column_rank_mask * adapter_scale_factor[:, None])[:, None, :]
     ).astype(jnp.bfloat16)
-    dy_full = lax.all_gather(grad_out, "tensor", axis=2, tiled=True)
-    weight_rows = lax.all_to_all(base_weight, "tensor", split_axis=1, concat_axis=2, tiled=True)
+    t_size = lax.axis_size("tensor")
+    dy_full = lax.all_gather(grad_out, "tensor", axis=2, tiled=False)
+    weight_split = base_weight.reshape(2, t_size, feat_shard, kv_shard)
+    weight_rows = lax.all_to_all(weight_split, "tensor", split_axis=1, concat_axis=1, tiled=True)
     frozen_gradient_share = jnp.einsum(
-        "tpk,pdk->td", dy_full, weight_rows, preferred_element_type=jnp.float32
+        "tpjk,pjdk->td", dy_full, weight_rows, preferred_element_type=jnp.float32
     )
     adapter_gradient_term = jnp.einsum(
         "bnc,bdc->bnd", backward_token_rows, a_blocks, preferred_element_type=jnp.float32
@@ -92,12 +98,7 @@
     b_flat = jnp.einsum("sb,bprk->sprk", one_hot, b_terms, precision=lax.Precision.HIGHEST).reshape(
         TENANTS * rank_width, kv_shard
     )
-    a_total, b_total = lax.psum((a_flat, b_flat), "dp")
-    owner_index = lax.axis_index("dp")
-    a_rows = a_flat.shape[0] // lax.axis_size("dp")
-    b_rows = b_flat.shape[0] // lax.axis_size("dp")
-    a_grad = lax.dynamic_slice_in_dim(a_total, owner_index * a_rows, a_rows, 0)
-    b_grad = lax.dynamic_slice_in_dim(b_total, owner_index * b_rows, b_rows, 0)
+    a_grad, b_grad = lax.psum_scatter((a_flat, b_flat), "dp", scatter_dimension=0, tiled=True)
     return (
         input_gradient_layer,
         a_grad,

time: 470 us -> 395 us (0.84)
  blocking collectives: 34.8 us -> 0 us
  local copies, waits for them, and re-layouts: 62.2 us -> 33.1 us
  waiting for transfers between devices: 311 us -> 302 us
    psum x1 -> x0, waiting for transfers between devices: 148 us -> none  [local(): a_total, b_total = lax.psum((a_flat, b_flat), 'dp')]
    reduce_scatter x0 -> x2, waiting for transfers between devices: none -> 100 us  [local(): lax.psum_scatter((a_flat, b_flat), 'dp', scatter_dimension=0, tiled=True)]
    all_gather x2, waiting for transfers between devices: 40.4 us -> 82.2 us  [the longest x1 82.2 us: local(): packed_all = lax.all_gather(packed, 'dp', axis=0, tiled=False)]
    all_gather x1 -> x0, blocking collectives: 34.8 us -> none  [local(): lax.all_gather(b_master.astype(jnp.bfloat16), 'dp', axis=0, tiled=True)]
    all_to_all x2 -> x0, local copies, waits for them, and re-layouts: 26.7 us -> none  [local(): lax.all_to_all(base_weight, 'tensor', split_axis=1, concat_axis=2, tiled=...]
    unnamed x22 -> x23, local copies, waits for them, and re-layouts: 17.3 us -> 1.48 us
    reshape x0 -> x4, local copies, waits for them, and re-layouts: none -> 8.22 us  [the longest x1 7.17 us: local(): weight_split = base_weight.reshape(2, t_size, feat_shard, kv_shard)]
    slice x0 -> x2, local copies, waits for them, and re-layouts: none -> 5.58 us  [the longest x1 4.5 us: local(): a_all = packed_all[:, :a_rows_own].reshape(TENANTS, feat_shard, rank_width)]
  transfers between devices with their start and end apart: 5 -> 6, of which waited for: 4 -> 4; matrix products, arithmetic and copies ran while one was open for 16% -> 13% of each run, Pallas kernels for 0% -> 0%
where the time goes in v1:
time: 395 us; the launch traced here: 394 us
  waiting for transfers between devices  302 us (76%)
  local copies, waits for them, and re-layouts  33.1 us (8%)
  matrix products  29.3 us (7%)
  between operations  14 us (4%)
  other arithmetic  9.41 us (2%)
  starting transfers between devices  6.21 us (2%)
    reduce_scatter x2, waiting for transfers between devices, local(): lax.psum_scatter((a_flat, b_flat), 'dp', scatter_dimension=0, tiled=True)  100 us
    all_to_all x1, waiting for transfers between devices, local(): lax.all_to_all(weight_split, 'tensor', split_axis=1, concat_axis=1, tiled...  90.3 us
    all_gather x1, waiting for transfers between devices, local(): packed_all = lax.all_gather(packed, 'dp', axis=0, tiled=False)  82.2 us
    psum x1, waiting for transfers between devices, local(): mid_sum, backward_gradient_sum = lax.psum((mid_part, back_part), 'tensor')  29.2 us
    dot_general x1, matrix products, local(): jnp.einsum('tpjk,pjdk->td', dy_full, weight_rows, preferred_element_type=...  12.1 us
  transfers between devices with their start and end apart: 6, of which 4 were waited for; matrix products, arithmetic and copies ran while one was open for 13% of the time, Pallas kernels for 0%

profile of v1, /device:TPU:0, one launch (start us, length us, event | category | flops | bytes accessed | tf_op | source)
XLA Modules:
  0.0 394.0 jit_solution(9366989404962711386)
XLA Ops:
  7.2 1.4 convert_element_type.41
  8.7 0.9 convert_element_type.42
  11.2 82.2 %all-gather.7.cloned.1.call-done = bf16[18432,128]{1,0:T(8,128)(2,1)} async-done(((bf16[2304,128]{1,0:T(8,128)(2,1)}), bf16[18432,128]{1,0:T(8,128)(2,1)}) %all-gather.7.cloned.1.call-update) | async-done | bytes 4718608 | tf_op jit(solution)/shard_map/all_gather | solution.py:48
  93.4 4.5 %slice.17 = bf16[8,2048,128]{2,1,0:T(8,128)(2,1)} slice(bf16[8,2304,128]{2,1,0:T(8,128)(2,1)} %bitcast.46), slice={[0:8], [0:2048], [0:128]} | slice | bytes 8388608 | tf_op jit(solution)/shard_map/slice | solution.py:49
  97.9 1.1 slice.16
  99.2 4.5 %gather_fusion.3 = bf16[4,2048,128]{2,1,0:T(8,128)(2,1)} fusion(bf16[8,2048,128]{2,1,0:T(8,128)(2,1)} %slice.17, s32[1024]{0:T(1024)S(1)} %pad_clamp_fusion), kind=kCustom, calls=%fused_computation.3 | custom fusion | bytes 4194320 | tf_op jit(solution)/shard_map/gather | solution.py:58
  105.4 3.2 convolution_bitcast_fusion
  108.6 1.4 copy.20
  110.8 29.2 %all-reduce.3.cloned.1.call-done = (f32[4,128,128]{2,1,0:T(8,128)}, f32[4,128,128]{1,2,0:T(8,128)}) async-done(((f32[4,128,128]{2,1,0:T(8,128)}, f32[4,128,128]{1,2,0:T(8,128)}), (f32[4,128,128]{2,1,0:T(8,128)}, f32[4,128,128]{1,2,0:T(8,128)})) %all-reduce.3.cloned.1.call-update) | async-done | bytes 524304 | tf_op jit(solution)/shard_map/psum | solution.py:66
  140.1 1.1 multiply_convert_fusion
  141.4 1.0 fusion.8
  142.4 1.3 copy.27
  143.8 2.8 fusion.19
  146.6 5.5 %copy.30 = f32[4,128,2048]{1,0,2:T(4,128)} copy(f32[4,128,2048]{2,1,0:T(8,128)} %fusion.19) | data formatting | bytes 8388608 | tf_op jit(solution)/shard_map/bnd,bnc->bdc/dot_general | solution.py:82
  152.1 7.0 %fusion = f32[8,2048,128]{2,0,1:T(8,128)S(1)} fusion(f32[4,128,2048]{1,0,2:T(4,128)} %copy.30, s32[4]{0:T(128)S(1)} %gather_fusion), kind=kOutput, calls=%fused_computation.5 | convolution fusion | flops 100663328 | bytes 12582928 | tf_op jit(solution)/shard_map/sb,bdc->sdc/dot_general | solution.py:95
  159.1 4.8 %copy.25 = f32[8,2048,128]{2,1,0:T(8,128)} copy(f32[8,2048,128]{2,0,1:T(8,128)S(1)} %fusion) | data formatting | bytes 16777216 | tf_op jit(solution)/shard_map/sb,bdc->sdc/dot_general | solution.py:95
  163.9 7.2 %copy.21 = bf16[2,4,2048,256]{3,2,0,1:T(8,128)(2,1)} copy(bf16[2,4,2048,256]{3,2,1,0:T(8,128)(2,1)} %bitcast.45) | data formatting | bytes 16777216 | tf_op jit(solution)/shard_map/reshape | solution.py:73
  171.1 6.0 %all-to-all-start = ((bf16[2,4,2048,256]{3,2,0,1:T(8,128)(2,1)}), bf16[2,4,2048,256]{3,2,0,1:T(8,128)(2,1)}, u32[]{:S(2)}, u32[]{:S(2)}) async-start(bf16[2,4,2048,256]{3,2,0,1:T(8,128)(2,1)} %copy.21), calls=%async_computation | async-start | bytes 16777216 | tf_op jit(solution)/shard_map/all_to_all | solution.py:74
  177.1 2.7 fusion.20
  179.8 90.3 %all-to-all-done = bf16[2,4,2048,256]{3,2,0,1:T(8,128)(2,1)} async-done(((bf16[2,4,2048,256]{3,2,0,1:T(8,128)(2,1)}), bf16[2,4,2048,256]{3,2,0,1:T(8,128)(2,1)}, u32[]{:S(2)}, u32[]{:S(2)}) %all-to-all-start) | async-done | bytes 8388640 | tf_op jit(solution)/shard_map/all_to_all | solution.py:74
  270.1 12.1 %bitcast_add_fusion = f32[512,2048]{1,0:T(8,128)} fusion(f32[4,128,2048]{2,1,0:T(8,128)} %fusion.20, bf16[2,4,2048,256]{3,2,0,1:T(8,128)(2,1)} %all-to-all-done, bf16[512,2,4,256]{0,3,2,1:T(8,128)(2,1)} %bitcast.54), kind=kOutput, calls=%fused_computation.4 | convolution fusion | flops 4296015872 | bytes 18874368 | tf_op jit(solution)/shard_map/tpjk,pjdk->td/dot_general | solution.py:75
  282.2 1.8 fusion.18
  284.0 100.2 %reduce-scatter.3.cloned.1.call-done = f32[2048,128]{1,0:T(8,128)} async-done(((f32[16384,128]{1,0:T(8,128)}), f32[2048,128]{1,0:T(8,128)}) %reduce-scatter.3.cloned.1.call-update) | async-done | bytes 1048592 | tf_op jit(solution)/shard_map/reduce_scatter | solution.py:101
  384.3 3.2 fusion.7
  (52 shorter events, 4.8 us)
Async XLA Ops:
  7.2 98.2 %copy-start = (bf16[512,2048]{1,0:T(8,128)(2,1)S(1)}, bf16[512,2048]{1,0:T(8,128)(2,1)}, u32[]{:S(2)}) copy-start(bf16[512,2048]{1,0:T(8,128)(2,1)} %param.12) | copy-start | bytes 6291460
  7.2 3.4 copy-start.10
  7.2 3.4 copy-start.2
  7.2 86.2 %all-gather.7.cloned.1.call-start = ((), (), s32[]{:S(2)}) async-start(), calls=%async_computation.6 | async-start | bytes 5308416 | tf_op jit(solution)/shard_map/all_gather | solution.py:48
  10.5 129.6 %all-reduce.3.cloned.1.call-start = ((), (), s32[]{:S(2)}) async-start(), calls=%async_computation.7 | async-start | bytes 1048576 | tf_op jit(solution)/shard_map/psum | solution.py:66
  99.2 5.0 %copy-start.5 = (bf16[512,2,256]{2,1,0:T(2,128)(2,1)S(1)}, bf16[512,2,256]{2,1,0:T(2,128)(2,1)}, u32[]{:S(2)}) copy-start(bf16[512,2,256]{2,1,0:T(2,128)(2,1)} %param.13) | copy-start | bytes 1572868
  108.5 1.6 copy-start.3
  108.5 71.3 %all-gather.5.cloned.1.call-start = ((), (), s32[]{:S(2)}) async-start(), calls=%async_computation.5 | async-start | bytes 2621440 | tf_op jit(solution)/shard_map/all_gather | solution.py:72
  110.0 172.2 %reduce-scatter.5.cloned.1.call-start = ((), (), s32[]{:S(2)}) async-start(), calls=%async_computation.4 | async-start | bytes 1179648 | tf_op jit(solution)/shard_map/reduce_scatter | solution.py:101
  141.4 2.5 copy-start.6
  143.7 240.5 %reduce-scatter.3.cloned.1.call-start = ((), (), s32[]{:S(2)}) async-start(), calls=%async_computation.3 | async-start | bytes 9437184 | tf_op jit(solution)/shard_map/reduce_scatter | solution.py:101
  171.1 6.0 %copy-start.4 = (bf16[4,2048,128]{2,1,0:T(8,128)(2,1)S(1)}, bf16[4,2048,128]{2,1,0:T(8,128)(2,1)}, u32[]{:S(2)}) copy-start(bf16[4,2048,128]{2,1,0:T(8,128)(2,1)} %gather_fusion.3) | copy-start | bytes 6291460
  171.1 99.0 %all-to-all-start = ((bf16[2,4,2048,256]{3,2,0,1:T(8,128)(2,1)}), bf16[2,4,2048,256]{3,2,0,1:T(8,128)(2,1)}, u32[]{:S(2)}, u32[]{:S(2)}) async-start(bf16[2,4,2048,256]{3,2,0,1:T(8,128)(2,1)} %copy.21), calls=%async_computation | async-start | bytes 16777216 | tf_op jit(solution)/shard_map/all_to_all | solution.py:74
  270.1 12.1 %copy-start.8 = (f32[128,256]{1,0:T(8,128)S(1)}, f32[128,256]{1,0:T(8,128)}, u32[]{:S(2)}) copy-start(f32[128,256]{1,0:T(8,128)} %param.20) | copy-start | bytes 393220
  270.1 12.1 %copy-start.9 = (f32[128,256]{1,0:T(8,128)S(1)}, f32[128,256]{1,0:T(8,128)}, u32[]{:S(2)}) copy-start(f32[128,256]{1,0:T(8,128)} %param.19) | copy-start | bytes 393220
  270.1 114.1 %copy-start.7 = (f32[2048,128]{1,0:T(8,128)S(1)}, f32[2048,128]{1,0:T(8,128)}, u32[]{:S(2)}) copy-start(f32[2048,128]{1,0:T(8,128)} %param.18) | copy-start | bytes 3145732
  282.2 105.2 %copy-start.1 = (bf16[512,2048]{1,0:T(8,128)(2,1)S(1)}, bf16[512,2048]{1,0:T(8,128)(2,1)}, u32[]{:S(2)}) copy-start(bf16[512,2048]{1,0:T(8,128)(2,1)} %param.12) | copy-start | bytes 6291460
Sparse Core Ops, SparseCore 0:
  10.8 82.5 all-gather.6
  108.7 31.3 all-reduce.2
  141.6 22.7 all-gather.4
  168.3 63.3 reduce-scatter.4
  236.2 148.0 reduce-scatter.2

commit v2 on v1

--- a/solution.py
+++ b/solution.py
@@ -20,6 +20,16 @@
     new_first = beta_one * first_moment + (1.0 - beta_one) * grad_value
     new_second = beta_two * second_moment + (1.0 - beta_two) * grad_value * grad_value
     return new_first / corr_one / (jnp.sqrt(new_second / corr_two) + adam_eps)
+
+
+def tensor_sum(parts):
+    size = lax.axis_size("tensor")
+    step = 1
+    while step < size:
+        pairs = [(i, i ^ step) for i in range(size)]
+        parts = tuple(p + lax.ppermute(p, "tensor", pairs) for p in parts)
+        step *= 2
+    return parts
 
 
 def local(
@@ -63,17 +73,22 @@
     back_part = jnp.einsum(
         "bnpk,bprk->bnpr", dy_blocks, b_blocks, preferred_element_type=jnp.float32
     ).reshape(block_count, TENANT_BLOCK, rank_width)
-    mid_sum, backward_gradient_sum = lax.psum((mid_part, back_part), "tensor")
+    mid_sum, backward_gradient_sum = tensor_sum((mid_part, back_part))
     middle_rank_rows = (mid_sum * column_rank_mask[:, None, :]).astype(jnp.bfloat16)
     backward_token_rows = (
         backward_gradient_sum * (column_rank_mask * adapter_scale_factor[:, None])[:, None, :]
     ).astype(jnp.bfloat16)
     t_size = lax.axis_size("tensor")
-    dy_full = lax.all_gather(grad_out, "tensor", axis=2, tiled=False)
-    weight_split = base_weight.reshape(2, t_size, feat_shard, kv_shard)
-    weight_rows = lax.all_to_all(weight_split, "tensor", split_axis=1, concat_axis=1, tiled=True)
+    weight_split = jnp.transpose(base_weight.reshape(2, t_size, feat_shard, kv_shard), (1, 0, 2, 3))
+    dy_copies = jnp.broadcast_to(
+        jnp.transpose(grad_out, (1, 0, 2))[None], (t_size, 2, tok_rows, kv_shard)
+    )
+    send = jnp.concatenate([weight_split, dy_copies], axis=2)
+    received = lax.all_to_all(send, "tensor", split_axis=0, concat_axis=0, tiled=True)
+    weight_rows = received[:, :, :feat_shard]
+    dy_full = received[:, :, feat_shard:]
     frozen_gradient_share = jnp.einsum(
-        "tpjk,pjdk->td", dy_full, weight_rows, preferred_element_type=jnp.float32
+        "jptk,jpdk->td", dy_full, weight_rows, preferred_element_type=jnp.float32
     )
     adapter_gradient_term = jnp.einsum(
         "bnc,bdc->bnd", backward_token_rows, a_blocks, preferred_element_type=jnp.float32
@@ -98,7 +113,19 @@
     b_flat = jnp.einsum("sb,bprk->sprk", one_hot, b_terms, precision=lax.Precision.HIGHEST).reshape(
         TENANTS * rank_width, kv_shard
     )
-    a_grad, b_grad = lax.psum_scatter((a_flat, b_flat), "dp", scatter_dimension=0, tiled=True)
+    a_per = a_flat.shape[0] // dp_size
+    b_per = b_flat.shape[0] // dp_size
+    b_wide = b_per * kv_shard // rank_width
+    grad_pack = jnp.concatenate(
+        [
+            a_flat.reshape(dp_size, a_per, rank_width),
+            b_flat.reshape(dp_size, b_wide, rank_width),
+        ],
+        axis=1,
+    ).reshape(dp_size * (a_per + b_wide), rank_width)
+    grad_own = lax.psum_scatter(grad_pack, "dp", scatter_dimension=0, tiled=True)
+    a_grad = grad_own[:a_per]
+    b_grad = grad_own[a_per:].reshape(b_per, kv_shard)
     return (
         input_gradient_layer,
         a_grad,

time: 395 us -> 326 us (0.83)
  waiting for transfers between devices: 302 us -> 212 us
  other arithmetic: 9.41 us -> 24.3 us
    reduce_scatter x2 -> x1, waiting for transfers between devices: 100 us -> 9.9 us  [local(): lax.psum_scatter(grad_pack, 'dp', scatter_dimension=0, tiled=True)]
    psum x1 -> x0, waiting for transfers between devices: 29.2 us -> none  [local(): mid_sum, backward_gradient_sum = lax.psum((mid_part, back_part), 'tensor')]
    all_to_all x1, waiting for transfers between devices: 90.3 us -> 113 us  [local(): lax.all_to_all(send, 'tensor', split_axis=0, concat_axis=0, tiled=True)]
    concatenate x0 -> x2, other arithmetic: none -> 14 us  [the longest x1 10.1 us: local(): send = jnp.concatenate([weight_split, dy_copies], axis=2)]
    ppermute x0 -> x4, waiting for transfers between devices: none -> 9.27 us  [tensor_sum(): parts = tuple((p + lax.ppermute(p, 'tensor', pairs) for p in parts))]
    dot_general x2 -> x0, local copies, waits for them, and re-layouts: 6.05 us -> none  [the longest x1 4.76 us: local(): jnp.einsum('sb,bdc->sdc', one_hot, a_terms, precision=lax.Precision.HIGHEST)]
    concatenate x0 -> x1, local copies, waits for them, and re-layouts: none -> 5.37 us  [local(): jnp.concatenate([a_flat.reshape(dp_size, a_per, rank_width), b_flat.resha...]
  transfers between devices with their start and end apart: 6 -> 7, of which waited for: 4 -> 5; matrix products, arithmetic and copies ran while one was open for 13% -> 14% of each run, Pallas kernels for 0% -> 0%
where the time goes in v2:
time: 326 us; the launch traced here: 325 us
  waiting for transfers between devices  212 us (65%)
  local copies, waits for them, and re-layouts  34.8 us (11%)
  matrix products  30 us (9%)
  other arithmetic  24.3 us (7%)
  between operations  14.2 us (4%)
  starting transfers between devices  9.29 us (3%)
    all_to_all x1, waiting for transfers between devices, local(): lax.all_to_all(send, 'tensor', split_axis=0, concat_axis=0, tiled=True)  113 us
    all_gather x1, waiting for transfers between devices, local(): packed_all = lax.all_gather(packed, 'dp', axis=0, tiled=False)  80.2 us
    dot_general x1, matrix products, local(): jnp.einsum('jptk,jpdk->td', dy_full, weight_rows, preferred_element_type=...  12 us
    concatenate x1, other arithmetic, local(): send = jnp.concatenate([weight_split, dy_copies], axis=2)  10.1 us
    reduce_scatter x1, waiting for transfers between devices, local(): lax.psum_scatter(grad_pack, 'dp', scatter_dimension=0, tiled=True)  9.9 us
    ppermute x4, waiting for transfers between devices, tensor_sum(): parts = tuple((p + lax.ppermute(p, 'tensor', pairs) for p in parts))  9.27 us
    reshape x1, local copies, waits for them, and re-layouts, local(): base_weight.reshape(2, t_size, feat_shard, kv_shard)  7.54 us
    dot_general x1, matrix products, local(): jnp.einsum('sb,bdc->sdc', one_hot, a_terms, precision=lax.Precision.HIGHEST)  6.82 us
  transfers between devices with their start and end apart: 7, of which 5 were waited for; matrix products, arithmetic and copies ran while one was open for 14% of the time, Pallas kernels for 0%

profile of v2, /device:TPU:0, one launch (start us, length us, event | category | flops | bytes accessed | tf_op | source)
XLA Modules:
  0.0 324.9 jit_solution(13983490879766905434)
XLA Ops:
  11.2 1.3 gather_fusion
  13.2 80.2 %all-gather.3.cloned.1.call-done = bf16[18432,128]{1,0:T(8,128)(2,1)} async-done(((bf16[2304,128]{1,0:T(8,128)(2,1)}), bf16[18432,128]{1,0:T(8,128)(2,1)}) %all-gather.3.cloned.1.call-update) | async-done | bytes 4718608 | tf_op jit(solution)/shard_map/all_gather | solution.py:58
  93.4 4.5 %slice.35 = bf16[8,2048,128]{2,1,0:T(8,128)(2,1)} slice(bf16[8,2304,128]{2,1,0:T(8,128)(2,1)} %bitcast.51), slice={[0:8], [0:2048], [0:128]} | slice | bytes 8388608 | tf_op jit(solution)/shard_map/slice | solution.py:59
  97.9 4.3 %gather_fusion.3 = bf16[4,2048,128]{2,1,0:T(8,128)(2,1)} fusion(bf16[8,2048,128]{2,1,0:T(8,128)(2,1)} %slice.35, s32[1024]{0:T(1024)S(1)} %pad_clamp_fusion), kind=kCustom, calls=%fused_computation.3 | custom fusion | bytes 4194320 | tf_op jit(solution)/shard_map/gather | solution.py:68
  102.2 2.5 convolution_bitcast_fusion
  106.9 1.6 gather_fusion.1
  112.2 1.5 collective-permute-start.3
  114.5 6.9 %collective-permute-done.3 = f32[4,128,128]{1,2,0:T(8,128)S(1)} collective-permute-done((f32[4,128,128]{1,2,0:T(8,128)S(1)}, f32[4,128,128]{1,2,0:T(8,128)S(1)}, u32[]{:S(2)}, u32[]{:S(2)}) %collective-permute-start.3) | collective-permute-done | bytes 262176 | tf_op jit(solution)/shard_map/ppermute | solution.py:30
  121.8 2.0 fusion.12
  123.8 2.3 collective-permute-done.1
  126.1 2.8 fusion.32
  128.9 5.2 %copy.30 = f32[4,128,2048]{1,0,2:T(4,128)} copy(f32[4,128,2048]{2,1,0:T(8,128)} %fusion.32) | data formatting | bytes 8388608 | tf_op jit(solution)/shard_map/bnd,bnc->bdc/dot_general | solution.py:97
  134.2 6.8 %fusion.2 = f32[8,2048,128]{2,0,1:T(8,128)S(1)} fusion(f32[4,128,2048]{1,0,2:T(4,128)} %copy.30, s32[4]{0:T(128)S(1)} %gather_fusion), kind=kOutput, calls=%fused_computation.10 | convolution fusion | flops 100663328 | bytes 12582928 | tf_op jit(solution)/shard_map/sb,bdc->sdc/dot_general | solution.py:110
  141.0 3.9 %pad_maximum_fusion.1 = f32[8,2304,128]{2,0,1:T(8,128)S(1)} fusion(f32[8,256,128]{2,0,1:T(8,128)S(1)} %bitcast.56, f32[8,2048,128]{2,0,1:T(8,128)S(1)} %fusion.2), kind=kLoop, calls=%fused_computation.5 | loop fusion | flops 2359296 | bytes 18874368 | tf_op jit(solution)/shard_map/concatenate | solution.py:119
  144.9 5.4 %copy.28 = f32[8,2304,128]{2,1,0:T(8,128)} copy(f32[8,2304,128]{2,0,1:T(8,128)S(1)} %pad_maximum_fusion.1) | data formatting | bytes 18874368 | tf_op jit(solution)/shard_map/concatenate | solution.py:119
  150.4 7.5 %copy.41 = bf16[2,4,2048,256]{3,2,0,1:T(8,128)(2,1)} copy(bf16[2,4,2048,256]{3,2,1,0:T(8,128)(2,1)} %bitcast.50) | data formatting | bytes 16777216 | tf_op jit(solution)/shard_map/reshape | solution.py:82
  158.1 10.1 %pad_maximum_fusion = bf16[4,2,2560,256]{3,2,1,0:T(8,128)(2,1)} fusion(bf16[4,2,512,256]{3,2,1,0:T(8,128)(2,1)S(1)} %broadcast_in_dim.4, bf16[4,2,2048,256]{3,2,1,0:T(8,128)(2,1)} %bitcast.49), kind=kLoop, calls=%fused_computation.4 | loop fusion | flops 20971520 | bytes 20971520 | tf_op jit(solution)/shard_map/concatenate | solution.py:86
  168.2 6.4 %all-to-all-start = ((bf16[4,2,2560,256]{3,2,1,0:T(8,128)(2,1)}), bf16[4,2,2560,256]{3,2,1,0:T(8,128)(2,1)}, u32[]{:S(2)}, u32[]{:S(2)}) async-start(bf16[4,2,2560,256]{3,2,1,0:T(8,128)(2,1)} %pad_maximum_fusion), calls=%async_computation | async-start | bytes 20971520 | tf_op jit(solution)/shard_map/all_to_all | solution.py:87
  174.6 2.7 fusion.31
  177.3 112.8 %all-to-all-done = bf16[4,2,2560,256]{3,2,1,0:T(8,128)(2,1)} async-done(((bf16[4,2,2560,256]{3,2,1,0:T(8,128)(2,1)}), bf16[4,2,2560,256]{3,2,1,0:T(8,128)(2,1)}, u32[]{:S(2)}, u32[]{:S(2)}) %all-to-all-start) | async-done | bytes 10485792 | tf_op jit(solution)/shard_map/all_to_all | solution.py:87
  290.0 12.0 %bitcast_add_fusion = f32[512,2048]{1,0:T(8,128)} fusion(f32[4,128,2048]{2,1,0:T(8,128)} %fusion.31, bf16[4,2,2560,256]{3,2,1,0:T(8,128)(2,1)} %all-to-all-done), kind=kOutput, calls=%fused_computation.9 | convolution fusion | flops 4296015872 | bytes 18874368 | tf_op jit(solution)/shard_map/jptk,jpdk->td/dot_general | solution.py:90
  302.0 9.9 %reduce-scatter.2.cloned.1.call-done = f32[2304,128]{1,0:T(8,128)} async-done(((f32[18432,128]{1,0:T(8,128)}), f32[2304,128]{1,0:T(8,128)}) %reduce-scatter.2.cloned.1.call-update) | async-done | bytes 1179664 | tf_op jit(solution)/shard_map/reduce_scatter | solution.py:126
  312.9 1.7 fusion.22
  314.6 3.4 %fusion.11 = (f32[2048,128]{1,0:T(8,128)}, f32[2048,128]{1,0:T(8,128)}) fusion(f32[2048,128]{1,0:T(8,128)S(1)} %copy-done.6, f32[2048,128]{1,0:T(8,128)} %param.17, f32[2304,128]{1,0:T(8,128)} %reduce-scatter.2.cloned.1.call-done), kind=kLoop, calls=%fused_computation.19 | loop fusion | flops 2883584 | bytes 5242880 | tf_op jit(solution)/shard_map/div | solution.py:22
  (54 shorter events, 12.8 us)
Async XLA Ops:
  7.2 95.0 %copy-start = (bf16[512,2048]{1,0:T(8,128)(2,1)S(1)}, bf16[512,2048]{1,0:T(8,128)(2,1)}, u32[]{:S(2)}) copy-start(bf16[512,2048]{1,0:T(8,128)(2,1)} %param.12) | copy-start | bytes 6291460
  7.2 5.3 %copy-start.2 = (s32[8]{0:T(128)S(1)}, s32[8]{0:T(128)}, u32[]{:S(2)}) copy-start(s32[8]{0:T(128)} %param.22) | copy-start | bytes 100
  7.2 86.2 %all-gather.3.cloned.1.call-start = ((), (), s32[]{:S(2)}) async-start(), calls=%async_computation.3 | async-start | bytes 5308416 | tf_op jit(solution)/shard_map/all_gather | solution.py:58
  10.5 301.4 %reduce-scatter.2.cloned.1.call-start = ((), (), s32[]{:S(2)}) async-start(), calls=%async_computation.2 | async-start | bytes 10616832 | tf_op jit(solution)/shard_map/reduce_scatter | solution.py:126
  102.2 6.3 %copy-start.4 = (bf16[512,2,256]{2,1,0:T(2,128)(2,1)S(1)}, bf16[512,2,256]{2,1,0:T(2,128)(2,1)}, u32[]{:S(2)}) copy-start(bf16[512,2,256]{2,1,0:T(2,128)(2,1)} %param.13) | copy-start | bytes 1572868
  104.7 6.5 %collective-permute-start.2 = (f32[4,128,128]{1,2,0:T(8,128)S(1)}, f32[4,128,128]{1,2,0:T(8,128)}, u32[]{:S(2)}, u32[]{:S(2)}) collective-permute-start(f32[4,128,128]{1,2,0:T(8,128)S(1)} %convolution_bitcast_fusion), channel_id=1, source_target_pairs={{0,1},{1,0},{2,3},{3,2},{4,5},{5,4},{6,7},{7,6},{8,9},{9,8},{10,11... | collective-permute-start | bytes 786440 | tf_op jit(solution)/shard_map/ppermute | solution.py:30
  110.6 3.2 collective-permute-start
  112.2 9.2 %collective-permute-start.3 = (f32[4,128,128]{1,2,0:T(8,128)S(1)}, f32[4,128,128]{1,2,0:T(8,128)S(1)}, u32[]{:S(2)}, u32[]{:S(2)}) collective-permute-start(f32[4,128,128]{1,2,0:T(8,128)S(1)} %add.72), channel_id=1, source_target_pairs={{0,2},{1,3},{2,0},{3,1},{4,6},{5,7},{6,4},{7,5},{8,10},{9,11},{10,... | collective-permute-start | bytes 786440 | tf_op jit(solution)/shard_map/ppermute | solution.py:30
  113.8 12.3 %collective-permute-start.1 = (f32[4,128,128]{2,1,0:T(8,128)S(1)}, f32[4,128,128]{2,1,0:T(8,128)S(1)}, u32[]{:S(2)}, u32[]{:S(2)}) collective-permute-start(f32[4,128,128]{2,1,0:T(8,128)S(1)} %add.68), channel_id=1, source_target_pairs={{0,2},{1,3},{2,0},{3,1},{4,6},{5,7},{6,4},{7,5},{8,10},{9,11},{10,... | collective-permute-start | bytes 786440 | tf_op jit(solution)/shard_map/ppermute | solution.py:30
  134.2 6.8 %copy-start.5 = (f32[8,2,64,256]{3,0,2,1:T(8,128)S(1)}, f32[8,2,64,256]{3,0,2,1:T(8,128)}, u32[]{:S(2)}) copy-start(f32[8,2,64,256]{3,0,2,1:T(8,128)} %fusion.12) | copy-start | bytes 3145732
  168.2 6.4 %copy-start.3 = (bf16[4,2048,128]{2,1,0:T(8,128)(2,1)S(1)}, bf16[4,2048,128]{2,1,0:T(8,128)(2,1)}, u32[]{:S(2)}) copy-start(bf16[4,2048,128]{2,1,0:T(8,128)(2,1)} %gather_fusion.3) | copy-start | bytes 6291460
  168.2 121.9 %all-to-all-start = ((bf16[4,2,2560,256]{3,2,1,0:T(8,128)(2,1)}), bf16[4,2,2560,256]{3,2,1,0:T(8,128)(2,1)}, u32[]{:S(2)}, u32[]{:S(2)}) async-start(bf16[4,2,2560,256]{3,2,1,0:T(8,128)(2,1)} %pad_maximum_fusion), calls=%async_computation | async-start | bytes 20971520 | tf_op jit(solution)/shard_map/all_to_all | solution.py:87
  177.3 135.6 %copy-start.8 = (f32[128,256]{1,0:T(8,128)S(1)}, f32[128,256]{1,0:T(8,128)}, u32[]{:S(2)}) copy-start(f32[128,256]{1,0:T(8,128)} %param.20) | copy-start | bytes 393220
  177.3 137.3 %copy-start.6 = (f32[2048,128]{1,0:T(8,128)S(1)}, f32[2048,128]{1,0:T(8,128)}, u32[]{:S(2)}) copy-start(f32[2048,128]{1,0:T(8,128)} %param.18) | copy-start | bytes 3145732
  290.0 28.0 %copy-start.1 = (bf16[512,2048]{1,0:T(8,128)(2,1)S(1)}, bf16[512,2048]{1,0:T(8,128)(2,1)}, u32[]{:S(2)}) copy-start(bf16[512,2048]{1,0:T(8,128)(2,1)} %param.12) | copy-start | bytes 6291460
  312.9 5.1 %copy-start.7 = (f32[128,256]{1,0:T(8,128)}, f32[128,256]{1,0:T(8,128)S(1)}, u32[]{:S(2)}) copy-start(f32[128,256]{1,0:T(8,128)S(1)} %reshape.146) | copy-start | bytes 393220
Sparse Core Ops, SparseCore 0:
  10.8 82.5 all-gather.2
  150.4 161.4 reduce-scatter.1

commit v3 on v2

--- a/solution.py
+++ b/solution.py
@@ -30,6 +30,39 @@
         parts = tuple(p + lax.ppermute(p, "tensor", pairs) for p in parts)
         step *= 2
     return parts
+
+
+def frozen_gradient(grad_out, base_weight, feat_shard):
+    tok_rows, _, kv_shard = grad_out.shape
+    t_size = lax.axis_size("tensor")
+    if t_size != 4:
+        weight_split = jnp.transpose(
+            base_weight.reshape(2, t_size, feat_shard, kv_shard), (1, 0, 2, 3)
+        )
+        weight_rows = lax.all_to_all(weight_split, "tensor", split_axis=0, concat_axis=0, tiled=True)
+        dy_full = lax.all_gather(grad_out, "tensor", axis=0, tiled=False)
+        return jnp.einsum("jtpk,jpdk->td", dy_full, weight_rows, preferred_element_type=jnp.float32)
+    me = lax.axis_index("tensor")
+    core_bit = me % 2
+    row_bit = me // 2
+    by_bits = base_weight.reshape(2, 2, 2, feat_shard, kv_shard)
+    to_partner = lax.dynamic_index_in_dim(by_bits, 1 - core_bit, axis=2, keepdims=False)
+    own_w = lax.dynamic_index_in_dim(by_bits, core_bit, axis=2, keepdims=False)
+    core_pairs = [(i, i ^ 1) for i in range(t_size)]
+    row_pairs = [(i, i ^ 2) for i in range(t_size)]
+    partner_w = lax.ppermute(to_partner, "tensor", core_pairs)
+    partner_dy = lax.ppermute(grad_out, "tensor", core_pairs)
+
+    def chip_partial(bit):
+        own = lax.dynamic_index_in_dim(own_w, bit, axis=1, keepdims=False)
+        other = lax.dynamic_index_in_dim(partner_w, bit, axis=1, keepdims=False)
+        first = jnp.einsum("tpk,pdk->td", grad_out, own, preferred_element_type=jnp.float32)
+        second = jnp.einsum("tpk,pdk->td", partner_dy, other, preferred_element_type=jnp.float32)
+        return first + second
+
+    far_part = chip_partial(1 - row_bit).astype(jnp.bfloat16)
+    far_in = lax.ppermute(far_part, "tensor", row_pairs)
+    return chip_partial(row_bit) + far_in.astype(jnp.float32)
 
 
 def local(
@@ -78,18 +111,7 @@
     backward_token_rows = (
         backward_gradient_sum * (column_rank_mask * adapter_scale_factor[:, None])[:, None, :]
     ).astype(jnp.bfloat16)
-    t_size = lax.axis_size("tensor")
-    weight_split = jnp.transpose(base_weight.reshape(2, t_size, feat_shard, kv_shard), (1, 0, 2, 3))
-    dy_copies = jnp.broadcast_to(
-        jnp.transpose(grad_out, (1, 0, 2))[None], (t_size, 2, tok_rows, kv_shard)
-    )
-    send = jnp.concatenate([weight_split, dy_copies], axis=2)
-    received = lax.all_to_all(send, "tensor", split_axis=0, concat_axis=0, tiled=True)
-    weight_rows = received[:, :, :feat_shard]
-    dy_full = received[:, :, feat_shard:]
-    frozen_gradient_share = jnp.einsum(
-        "jptk,jpdk->td", dy_full, weight_rows, preferred_element_type=jnp.float32
-    )
+    frozen_gradient_share = frozen_gradient(grad_out, base_weight, feat_shard)
     adapter_gradient_term = jnp.einsum(
         "bnc,bdc->bnd", backward_token_rows, a_blocks, preferred_element_type=jnp.float32
     ).reshape(tok_rows, feat_shard)
@@ -123,7 +145,14 @@
         ],
         axis=1,
     ).reshape(dp_size * (a_per + b_wide), rank_width)
-    grad_own = lax.psum_scatter(grad_pack, "dp", scatter_dimension=0, tiled=True)
+    grad_parts = lax.all_to_all(
+        grad_pack.astype(jnp.bfloat16).reshape(dp_size, a_per + b_wide, rank_width),
+        "dp",
+        split_axis=0,
+        concat_axis=0,
+        tiled=True,
+    )
+    grad_own = jnp.sum(grad_parts.astype(jnp.float32), axis=0)
     a_grad = grad_own[:a_per]
     b_grad = grad_own[a_per:].reshape(b_per, kv_shard)
     return (

time: 326 us -> 275 us (0.84)
  waiting for transfers between devices: 212 us -> 155 us
  matrix products: 30 us -> 36.7 us
    all_to_all x1, waiting for transfers between devices: 113 us -> 25.5 us  [local(): lax.all_to_all(grad_pack.astype(jnp.bfloat16).reshape(dp_size, a_per + b_...]
    ppermute x0 -> x3, waiting for transfers between devices: none -> 38.1 us  [the longest x1 33.4 us: frozen_gradient(): far_in = lax.ppermute(far_part, 'tensor', row_pairs)]
    concatenate x1 -> x0, other arithmetic: 10.1 us -> none  [local(): send = jnp.concatenate([weight_split, dy_copies], axis=2)]
    reduce_scatter x1 -> x0, waiting for transfers between devices: 9.9 us -> none  [local(): lax.psum_scatter(grad_pack, 'dp', scatter_dimension=0, tiled=True)]
    dot_general x1 -> x4, matrix products: 12 us -> 20.2 us  [the longest x2 12.4 us: chip_partial(): jnp.einsum('tpk,pdk->td', partner_dy, other, preferred_element_type=jnp.f...]
    concatenate x1, other arithmetic: 3.91 us -> 11.2 us  [local(): jnp.concatenate([a_flat.reshape(dp_size, a_per, rank_width), b_flat.resha...]
    unnamed x18, local copies, waits for them, and re-layouts: 0.04 us -> 5.46 us
    squeeze x0 -> x1, local copies, waits for them, and re-layouts: none -> 4.48 us  [frozen_gradient(): lax.dynamic_index_in_dim(by_bits, 1 - core_bit, axis=2, keepdims=False)]
  transfers between devices with their start and end apart: 7 -> 9, of which waited for: 5 -> 8; matrix products, arithmetic and copies ran while one was open for 14% -> 16% of each run, Pallas kernels for 0% -> 0%
where the time goes in v3:
time: 275 us
  waiting for transfers between devices  155 us (56%)
  matrix products  36.7 us (13%)
  local copies, waits for them, and re-layouts  36.2 us (13%)
  other arithmetic  23 us (8%)
  between operations  14.3 us (5%)
  starting transfers between devices  9.67 us (4%)
    all_gather x1, waiting for transfers between devices, local(): packed_all = lax.all_gather(packed, 'dp', axis=0, tiled=False)  80.3 us
    ppermute x1, waiting for transfers between devices, frozen_gradient(): far_in = lax.ppermute(far_part, 'tensor', row_pairs)  33.4 us
    all_to_all x1, waiting for transfers between devices, local(): lax.all_to_all(grad_pack.astype(jnp.bfloat16).reshape(dp_size, a_per + b_...  25.5 us
    dot_general x2, matrix products, chip_partial(): jnp.einsum('tpk,pdk->td', partner_dy, other, preferred_element_type=jnp.f...  12.4 us
    concatenate x1, other arithmetic, local(): jnp.concatenate([a_flat.reshape(dp_size, a_per, rank_width), b_flat.resha...  11.2 us
    ppermute x4, waiting for transfers between devices, tensor_sum(): parts = tuple((p + lax.ppermute(p, 'tensor', pairs) for p in parts))  11 us
    dot_general x2, matrix products, chip_partial(): jnp.einsum('tpk,pdk->td', grad_out, own, preferred_element_type=jnp.float32)  7.86 us
    dot_general x1, matrix products, local(): jnp.einsum('sb,bdc->sdc', one_hot, a_terms, precision=lax.Precision.HIGHEST)  7.03 us
  transfers between devices with their start and end apart: 9, of which 8 were waited for; matrix products, arithmetic and copies ran while one was open for 16% of the time, Pallas kernels for 0%

profile of v3, /device:TPU:0, one launch (start us, length us, event | category | flops | bytes accessed | tf_op | source)
XLA Modules:
  0.0 274.8 jit_solution(533665738353676574)
XLA Ops:
  13.1 80.3 %all-gather.3.cloned.1.call-done = bf16[18432,128]{1,0:T(8,128)(2,1)} async-done(((bf16[2304,128]{1,0:T(8,128)(2,1)}), bf16[18432,128]{1,0:T(8,128)(2,1)}) %all-gather.3.cloned.1.call-update) | async-done | bytes 4718608 | tf_op jit(solution)/shard_map/all_gather | solution.py:91
  94.5 4.5 %slice.25 = bf16[8,2048,128]{2,1,0:T(8,128)(2,1)} slice(bf16[8,2304,128]{2,1,0:T(8,128)(2,1)} %bitcast.83), slice={[0:8], [0:2048], [0:128]} | slice | bytes 8388608 | tf_op jit(solution)/shard_map/slice | solution.py:92
  99.8 4.4 %gather_fusion.3 = bf16[4,2048,128]{2,1,0:T(8,128)(2,1)} fusion(bf16[8,2048,128]{2,1,0:T(8,128)(2,1)} %slice.25, s32[1024]{0:T(1024)S(1)} %pad_clamp_fusion), kind=kCustom, calls=%fused_computation.3 | custom fusion | bytes 4194320 | tf_op jit(solution)/shard_map/gather | solution.py:101
  110.5 7.0 %collective-permute-done.6 = f32[4,128,128]{1,2,0:T(8,128)S(1)} collective-permute-done((f32[4,128,128]{1,2,0:T(8,128)S(1)}, f32[4,128,128]{1,2,0:T(8,128)S(1)}, u32[]{:S(2)}, u32[]{:S(2)}) %collective-permute-start.6) | collective-permute-done | bytes 262176 | tf_op jit(solution)/shard_map/ppermute | solution.py:30
  118.8 3.4 %collective-permute-done.4 = f32[4,128,128]{1,2,0:T(8,128)S(1)} collective-permute-done((f32[4,128,128]{1,2,0:T(8,128)S(1)}, f32[4,128,128]{1,2,0:T(8,128)S(1)}, u32[]{:S(2)}, u32[]{:S(2)}) %collective-permute-start.4) | collective-permute-done | bytes 262176 | tf_op jit(solution)/shard_map/ppermute | solution.py:30
  122.4 2.7 convolution_bitcast_fusion
  125.1 5.3 %copy.50 = f32[4,2048,128]{2,0,1:T(4,128)} copy(f32[4,2048,128]{1,2,0:T(8,128)} %convolution_bitcast_fusion) | data formatting | bytes 8388608 | tf_op jit(solution)/shard_map/bnd,bnc->bdc/dot_general | solution.py:119
  130.3 7.0 %convolution_convert_fusion = bf16[8,2048,128]{2,0,1:T(8,128)(2,1)S(1)} fusion(f32[4,2048,128]{2,0,1:T(4,128)} %copy.50, s32[4]{0:T(128)S(1)} %gather_fusion), kind=kOutput, calls=%fused_computation.14 | convolution fusion | flops 102760480 | bytes 8388624 | tf_op jit(solution)/shard_map/sb,bdc->sdc/dot_general | solution.py:132
  137.4 11.2 %pad_maximum_fusion = bf16[8,2304,128]{2,0,1:T(8,128)(2,1)S(1)} fusion(bf16[8,256,128]{2,0,1:T(8,128)(2,1)S(1)} %bitcast.86, bf16[8,2048,128]{2,0,1:T(8,128)(2,1)S(1)} %convolution_convert_fusion), kind=kLoop, calls=%fused_computation.5 | loop fusion | flops 2359296 | bytes 9437184 | tf_op jit(solution)/shard_map/concatenate | solution.py:141
  148.6 2.9 %copy.54 = bf16[8,2304,128]{2,1,0:T(8,128)(2,1)} copy(bf16[8,2304,128]{2,0,1:T(8,128)(2,1)S(1)} %pad_maximum_fusion) | data formatting | bytes 9437184 | tf_op jit(solution)/shard_map/concatenate | solution.py:141
  151.5 4.8 %all-to-all-start = ((bf16[8,2304,128]{2,1,0:T(8,128)(2,1)}), bf16[8,2304,128]{2,1,0:T(8,128)(2,1)}, u32[]{:S(2)}, u32[]{:S(2)}) async-start(bf16[8,2304,128]{2,1,0:T(8,128)(2,1)} %copy.54), calls=%async_computation | async-start | bytes 9437184 | tf_op jit(solution)/shard_map/all_to_all | solution.py:148
  156.4 4.5 %copy_bitcast_fusion = bf16[2,2,2048,256]{3,2,0,1:T(8,128)(2,1)} fusion(bf16[2,2,2,2048,256]{4,3,2,1,0:T(8,128)(2,1)} %bitcast.87, s32[]{:T(128)S(6)} %select_n.64), kind=kLoop, calls=%fused_computation.11 | loop fusion | bytes 8388612 | tf_op jit(solution)/shard_map/jit(dynamic_index_in_dim)/squeeze | solution.py:49
  161.5 2.9 %fusion.3 = f32[2048,512,1]{1,0,2:T(8,128)S(1)} fusion(bf16[2,2,2,2048,256]{4,3,2,1,0:T(8,128)(2,1)} %bitcast.88, s32[]{:T(128)S(6)} %select_n.66, s32[]{:T(128)S(6)} %select_n.63, bf16[512,2,256]{2,1,0:T(2,128)(2,1)S(1)} %copy-done.4), kind=kOutput, calls=%fused_computation.15 | convolution fusion | flops 1073741824 | bytes 6815752 | tf_op jit(solution)/shard_map/tpk,pdk->td/dot_general | solution.py:59
  164.4 4.0 %collective-permute-done.1 = bf16[512,2,256]{2,0,1:T(8,128)(2,1)S(1)} collective-permute-done((bf16[512,2,256]{2,0,1:T(8,128)(2,1)S(1)}, bf16[512,2,256]{2,0,1:T(8,128)(2,1)S(1)}, u32[]{:S(2)}, u32[]{:S(2)}) %collective-permute-start.1) | collective-permute-done | bytes 524320 | tf_op jit(solution)/shard_map/ppermute | solution.py:54
  169.1 4.3 %fusion.2 = bf16[512,2048]{0,1:T(8,128)(2,1)} fusion(bf16[512,2,256]{2,0,1:T(8,128)(2,1)S(1)} %collective-permute-done.1, f32[2048,512,1]{1,0,2:T(8,128)S(1)} %fusion.3, bf16[2,2,2048,256]{3,2,0,1:T(8,128)(2,1)} %collective-permute-done, s32[]{:T(128)S(6)} %select_n.65), kind=kOutput, calls=%fused_computation.13 | convolution fusion | flops 1075838976 | bytes 8912900 | tf_op jit(solution)/shard_map/tpk,pdk->td/dot_general | solution.py:60
  174.8 5.0 %fusion.5 = f32[2048,512,1]{1,0,2:T(8,128)} fusion(bf16[2,2,2,2048,256]{4,3,2,1,0:T(8,128)(2,1)} %bitcast.89, s32[]{:T(128)S(6)} %select_n.60, s32[]{:T(128)S(6)} %select_n.63, bf16[512,2,256]{2,1,0:T(2,128)(2,1)S(1)} %copy-done.4), kind=kOutput, calls=%fused_computation.17 | convolution fusion | flops 1073741824 | bytes 6815752 | tf_op jit(solution)/shard_map/tpk,pdk->td/dot_general | solution.py:59
  179.8 2.8 %fusion.41 = f32[4,128,2048]{2,1,0:T(8,128)} fusion(bf16[4,128,128]{1,2,0:T(8,128)(2,1)S(1)} %multiply_convert_fusion.1, bf16[4,2048,128]{2,1,0:T(8,128)(2,1)S(1)} %copy-done.3), kind=kOutput, calls=%fused_computation.70 | convolution fusion | flops 268435456 | bytes 6422528 | tf_op jit(solution)/shard_map/bnc,bdc->bnd/dot_general | solution.py:115
  182.6 5.3 %copy.59 = f32[512,2048]{0,1:T(8,128)} copy(f32[512,2048]{1,0:T(8,128)} %bitcast.81) | data formatting | bytes 8388608 | tf_op jit(solution)/shard_map/reshape | solution.py:117
  187.9 33.4 %collective-permute-done.2 = bf16[512,2048]{0,1:T(8,128)(2,1)} collective-permute-done((bf16[512,2048]{0,1:T(8,128)(2,1)}, bf16[512,2048]{0,1:T(8,128)(2,1)}, u32[]{:S(2)}, u32[]{:S(2)}) %collective-permute-start.2) | collective-permute-done | bytes 2097184 | tf_op jit(solution)/shard_map/ppermute | solution.py:64
  221.4 8.1 %fusion.1 = f32[512,2048]{0,1:T(8,128)} fusion(f32[512,2048]{0,1:T(8,128)} %copy.59, f32[2048,512,1]{1,0,2:T(8,128)} %fusion.5, bf16[512,2048]{0,1:T(8,128)(2,1)} %collective-permute-done.2, bf16[512,2,256]{2,0,1:T(8,128)(2,1)S(1)} %collective-permute-done.1, bf16[2,2,2048,256]{3,2,0,1:T(8,128)(2,1)} %collective-permute-done, s32[]{:T(128)S(6)} %select_n.59), kind=kOutput, calls=%fused_computation.9 | convolution fusion | flops 1077936128 | bytes 17301508 | tf_op jit(solution)/shard_map/tpk,pdk->td/dot_general | solution.py:60
  229.5 5.3 %copy.55 = f32[512,2048]{1,0:T(8,128)} copy(f32[512,2048]{0,1:T(8,128)} %fusion.1) | data formatting | bytes 8388608
  234.8 25.5 %all-to-all-done = bf16[8,2304,128]{2,1,0:T(8,128)(2,1)} async-done(((bf16[8,2304,128]{2,1,0:T(8,128)(2,1)}), bf16[8,2304,128]{2,1,0:T(8,128)(2,1)}, u32[]{:S(2)}, u32[]{:S(2)}) %all-to-all-start) | async-done | bytes 4718624 | tf_op jit(solution)/shard_map/all_to_all | solution.py:148
  260.3 3.2 %convert_reduce_fusion = f32[2304,128]{1,0:T(8,128)S(1)} fusion(bf16[8,2304,128]{2,1,0:T(8,128)(2,1)} %all-to-all-done), kind=kLoop, calls=%fused_computation.4 | loop fusion | flops 4423680 | bytes 5898240 | tf_op jit(solution)/shard_map/reduce_sum | solution.py:155
  263.6 3.5 %fusion.17 = (f32[2048,128]{1,0:T(8,128)}, f32[2048,128]{1,0:T(8,128)}) fusion(f32[2048,128]{1,0:T(8,128)} %param.18, f32[2048,128]{1,0:T(8,128)} %param.17, f32[2304,128]{1,0:T(8,128)S(1)} %convert_reduce_fusion), kind=kLoop, calls=%fused_computation.33 | loop fusion | flops 2883584 | bytes 5242880 | tf_op jit(solution)/shard_map/div | solution.py:22
  (58 shorter events, 19.2 us)
Async XLA Ops:
  7.2 97.0 %copy-start = (bf16[512,2048]{1,0:T(8,128)(2,1)S(1)}, bf16[512,2048]{1,0:T(8,128)(2,1)}, u32[]{:S(2)}) copy-start(bf16[512,2048]{1,0:T(8,128)(2,1)} %param.12) | copy-start | bytes 6291460
  7.2 5.3 %copy-start.2 = (s32[8]{0:T(128)S(1)}, s32[8]{0:T(128)}, u32[]{:S(2)}) copy-start(s32[8]{0:T(128)} %param.22) | copy-start | bytes 100
  7.2 86.2 %all-gather.3.cloned.1.call-start = ((), (), s32[]{:S(2)}) async-start(), calls=%async_computation.1 | async-start | bytes 5308416 | tf_op jit(solution)/shard_map/all_gather | solution.py:91
  99.7 6.9 %copy-start.4 = (bf16[512,2,256]{2,1,0:T(2,128)(2,1)S(1)}, bf16[512,2,256]{2,1,0:T(2,128)(2,1)}, u32[]{:S(2)}) copy-start(bf16[512,2,256]{2,1,0:T(2,128)(2,1)} %param.13) | copy-start | bytes 1572868
  106.6 1.6 collective-permute-start.5
  107.0 2.9 %collective-permute-start.3 = (f32[4,128,128]{1,2,0:T(8,128)S(1)}, f32[4,128,128]{1,2,0:T(8,128)S(1)}, u32[]{:S(2)}, u32[]{:S(2)}) collective-permute-start(f32[4,128,128]{1,2,0:T(8,128)S(1)} %bitcast.90), channel_id=1, source_target_pairs={{0,1},{1,0},{2,3},{3,2},{4,5},{5,4},{6,7},{7,6},{8,9},{9,8},{10,11... | collective-permute-start | bytes 786440 | tf_op jit(solution)/shard_map/ppermute | solution.py:30
  108.2 9.2 %collective-permute-start.6 = (f32[4,128,128]{1,2,0:T(8,128)S(1)}, f32[4,128,128]{1,2,0:T(8,128)S(1)}, u32[]{:S(2)}, u32[]{:S(2)}) collective-permute-start(f32[4,128,128]{1,2,0:T(8,128)S(1)} %add.125), channel_id=1, source_target_pairs={{0,2},{1,3},{2,0},{3,1},{4,6},{5,7},{6,4},{7,5},{8,10},{9,11},{10,... | collective-permute-start | bytes 786440 | tf_op jit(solution)/shard_map/ppermute | solution.py:30
  109.9 12.4 %collective-permute-start.4 = (f32[4,128,128]{1,2,0:T(8,128)S(1)}, f32[4,128,128]{1,2,0:T(8,128)S(1)}, u32[]{:S(2)}, u32[]{:S(2)}) collective-permute-start(f32[4,128,128]{1,2,0:T(8,128)S(1)} %bitcast_add_fusion.3), channel_id=1, source_target_pairs={{0,2},{1,3},{2,0},{3,1},{4,6},{5,7},{6,4},{7,5},{8,10},{9,11},{10,... | collective-permute-start | bytes 786440 | tf_op jit(solution)/shard_map/ppermute | solution.py:30
  151.5 108.8 %all-to-all-start = ((bf16[8,2304,128]{2,1,0:T(8,128)(2,1)}), bf16[8,2304,128]{2,1,0:T(8,128)(2,1)}, u32[]{:S(2)}, u32[]{:S(2)}) async-start(bf16[8,2304,128]{2,1,0:T(8,128)(2,1)} %copy.54), calls=%async_computation | async-start | bytes 9437184 | tf_op jit(solution)/shard_map/all_to_all | solution.py:148
  160.9 8.3 %collective-permute-start = (bf16[2,2,2048,256]{3,2,0,1:T(8,128)(2,1)}, bf16[2,2,2048,256]{3,2,0,1:T(8,128)(2,1)}, u32[]{:S(2)}, u32[]{:S(2)}) collective-permute-start(bf16[2,2,2048,256]{3,2,0,1:T(8,128)(2,1)} %copy_bitcast_fusion), channel_id=1, source_target_pairs={{0,1},{1,0},{2,3},{3,2},{4,5},{5,4},{6,7},{7,6},{8,9},{9,8},{10,11... | collective-permute-start | bytes 12582920 | tf_op jit(solution)/shard_map/ppermute | solution.py:53
  160.9 7.5 %collective-permute-start.1 = (bf16[512,2,256]{2,0,1:T(8,128)(2,1)S(1)}, bf16[512,2,256]{2,0,1:T(8,128)(2,1)S(1)}, u32[]{:S(2)}, u32[]{:S(2)}) collective-permute-start(bf16[512,2,256]{2,0,1:T(8,128)(2,1)S(1)} %copy.42), channel_id=1, source_target_pairs={{0,1},{1,0},{2,3},{3,2},{4,5},{5,4},{6,7},{7,6},{8,9},{9,8},{10,11... | collective-permute-start | bytes 1572872 | tf_op jit(solution)/shard_map/ppermute | solution.py:54
  173.4 48.0 %collective-permute-start.2 = (bf16[512,2048]{0,1:T(8,128)(2,1)}, bf16[512,2048]{0,1:T(8,128)(2,1)}, u32[]{:S(2)}, u32[]{:S(2)}) collective-permute-start(bf16[512,2048]{0,1:T(8,128)(2,1)} %fusion.2), channel_id=1, source_target_pairs={{0,2},{1,3},{2,0},{3,1},{4,6},{5,7},{6,4},{7,5},{8,10},{9,11},{10,... | collective-permute-start | bytes 6291464 | tf_op jit(solution)/shard_map/ppermute | solution.py:64
  174.8 5.0 %copy-start.3 = (bf16[4,2048,128]{2,1,0:T(8,128)(2,1)S(1)}, bf16[4,2048,128]{2,1,0:T(8,128)(2,1)}, u32[]{:S(2)}) copy-start(bf16[4,2048,128]{2,1,0:T(8,128)(2,1)} %gather_fusion.3) | copy-start | bytes 6291460
  260.3 7.6 %copy-start.1 = (bf16[512,2048]{1,0:T(8,128)(2,1)S(1)}, bf16[512,2048]{1,0:T(8,128)(2,1)}, u32[]{:S(2)}) copy-start(bf16[512,2048]{1,0:T(8,128)(2,1)} %param.12) | copy-start | bytes 6291460
  263.6 4.3 %copy-start.5 = (f32[128,256]{1,0:T(8,128)}, f32[128,256]{1,0:T(8,128)S(1)}, u32[]{:S(2)}) copy-start(f32[128,256]{1,0:T(8,128)S(1)} %reshape.147) | copy-start | bytes 393220
  263.6 3.5 %copy-start.6 = (f32[128,256]{1,0:T(8,128)S(1)}, f32[128,256]{1,0:T(8,128)}, u32[]{:S(2)}) copy-start(f32[128,256]{1,0:T(8,128)} %param.20) | copy-start | bytes 393220
  263.6 3.5 %copy-start.7 = (f32[128,256]{1,0:T(8,128)S(1)}, f32[128,256]{1,0:T(8,128)}, u32[]{:S(2)}) copy-start(f32[128,256]{1,0:T(8,128)} %param.19) | copy-start | bytes 393220
Sparse Core Ops, SparseCore 0:
  10.8 82.5 all-gather.2

commit v4 on v3

--- a/solution.py
+++ b/solution.py
@@ -89,6 +89,8 @@
     b_as_a = b_master.astype(jnp.bfloat16).reshape(b_rows_own * kv_shard // rank_width, rank_width)
     packed = jnp.concatenate([a_master.astype(jnp.bfloat16), b_as_a], axis=0)
     packed_all = lax.all_gather(packed, "dp", axis=0, tiled=False)
+    frozen_gradient_share = frozen_gradient(grad_out, base_weight, feat_shard)
+    frozen_gradient_share, packed_all = lax.optimization_barrier((frozen_gradient_share, packed_all))
     a_all = packed_all[:, :a_rows_own].reshape(TENANTS, feat_shard, rank_width)
     b_all = packed_all[:, a_rows_own:].reshape(dp_size, b_rows_own, kv_shard).reshape(
         TENANTS, rank_width, kv_shard
@@ -106,12 +108,13 @@
     back_part = jnp.einsum(
         "bnpk,bprk->bnpr", dy_blocks, b_blocks, preferred_element_type=jnp.float32
     ).reshape(block_count, TENANT_BLOCK, rank_width)
-    mid_sum, backward_gradient_sum = tensor_sum((mid_part, back_part))
+    both_sum = tensor_sum((jnp.concatenate([mid_part, back_part], axis=2),))[0]
+    mid_sum = both_sum[:, :, :rank_width]
+    backward_gradient_sum = both_sum[:, :, rank_width:]
     middle_rank_rows = (mid_sum * column_rank_mask[:, None, :]).astype(jnp.bfloat16)
     backward_token_rows = (
         backward_gradient_sum * (column_rank_mask * adapter_scale_factor[:, None])[:, None, :]
     ).astype(jnp.bfloat16)
-    frozen_gradient_share = frozen_gradient(grad_out, base_weight, feat_shard)
     adapter_gradient_term = jnp.einsum(
         "bnc,bdc->bnd", backward_token_rows, a_blocks, preferred_element_type=jnp.float32
     ).reshape(tok_rows, feat_shard)

time: 275 us -> 281 us (1.022)
  other arithmetic: 23 us -> 30.7 us
  matrix products: 36.7 us -> 32.4 us
    all_gather x1, waiting for transfers between devices: 80.3 us -> 11.2 us  [local(): packed_all = lax.all_gather(packed, 'dp', axis=0, tiled=False)]
    all_to_all x1, waiting for transfers between devices: 25.5 us -> 83.8 us  [local(): lax.all_to_all(grad_pack.astype(jnp.bfloat16).reshape(dp_size, a_per + b_...]
    ppermute x1, waiting for transfers between devices: 33.4 us -> 42.6 us  [frozen_gradient(): far_in = lax.ppermute(far_part, 'tensor', row_pairs)]
    add x0 -> x1, other arithmetic: none -> 6.43 us  [local(): input_gradient_layer = frozen_gradient_share + adapter_gradient_term]
    ppermute x4 -> x2, waiting for transfers between devices: 11 us -> 14 us  [tensor_sum(): parts = tuple((p + lax.ppermute(p, 'tensor', pairs) for p in parts))]
    unnamed x18 -> x24, local copies, waits for them, and re-layouts: 5.46 us -> 6.27 us
  transfers between devices with their start and end apart: 9 -> 7, of which waited for: 8 -> 6; matrix products, arithmetic and copies ran while one was open for 16% -> 15% of each run, Pallas kernels for 0% -> 0%
where the time goes in v4:
time: 281 us; the launch traced here: 280 us
  waiting for transfers between devices  156 us (56%)
  local copies, waits for them, and re-layouts  37.2 us (13%)
  matrix products  32.4 us (12%)
  other arithmetic  30.7 us (11%)
  between operations  14.3 us (5%)
  starting transfers between devices  9.89 us (4%)
    all_to_all x1, waiting for transfers between devices, local(): lax.all_to_all(grad_pack.astype(jnp.bfloat16).reshape(dp_size, a_per + b_...  83.8 us
    ppermute x1, waiting for transfers between devices, frozen_gradient(): far_in = lax.ppermute(far_part, 'tensor', row_pairs)  42.6 us
    ppermute x2, waiting for transfers between devices, tensor_sum(): parts = tuple((p + lax.ppermute(p, 'tensor', pairs) for p in parts))  14 us
    concatenate x1, other arithmetic, local(): jnp.concatenate([a_flat.reshape(dp_size, a_per, rank_width), b_flat.resha...  11.2 us
    all_gather x1, waiting for transfers between devices, local(): packed_all = lax.all_gather(packed, 'dp', axis=0, tiled=False)  11.2 us
    dot_general x2, matrix products, chip_partial(): jnp.einsum('tpk,pdk->td', partner_dy, other, preferred_element_type=jnp.f...  9.89 us
    dot_general x1, matrix products, local(): jnp.einsum('sb,bdc->sdc', one_hot, a_terms, precision=lax.Precision.HIGHEST)  7.03 us
    add x1, other arithmetic, local(): input_gradient_layer = frozen_gradient_share + adapter_gradient_term  6.43 us
  transfers between devices with their start and end apart: 7, of which 6 were waited for; matrix products, arithmetic and copies ran while one was open for 15% of the time, Pallas kernels for 0%

profile of v4, /device:TPU:0, one launch (start us, length us, event | category | flops | bytes accessed | tf_op | source)
XLA Modules:
  0.0 279.9 jit_solution(4975846280051287860)
XLA Ops:
  10.5 4.5 %copy_bitcast_fusion = bf16[2,2,2048,256]{3,2,0,1:T(8,128)(2,1)} fusion(bf16[2,2,2,2048,256]{4,3,2,1,0:T(8,128)(2,1)} %bitcast.84, s32[]{:T(128)S(6)} %select_n.64), kind=kLoop, calls=%fused_computation.10 | loop fusion | bytes 8388612 | tf_op jit(solution)/shard_map/jit(dynamic_index_in_dim)/squeeze | solution.py:49
  16.4 2.9 %fusion.2 = f32[2048,512,1]{1,0,2:T(8,128)S(1)} fusion(bf16[2,2,2,2048,256]{4,3,2,1,0:T(8,128)(2,1)} %bitcast.85, s32[]{:T(128)S(6)} %select_n.66, s32[]{:T(128)S(6)} %select_n.63, bf16[512,2,256]{2,1,0:T(2,128)(2,1)S(1)} %copy-done.5), kind=kOutput, calls=%fused_computation.14 | convolution fusion | flops 1073741824 | bytes 6815752 | tf_op jit(solution)/shard_map/tpk,pdk->td/dot_general | solution.py:59
  19.3 3.9 %collective-permute-done.1 = bf16[512,2,256]{2,0,1:T(8,128)(2,1)S(1)} collective-permute-done((bf16[512,2,256]{2,0,1:T(8,128)(2,1)}, bf16[512,2,256]{2,0,1:T(8,128)(2,1)S(1)}, u32[]{:S(2)}, u32[]{:S(2)}) %collective-permute-start.1) | collective-permute-done | bytes 524320 | tf_op jit(solution)/shard_map/ppermute | solution.py:54
  23.2 4.2 %fusion.1 = bf16[512,2048]{0,1:T(8,128)(2,1)} fusion(bf16[512,2,256]{2,0,1:T(8,128)(2,1)S(1)} %collective-permute-done.1, f32[2048,512,1]{1,0,2:T(8,128)S(1)} %fusion.2, bf16[2,2,2048,256]{3,2,0,1:T(8,128)(2,1)} %collective-permute-done, s32[]{:T(128)S(6)} %select_n.65), kind=kOutput, calls=%fused_computation.12 | convolution fusion | flops 1075838976 | bytes 8912900 | tf_op jit(solution)/shard_map/tpk,pdk->td/dot_general | solution.py:60
  27.4 2.9 %collective-permute-start.2 = (bf16[512,2048]{0,1:T(8,128)(2,1)}, bf16[512,2048]{0,1:T(8,128)(2,1)}, u32[]{:S(2)}, u32[]{:S(2)}) collective-permute-start(bf16[512,2048]{0,1:T(8,128)(2,1)} %fusion.1), channel_id=1, source_target_pairs={{0,2},{1,3},{2,0},{3,1},{4,6},{5,7},{6,4},{7,5},{8,10},{9,11},{10,... | collective-permute-start | bytes 6291464 | tf_op jit(solution)/shard_map/ppermute | solution.py:64
  31.0 2.9 %fusion.4 = f32[2048,512,1]{1,0,2:T(8,128)S(1)} fusion(bf16[2,2,2,2048,256]{4,3,2,1,0:T(8,128)(2,1)} %bitcast.86, s32[]{:T(128)S(6)} %select_n.60, s32[]{:T(128)S(6)} %select_n.63, bf16[512,2,256]{2,1,0:T(2,128)(2,1)S(1)} %copy-done.5), kind=kOutput, calls=%fused_computation.16 | convolution fusion | flops 1073741824 | bytes 6815752 | tf_op jit(solution)/shard_map/tpk,pdk->td/dot_general | solution.py:59
  33.9 42.6 %collective-permute-done.2 = bf16[512,2048]{0,1:T(8,128)(2,1)} collective-permute-done((bf16[512,2048]{0,1:T(8,128)(2,1)}, bf16[512,2048]{0,1:T(8,128)(2,1)}, u32[]{:S(2)}, u32[]{:S(2)}) %collective-permute-start.2) | collective-permute-done | bytes 2097184 | tf_op jit(solution)/shard_map/ppermute | solution.py:64
  76.5 5.7 %bitcast_add_fusion.1 = f32[512,2048]{0,1:T(8,128)} fusion(f32[2048,512,1]{1,0,2:T(8,128)S(1)} %fusion.4, bf16[512,2048]{0,1:T(8,128)(2,1)} %collective-permute-done.2, bf16[512,2,256]{2,0,1:T(8,128)(2,1)S(1)} %collective-permute-done.1, bf16[2,2,2048,256]{3,2,0,1:T(8,128)(2,1)} %collective-permute-done, s32[]{:T(128)S(6)} %select_n.59), kind=kOutput, calls=%fused_computation.8 | convolution fusion | flops 1076887552 | bytes 13107204 | tf_op jit(solution)/shard_map/tpk,pdk->td/dot_general | solution.py:60
  82.2 11.2 %all-gather.3.cloned.1.call-done = bf16[18432,128]{1,0:T(8,128)(2,1)} async-done(((bf16[2304,128]{1,0:T(8,128)(2,1)}), bf16[18432,128]{1,0:T(8,128)(2,1)}) %all-gather.3.cloned.1.call-update) | async-done | bytes 4718608 | tf_op jit(solution)/shard_map/all_gather | solution.py:91
  93.4 4.5 %slice.18 = bf16[8,2048,128]{2,1,0:T(8,128)(2,1)} slice(bf16[8,2304,128]{2,1,0:T(8,128)(2,1)} %bitcast.77), slice={[0:8], [0:2048], [0:128]} | slice | bytes 8388608 | tf_op jit(solution)/shard_map/slice | solution.py:94
  99.9 4.4 %gather_fusion.1 = bf16[4,2048,128]{2,1,0:T(8,128)(2,1)} fusion(bf16[8,2048,128]{2,1,0:T(8,128)(2,1)} %slice.18, s32[1024]{0:T(1024)S(1)} %pad_clamp_fusion), kind=kCustom, calls=%fused_computation.1 | custom fusion | bytes 4194320 | tf_op jit(solution)/shard_map/gather | solution.py:103
  113.5 12.4 %collective-permute-done.4 = f32[4,128,256]{1,2,0:T(8,128)S(1)} collective-permute-done((f32[4,128,256]{1,2,0:T(8,128)S(1)}, f32[4,128,256]{1,2,0:T(8,128)S(1)}, u32[]{:S(2)}, u32[]{:S(2)}) %collective-permute-start.4) | collective-permute-done | bytes 524320 | tf_op jit(solution)/shard_map/ppermute | solution.py:30
  128.7 5.3 %copy.49 = f32[4,2048,128]{2,0,1:T(4,128)} copy(f32[4,2048,128]{1,2,0:T(8,128)} %convolution_bitcast_fusion) | data formatting | bytes 8388608 | tf_op jit(solution)/shard_map/bnd,bnc->bdc/dot_general | solution.py:122
  134.0 7.0 %convolution_convert_fusion = bf16[8,2048,128]{2,0,1:T(8,128)(2,1)S(1)} fusion(f32[4,2048,128]{2,0,1:T(4,128)} %copy.49, s32[4]{0:T(128)S(1)} %gather_fusion), kind=kOutput, calls=%fused_computation.13 | convolution fusion | flops 102760480 | bytes 8388624 | tf_op jit(solution)/shard_map/sb,bdc->sdc/dot_general | solution.py:135
  142.4 11.2 %pad_maximum_fusion = bf16[8,2304,128]{2,0,1:T(8,128)(2,1)S(1)} fusion(bf16[8,256,128]{2,0,1:T(8,128)(2,1)S(1)} %bitcast.83, bf16[8,2048,128]{2,0,1:T(8,128)(2,1)S(1)} %convolution_convert_fusion), kind=kLoop, calls=%fused_computation.5 | loop fusion | flops 2359296 | bytes 9437184 | tf_op jit(solution)/shard_map/concatenate | solution.py:144
  153.6 2.9 %copy.52 = bf16[8,2304,128]{2,1,0:T(8,128)(2,1)} copy(bf16[8,2304,128]{2,0,1:T(8,128)(2,1)S(1)} %pad_maximum_fusion) | data formatting | bytes 9437184 | tf_op jit(solution)/shard_map/concatenate | solution.py:144
  156.6 5.0 %all-to-all-start = ((bf16[8,2304,128]{2,1,0:T(8,128)(2,1)}), bf16[8,2304,128]{2,1,0:T(8,128)(2,1)}, u32[]{:S(2)}, u32[]{:S(2)}) async-start(bf16[8,2304,128]{2,1,0:T(8,128)(2,1)} %copy.52), calls=%async_computation | async-start | bytes 9437184 | tf_op jit(solution)/shard_map/all_to_all | solution.py:151
  161.5 3.0 %fusion.29 = f32[4,128,2048]{2,1,0:T(8,128)} fusion(bf16[4,2048,128]{2,1,0:T(8,128)(2,1)S(1)} %copy-done.4, f32[4,128,256]{1,2,0:T(8,128)S(1)} %add.116, f32[4,128]{1,0:T(4,128)S(1)} %compare_select_fusion.2), kind=kOutput, calls=%fused_computation.49 | convolution fusion | flops 268566528 | bytes 6555648 | tf_op jit(solution)/shard_map/bnc,bdc->bnd/dot_general | solution.py:118
  164.6 5.3 %copy.57 = f32[512,2048]{0,1:T(8,128)} copy(f32[512,2048]{1,0:T(8,128)} %bitcast.76) | data formatting | bytes 8388608 | tf_op jit(solution)/shard_map/reshape | solution.py:120
  169.9 6.4 %add.118 = f32[512,2048]{0,1:T(8,128)} add(f32[512,2048]{0,1:T(8,128)} %bitcast_add_fusion.1, f32[512,2048]{0,1:T(8,128)} %copy.57) | non-fusion elementwise | flops 1048576 | bytes 12582912 | tf_op jit(solution)/shard_map/add | solution.py:121
  176.3 5.3 %copy.53 = f32[512,2048]{1,0:T(8,128)} copy(f32[512,2048]{0,1:T(8,128)} %add.118) | data formatting | bytes 8388608
  181.7 83.8 %all-to-all-done = bf16[8,2304,128]{2,1,0:T(8,128)(2,1)} async-done(((bf16[8,2304,128]{2,1,0:T(8,128)(2,1)}), bf16[8,2304,128]{2,1,0:T(8,128)(2,1)}, u32[]{:S(2)}, u32[]{:S(2)}) %all-to-all-start) | async-done | bytes 4718624 | tf_op jit(solution)/shard_map/all_to_all | solution.py:151
  265.5 3.2 %convert_reduce_fusion = f32[2304,128]{1,0:T(8,128)S(1)} fusion(bf16[8,2304,128]{2,1,0:T(8,128)(2,1)} %all-to-all-done), kind=kLoop, calls=%fused_computation.4 | loop fusion | flops 4423680 | bytes 5898240 | tf_op jit(solution)/shard_map/reduce_sum | solution.py:158
  268.8 3.5 %fusion.16 = (f32[2048,128]{1,0:T(8,128)}, f32[2048,128]{1,0:T(8,128)}) fusion(f32[2048,128]{1,0:T(8,128)} %param.18, f32[2048,128]{1,0:T(8,128)} %param.17, f32[2304,128]{1,0:T(8,128)S(1)} %convert_reduce_fusion), kind=kLoop, calls=%fused_computation.32 | loop fusion | flops 2883584 | bytes 5242880 | tf_op jit(solution)/shard_map/div | solution.py:22
  (61 shorter events, 21.6 us)
Async XLA Ops:
  7.2 97.7 %copy-start = (bf16[512,2048]{1,0:T(8,128)(2,1)S(1)}, bf16[512,2048]{1,0:T(8,128)(2,1)}, u32[]{:S(2)}) copy-start(bf16[512,2048]{1,0:T(8,128)(2,1)} %param.12) | copy-start | bytes 6291460
  7.2 86.2 %all-gather.3.cloned.1.call-start = ((), (), s32[]{:S(2)}) async-start(), calls=%async_computation.1 | async-start | bytes 5308416 | tf_op jit(solution)/shard_map/all_gather | solution.py:91
  10.5 5.0 %copy-start.5 = (bf16[512,2,256]{2,1,0:T(2,128)(2,1)S(1)}, bf16[512,2,256]{2,1,0:T(2,128)(2,1)}, u32[]{:S(2)}) copy-start(bf16[512,2,256]{2,1,0:T(2,128)(2,1)} %param.13) | copy-start | bytes 1572868
  15.0 8.2 %collective-permute-start = (bf16[2,2,2048,256]{3,2,0,1:T(8,128)(2,1)}, bf16[2,2,2048,256]{3,2,0,1:T(8,128)(2,1)}, u32[]{:S(2)}, u32[]{:S(2)}) collective-permute-start(bf16[2,2,2048,256]{3,2,0,1:T(8,128)(2,1)} %copy_bitcast_fusion), channel_id=1, source_target_pairs={{0,1},{1,0},{2,3},{3,2},{4,5},{5,4},{6,7},{7,6},{8,9},{9,8},{10,11... | collective-permute-start | bytes 12582920 | tf_op jit(solution)/shard_map/ppermute | solution.py:53
  16.4 6.9 %collective-permute-start.1 = (bf16[512,2,256]{2,0,1:T(8,128)(2,1)}, bf16[512,2,256]{2,0,1:T(8,128)(2,1)S(1)}, u32[]{:S(2)}, u32[]{:S(2)}) collective-permute-start(bf16[512,2,256]{2,0,1:T(8,128)(2,1)} %copy.40), channel_id=1, source_target_pairs={{0,1},{1,0},{2,3},{3,2},{4,5},{5,4},{6,7},{7,6},{8,9},{9,8},{10,11... | collective-permute-start | bytes 1572872 | tf_op jit(solution)/shard_map/ppermute | solution.py:54
  19.3 11.0 %copy-start.10 = (s32[4]{0:T(128)S(1)}, s32[4]{0:T(128)}, u32[]{:S(2)}) copy-start(s32[4]{0:T(128)} %param.21) | copy-start | bytes 52
  19.3 11.0 %copy-start.2 = (s32[8]{0:T(128)S(1)}, s32[8]{0:T(128)}, u32[]{:S(2)}) copy-start(s32[8]{0:T(128)} %param.23) | copy-start | bytes 100
  27.4 49.1 %collective-permute-start.2 = (bf16[512,2048]{0,1:T(8,128)(2,1)}, bf16[512,2048]{0,1:T(8,128)(2,1)}, u32[]{:S(2)}, u32[]{:S(2)}) collective-permute-start(bf16[512,2048]{0,1:T(8,128)(2,1)} %fusion.1), channel_id=1, source_target_pairs={{0,2},{1,3},{2,0},{3,1},{4,6},{5,7},{6,4},{7,5},{8,10},{9,11},{10,... | collective-permute-start | bytes 6291464 | tf_op jit(solution)/shard_map/ppermute | solution.py:64
  99.9 4.4 %copy-start.6 = (bf16[8,128,256]{2,1,0:T(8,128)(2,1)S(1)}, bf16[8,128,256]{2,1,0:T(8,128)(2,1)}, u32[]{:S(2)}) copy-start(bf16[8,128,256]{2,1,0:T(8,128)(2,1)} %reshape.141) | copy-start | bytes 1572868
  104.3 4.2 %copy-start.3 = (s32[8]{0:T(128)S(1)}, s32[8]{0:T(128)}, u32[]{:S(2)}) copy-start(s32[8]{0:T(128)} %param.22) | copy-start | bytes 100
  108.5 2.3 collective-permute-start.3
  111.9 14.0 %collective-permute-start.4 = (f32[4,128,256]{1,2,0:T(8,128)S(1)}, f32[4,128,256]{1,2,0:T(8,128)S(1)}, u32[]{:S(2)}, u32[]{:S(2)}) collective-permute-start(f32[4,128,256]{1,2,0:T(8,128)S(1)} %fusion.43), channel_id=1, source_target_pairs={{0,2},{1,3},{2,0},{3,1},{4,6},{5,7},{6,4},{7,5},{8,10},{9,11},{10,... | collective-permute-start | bytes 1572872 | tf_op jit(solution)/shard_map/ppermute | solution.py:30
  156.6 5.0 %copy-start.4 = (bf16[4,2048,128]{2,1,0:T(8,128)(2,1)S(1)}, bf16[4,2048,128]{2,1,0:T(8,128)(2,1)}, u32[]{:S(2)}) copy-start(bf16[4,2048,128]{2,1,0:T(8,128)(2,1)} %gather_fusion.1) | copy-start | bytes 6291460
  156.6 108.9 %all-to-all-start = ((bf16[8,2304,128]{2,1,0:T(8,128)(2,1)}), bf16[8,2304,128]{2,1,0:T(8,128)(2,1)}, u32[]{:S(2)}, u32[]{:S(2)}) async-start(bf16[8,2304,128]{2,1,0:T(8,128)(2,1)} %copy.52), calls=%async_computation | async-start | bytes 9437184 | tf_op jit(solution)/shard_map/all_to_all | solution.py:151
  265.5 7.6 %copy-start.1 = (bf16[512,2048]{1,0:T(8,128)(2,1)S(1)}, bf16[512,2048]{1,0:T(8,128)(2,1)}, u32[]{:S(2)}) copy-start(bf16[512,2048]{1,0:T(8,128)(2,1)} %param.12) | copy-start | bytes 6291460
  268.8 4.3 %copy-start.7 = (f32[128,256]{1,0:T(8,128)}, f32[128,256]{1,0:T(8,128)S(1)}, u32[]{:S(2)}) copy-start(f32[128,256]{1,0:T(8,128)S(1)} %reshape.147) | copy-start | bytes 393220
  268.8 3.5 %copy-start.8 = (f32[128,256]{1,0:T(8,128)S(1)}, f32[128,256]{1,0:T(8,128)}, u32[]{:S(2)}) copy-start(f32[128,256]{1,0:T(8,128)} %param.20) | copy-start | bytes 393220
  268.8 3.5 %copy-start.9 = (f32[128,256]{1,0:T(8,128)S(1)}, f32[128,256]{1,0:T(8,128)}, u32[]{:S(2)}) copy-start(f32[128,256]{1,0:T(8,128)} %param.19) | copy-start | bytes 393220
Sparse Core Ops, SparseCore 0:
  10.8 82.5 all-gather.2

commit v5 on v4

--- a/solution.py
+++ b/solution.py
@@ -141,21 +141,29 @@
     a_per = a_flat.shape[0] // dp_size
     b_per = b_flat.shape[0] // dp_size
     b_wide = b_per * kv_shard // rank_width
+    rows = a_per + b_wide
     grad_pack = jnp.concatenate(
         [
             a_flat.reshape(dp_size, a_per, rank_width),
             b_flat.reshape(dp_size, b_wide, rank_width),
         ],
         axis=1,
-    ).reshape(dp_size * (a_per + b_wide), rank_width)
-    grad_parts = lax.all_to_all(
-        grad_pack.astype(jnp.bfloat16).reshape(dp_size, a_per + b_wide, rank_width),
+    )
+    sc_rows = (rows * 2 // 5) // 8 * 8
+    sc_own = lax.psum_scatter(
+        grad_pack[:, :sc_rows].reshape(dp_size * sc_rows, rank_width),
+        "dp",
+        scatter_dimension=0,
+        tiled=True,
+    )
+    tc_parts = lax.all_to_all(
+        grad_pack[:, sc_rows:].astype(jnp.bfloat16),
         "dp",
         split_axis=0,
         concat_axis=0,
         tiled=True,
     )
-    grad_own = jnp.sum(grad_parts.astype(jnp.float32), axis=0)
+    grad_own = jnp.concatenate([sc_own, jnp.sum(tc_parts.astype(jnp.float32), axis=0)], axis=0)
     a_grad = grad_own[:a_per]
     b_grad = grad_own[a_per:].reshape(b_per, kv_shard)
     return (

time: 281 us -> 287 us (1.021)
  waiting for transfers between devices: 156 us -> 164 us
  other arithmetic: 30.7 us -> 25.5 us
    unnamed x1 -> x3, waiting for transfers between devices: 0.02 us -> 27.2 us
    all_to_all x1, waiting for transfers between devices: 83.8 us -> 64.8 us  [local(): lax.all_to_all(grad_pack[:, sc_rows:].astype(jnp.bfloat16), 'dp', split_a...]
    slice x0 -> x3, local copies, waits for them, and re-layouts: none -> 4.64 us  [the longest x2 2.74 us: local(): grad_pack[:, :sc_rows].reshape(dp_size * sc_rows, rank_width)]
    concatenate x1, other arithmetic: 11.2 us -> 6.92 us  [local(): jnp.concatenate([a_flat.reshape(dp_size, a_per, rank_width), b_flat.resha...]
    concatenate x1 -> x0, local copies, waits for them, and re-layouts: 2.94 us -> none  [local(): jnp.concatenate([a_flat.reshape(dp_size, a_per, rank_width), b_flat.resha...]
  transfers between devices with their start and end apart: 7 -> 8, of which waited for: 6 -> 7; matrix products, arithmetic and copies ran while one was open for 15% -> 20% of each run, Pallas kernels for 0% -> 0%
where the time goes in v5:
time: 287 us; the launch traced here: 286 us
  waiting for transfers between devices  164 us (57%)
  local copies, waits for them, and re-layouts  39.2 us (14%)
  matrix products  33.7 us (12%)
  other arithmetic  25.5 us (9%)
  between operations  14.3 us (5%)
  starting transfers between devices  9.77 us (3%)
    all_to_all x1, waiting for transfers between devices, local(): lax.all_to_all(grad_pack[:, sc_rows:].astype(jnp.bfloat16), 'dp', split_a...  64.8 us
    ppermute x1, waiting for transfers between devices, frozen_gradient(): far_in = lax.ppermute(far_part, 'tensor', row_pairs)  42.6 us
    unnamed x3, waiting for transfers between devices  27.2 us
    ppermute x2, waiting for transfers between devices, tensor_sum(): parts = tuple((p + lax.ppermute(p, 'tensor', pairs) for p in parts))  14 us
    all_gather x1, waiting for transfers between devices, local(): packed_all = lax.all_gather(packed, 'dp', axis=0, tiled=False)  11.1 us
    dot_general x2, matrix products, chip_partial(): jnp.einsum('tpk,pdk->td', partner_dy, other, preferred_element_type=jnp.f...  9.89 us
    dot_general x1, matrix products, local(): jnp.einsum('sb,bdc->sdc', one_hot, a_terms, precision=lax.Precision.HIGHEST)  8.45 us
    concatenate x1, other arithmetic, local(): jnp.concatenate([a_flat.reshape(dp_size, a_per, rank_width), b_flat.resha...  6.92 us
  transfers between devices with their start and end apart: 8, of which 7 were waited for; matrix products, arithmetic and copies ran while one was open for 20% of the time, Pallas kernels for 0%

profile of v5, /device:TPU:0, one launch (start us, length us, event | category | flops | bytes accessed | tf_op | source)
XLA Modules:
  0.0 286.1 jit_solution(2693082093097554631)
XLA Ops:
  10.6 4.5 %copy_bitcast_fusion = bf16[2,2,2048,256]{3,2,0,1:T(8,128)(2,1)} fusion(bf16[2,2,2,2048,256]{4,3,2,1,0:T(8,128)(2,1)} %bitcast.89, s32[]{:T(128)S(6)} %select_n.64), kind=kLoop, calls=%fused_computation.9 | loop fusion | bytes 8388612 | tf_op jit(solution)/shard_map/jit(dynamic_index_in_dim)/squeeze | solution.py:49
  16.5 2.9 %fusion.2 = f32[2048,512,1]{1,0,2:T(8,128)S(1)} fusion(bf16[2,2,2,2048,256]{4,3,2,1,0:T(8,128)(2,1)} %bitcast.90, s32[]{:T(128)S(6)} %select_n.66, s32[]{:T(128)S(6)} %select_n.63, bf16[512,2,256]{2,1,0:T(2,128)(2,1)S(1)} %copy-done.5), kind=kOutput, calls=%fused_computation.13 | convolution fusion | flops 1073741824 | bytes 6815752 | tf_op jit(solution)/shard_map/tpk,pdk->td/dot_general | solution.py:59
  19.4 3.9 %collective-permute-done.1 = bf16[512,2,256]{2,0,1:T(8,128)(2,1)S(1)} collective-permute-done((bf16[512,2,256]{2,0,1:T(8,128)(2,1)}, bf16[512,2,256]{2,0,1:T(8,128)(2,1)S(1)}, u32[]{:S(2)}, u32[]{:S(2)}) %collective-permute-start.1) | collective-permute-done | bytes 524320 | tf_op jit(solution)/shard_map/ppermute | solution.py:54
  23.3 4.2 %fusion.1 = bf16[512,2048]{0,1:T(8,128)(2,1)} fusion(bf16[512,2,256]{2,0,1:T(8,128)(2,1)S(1)} %collective-permute-done.1, f32[2048,512,1]{1,0,2:T(8,128)S(1)} %fusion.2, bf16[2,2,2048,256]{3,2,0,1:T(8,128)(2,1)} %collective-permute-done, s32[]{:T(128)S(6)} %select_n.65), kind=kOutput, calls=%fused_computation.12 | convolution fusion | flops 1075838976 | bytes 8912900 | tf_op jit(solution)/shard_map/tpk,pdk->td/dot_general | solution.py:60
  27.5 2.9 collective-permute-start.2
  31.0 2.9 %fusion.4 = f32[2048,512,1]{1,0,2:T(8,128)S(1)} fusion(bf16[2,2,2,2048,256]{4,3,2,1,0:T(8,128)(2,1)} %bitcast.91, s32[]{:T(128)S(6)} %select_n.60, s32[]{:T(128)S(6)} %select_n.63, bf16[512,2,256]{2,1,0:T(2,128)(2,1)S(1)} %copy-done.5), kind=kOutput, calls=%fused_computation.15 | convolution fusion | flops 1073741824 | bytes 6815752 | tf_op jit(solution)/shard_map/tpk,pdk->td/dot_general | solution.py:59
  34.0 42.6 %collective-permute-done.2 = bf16[512,2048]{0,1:T(8,128)(2,1)} collective-permute-done((bf16[512,2048]{0,1:T(8,128)(2,1)}, bf16[512,2048]{0,1:T(8,128)(2,1)}, u32[]{:S(2)}, u32[]{:S(2)}) %collective-permute-start.2) | collective-permute-done | bytes 2097184 | tf_op jit(solution)/shard_map/ppermute | solution.py:64
  76.6 5.7 %bitcast_add_fusion.1 = f32[512,2048]{0,1:T(8,128)} fusion(f32[2048,512,1]{1,0,2:T(8,128)S(1)} %fusion.4, bf16[512,2048]{0,1:T(8,128)(2,1)} %collective-permute-done.2, bf16[512,2,256]{2,0,1:T(8,128)(2,1)S(1)} %collective-permute-done.1, bf16[2,2,2048,256]{3,2,0,1:T(8,128)(2,1)} %collective-permute-done, s32[]{:T(128)S(6)} %select_n.59), kind=kOutput, calls=%fused_computation.7 | convolution fusion | flops 1076887552 | bytes 13107204 | tf_op jit(solution)/shard_map/tpk,pdk->td/dot_general | solution.py:60
  82.3 11.1 %all-gather.3.cloned.1.call-done = bf16[18432,128]{1,0:T(8,128)(2,1)} async-done(((bf16[2304,128]{1,0:T(8,128)(2,1)}), bf16[18432,128]{1,0:T(8,128)(2,1)}) %all-gather.3.cloned.1.call-update) | async-done | bytes 4718608 | tf_op jit(solution)/shard_map/all_gather | solution.py:91
  93.4 4.5 %slice.25 = bf16[8,2048,128]{2,1,0:T(8,128)(2,1)} slice(bf16[8,2304,128]{2,1,0:T(8,128)(2,1)} %bitcast.82), slice={[0:8], [0:2048], [0:128]} | slice | bytes 8388608 | tf_op jit(solution)/shard_map/slice | solution.py:94
  100.0 4.4 %gather_fusion.1 = bf16[4,2048,128]{2,1,0:T(8,128)(2,1)} fusion(bf16[8,2048,128]{2,1,0:T(8,128)(2,1)} %slice.25, s32[1024]{0:T(1024)S(1)} %pad_clamp_fusion), kind=kCustom, calls=%fused_computation.1 | custom fusion | bytes 4194320 | tf_op jit(solution)/shard_map/gather | solution.py:103
  113.5 12.4 %collective-permute-done.4 = f32[4,128,256]{1,2,0:T(8,128)S(1)} collective-permute-done((f32[4,128,256]{1,2,0:T(8,128)S(1)}, f32[4,128,256]{1,2,0:T(8,128)S(1)}, u32[]{:S(2)}, u32[]{:S(2)}) %collective-permute-start.4) | collective-permute-done | bytes 524320 | tf_op jit(solution)/shard_map/ppermute | solution.py:30
  126.0 2.7 convolution_bitcast_fusion
  128.7 5.3 %copy.50 = f32[4,2048,128]{2,0,1:T(4,128)} copy(f32[4,2048,128]{1,2,0:T(8,128)} %convolution_bitcast_fusion) | data formatting | bytes 8388608 | tf_op jit(solution)/shard_map/bnd,bnc->bdc/dot_general | solution.py:122
  134.0 8.5 %fusion.47 = (bf16[8,2048,128]{2,0,1:T(8,128)(2,1)}, f32[8,2048,128]{2,0,1:T(8,128)S(1)}) fusion(f32[4,2048,128]{2,0,1:T(4,128)} %copy.50, s32[4]{0:T(128)S(1)} %gather_fusion), kind=kOutput, calls=%fused_computation.74 | convolution fusion | flops 102760480 | bytes 16777232 | tf_op jit(solution)/shard_map/sb,bdc->sdc/dot_general | solution.py:135
  146.7 6.9 %pad_maximum_fusion = bf16[8,1384,128]{2,0,1:T(8,128)(2,1)S(1)} fusion(bf16[8,256,128]{2,0,1:T(8,128)(2,1)S(1)} %bitcast.88, bf16[8,2048,128]{2,0,1:T(8,128)(2,1)} %get-tuple-element.26), kind=kLoop, calls=%fused_computation.11 | loop fusion | flops 1417216 | bytes 7553024 | tf_op jit(solution)/shard_map/concatenate | solution.py:145
  155.5 4.8 %all-to-all-start = ((bf16[8,1384,128]{2,1,0:T(8,128)(2,1)}), bf16[8,1384,128]{2,1,0:T(8,128)(2,1)}, u32[]{:S(2)}, u32[]{:S(2)}) async-start(bf16[8,1384,128]{2,1,0:T(8,128)(2,1)} %copy.54), calls=%async_computation | async-start | bytes 5668864 | tf_op jit(solution)/shard_map/all_to_all | solution.py:159
  160.3 2.9 fusion.29
  163.1 5.4 %copy.59 = f32[512,2048]{0,1:T(8,128)} copy(f32[512,2048]{1,0:T(8,128)} %bitcast.80) | data formatting | bytes 8388608 | tf_op jit(solution)/shard_map/reshape | solution.py:120
  168.6 6.5 %add.120 = f32[512,2048]{0,1:T(8,128)} add(f32[512,2048]{0,1:T(8,128)} %bitcast_add_fusion.1, f32[512,2048]{0,1:T(8,128)} %copy.59) | non-fusion elementwise | flops 1048576 | bytes 12582912 | tf_op jit(solution)/shard_map/add | solution.py:121
  175.1 5.5 %copy.55 = f32[512,2048]{1,0:T(8,128)} copy(f32[512,2048]{0,1:T(8,128)} %add.120) | data formatting | bytes 8388608
  180.6 64.8 %all-to-all-done = bf16[8,1384,128]{2,1,0:T(8,128)(2,1)} async-done(((bf16[8,1384,128]{2,1,0:T(8,128)(2,1)}), bf16[8,1384,128]{2,1,0:T(8,128)(2,1)}, u32[]{:S(2)}, u32[]{:S(2)}) %all-to-all-start) | async-done | bytes 2834464 | tf_op jit(solution)/shard_map/all_to_all | solution.py:159
  248.5 27.2 %reduce-scatter.4.cloned.1.call-done = f32[920,128]{1,0:T(8,128)} async-done(((f32[7360,128]{1,0:T(8,128)}), f32[920,128]{1,0:T(8,128)}) %reduce-scatter.4.cloned.1.call-update) | async-done | bytes 471056
  275.7 3.5 %fusion.16 = (f32[2048,128]{1,0:T(8,128)}, f32[2048,128]{1,0:T(8,128)}) fusion(f32[2048,128]{1,0:T(8,128)} %param.18, f32[2048,128]{1,0:T(8,128)} %param.17, f32[1384,128]{1,0:T(8,128)S(1)} %convert_reduce_fusion, f32[920,128]{1,0:T(8,128)} %reduce-scatter.4.cloned.1.call-done), kind=kLoop, calls=%fused_computation.31 | loop fusion | flops 3145728 | bytes 5373952 | tf_op jit(solution)/shard_map/div | solution.py:22
  (66 shorter events, 25.8 us)
Async XLA Ops:
  7.2 98.0 %copy-start = (bf16[512,2048]{1,0:T(8,128)(2,1)S(1)}, bf16[512,2048]{1,0:T(8,128)(2,1)}, u32[]{:S(2)}) copy-start(bf16[512,2048]{1,0:T(8,128)(2,1)} %param.12) | copy-start | bytes 6291460
  7.2 86.2 %all-gather.3.cloned.1.call-start = ((), (), s32[]{:S(2)}) async-start(), calls=%async_computation.2 | async-start | bytes 5308416 | tf_op jit(solution)/shard_map/all_gather | solution.py:91
  10.5 265.2 %reduce-scatter.4.cloned.1.call-start = ((), (), s32[]{:S(2)}) async-start(), calls=%async_computation.3 | async-start | bytes 4239360
  10.5 5.0 %copy-start.5 = (bf16[512,2,256]{2,1,0:T(2,128)(2,1)S(1)}, bf16[512,2,256]{2,1,0:T(2,128)(2,1)}, u32[]{:S(2)}) copy-start(bf16[512,2,256]{2,1,0:T(2,128)(2,1)} %param.13) | copy-start | bytes 1572868
  15.1 8.2 %collective-permute-start = (bf16[2,2,2048,256]{3,2,0,1:T(8,128)(2,1)}, bf16[2,2,2048,256]{3,2,0,1:T(8,128)(2,1)}, u32[]{:S(2)}, u32[]{:S(2)}) collective-permute-start(bf16[2,2,2048,256]{3,2,0,1:T(8,128)(2,1)} %copy_bitcast_fusion), channel_id=1, source_target_pairs={{0,1},{1,0},{2,3},{3,2},{4,5},{5,4},{6,7},{7,6},{8,9},{9,8},{10,11... | collective-permute-start | bytes 12582920 | tf_op jit(solution)/shard_map/ppermute | solution.py:53
  16.4 6.9 %collective-permute-start.1 = (bf16[512,2,256]{2,0,1:T(8,128)(2,1)}, bf16[512,2,256]{2,0,1:T(8,128)(2,1)S(1)}, u32[]{:S(2)}, u32[]{:S(2)}) collective-permute-start(bf16[512,2,256]{2,0,1:T(8,128)(2,1)} %copy.41), channel_id=1, source_target_pairs={{0,1},{1,0},{2,3},{3,2},{4,5},{5,4},{6,7},{7,6},{8,9},{9,8},{10,11... | collective-permute-start | bytes 1572872 | tf_op jit(solution)/shard_map/ppermute | solution.py:54
  19.3 11.0 %copy-start.10 = (s32[4]{0:T(128)S(1)}, s32[4]{0:T(128)}, u32[]{:S(2)}) copy-start(s32[4]{0:T(128)} %param.21) | copy-start | bytes 52
  19.4 11.0 %copy-start.2 = (s32[8]{0:T(128)S(1)}, s32[8]{0:T(128)}, u32[]{:S(2)}) copy-start(s32[8]{0:T(128)} %param.23) | copy-start | bytes 100
  27.5 49.1 %collective-permute-start.2 = (bf16[512,2048]{0,1:T(8,128)(2,1)}, bf16[512,2048]{0,1:T(8,128)(2,1)}, u32[]{:S(2)}, u32[]{:S(2)}) collective-permute-start(bf16[512,2048]{0,1:T(8,128)(2,1)} %fusion.1), channel_id=1, source_target_pairs={{0,2},{1,3},{2,0},{3,1},{4,6},{5,7},{6,4},{7,5},{8,10},{9,11},{10,... | collective-permute-start | bytes 6291464 | tf_op jit(solution)/shard_map/ppermute | solution.py:64
  100.0 4.4 %copy-start.6 = (bf16[8,128,256]{2,1,0:T(8,128)(2,1)S(1)}, bf16[8,128,256]{2,1,0:T(8,128)(2,1)}, u32[]{:S(2)}) copy-start(bf16[8,128,256]{2,1,0:T(8,128)(2,1)} %reshape.142) | copy-start | bytes 1572868
  104.3 4.2 %copy-start.3 = (s32[8]{0:T(128)S(1)}, s32[8]{0:T(128)}, u32[]{:S(2)}) copy-start(s32[8]{0:T(128)} %param.22) | copy-start | bytes 100
  108.5 2.3 collective-permute-start.3
  111.8 14.0 %collective-permute-start.4 = (f32[4,128,256]{1,2,0:T(8,128)S(1)}, f32[4,128,256]{1,2,0:T(8,128)S(1)}, u32[]{:S(2)}, u32[]{:S(2)}) collective-permute-start(f32[4,128,256]{1,2,0:T(8,128)S(1)} %fusion.44), channel_id=1, source_target_pairs={{0,2},{1,3},{2,0},{3,1},{4,6},{5,7},{6,4},{7,5},{8,10},{9,11},{10,... | collective-permute-start | bytes 1572872 | tf_op jit(solution)/shard_map/ppermute | solution.py:30
  155.5 4.8 %copy-start.4 = (bf16[4,2048,128]{2,1,0:T(8,128)(2,1)S(1)}, bf16[4,2048,128]{2,1,0:T(8,128)(2,1)}, u32[]{:S(2)}) copy-start(bf16[4,2048,128]{2,1,0:T(8,128)(2,1)} %gather_fusion.1) | copy-start | bytes 6291460
  155.5 89.9 %all-to-all-start = ((bf16[8,1384,128]{2,1,0:T(8,128)(2,1)}), bf16[8,1384,128]{2,1,0:T(8,128)(2,1)}, u32[]{:S(2)}, u32[]{:S(2)}) async-start(bf16[8,1384,128]{2,1,0:T(8,128)(2,1)} %copy.54), calls=%async_computation | async-start | bytes 5668864 | tf_op jit(solution)/shard_map/all_to_all | solution.py:159
  175.1 72.6 %copy-start.8 = (f32[128,256]{1,0:T(8,128)S(1)}, f32[128,256]{1,0:T(8,128)}, u32[]{:S(2)}) copy-start(f32[128,256]{1,0:T(8,128)} %param.20) | copy-start | bytes 393220
  175.1 72.6 %copy-start.9 = (f32[128,256]{1,0:T(8,128)S(1)}, f32[128,256]{1,0:T(8,128)}, u32[]{:S(2)}) copy-start(f32[128,256]{1,0:T(8,128)} %param.19) | copy-start | bytes 393220
  175.1 104.2 %copy-start.1 = (bf16[512,2048]{1,0:T(8,128)(2,1)S(1)}, bf16[512,2048]{1,0:T(8,128)(2,1)}, u32[]{:S(2)}) copy-start(bf16[512,2048]{1,0:T(8,128)(2,1)} %param.12) | copy-start | bytes 6291460
  247.7 31.5 %copy-start.7 = (f32[128,256]{1,0:T(8,128)}, f32[128,256]{1,0:T(8,128)S(1)}, u32[]{:S(2)}) copy-start(f32[128,256]{1,0:T(8,128)S(1)} %reshape.149) | copy-start | bytes 393220
Sparse Core Ops, SparseCore 0:
  10.8 82.5 all-gather.2
  145.3 130.3 reduce-scatter.3

commit v6 on v4

--- a/solution.py
+++ b/solution.py
@@ -20,6 +20,35 @@
     new_first = beta_one * first_moment + (1.0 - beta_one) * grad_value
     new_second = beta_two * second_moment + (1.0 - beta_two) * grad_value * grad_value
     return new_first / corr_one / (jnp.sqrt(new_second / corr_two) + adam_eps)
+
+
+def ring_order(n):
+    if n % 2:
+        return list(range(n))
+    return list(range(0, n, 2)) + list(range(n - 1, 0, -2))
+
+
+def ring_all_gather(x):
+    n = lax.axis_size("dp")
+    order = ring_order(n)
+    pos_of = [0] * n
+    for p, d in enumerate(order):
+        pos_of[d] = p
+    fwd = [(order[p], order[(p + 1) % n]) for p in range(n)]
+    bwd = [(order[p], order[(p - 1) % n]) for p in range(n)]
+    half = x.shape[0] // 2
+    cw, ccw = x[:half], x[half:]
+    cw_steps, ccw_steps = [cw], [ccw]
+    for _ in range(n - 1):
+        cw = lax.ppermute(cw, "dp", fwd)
+        ccw = lax.ppermute(ccw, "dp", bwd)
+        cw_steps.append(cw)
+        ccw_steps.append(ccw)
+    ring_pos = jnp.asarray(pos_of, jnp.int32)
+    pos = ring_pos[lax.axis_index("dp")]
+    cw_all = jnp.take(jnp.stack(cw_steps), (pos - ring_pos) % n, axis=0)
+    ccw_all = jnp.take(jnp.stack(ccw_steps), (ring_pos - pos) % n, axis=0)
+    return jnp.concatenate([cw_all, ccw_all], axis=1)
 
 
 def tensor_sum(parts):
@@ -88,7 +117,7 @@
     b_rows_own = b_master.shape[0]
     b_as_a = b_master.astype(jnp.bfloat16).reshape(b_rows_own * kv_shard // rank_width, rank_width)
     packed = jnp.concatenate([a_master.astype(jnp.bfloat16), b_as_a], axis=0)
-    packed_all = lax.all_gather(packed, "dp", axis=0, tiled=False)
+    packed_all = ring_all_gather(packed)
     frozen_gradient_share = frozen_gradient(grad_out, base_weight, feat_shard)
     frozen_gradient_share, packed_all = lax.optimization_barrier((frozen_gradient_share, packed_all))
     a_all = packed_all[:, :a_rows_own].reshape(TENANTS, feat_shard, rank_width)

time: 281 us -> 299 us (1.064)
  local copies, waits for them, and re-layouts: 37.2 us -> 56.6 us
  starting transfers between devices: 9.89 us -> 23.9 us
  between operations: 14.3 us -> 0.95 us
  waiting for transfers between devices: 156 us -> 147 us
  other arithmetic: 30.7 us -> 35.2 us
    ppermute x0 -> x14, waiting for transfers between devices: none -> 22.7 us  [the longest x7 18.2 us: ring_all_gather(): ccw = lax.ppermute(ccw, 'dp', bwd)]
    ppermute x1, waiting for transfers between devices: 42.6 us -> 26.1 us  [frozen_gradient(): far_in = lax.ppermute(far_part, 'tensor', row_pairs)]
    ppermute x0 -> x14, starting transfers between devices: none -> 14.2 us  [the longest x7 12 us: ring_all_gather(): ccw = lax.ppermute(ccw, 'dp', bwd)]
    all_gather x1 -> x0, waiting for transfers between devices: 11.2 us -> none  [local(): packed_all = lax.all_gather(packed, 'dp', axis=0, tiled=False)]
    unnamed x24 -> x42, local copies, waits for them, and re-layouts: 6.27 us -> 17.1 us
    gather x0 -> x2, local copies, waits for them, and re-layouts: none -> 7.95 us  [the longest x1 4 us: ring_all_gather(): cw_all = jnp.take(jnp.stack(cw_steps), (pos - ring_pos) % n, axis=0)]
    ppermute x1, waiting for transfers between devices: 3.92 us -> 0.01 us  [frozen_gradient(): partner_dy = lax.ppermute(grad_out, 'tensor', core_pairs)]
  transfers between devices with their start and end apart: 7 -> 20, of which waited for: 6 -> 14; matrix products, arithmetic and copies ran while one was open for 15% -> 22% of each run, Pallas kernels for 0% -> 0%
where the time goes in v6:
time: 299 us; the launch traced here: 298 us
  waiting for transfers between devices  147 us (49%)
  local copies, waits for them, and re-layouts  56.6 us (19%)
  other arithmetic  35.2 us (12%)
  matrix products  34.4 us (12%)
  starting transfers between devices  23.9 us (8%)
    all_to_all x1, waiting for transfers between devices, local(): lax.all_to_all(grad_pack.astype(jnp.bfloat16).reshape(dp_size, a_per + b_...  83.9 us
    ppermute x1, waiting for transfers between devices, frozen_gradient(): far_in = lax.ppermute(far_part, 'tensor', row_pairs)  26.1 us
    ppermute x7, waiting for transfers between devices, ring_all_gather(): ccw = lax.ppermute(ccw, 'dp', bwd)  18.2 us
    unnamed x42, local copies, waits for them, and re-layouts  17.1 us
    ppermute x2, waiting for transfers between devices, tensor_sum(): parts = tuple((p + lax.ppermute(p, 'tensor', pairs) for p in parts))  14.1 us
    ppermute x7, starting transfers between devices, ring_all_gather(): ccw = lax.ppermute(ccw, 'dp', bwd)  12 us
    concatenate x1, other arithmetic, local(): jnp.concatenate([a_flat.reshape(dp_size, a_per, rank_width), b_flat.resha...  11.2 us
    dot_general x2, matrix products, chip_partial(): jnp.einsum('tpk,pdk->td', partner_dy, other, preferred_element_type=jnp.f...  9.83 us
  transfers between devices with their start and end apart: 20, of which 14 were waited for; matrix products, arithmetic and copies ran while one was open for 22% of the time, Pallas kernels for 0%

profile of v6, /device:TPU:0, one launch (start us, length us, event | category | flops | bytes accessed | tf_op | source)
XLA Modules:
  0.0 297.8 jit_solution(7615908155814622352)
XLA Ops:
  7.7 4.5 %copy_bitcast_fusion = bf16[2,2,2048,256]{3,2,0,1:T(8,128)(2,1)} fusion(bf16[2,2,2,2048,256]{4,3,2,1,0:T(8,128)(2,1)} %bitcast.114, s32[]{:T(128)S(6)} %select_n.84), kind=kLoop, calls=%fused_computation.13 | loop fusion | bytes 8388612 | tf_op jit(solution)/shard_map/jit(dynamic_index_in_dim)/squeeze | solution.py:78
  19.2 4.9 %fusion.4 = f32[2048,512,1]{1,0,2:T(8,128)} fusion(bf16[2,2,2,2048,256]{4,3,2,1,0:T(8,128)(2,1)} %bitcast.116, s32[]{:T(128)S(6)} %select_n.80, s32[]{:T(128)S(6)} %select_n.83, bf16[512,2,256]{2,1,0:T(2,128)(2,1)S(1)} %copy-done.5), kind=kOutput, calls=%fused_computation.21 | convolution fusion | flops 1073741824 | bytes 6815752 | tf_op jit(solution)/shard_map/tpk,pdk->td/dot_general | solution.py:88
  29.6 3.9 %collective-permute-done.11 = bf16[1152,128]{1,0:T(8,128)(2,1)S(1)} collective-permute-done((bf16[1152,128]{1,0:T(8,128)(2,1)}, bf16[1152,128]{1,0:T(8,128)(2,1)S(1)}, u32[]{:S(2)}, u32[]{:S(2)}) %collective-permute-start.11) | collective-permute-done | bytes 294944 | tf_op jit(solution)/shard_map/ppermute | solution.py:44
  37.7 4.2 %collective-permute-done.12 = bf16[1152,128]{1,0:T(8,128)(2,1)S(1)} collective-permute-done((bf16[1152,128]{1,0:T(8,128)(2,1)S(1)}, bf16[1152,128]{1,0:T(8,128)(2,1)S(1)}, u32[]{:S(2)}, u32[]{:S(2)}) %collective-permute-start.12) | collective-permute-done | bytes 294944 | tf_op jit(solution)/shard_map/ppermute | solution.py:44
  53.7 3.2 %collective-permute-done.14 = bf16[1152,128]{1,0:T(8,128)(2,1)S(1)} collective-permute-done((bf16[1152,128]{1,0:T(8,128)(2,1)S(1)}, bf16[1152,128]{1,0:T(8,128)(2,1)S(1)}, u32[]{:S(2)}, u32[]{:S(2)}) %collective-permute-start.14) | collective-permute-done | bytes 294944 | tf_op jit(solution)/shard_map/ppermute | solution.py:44
  61.3 4.1 %collective-permute-done.15 = bf16[1152,128]{1,0:T(8,128)(2,1)S(1)} collective-permute-done((bf16[1152,128]{1,0:T(8,128)(2,1)S(1)}, bf16[1152,128]{1,0:T(8,128)(2,1)S(1)}, u32[]{:S(2)}, u32[]{:S(2)}) %collective-permute-start.15) | collective-permute-done | bytes 294944 | tf_op jit(solution)/shard_map/ppermute | solution.py:44
  68.9 4.2 %fusion.1 = bf16[512,2048]{0,1:T(8,128)(2,1)} fusion(bf16[512,2,256]{2,0,1:T(8,128)(2,1)S(1)} %collective-permute-done.1, f32[2048,512,1]{1,0,2:T(8,128)S(1)} %fusion.2, bf16[2,2,2048,256]{3,2,0,1:T(8,128)(2,1)} %collective-permute-done, s32[]{:T(128)S(6)} %select_n.85), kind=kOutput, calls=%fused_computation.15 | convolution fusion | flops 1075838976 | bytes 8912900 | tf_op jit(solution)/shard_map/tpk,pdk->td/dot_general | solution.py:89
  75.8 3.9 %gather_fusion.5 = bf16[8,1152,128]{2,1,0:T(8,128)(2,1)} fusion(bf16[8,1152,128]{2,1,0:T(8,128)(2,1)} %bitcast_dynamic-update-slice_fusion, s32[1024]{0:T(1024)S(1)} %pad_clamp_fusion.2), kind=kCustom, calls=%fused_computation.1.clone | custom fusion | bytes 4718624 | tf_op jit(solution)/shard_map/jit(_take)/gather | solution.py:50
  81.5 4.0 %gather_fusion.4 = bf16[8,1152,128]{2,1,0:T(8,128)(2,1)} fusion(bf16[8,1152,128]{2,1,0:T(8,128)(2,1)} %bitcast_dynamic-update-slice_fusion.8, s32[1024]{0:T(1024)S(1)} %pad_clamp_fusion.3), kind=kCustom, calls=%fused_computation.clone | custom fusion | bytes 4718624 | tf_op jit(solution)/shard_map/jit(_take)/gather | solution.py:49
  88.7 26.1 %collective-permute-done.2 = bf16[512,2048]{0,1:T(8,128)(2,1)} collective-permute-done((bf16[512,2048]{0,1:T(8,128)(2,1)}, bf16[512,2048]{0,1:T(8,128)(2,1)}, u32[]{:S(2)}, u32[]{:S(2)}) %collective-permute-start.2) | collective-permute-done | bytes 2097184 | tf_op jit(solution)/shard_map/ppermute | solution.py:93
  114.7 5.7 %bitcast_add_fusion.1 = f32[512,2048]{0,1:T(8,128)} fusion(f32[2048,512,1]{1,0,2:T(8,128)S(1)} %copy-done.6, bf16[512,2048]{0,1:T(8,128)(2,1)} %collective-permute-done.2, bf16[512,2,256]{2,0,1:T(8,128)(2,1)S(1)} %collective-permute-done.1, bf16[2,2,2048,256]{3,2,0,1:T(8,128)(2,1)} %collective-permute-done, s32[]{:T(128)S(6)} %select_n.79), kind=kOutput, calls=%fused_computation.11 | convolution fusion | flops 1076887552 | bytes 13107204 | tf_op jit(solution)/shard_map/tpk,pdk->td/dot_general | solution.py:89
  123.7 4.4 %gather_fusion.1 = bf16[4,2048,128]{2,1,0:T(8,128)(2,1)} fusion(bf16[8,2048,128]{2,1,0:T(8,128)(2,1)} %slice.26, s32[1024]{0:T(1024)S(1)} %pad_clamp_fusion), kind=kCustom, calls=%fused_computation.3 | custom fusion | bytes 4194320 | tf_op jit(solution)/shard_map/gather | solution.py:132
  137.2 12.5 %collective-permute-done.18 = f32[4,128,256]{1,2,0:T(8,128)S(1)} collective-permute-done((f32[4,128,256]{1,2,0:T(8,128)S(1)}, f32[4,128,256]{1,2,0:T(8,128)S(1)}, u32[]{:S(2)}, u32[]{:S(2)}) %collective-permute-start.18) | collective-permute-done | bytes 524320 | tf_op jit(solution)/shard_map/ppermute | solution.py:59
  152.5 5.3 %copy.50 = f32[4,2048,128]{2,0,1:T(4,128)} copy(f32[4,2048,128]{1,2,0:T(8,128)} %convolution_bitcast_fusion) | data formatting | bytes 8388608 | tf_op jit(solution)/shard_map/bnd,bnc->bdc/dot_general | solution.py:151
  157.8 7.0 %convolution_convert_fusion = bf16[8,2048,128]{2,0,1:T(8,128)(2,1)S(1)} fusion(f32[4,2048,128]{2,0,1:T(4,128)} %copy.50, s32[4]{0:T(128)S(1)} %gather_fusion), kind=kOutput, calls=%fused_computation.16 | convolution fusion | flops 102760480 | bytes 8388624 | tf_op jit(solution)/shard_map/sb,bdc->sdc/dot_general | solution.py:164
  166.2 11.2 %pad_maximum_fusion.1 = bf16[8,2304,128]{2,0,1:T(8,128)(2,1)S(1)} fusion(bf16[8,256,128]{2,0,1:T(8,128)(2,1)S(1)} %bitcast.113, bf16[8,2048,128]{2,0,1:T(8,128)(2,1)S(1)} %convolution_convert_fusion), kind=kLoop, calls=%fused_computation.8 | loop fusion | flops 2359296 | bytes 9437184 | tf_op jit(solution)/shard_map/concatenate | solution.py:173
  180.4 5.8 %all-to-all-start = ((bf16[8,2304,128]{2,1,0:T(8,128)(2,1)}), bf16[8,2304,128]{2,1,0:T(8,128)(2,1)}, u32[]{:S(2)}, u32[]{:S(2)}) async-start(bf16[8,2304,128]{2,1,0:T(8,128)(2,1)} %copy.53), calls=%async_computation | async-start | bytes 9437184 | tf_op jit(solution)/shard_map/all_to_all | solution.py:180
  186.2 3.0 %fusion.29 = f32[4,128,2048]{2,1,0:T(8,128)} fusion(bf16[4,2048,128]{2,1,0:T(8,128)(2,1)S(1)} %copy-done.4, f32[4,128,256]{1,2,0:T(8,128)S(1)} %add.135, f32[4,128]{1,0:T(4,128)S(1)} %compare_select_fusion.4), kind=kOutput, calls=%fused_computation.70 | convolution fusion | flops 268566528 | bytes 6555648 | tf_op jit(solution)/shard_map/bnc,bdc->bnd/dot_general | solution.py:147
  189.2 5.3 %copy.58 = f32[512,2048]{0,1:T(8,128)} copy(f32[512,2048]{1,0:T(8,128)} %bitcast.108) | data formatting | bytes 8388608 | tf_op jit(solution)/shard_map/reshape | solution.py:149
  194.6 6.4 %add.137 = f32[512,2048]{0,1:T(8,128)} add(f32[512,2048]{0,1:T(8,128)} %bitcast_add_fusion.1, f32[512,2048]{0,1:T(8,128)} %copy.58) | non-fusion elementwise | flops 1048576 | bytes 12582912 | tf_op jit(solution)/shard_map/add | solution.py:150
  201.0 5.3 %copy.54 = f32[512,2048]{1,0:T(8,128)} copy(f32[512,2048]{0,1:T(8,128)} %add.137) | data formatting | bytes 8388608
  206.3 83.9 %all-to-all-done = bf16[8,2304,128]{2,1,0:T(8,128)(2,1)} async-done(((bf16[8,2304,128]{2,1,0:T(8,128)(2,1)}), bf16[8,2304,128]{2,1,0:T(8,128)(2,1)}, u32[]{:S(2)}, u32[]{:S(2)}) %all-to-all-start) | async-done | bytes 4718624 | tf_op jit(solution)/shard_map/all_to_all | solution.py:180
  290.2 3.1 %convert_reduce_fusion = f32[2304,128]{1,0:T(8,128)S(1)} fusion(bf16[8,2304,128]{2,1,0:T(8,128)(2,1)} %all-to-all-done), kind=kLoop, calls=%fused_computation.6 | loop fusion | flops 4423680 | bytes 5898240 | tf_op jit(solution)/shard_map/reduce_sum | solution.py:187
  293.4 3.6 %fusion.16 = (f32[2048,128]{1,0:T(8,128)}, f32[2048,128]{1,0:T(8,128)}) fusion(f32[2048,128]{1,0:T(8,128)} %param.21, f32[2048,128]{1,0:T(8,128)} %param.20, f32[2304,128]{1,0:T(8,128)S(1)} %convert_reduce_fusion), kind=kLoop, calls=%fused_computation.37 | loop fusion | flops 2883584 | bytes 5242880 | tf_op jit(solution)/shard_map/div | solution.py:22
  (116 shorter events, 71.2 us)
Async XLA Ops:
  0.6 128.0 %copy-start = (bf16[512,2048]{1,0:T(8,128)(2,1)S(1)}, bf16[512,2048]{1,0:T(8,128)(2,1)}, u32[]{:S(2)}) copy-start(bf16[512,2048]{1,0:T(8,128)(2,1)} %param.15) | copy-start | bytes 6291460
  4.0 20.2 %collective-permute-start.10 = (bf16[1152,128]{1,0:T(8,128)(2,1)S(1)}, bf16[1152,128]{1,0:T(8,128)(2,1)}, u32[]{:S(2)}, u32[]{:S(2)}) collective-permute-start(bf16[1152,128]{1,0:T(8,128)(2,1)S(1)} %get-tuple-element.32), channel_id=1, source_target_pairs={{0,4},{8,0},{16,8},{24,16},{28,24},{20,28},{12,20},{4,12},{1,5},{9... | collective-permute-start | bytes 884744 | tf_op jit(solution)/shard_map/ppermute | solution.py:44
  7.7 20.2 %collective-permute-start.3 = (bf16[1152,128]{1,0:T(8,128)(2,1)}, bf16[1152,128]{1,0:T(8,128)(2,1)}, u32[]{:S(2)}, u32[]{:S(2)}) collective-permute-start(bf16[1152,128]{1,0:T(8,128)(2,1)} %slice.44), channel_id=1, source_target_pairs={{0,8},{8,16},{16,24},{24,28},{28,20},{20,12},{12,4},{4,0},{1,9},{9... | collective-permute-start | bytes 884744 | tf_op jit(solution)/shard_map/ppermute | solution.py:43
  7.7 7.9 %copy-start.13 = (s32[4]{0:T(128)S(1)}, s32[4]{0:T(128)}, u32[]{:S(2)}) copy-start(s32[4]{0:T(128)} %param.24) | copy-start | bytes 52
  7.7 8.0 %copy-start.2 = (s32[8]{0:T(128)S(1)}, s32[8]{0:T(128)}, u32[]{:S(2)}) copy-start(s32[8]{0:T(128)} %param.26) | copy-start | bytes 100
  12.3 56.6 %collective-permute-start = (bf16[2,2,2048,256]{3,2,0,1:T(8,128)(2,1)}, bf16[2,2,2048,256]{3,2,0,1:T(8,128)(2,1)}, u32[]{:S(2)}, u32[]{:S(2)}) collective-permute-start(bf16[2,2,2048,256]{3,2,0,1:T(8,128)(2,1)} %copy_bitcast_fusion), channel_id=1, source_target_pairs={{0,1},{1,0},{2,3},{3,2},{4,5},{5,4},{6,7},{7,6},{8,9},{9,8},{10,11... | collective-permute-start | bytes 12582920 | tf_op jit(solution)/shard_map/ppermute | solution.py:82
  13.1 55.7 %collective-permute-start.1 = (bf16[512,2,256]{2,0,1:T(8,128)(2,1)}, bf16[512,2,256]{2,0,1:T(8,128)(2,1)S(1)}, u32[]{:S(2)}, u32[]{:S(2)}) collective-permute-start(bf16[512,2,256]{2,0,1:T(8,128)(2,1)} %copy.41), channel_id=1, source_target_pairs={{0,1},{1,0},{2,3},{3,2},{4,5},{5,4},{6,7},{7,6},{8,9},{9,8},{10,11... | collective-permute-start | bytes 1572872 | tf_op jit(solution)/shard_map/ppermute | solution.py:83
  24.1 9.4 %collective-permute-start.11 = (bf16[1152,128]{1,0:T(8,128)(2,1)}, bf16[1152,128]{1,0:T(8,128)(2,1)S(1)}, u32[]{:S(2)}, u32[]{:S(2)}) collective-permute-start(bf16[1152,128]{1,0:T(8,128)(2,1)} %collective-permute-done.10), channel_id=1, source_target_pairs={{0,4},{8,0},{16,8},{24,16},{28,24},{20,28},{12,20},{4,12},{1,5},{9... | collective-permute-start | bytes 884744 | tf_op jit(solution)/shard_map/ppermute | solution.py:44
  27.8 8.8 %collective-permute-start.4 = (bf16[1152,128]{1,0:T(8,128)(2,1)}, bf16[1152,128]{1,0:T(8,128)(2,1)S(1)}, u32[]{:S(2)}, u32[]{:S(2)}) collective-permute-start(bf16[1152,128]{1,0:T(8,128)(2,1)} %collective-permute-done.3), channel_id=1, source_target_pairs={{0,8},{8,16},{16,24},{24,28},{28,20},{20,12},{12,4},{4,0},{1,9},{9... | collective-permute-start | bytes 884744 | tf_op jit(solution)/shard_map/ppermute | solution.py:43
  33.5 8.4 %collective-permute-start.12 = (bf16[1152,128]{1,0:T(8,128)(2,1)S(1)}, bf16[1152,128]{1,0:T(8,128)(2,1)S(1)}, u32[]{:S(2)}, u32[]{:S(2)}) collective-permute-start(bf16[1152,128]{1,0:T(8,128)(2,1)S(1)} %collective-permute-done.11), channel_id=1, source_target_pairs={{0,4},{8,0},{16,8},{24,16},{28,24},{20,28},{12,20},{4,12},{1,5},{9... | collective-permute-start | bytes 884744 | tf_op jit(solution)/shard_map/ppermute | solution.py:44
  36.7 7.7 %collective-permute-start.5 = (bf16[1152,128]{1,0:T(8,128)(2,1)S(1)}, bf16[1152,128]{1,0:T(8,128)(2,1)S(1)}, u32[]{:S(2)}, u32[]{:S(2)}) collective-permute-start(bf16[1152,128]{1,0:T(8,128)(2,1)S(1)} %collective-permute-done.4), channel_id=1, source_target_pairs={{0,8},{8,16},{16,24},{24,28},{28,20},{20,12},{12,4},{4,0},{1,9},{9... | collective-permute-start | bytes 884744 | tf_op jit(solution)/shard_map/ppermute | solution.py:43
  41.9 7.5 %collective-permute-start.13 = (bf16[1152,128]{1,0:T(8,128)(2,1)S(1)}, bf16[1152,128]{1,0:T(8,128)(2,1)S(1)}, u32[]{:S(2)}, u32[]{:S(2)}) collective-permute-start(bf16[1152,128]{1,0:T(8,128)(2,1)S(1)} %collective-permute-done.12), channel_id=1, source_target_pairs={{0,4},{8,0},{16,8},{24,16},{28,24},{20,28},{12,20},{4,12},{1,5},{9... | collective-permute-start | bytes 884744 | tf_op jit(solution)/shard_map/ppermute | solution.py:44
  44.4 7.2 %collective-permute-start.6 = (bf16[1152,128]{1,0:T(8,128)(2,1)S(1)}, bf16[1152,128]{1,0:T(8,128)(2,1)S(1)}, u32[]{:S(2)}, u32[]{:S(2)}) collective-permute-start(bf16[1152,128]{1,0:T(8,128)(2,1)S(1)} %collective-permute-done.5), channel_id=1, source_target_pairs={{0,8},{8,16},{16,24},{24,28},{28,20},{20,12},{12,4},{4,0},{1,9},{9... | collective-permute-start | bytes 884744 | tf_op jit(solution)/shard_map/ppermute | solution.py:43
  49.4 7.6 %collective-permute-start.14 = (bf16[1152,128]{1,0:T(8,128)(2,1)S(1)}, bf16[1152,128]{1,0:T(8,128)(2,1)S(1)}, u32[]{:S(2)}, u32[]{:S(2)}) collective-permute-start(bf16[1152,128]{1,0:T(8,128)(2,1)S(1)} %collective-permute-done.13), channel_id=1, source_target_pairs={{0,4},{8,0},{16,8},{24,16},{28,24},{20,28},{12,20},{4,12},{1,5},{9... | collective-permute-start | bytes 884744 | tf_op jit(solution)/shard_map/ppermute | solution.py:44
  51.6 7.9 %collective-permute-start.7 = (bf16[1152,128]{1,0:T(8,128)(2,1)S(1)}, bf16[1152,128]{1,0:T(8,128)(2,1)S(1)}, u32[]{:S(2)}, u32[]{:S(2)}) collective-permute-start(bf16[1152,128]{1,0:T(8,128)(2,1)S(1)} %collective-permute-done.6), channel_id=1, source_target_pairs={{0,8},{8,16},{16,24},{24,28},{28,20},{20,12},{12,4},{4,0},{1,9},{9... | collective-permute-start | bytes 884744 | tf_op jit(solution)/shard_map/ppermute | solution.py:43
  57.0 8.4 %collective-permute-start.15 = (bf16[1152,128]{1,0:T(8,128)(2,1)S(1)}, bf16[1152,128]{1,0:T(8,128)(2,1)S(1)}, u32[]{:S(2)}, u32[]{:S(2)}) collective-permute-start(bf16[1152,128]{1,0:T(8,128)(2,1)S(1)} %collective-permute-done.14), channel_id=1, source_target_pairs={{0,4},{8,0},{16,8},{24,16},{28,24},{20,28},{12,20},{4,12},{1,5},{9... | collective-permute-start | bytes 884744 | tf_op jit(solution)/shard_map/ppermute | solution.py:44
  59.5 8.7 %collective-permute-start.8 = (bf16[1152,128]{1,0:T(8,128)(2,1)S(1)}, bf16[1152,128]{1,0:T(8,128)(2,1)S(1)}, u32[]{:S(2)}, u32[]{:S(2)}) collective-permute-start(bf16[1152,128]{1,0:T(8,128)(2,1)S(1)} %collective-permute-done.7), channel_id=1, source_target_pairs={{0,8},{8,16},{16,24},{24,28},{28,20},{20,12},{12,4},{4,0},{1,9},{9... | collective-permute-start | bytes 884744 | tf_op jit(solution)/shard_map/ppermute | solution.py:43
  65.3 9.7 %collective-permute-start.16 = (bf16[1152,128]{1,0:T(8,128)(2,1)S(1)}, bf16[1152,128]{1,0:T(8,128)(2,1)S(1)}, u32[]{:S(2)}, u32[]{:S(2)}) collective-permute-start(bf16[1152,128]{1,0:T(8,128)(2,1)S(1)} %collective-permute-done.15), channel_id=1, source_target_pairs={{0,4},{8,0},{16,8},{24,16},{28,24},{20,28},{12,20},{4,12},{1,5},{9... | collective-permute-start | bytes 884744 | tf_op jit(solution)/shard_map/ppermute | solution.py:44
  68.1 11.6 %collective-permute-start.9 = (bf16[1152,128]{1,0:T(8,128)(2,1)S(1)}, bf16[1152,128]{1,0:T(8,128)(2,1)}, u32[]{:S(2)}, u32[]{:S(2)}) collective-permute-start(bf16[1152,128]{1,0:T(8,128)(2,1)S(1)} %collective-permute-done.8), channel_id=1, source_target_pairs={{0,8},{8,16},{16,24},{24,28},{28,20},{20,12},{12,4},{4,0},{1,9},{9... | collective-permute-start | bytes 884744 | tf_op jit(solution)/shard_map/ppermute | solution.py:43
  73.1 41.7 %collective-permute-start.2 = (bf16[512,2048]{0,1:T(8,128)(2,1)}, bf16[512,2048]{0,1:T(8,128)(2,1)}, u32[]{:S(2)}, u32[]{:S(2)}) collective-permute-start(bf16[512,2048]{0,1:T(8,128)(2,1)} %fusion.1), channel_id=1, source_target_pairs={{0,2},{1,3},{2,0},{3,1},{4,6},{5,7},{6,4},{7,5},{8,10},{9,11},{10,... | collective-permute-start | bytes 6291464 | tf_op jit(solution)/shard_map/ppermute | solution.py:93
  88.3 26.4 %copy-start.6 = (f32[2048,512,1]{1,0,2:T(8,128)S(1)}, f32[2048,512,1]{1,0,2:T(8,128)}, u32[]{:S(2)}) copy-start(f32[2048,512,1]{1,0,2:T(8,128)} %fusion.4) | copy-start | bytes 12582916
  132.2 2.3 collective-permute-start.17
  135.6 14.0 %collective-permute-start.18 = (f32[4,128,256]{1,2,0:T(8,128)S(1)}, f32[4,128,256]{1,2,0:T(8,128)S(1)}, u32[]{:S(2)}, u32[]{:S(2)}) collective-permute-start(f32[4,128,256]{1,2,0:T(8,128)S(1)} %fusion.45), channel_id=1, source_target_pairs={{0,2},{1,3},{2,0},{3,1},{4,6},{5,7},{6,4},{7,5},{8,10},{9,11},{10,... | collective-permute-start | bytes 1572872 | tf_op jit(solution)/shard_map/ppermute | solution.py:59
  180.4 109.8 %all-to-all-start = ((bf16[8,2304,128]{2,1,0:T(8,128)(2,1)}), bf16[8,2304,128]{2,1,0:T(8,128)(2,1)}, u32[]{:S(2)}, u32[]{:S(2)}) async-start(bf16[8,2304,128]{2,1,0:T(8,128)(2,1)} %copy.53), calls=%async_computation | async-start | bytes 9437184 | tf_op jit(solution)/shard_map/all_to_all | solution.py:180
  (10 other events, 46.8 us)

commit v7 on v3

--- a/solution.py
+++ b/solution.py
@@ -20,6 +20,21 @@
     new_first = beta_one * first_moment + (1.0 - beta_one) * grad_value
     new_second = beta_two * second_moment + (1.0 - beta_two) * grad_value * grad_value
     return new_first / corr_one / (jnp.sqrt(new_second / corr_two) + adam_eps)
+
+
+def tensor_sum_pair(first, second):
+    size = lax.axis_size("tensor")
+    width = first.shape[-1]
+    both = jnp.concatenate([first, second], axis=-1)
+    both = both + lax.ppermute(both, "tensor", [(i, i ^ 1) for i in range(size)])
+    first, second = both[..., :width], both[..., width:]
+    step = 2
+    while step < size:
+        pairs = [(i, i ^ step) for i in range(size)]
+        first = first + lax.ppermute(first, "tensor", pairs)
+        second = second + lax.ppermute(second, "tensor", pairs)
+        step *= 2
+    return first, second
 
 
 def tensor_sum(parts):
@@ -61,8 +76,46 @@
         return first + second
 
     far_part = chip_partial(1 - row_bit).astype(jnp.bfloat16)
-    far_in = lax.ppermute(far_part, "tensor", row_pairs)
+    half = tok_rows // 2
+    far_in = jnp.concatenate(
+        [
+            lax.ppermute(far_part[:half], "tensor", row_pairs),
+            lax.ppermute(far_part[half:], "tensor", row_pairs),
+        ],
+        axis=0,
+    )
     return chip_partial(row_bit) + far_in.astype(jnp.float32)
+
+
+def slot_major_grads(
+    tokens_in, grad_out, middle_rank_rows, backward_token_rows, block_slot, tenant_rank, tenant_slot
+):
+    tok_rows, feat_shard = tokens_in.shape
+    kv_shard = grad_out.shape[2]
+    rank_width = backward_token_rows.shape[-1]
+    token_slot = jnp.repeat(block_slot, TENANT_BLOCK)
+    slot_hot = token_slot[:, None] == jnp.arange(TENANTS)[None, :]
+    back_rows = backward_token_rows.reshape(tok_rows, rank_width)
+    back_sel = jnp.where(slot_hot[:, :, None], back_rows[:, None, :], jnp.zeros((), back_rows.dtype))
+    a_sc = jnp.einsum("nsc,nd->scd", back_sel, tokens_in, preferred_element_type=jnp.float32)
+    mid_rows = middle_rank_rows.reshape(tok_rows, 2, PADDED_RANK)
+    mid_sel = jnp.where(
+        slot_hot[:, :, None, None], mid_rows[:, None, :, :], jnp.zeros((), mid_rows.dtype)
+    )
+    b_sc = jnp.einsum("nspr,npk->sprk", mid_sel, grad_out, preferred_element_type=jnp.float32)
+    slot_tenant = jnp.argsort(tenant_slot)
+    slot_scale = adapter_alpha_factor / tenant_rank[slot_tenant].astype(jnp.float32)
+    b_sc = b_sc * slot_scale[:, None, None, None]
+    send = jnp.concatenate(
+        [
+            a_sc.astype(jnp.bfloat16),
+            b_sc.reshape(TENANTS, rank_width, kv_shard).astype(jnp.bfloat16),
+        ],
+        axis=2,
+    )
+    recv = lax.all_to_all(send, "dp", split_axis=0, concat_axis=0, tiled=True)
+    own = jnp.sum(recv.astype(jnp.float32), axis=0)
+    return own[:, :feat_shard].T, own[:, feat_shard:]
 
 
 def local(
@@ -89,24 +142,30 @@
     b_as_a = b_master.astype(jnp.bfloat16).reshape(b_rows_own * kv_shard // rank_width, rank_width)
     packed = jnp.concatenate([a_master.astype(jnp.bfloat16), b_as_a], axis=0)
     packed_all = lax.all_gather(packed, "dp", axis=0, tiled=False)
-    a_all = packed_all[:, :a_rows_own].reshape(TENANTS, feat_shard, rank_width)
-    b_all = packed_all[:, a_rows_own:].reshape(dp_size, b_rows_own, kv_shard).reshape(
-        TENANTS, rank_width, kv_shard
-    )
     block_slot = tenant_slot[block_tenant]
+    slot_major = dp_size == TENANTS
+    if slot_major:
+        picked = jnp.take(packed_all, block_slot, axis=0)
+        a_blocks = picked[:, :a_rows_own]
+        b_blocks = picked[:, a_rows_own:].reshape(block_count, 2, PADDED_RANK, kv_shard)
+    else:
+        a_all = packed_all[:, :a_rows_own].reshape(TENANTS, feat_shard, rank_width)
+        b_all = packed_all[:, a_rows_own:].reshape(dp_size, b_rows_own, kv_shard).reshape(
+            TENANTS, rank_width, kv_shard
+        )
+        a_blocks = a_all[block_slot]
+        b_blocks = b_all[block_slot].reshape(block_count, 2, PADDED_RANK, kv_shard)
     rank_of_block = tenant_rank[block_tenant].astype(jnp.float32)
     column_rank = (jnp.arange(rank_width) % PADDED_RANK).astype(jnp.float32)
     column_rank_mask = (column_rank[None, :] < rank_of_block[:, None]).astype(jnp.float32)
     adapter_scale_factor = adapter_alpha_factor / rank_of_block
-    a_blocks = a_all[block_slot]
-    b_blocks = b_all[block_slot].reshape(block_count, 2, PADDED_RANK, kv_shard)
     x_blocks = tokens_in.reshape(block_count, TENANT_BLOCK, feat_shard)
     dy_blocks = grad_out.reshape(block_count, TENANT_BLOCK, 2, kv_shard)
     mid_part = jnp.einsum("bnd,bdc->bnc", x_blocks, a_blocks, preferred_element_type=jnp.float32)
     back_part = jnp.einsum(
         "bnpk,bprk->bnpr", dy_blocks, b_blocks, preferred_element_type=jnp.float32
     ).reshape(block_count, TENANT_BLOCK, rank_width)
-    mid_sum, backward_gradient_sum = tensor_sum((mid_part, back_part))
+    mid_sum, backward_gradient_sum = tensor_sum_pair(mid_part, back_part)
     middle_rank_rows = (mid_sum * column_rank_mask[:, None, :]).astype(jnp.bfloat16)
     backward_token_rows = (
         backward_gradient_sum * (column_rank_mask * adapter_scale_factor[:, None])[:, None, :]
@@ -116,45 +175,51 @@
         "bnc,bdc->bnd", backward_token_rows, a_blocks, preferred_element_type=jnp.float32
     ).reshape(tok_rows, feat_shard)
     input_gradient_layer = frozen_gradient_share + adapter_gradient_term
-    a_terms = jnp.einsum(
-        "bnd,bnc->bdc", x_blocks, backward_token_rows, preferred_element_type=jnp.float32
-    )
-    b_terms = (
-        jnp.einsum(
-            "bnpr,bnpk->bprk",
-            middle_rank_rows.reshape(block_count, TENANT_BLOCK, 2, PADDED_RANK),
-            dy_blocks,
-            preferred_element_type=jnp.float32,
-        )
-        * adapter_scale_factor[:, None, None, None]
-    )
-    one_hot = (block_slot[None, :] == jnp.arange(TENANTS)[:, None]).astype(jnp.float32)
-    a_flat = jnp.einsum("sb,bdc->sdc", one_hot, a_terms, precision=lax.Precision.HIGHEST).reshape(
-        TENANTS * feat_shard, rank_width
-    )
-    b_flat = jnp.einsum("sb,bprk->sprk", one_hot, b_terms, precision=lax.Precision.HIGHEST).reshape(
-        TENANTS * rank_width, kv_shard
-    )
-    a_per = a_flat.shape[0] // dp_size
-    b_per = b_flat.shape[0] // dp_size
-    b_wide = b_per * kv_shard // rank_width
-    grad_pack = jnp.concatenate(
-        [
-            a_flat.reshape(dp_size, a_per, rank_width),
-            b_flat.reshape(dp_size, b_wide, rank_width),
-        ],
-        axis=1,
-    ).reshape(dp_size * (a_per + b_wide), rank_width)
-    grad_parts = lax.all_to_all(
-        grad_pack.astype(jnp.bfloat16).reshape(dp_size, a_per + b_wide, rank_width),
-        "dp",
-        split_axis=0,
-        concat_axis=0,
-        tiled=True,
-    )
-    grad_own = jnp.sum(grad_parts.astype(jnp.float32), axis=0)
-    a_grad = grad_own[:a_per]
-    b_grad = grad_own[a_per:].reshape(b_per, kv_shard)
+    if slot_major:
+        a_grad, b_grad = slot_major_grads(
+            tokens_in, grad_out, middle_rank_rows, backward_token_rows, block_slot,
+            tenant_rank, tenant_slot,
+        )
+    else:
+        a_terms = jnp.einsum(
+            "bnd,bnc->bdc", x_blocks, backward_token_rows, preferred_element_type=jnp.float32
+        )
+        b_terms = (
+            jnp.einsum(
+                "bnpr,bnpk->bprk",
+                middle_rank_rows.reshape(block_count, TENANT_BLOCK, 2, PADDED_RANK),
+                dy_blocks,
+                preferred_element_type=jnp.float32,
+            )
+            * adapter_scale_factor[:, None, None, None]
+        )
+        one_hot = (block_slot[None, :] == jnp.arange(TENANTS)[:, None]).astype(jnp.float32)
+        a_flat = jnp.einsum("sb,bdc->sdc", one_hot, a_terms, precision=lax.Precision.HIGHEST).reshape(
+            TENANTS * feat_shard, rank_width
+        )
+        b_flat = jnp.einsum("sb,bprk->sprk", one_hot, b_terms, precision=lax.Precision.HIGHEST).reshape(
+            TENANTS * rank_width, kv_shard
+        )
+        a_per = a_flat.shape[0] // dp_size
+        b_per = b_flat.shape[0] // dp_size
+        b_wide = b_per * kv_shard // rank_width
+        grad_pack = jnp.concatenate(
+            [
+                a_flat.reshape(dp_size, a_per, rank_width),
+                b_flat.reshape(dp_size, b_wide, rank_width),
+            ],
+            axis=1,
+        ).reshape(dp_size * (a_per + b_wide), rank_width)
+        grad_parts = lax.all_to_all(
+            grad_pack.astype(jnp.bfloat16).reshape(dp_size, a_per + b_wide, rank_width),
+            "dp",
+            split_axis=0,
+            concat_axis=0,
+            tiled=True,
+        )
+        grad_own = jnp.sum(grad_parts.astype(jnp.float32), axis=0)
+        a_grad = grad_own[:a_per]
+        b_grad = grad_own[a_per:].reshape(b_per, kv_shard)
     return (
         input_gradient_layer,
         a_grad,

time: 275 us -> 258 us (0.938)
  matrix products: 36.7 us -> 26.5 us
  other arithmetic: 23 us -> 17.4 us
    concatenate x1 -> x2, other arithmetic: 11.2 us -> 2.66 us  [the longest x1 2.61 us: slot_major_grads(): jnp.concatenate([a_sc.astype(jnp.bfloat16), b_sc.reshape(TENANTS, rank_wi...]
    dot_general x4 -> x2, matrix products: 11 us -> 2.78 us  [the longest x1 2.34 us: slot_major_grads(): jnp.einsum('nsc,nd->scd', back_sel, tokens_in, preferred_element_type=jnp...]
    dot_general x1 -> x0, local copies, waits for them, and re-layouts: 5.25 us -> none  [local(): jnp.einsum('bnd,bnc->bdc', x_blocks, backward_token_rows, preferred_eleme...]
    gather x2 -> x3, local copies, waits for them, and re-layouts: 4.93 us -> 9.53 us  [the longest x2 8.89 us: local(): picked = jnp.take(packed_all, block_slot, axis=0)]
    slice x3 -> x4, local copies, waits for them, and re-layouts: 5.6 us -> 1.68 us  [the longest x1 1.45 us: frozen_gradient(): far_part[:half]]
    unnamed x18 -> x21, local copies, waits for them, and re-layouts: 5.46 us -> 9.35 us
    concatenate x1 -> x0, local copies, waits for them, and re-layouts: 2.93 us -> none  [local(): jnp.concatenate([a_flat.reshape(dp_size, a_per, rank_width), b_flat.resha...]
  transfers between devices with their start and end apart: 9 -> 9, of which waited for: 8 -> 9; matrix products, arithmetic and copies ran while one was open for 16% -> 16% of each run, Pallas kernels for 0% -> 0%
where the time goes in v7:
time: 258 us
  waiting for transfers between devices  156 us (60%)
  local copies, waits for them, and re-layouts  34 us (13%)
  matrix products  26.5 us (10%)
  other arithmetic  17.4 us (7%)
  between operations  14.3 us (6%)
  starting transfers between devices  9.58 us (4%)
    all_gather x1, waiting for transfers between devices, local(): packed_all = lax.all_gather(packed, 'dp', axis=0, tiled=False)  78.6 us
    all_to_all x1, waiting for transfers between devices, slot_major_grads(): recv = lax.all_to_all(send, 'dp', split_axis=0, concat_axis=0, tiled=True)  26.2 us
    ppermute x1, waiting for transfers between devices, frozen_gradient(): lax.ppermute(far_part[half:], 'tensor', row_pairs)  21.7 us
    ppermute x1, waiting for transfers between devices, frozen_gradient(): lax.ppermute(far_part[:half], 'tensor', row_pairs)  10.9 us
    dot_general x2, matrix products, chip_partial(): jnp.einsum('tpk,pdk->td', partner_dy, other, preferred_element_type=jnp.f...  10.4 us
    unnamed x21, local copies, waits for them, and re-layouts  9.35 us
    gather x2, local copies, waits for them, and re-layouts, local(): picked = jnp.take(packed_all, block_slot, axis=0)  8.89 us
    dot_general x2, matrix products, chip_partial(): jnp.einsum('tpk,pdk->td', grad_out, own, preferred_element_type=jnp.float32)  8.01 us
  transfers between devices with their start and end apart: 9, of which 9 were waited for; matrix products, arithmetic and copies ran while one was open for 16% of the time, Pallas kernels for 0%

profile of v7, /device:TPU:0, one launch (start us, length us, event | category | flops | bytes accessed | tf_op | source)
XLA Modules:
  0.0 257.5 jit_solution(13752189500073999148)
XLA Ops:
  14.8 78.6 %all-gather.3.cloned.1.call-done = bf16[18432,128]{1,0:T(8,128)(2,1)} async-done(((bf16[2304,128]{1,0:T(8,128)(2,1)}), bf16[18432,128]{1,0:T(8,128)(2,1)}) %all-gather.3.cloned.1.call-update) | async-done | bytes 4718608 | tf_op jit(solution)/shard_map/all_gather | solution.py:144
  93.4 4.6 %gather_fusion.1 = bf16[4,2304,128]{2,1,0:T(8,128)(2,1)} fusion(bf16[8,2304,128]{2,1,0:T(8,128)(2,1)} %bitcast.83, s32[1024]{0:T(1024)S(1)} %pad_clamp_fusion.1), kind=kCustom, calls=%fused_computation.1 | custom fusion | bytes 4718608 | tf_op jit(solution)/shard_map/jit(_take)/gather | solution.py:148
  98.0 4.3 %copy.40 = bf16[4,2304,128]{1,2,0:T(8,128)(2,1)} copy(bf16[4,2304,128]{2,1,0:T(8,128)(2,1)} %gather_fusion.1) | data formatting | bytes 4718592 | tf_op jit(solution)/shard_map/jit(_take)/gather | solution.py:148
  105.9 2.3 fusion.20
  112.8 7.1 %collective-permute-done.5 = f32[4,128,128]{1,2,0:T(8,128)S(1)} collective-permute-done((f32[4,128,128]{1,2,0:T(8,128)S(1)}, f32[4,128,128]{1,2,0:T(8,128)S(1)}, u32[]{:S(2)}, u32[]{:S(2)}) %collective-permute-start.5) | collective-permute-done | bytes 262176 | tf_op jit(solution)/shard_map/ppermute | solution.py:35
  119.9 4.8 %collective-permute-done.6 = f32[4,128,128]{1,2,0:T(8,128)S(1)} collective-permute-done((f32[4,128,128]{1,2,0:T(8,128)S(1)}, f32[4,128,128]{1,2,0:T(8,128)S(1)}, u32[]{:S(2)}, u32[]{:S(2)}) %collective-permute-start.6) | collective-permute-done | bytes 262176 | tf_op jit(solution)/shard_map/ppermute | solution.py:34
  125.4 2.3 convolution_convert_fusion
  128.2 2.6 %pad_maximum_fusion = bf16[8,128,2304]{2,1,0:T(8,128)(2,1)} fusion(bf16[8,128,256]{2,1,0:T(8,128)(2,1)S(1)} %bitcast.77, bf16[8,128,2048]{2,1,0:T(8,128)(2,1)S(1)} %convolution_convert_fusion), kind=kLoop, calls=%fused_computation.5 | loop fusion | flops 9437184 | bytes 9437184 | tf_op jit(solution)/shard_map/concatenate | solution.py:109
  130.8 4.8 %all-to-all-start = ((bf16[8,128,2304]{2,1,0:T(8,128)(2,1)}), bf16[8,128,2304]{2,1,0:T(8,128)(2,1)}, u32[]{:S(2)}, u32[]{:S(2)}) async-start(bf16[8,128,2304]{2,1,0:T(8,128)(2,1)} %pad_maximum_fusion), calls=%async_computation | async-start | bytes 9437184 | tf_op jit(solution)/shard_map/all_to_all | solution.py:116
  135.6 4.5 %copy_bitcast_fusion = bf16[2,2,2048,256]{3,2,0,1:T(8,128)(2,1)} fusion(bf16[2,2,2,2048,256]{4,3,2,1,0:T(8,128)(2,1)} %bitcast.78, s32[]{:T(128)S(6)} %select_n.84), kind=kLoop, calls=%fused_computation.11 | loop fusion | bytes 8388612 | tf_op jit(solution)/shard_map/jit(dynamic_index_in_dim)/squeeze | solution.py:64
  140.8 2.9 %fusion.3 = f32[2048,512,1]{1,0,2:T(8,128)S(1)} fusion(bf16[2,2,2,2048,256]{4,3,2,1,0:T(8,128)(2,1)} %bitcast.79, s32[]{:T(128)S(6)} %select_n.86, s32[]{:T(128)S(6)} %select_n.83, bf16[512,2,256]{2,1,0:T(2,128)(2,1)S(1)} %copy-done.6), kind=kOutput, calls=%fused_computation.15 | convolution fusion | flops 1073741824 | bytes 6815752 | tf_op jit(solution)/shard_map/tpk,pdk->td/dot_general | solution.py:74
  143.7 4.0 %collective-permute-done.1 = bf16[512,2,256]{2,0,1:T(8,128)(2,1)S(1)} collective-permute-done((bf16[512,2,256]{2,0,1:T(8,128)(2,1)S(1)}, bf16[512,2,256]{2,0,1:T(8,128)(2,1)S(1)}, u32[]{:S(2)}, u32[]{:S(2)}) %collective-permute-start.1) | collective-permute-done | bytes 524320 | tf_op jit(solution)/shard_map/ppermute | solution.py:69
  148.4 2.9 %fusion.2 = bf16[512,2048]{0,1:T(8,128)(2,1)S(1)} fusion(bf16[512,2,256]{2,0,1:T(8,128)(2,1)S(1)} %collective-permute-done.1, f32[2048,512,1]{1,0,2:T(8,128)S(1)} %fusion.3, bf16[2,2,2048,256]{3,2,0,1:T(8,128)(2,1)} %collective-permute-done, s32[]{:T(128)S(6)} %select_n.85), kind=kOutput, calls=%fused_computation.13 | convolution fusion | flops 1075838976 | bytes 8912900 | tf_op jit(solution)/shard_map/tpk,pdk->td/dot_general | solution.py:75
  154.7 5.1 %fusion.5 = f32[2048,512,1]{1,0,2:T(8,128)} fusion(bf16[2,2,2,2048,256]{4,3,2,1,0:T(8,128)(2,1)} %bitcast.80, s32[]{:T(128)S(6)} %select_n.80, s32[]{:T(128)S(6)} %select_n.83, bf16[512,2,256]{2,1,0:T(2,128)(2,1)S(1)} %copy-done.6), kind=kOutput, calls=%fused_computation.17 | convolution fusion | flops 1073741824 | bytes 6815752 | tf_op jit(solution)/shard_map/tpk,pdk->td/dot_general | solution.py:74
  159.9 2.8 %fusion.14 = f32[4,128,2048]{2,1,0:T(8,128)} fusion(bf16[4,128,128]{1,2,0:T(8,128)(2,1)S(1)} %get-tuple-element.22, bf16[4,2304,128]{1,2,0:T(8,128)(2,1)S(1)} %copy-done.5), kind=kOutput, calls=%fused_computation.26 | convolution fusion | flops 268435456 | bytes 6422528 | tf_op jit(solution)/shard_map/bnc,bdc->bnd/dot_general | solution.py:174
  162.6 5.3 %copy.59 = f32[512,2048]{0,1:T(8,128)} copy(f32[512,2048]{1,0:T(8,128)} %bitcast.74) | data formatting | bytes 8388608 | tf_op jit(solution)/shard_map/reshape | solution.py:176
  168.0 10.9 %collective-permute-done.2 = bf16[256,2048]{0,1:T(8,128)(2,1)S(1)} collective-permute-done((bf16[256,2048]{0,1:T(8,128)(2,1)}, bf16[256,2048]{0,1:T(8,128)(2,1)S(1)}, u32[]{:S(2)}, u32[]{:S(2)}) %collective-permute-start.2) | collective-permute-done | bytes 1048608 | tf_op jit(solution)/shard_map/ppermute | solution.py:82
  178.9 21.7 %collective-permute-done.3 = bf16[256,2048]{0,1:T(8,128)(2,1)S(1)} collective-permute-done((bf16[256,2048]{0,1:T(8,128)(2,1)}, bf16[256,2048]{0,1:T(8,128)(2,1)S(1)}, u32[]{:S(2)}, u32[]{:S(2)}) %collective-permute-start.3) | collective-permute-done | bytes 1048608 | tf_op jit(solution)/shard_map/ppermute | solution.py:83
  200.6 7.5 %fusion.1 = f32[512,2048]{0,1:T(8,128)} fusion(f32[512,2048]{0,1:T(8,128)} %copy.59, f32[2048,512,1]{1,0,2:T(8,128)} %fusion.5, bf16[512,2,256]{2,0,1:T(8,128)(2,1)S(1)} %collective-permute-done.1, bf16[256,2048]{0,1:T(8,128)(2,1)S(1)} %collective-permute-done.3, bf16[256,2048]{0,1:T(8,128)(2,1)S(1)} %collective-permute-done.2, ...), kind=kOutput, calls=%fused_computation.9 | convolution fusion | flops 1081081856 | bytes 17301508 | tf_op jit(solution)/shard_map/tpk,pdk->td/dot_general | solution.py:75
  208.1 5.3 %copy.54 = f32[512,2048]{1,0:T(8,128)} copy(f32[512,2048]{0,1:T(8,128)} %fusion.1) | data formatting | bytes 8388608
  213.5 26.2 %all-to-all-done = bf16[8,128,2304]{2,1,0:T(8,128)(2,1)} async-done(((bf16[8,128,2304]{2,1,0:T(8,128)(2,1)}), bf16[8,128,2304]{2,1,0:T(8,128)(2,1)}, u32[]{:S(2)}, u32[]{:S(2)}) %all-to-all-start) | async-done | bytes 4718624 | tf_op jit(solution)/shard_map/all_to_all | solution.py:116
  239.6 3.2 %convert_reduce_fusion = f32[128,2304]{1,0:T(8,128)S(1)} fusion(bf16[8,128,2304]{2,1,0:T(8,128)(2,1)} %all-to-all-done), kind=kLoop, calls=%fused_computation.4 | loop fusion | flops 4423680 | bytes 5898240 | tf_op jit(solution)/shard_map/reduce_sum | solution.py:117
  243.9 2.5 copy.55
  247.2 3.5 %fusion.27 = f32[2048,128]{1,0:T(8,128)} fusion(f32[2048,128]{1,0:T(8,128)} %copy.55, f32[2048,128]{1,0:T(8,128)} %param.18, f32[2048,128]{1,0:T(8,128)} %param.17), kind=kLoop, calls=%fused_computation.39 | loop fusion | flops 2883584 | bytes 4194304 | tf_op jit(solution)/shard_map/div | solution.py:22
  (72 shorter events, 23.5 us)
Async XLA Ops:
  7.2 98.8 %copy-start = (bf16[512,2048]{1,0:T(8,128)(2,1)S(1)}, bf16[512,2048]{1,0:T(8,128)(2,1)}, u32[]{:S(2)}) copy-start(bf16[512,2048]{1,0:T(8,128)(2,1)} %param.12) | copy-start | bytes 6291460
  7.2 5.9 %copy-start.3 = (s32[8]{0:T(128)S(1)}, s32[8]{0:T(128)}, u32[]{:S(2)}) copy-start(s32[8]{0:T(128)} %param.23) | copy-start | bytes 100
  7.2 5.3 %copy-start.2 = (s32[8]{0:T(128)S(1)}, s32[8]{0:T(128)}, u32[]{:S(2)}) copy-start(s32[8]{0:T(128)} %param.22) | copy-start | bytes 100
  7.2 86.2 %all-gather.3.cloned.1.call-start = ((), (), s32[]{:S(2)}) async-start(), calls=%async_computation.1 | async-start | bytes 5308416 | tf_op jit(solution)/shard_map/all_gather | solution.py:144
  104.3 1.4 copy-start.4
  105.6 2.6 %copy-start.6 = (bf16[512,2,256]{2,1,0:T(2,128)(2,1)S(1)}, bf16[512,2,256]{2,1,0:T(2,128)(2,1)}, u32[]{:S(2)}) copy-start(bf16[512,2,256]{2,1,0:T(2,128)(2,1)} %param.13) | copy-start | bytes 1572868
  108.6 2.0 collective-permute-start.4
  110.7 9.2 %collective-permute-start.5 = (f32[4,128,128]{1,2,0:T(8,128)S(1)}, f32[4,128,128]{1,2,0:T(8,128)S(1)}, u32[]{:S(2)}, u32[]{:S(2)}) collective-permute-start(f32[4,128,128]{1,2,0:T(8,128)S(1)} %get-tuple-element.24), channel_id=1, source_target_pairs={{0,2},{1,3},{2,0},{3,1},{4,6},{5,7},{6,4},{7,5},{8,10},{9,11},{10,... | collective-permute-start | bytes 786440 | tf_op jit(solution)/shard_map/ppermute | solution.py:35
  112.2 12.5 %collective-permute-start.6 = (f32[4,128,128]{1,2,0:T(8,128)S(1)}, f32[4,128,128]{1,2,0:T(8,128)S(1)}, u32[]{:S(2)}, u32[]{:S(2)}) collective-permute-start(f32[4,128,128]{1,2,0:T(8,128)S(1)} %get-tuple-element.23), channel_id=1, source_target_pairs={{0,2},{1,3},{2,0},{3,1},{4,6},{5,7},{6,4},{7,5},{8,10},{9,11},{10,... | collective-permute-start | bytes 786440 | tf_op jit(solution)/shard_map/ppermute | solution.py:34
  130.8 108.8 %all-to-all-start = ((bf16[8,128,2304]{2,1,0:T(8,128)(2,1)}), bf16[8,128,2304]{2,1,0:T(8,128)(2,1)}, u32[]{:S(2)}, u32[]{:S(2)}) async-start(bf16[8,128,2304]{2,1,0:T(8,128)(2,1)} %pad_maximum_fusion), calls=%async_computation | async-start | bytes 9437184 | tf_op jit(solution)/shard_map/all_to_all | solution.py:116
  140.1 8.3 %collective-permute-start = (bf16[2,2,2048,256]{3,2,0,1:T(8,128)(2,1)}, bf16[2,2,2048,256]{3,2,0,1:T(8,128)(2,1)}, u32[]{:S(2)}, u32[]{:S(2)}) collective-permute-start(bf16[2,2,2048,256]{3,2,0,1:T(8,128)(2,1)} %copy_bitcast_fusion), channel_id=1, source_target_pairs={{0,1},{1,0},{2,3},{3,2},{4,5},{5,4},{6,7},{7,6},{8,9},{9,8},{10,11... | collective-permute-start | bytes 12582920 | tf_op jit(solution)/shard_map/ppermute | solution.py:68
  140.2 7.5 %collective-permute-start.1 = (bf16[512,2,256]{2,0,1:T(8,128)(2,1)S(1)}, bf16[512,2,256]{2,0,1:T(8,128)(2,1)S(1)}, u32[]{:S(2)}, u32[]{:S(2)}) collective-permute-start(bf16[512,2,256]{2,0,1:T(8,128)(2,1)S(1)} %copy.35), channel_id=1, source_target_pairs={{0,1},{1,0},{2,3},{3,2},{4,5},{5,4},{6,7},{7,6},{8,9},{9,8},{10,11... | collective-permute-start | bytes 1572872 | tf_op jit(solution)/shard_map/ppermute | solution.py:69
  152.7 26.2 %collective-permute-start.2 = (bf16[256,2048]{0,1:T(8,128)(2,1)}, bf16[256,2048]{0,1:T(8,128)(2,1)S(1)}, u32[]{:S(2)}, u32[]{:S(2)}) collective-permute-start(bf16[256,2048]{0,1:T(8,128)(2,1)} %get-tuple-element.19), channel_id=1, source_target_pairs={{0,2},{1,3},{2,0},{3,1},{4,6},{5,7},{6,4},{7,5},{8,10},{9,11},{10,... | collective-permute-start | bytes 3145736 | tf_op jit(solution)/shard_map/ppermute | solution.py:82
  154.2 46.4 %collective-permute-start.3 = (bf16[256,2048]{0,1:T(8,128)(2,1)}, bf16[256,2048]{0,1:T(8,128)(2,1)S(1)}, u32[]{:S(2)}, u32[]{:S(2)}) collective-permute-start(bf16[256,2048]{0,1:T(8,128)(2,1)} %get-tuple-element.20), channel_id=1, source_target_pairs={{0,2},{1,3},{2,0},{3,1},{4,6},{5,7},{6,4},{7,5},{8,10},{9,11},{10,... | collective-permute-start | bytes 3145736 | tf_op jit(solution)/shard_map/ppermute | solution.py:83
  154.7 5.1 %copy-start.5 = (bf16[4,2304,128]{1,2,0:T(8,128)(2,1)S(1)}, bf16[4,2304,128]{1,2,0:T(8,128)(2,1)}, u32[]{:S(2)}) copy-start(bf16[4,2304,128]{1,2,0:T(8,128)(2,1)} %copy-done.4) | copy-start | bytes 7077892
  213.4 33.0 %copy-start.7 = (f32[128,256]{1,0:T(8,128)S(1)}, f32[128,256]{1,0:T(8,128)}, u32[]{:S(2)}) copy-start(f32[128,256]{1,0:T(8,128)} %param.20) | copy-start | bytes 393220
  213.5 33.0 %copy-start.8 = (f32[128,256]{1,0:T(8,128)S(1)}, f32[128,256]{1,0:T(8,128)}, u32[]{:S(2)}) copy-start(f32[128,256]{1,0:T(8,128)} %param.19) | copy-start | bytes 393220
  239.6 11.1 %copy-start.1 = (bf16[512,2048]{1,0:T(8,128)(2,1)S(1)}, bf16[512,2048]{1,0:T(8,128)(2,1)}, u32[]{:S(2)}) copy-start(bf16[512,2048]{1,0:T(8,128)(2,1)} %param.12) | copy-start | bytes 6291460
Sparse Core Ops, SparseCore 0:
  10.8 82.5 all-gather.2

commit v8 on v7

--- a/solution.py
+++ b/solution.py
@@ -106,16 +106,32 @@
     slot_tenant = jnp.argsort(tenant_slot)
     slot_scale = adapter_alpha_factor / tenant_rank[slot_tenant].astype(jnp.float32)
     b_sc = b_sc * slot_scale[:, None, None, None]
-    send = jnp.concatenate(
-        [
-            a_sc.astype(jnp.bfloat16),
-            b_sc.reshape(TENANTS, rank_width, kv_shard).astype(jnp.bfloat16),
-        ],
-        axis=2,
-    )
-    recv = lax.all_to_all(send, "dp", split_axis=0, concat_axis=0, tiled=True)
-    own = jnp.sum(recv.astype(jnp.float32), axis=0)
+    full = jnp.concatenate([a_sc, b_sc.reshape(TENANTS, rank_width, kv_shard)], axis=2)
+    own = grouped_exchange(full)
     return own[:, :feat_shard].T, own[:, feat_shard:]
+
+
+def grouped_exchange(full):
+    n = full.shape[0]
+    if n % 4:
+        recv = lax.all_to_all(full.astype(jnp.bfloat16), "dp", split_axis=0, concat_axis=0, tiled=True)
+        return jnp.sum(recv.astype(jnp.float32), axis=0)
+    groups = n // 4
+    me = lax.axis_index("dp")
+    member = me % 4
+    group = me // 4
+    by_member = full.reshape(groups, 4, *full.shape[1:])
+    acc = lax.dynamic_index_in_dim(by_member, member, axis=1, keepdims=False)
+    for m in (1, 2, 3):
+        pairs = [(i, (i // 4) * 4 + ((i % 4) ^ m)) for i in range(n)]
+        part = lax.dynamic_index_in_dim(by_member, member ^ m, axis=1, keepdims=False)
+        acc = acc + lax.ppermute(part.astype(jnp.bfloat16), "dp", pairs).astype(jnp.float32)
+    total = lax.dynamic_index_in_dim(acc, group, axis=0, keepdims=False)
+    for m in range(1, groups):
+        pairs = [(i, ((i // 4 + m) % groups) * 4 + i % 4) for i in range(n)]
+        part = lax.dynamic_index_in_dim(acc, (group + m) % groups, axis=0, keepdims=False)
+        total = total + lax.ppermute(part.astype(jnp.bfloat16), "dp", pairs).astype(jnp.float32)
+    return total
 
 
 def local(

time: 258 us -> 246 us (0.953)
  waiting for transfers between devices: 156 us -> 132 us
  local copies, waits for them, and re-layouts: 34 us -> 42.8 us
    ppermute x0 -> x4, waiting for transfers between devices: none -> 51.1 us  [grouped_exchange(): lax.ppermute(part.astype(jnp.bfloat16), 'dp', pairs).astype(jnp.float32)]
    all_to_all x1 -> x0, waiting for transfers between devices: 26.2 us -> none  [slot_major_grads(): recv = lax.all_to_all(send, 'dp', split_axis=0, concat_axis=0, tiled=True)]
    ppermute x1, waiting for transfers between devices: 21.7 us -> 0.01 us  [frozen_gradient(): lax.ppermute(far_part[half:], 'tensor', row_pairs)]
    ppermute x1, waiting for transfers between devices: 10.9 us -> 0.01 us  [frozen_gradient(): lax.ppermute(far_part[:half], 'tensor', row_pairs)]
    all_gather x1, waiting for transfers between devices: 78.6 us -> 68.7 us  [local(): packed_all = lax.all_gather(packed, 'dp', axis=0, tiled=False)]
    unnamed x21 -> x39, local copies, waits for them, and re-layouts: 9.35 us -> 15.3 us
    ppermute x0 -> x4, starting transfers between devices: none -> 5.02 us  [grouped_exchange(): lax.ppermute(part.astype(jnp.bfloat16), 'dp', pairs).astype(jnp.float32)]
    all_to_all x1 -> x0, starting transfers between devices: 4.78 us -> none  [slot_major_grads(): recv = lax.all_to_all(send, 'dp', split_axis=0, concat_axis=0, tiled=True)]
  transfers between devices with their start and end apart: 9 -> 12, of which waited for: 9 -> 7; matrix products, arithmetic and copies ran while one was open for 16% -> 29% of each run, Pallas kernels for 0% -> 0%
where the time goes in v8:
time: 246 us; the launch traced here: 245 us
  waiting for transfers between devices  132 us (54%)
  local copies, waits for them, and re-layouts  42.8 us (17%)
  matrix products  27.8 us (11%)
  other arithmetic  18.7 us (8%)
  between operations  14.4 us (6%)
  starting transfers between devices  9.69 us (4%)
    all_gather x1, waiting for transfers between devices, local(): packed_all = lax.all_gather(packed, 'dp', axis=0, tiled=False)  68.7 us
    ppermute x4, waiting for transfers between devices, grouped_exchange(): lax.ppermute(part.astype(jnp.bfloat16), 'dp', pairs).astype(jnp.float32)  51.1 us
    unnamed x39, local copies, waits for them, and re-layouts  15.3 us
    dot_general x2, matrix products, chip_partial(): jnp.einsum('tpk,pdk->td', grad_out, own, preferred_element_type=jnp.float32)  10.1 us
    gather x2, local copies, waits for them, and re-layouts, local(): picked = jnp.take(packed_all, block_slot, axis=0)  8.97 us
    dot_general x2, matrix products, chip_partial(): jnp.einsum('tpk,pdk->td', partner_dy, other, preferred_element_type=jnp.f...  8.65 us
    ppermute x1, waiting for transfers between devices, tensor_sum_pair(): second = second + lax.ppermute(second, 'tensor', pairs)  7.27 us
    reshape x1, local copies, waits for them, and re-layouts, local(): adapter_gradient_term = jnp.einsum('bnc,bdc->bnd', backward_token_rows, a...  5.38 us
  transfers between devices with their start and end apart: 12, of which 7 were waited for; matrix products, arithmetic and copies ran while one was open for 29% of the time, Pallas kernels for 0%

profile of v8, /device:TPU:0, one launch (start us, length us, event | category | flops | bytes accessed | tf_op | source)
XLA Modules:
  0.0 245.0 jit_solution(6852486175081633792)
XLA Ops:
  10.5 4.5 %copy_bitcast_fusion = bf16[2,2,2048,256]{3,2,0,1:T(8,128)(2,1)} fusion(bf16[2,2,2,2048,256]{4,3,2,1,0:T(8,128)(2,1)} %bitcast.120, s32[]{:T(128)S(6)} %select_n.115), kind=kLoop, calls=%fused_computation.17 | loop fusion | bytes 8388612 | tf_op jit(solution)/shard_map/jit(dynamic_index_in_dim)/squeeze | solution.py:64
  19.6 5.2 %fusion.17 = f32[2048,512,1]{1,0,2:T(8,128)} fusion(bf16[2,2,2,2048,256]{4,3,2,1,0:T(8,128)(2,1)} %bitcast.121, s32[]{:T(128)S(6)} %select_n.117, s32[]{:T(128)S(6)} %select_n.114, bf16[512,2,256]{2,1,0:T(2,128)(2,1)} %param.13), kind=kOutput, calls=%fused_computation.34 | convolution fusion | flops 1073741824 | bytes 6815752 | tf_op jit(solution)/shard_map/tpk,pdk->td/dot_general | solution.py:74
  24.7 68.7 %all-gather.3.cloned.1.call-done = bf16[18432,128]{1,0:T(8,128)(2,1)} async-done(((bf16[2304,128]{1,0:T(8,128)(2,1)}), bf16[18432,128]{1,0:T(8,128)(2,1)}) %all-gather.3.cloned.1.call-update) | async-done | bytes 4718608 | tf_op jit(solution)/shard_map/all_gather | solution.py:160
  93.4 4.6 %gather_fusion.1 = bf16[4,2304,128]{2,1,0:T(8,128)(2,1)} fusion(bf16[8,2304,128]{2,1,0:T(8,128)(2,1)} %bitcast.125, s32[1024]{0:T(1024)S(1)} %pad_clamp_fusion.1), kind=kCustom, calls=%fused_computation.1 | custom fusion | bytes 4718608 | tf_op jit(solution)/shard_map/jit(_take)/gather | solution.py:164
  98.1 4.3 %copy.40 = bf16[4,2304,128]{1,2,0:T(8,128)(2,1)} copy(bf16[4,2304,128]{2,1,0:T(8,128)(2,1)} %gather_fusion.1) | data formatting | bytes 4718592 | tf_op jit(solution)/shard_map/jit(_take)/gather | solution.py:164
  102.4 2.0 broadcast_select_fusion
  109.7 2.3 fusion.37
  112.2 4.9 %fusion.19 = f32[2048,512,1]{1,0,2:T(8,128)} fusion(bf16[2,2,2,2048,256]{4,3,2,1,0:T(8,128)(2,1)} %bitcast.122, s32[]{:T(128)S(6)} %select_n.111, s32[]{:T(128)S(6)} %select_n.114, bf16[512,2,256]{2,1,0:T(2,128)(2,1)S(1)} %copy-done.12), kind=kOutput, calls=%fused_computation.36 | convolution fusion | flops 1073741824 | bytes 6815752 | tf_op jit(solution)/shard_map/tpk,pdk->td/dot_general | solution.py:74
  120.1 7.3 %collective-permute-done.5 = f32[4,128,128]{1,2,0:T(8,128)S(1)} collective-permute-done((f32[4,128,128]{1,2,0:T(8,128)}, f32[4,128,128]{1,2,0:T(8,128)S(1)}, u32[]{:S(2)}, u32[]{:S(2)}) %collective-permute-start.5) | collective-permute-done | bytes 262176 | tf_op jit(solution)/shard_map/ppermute | solution.py:35
  128.0 4.6 %collective-permute-done.6 = f32[4,128,128]{1,2,0:T(8,128)} collective-permute-done((f32[4,128,128]{1,2,0:T(8,128)}, f32[4,128,128]{1,2,0:T(8,128)}, u32[]{:S(2)}, u32[]{:S(2)}) %collective-permute-start.6) | collective-permute-done | bytes 262176 | tf_op jit(solution)/shard_map/ppermute | solution.py:34
  134.3 2.3 fusion.21
  139.2 2.9 %copy-done.4 = f32[8,128,2048]{2,1,0:T(8,128)} copy-done((f32[8,128,2048]{2,1,0:T(8,128)}, f32[8,128,2048]{2,1,0:T(8,128)S(1)}, u32[]{:S(2)}) %copy-start.4) | copy-done | bytes 8388632
  143.2 2.4 collective-permute-start.9
  145.6 3.0 %fusion.2 = bf16[512,2048]{0,1:T(8,128)(2,1)S(1)} fusion(bf16[512,2,256]{2,0,1:T(8,128)(2,1)S(1)} %collective-permute-done.1, f32[2048,512,1]{1,0,2:T(8,128)S(1)} %copy-done.10, bf16[2,2,2048,256]{3,2,0,1:T(8,128)(2,1)} %collective-permute-done, s32[]{:T(128)S(6)} %select_n.116), kind=kOutput, calls=%fused_computation.18 | convolution fusion | flops 1075838976 | bytes 8912900 | tf_op jit(solution)/shard_map/tpk,pdk->td/dot_general | solution.py:75
  152.1 2.8 %fusion.29 = f32[4,128,2048]{2,1,0:T(8,128)} fusion(bf16[4,128,128]{1,2,0:T(8,128)(2,1)S(1)} %get-tuple-element.25, bf16[4,2304,128]{1,2,0:T(8,128)(2,1)S(1)} %copy-done.7), kind=kOutput, calls=%fused_computation.46 | convolution fusion | flops 268435456 | bytes 6422528 | tf_op jit(solution)/shard_map/bnc,bdc->bnd/dot_general | solution.py:190
  154.9 5.4 %copy.61 = f32[512,2048]{0,1:T(8,128)} copy(f32[512,2048]{1,0:T(8,128)} %bitcast.115) | data formatting | bytes 8388608 | tf_op jit(solution)/shard_map/reshape | solution.py:192
  160.2 10.1 %collective-permute-done.7 = bf16[2,128,2304]{2,1,0:T(8,128)(2,1)} collective-permute-done((bf16[2,128,2304]{2,1,0:T(8,128)(2,1)}, bf16[2,128,2304]{2,1,0:T(8,128)(2,1)}, u32[]{:S(2)}, u32[]{:S(2)}) %collective-permute-start.7) | collective-permute-done | bytes 1179680 | tf_op jit(solution)/shard_map/ppermute | solution.py:128
  171.8 24.6 %collective-permute-done.9 = bf16[2,128,2304]{2,1,0:T(8,128)(2,1)} collective-permute-done((bf16[2,128,2304]{2,1,0:T(8,128)(2,1)}, bf16[2,128,2304]{2,1,0:T(8,128)(2,1)}, u32[]{:S(2)}, u32[]{:S(2)}) %collective-permute-start.9) | collective-permute-done | bytes 1179680 | tf_op jit(solution)/shard_map/ppermute | solution.py:128
  196.4 3.2 %fusion.10 = f32[2,128,2304]{2,1,0:T(8,128)S(1)} fusion(s32[]{:T(128)S(6)} %select_n.127, f32[2,4,128,2048]{3,2,1,0:T(8,128)} %bitcast.114, f32[2,4,128,256]{3,2,1,0:T(8,128)S(1)} %bitcast.117, bf16[2,128,2304]{2,1,0:T(8,128)(2,1)} %collective-permute-done.9, bf16[2,128,2304]{2,1,0:T(8,128)(2,1)} %collective-permute-done.8, ...), kind=kLoop, calls=%fused_computation.26 | loop fusion | flops 4128768 | bytes 15335428 | tf_op jit(solution)/shard_map/add | solution.py:128
  202.7 5.6 %fusion.1 = f32[512,2048]{0,1:T(8,128)} fusion(f32[512,2048]{0,1:T(8,128)S(1)} %copy-done.5, f32[2048,512,1]{1,0,2:T(8,128)S(1)} %copy-done.9, bf16[512,2,256]{2,0,1:T(8,128)(2,1)S(1)} %collective-permute-done.1, bf16[256,2048]{0,1:T(8,128)(2,1)} %collective-permute-done.3, bf16[256,2048]{0,1:T(8,128)(2,1)S(1)} %collective-permute-done.2, ...), kind=kOutput, calls=%fused_computation.15 | convolution fusion | flops 1081081856 | bytes 17301508 | tf_op jit(solution)/shard_map/tpk,pdk->td/dot_general | solution.py:75
  208.3 5.3 %copy.56 = f32[512,2048]{1,0:T(8,128)} copy(f32[512,2048]{0,1:T(8,128)} %fusion.1) | data formatting | bytes 8388608
  213.7 14.9 %collective-permute-done.10 = bf16[128,2304]{1,0:T(8,128)(2,1)} collective-permute-done((bf16[128,2304]{1,0:T(8,128)(2,1)S(1)}, bf16[128,2304]{1,0:T(8,128)(2,1)}, u32[]{:S(2)}, u32[]{:S(2)}) %collective-permute-start.10) | collective-permute-done | bytes 589856 | tf_op jit(solution)/shard_map/ppermute | solution.py:133
  231.2 2.7 %copy.57 = f32[2048,128]{1,0:T(8,128)} copy(f32[2048,128]{0,1:T(8,128)} %slice_bitcast_fusion) | data formatting | bytes 2097152
  234.7 3.5 %fusion.44 = f32[2048,128]{1,0:T(8,128)} fusion(f32[2048,128]{1,0:T(8,128)} %copy.57, f32[2048,128]{1,0:T(8,128)} %param.18, f32[2048,128]{1,0:T(8,128)} %param.17), kind=kLoop, calls=%fused_computation.63 | loop fusion | flops 2883584 | bytes 4194304 | tf_op jit(solution)/shard_map/div | solution.py:22
  (98 shorter events, 33.4 us)
Async XLA Ops:
  7.2 102.5 %copy-start = (bf16[512,2048]{1,0:T(8,128)(2,1)S(1)}, bf16[512,2048]{1,0:T(8,128)(2,1)}, u32[]{:S(2)}) copy-start(bf16[512,2048]{1,0:T(8,128)(2,1)} %param.12) | copy-start | bytes 6291460
  7.2 86.3 %all-gather.3.cloned.1.call-start = ((), (), s32[]{:S(2)}) async-start(), calls=%async_computation | async-start | bytes 5308416 | tf_op jit(solution)/shard_map/all_gather | solution.py:160
  10.5 5.0 %copy-start.11 = (bf16[512,2,256]{2,1,0:T(2,128)(2,1)S(1)}, bf16[512,2,256]{2,1,0:T(2,128)(2,1)}, u32[]{:S(2)}) copy-start(bf16[512,2,256]{2,1,0:T(2,128)(2,1)} %param.13) | copy-start | bytes 1572868
  10.5 5.9 %copy-start.17 = (s32[4]{0:T(128)S(1)}, s32[4]{0:T(128)}, u32[]{:S(2)}) copy-start(s32[4]{0:T(128)} %param.21) | copy-start | bytes 52
  10.5 5.9 %copy-start.3 = (s32[8]{0:T(128)S(1)}, s32[8]{0:T(128)}, u32[]{:S(2)}) copy-start(s32[8]{0:T(128)} %param.23) | copy-start | bytes 100
  10.5 6.6 %copy-start.2 = (s32[8]{0:T(128)S(1)}, s32[8]{0:T(128)}, u32[]{:S(2)}) copy-start(s32[8]{0:T(128)} %param.22) | copy-start | bytes 100
  15.0 130.5 %collective-permute-start = (bf16[2,2,2048,256]{3,2,0,1:T(8,128)(2,1)}, bf16[2,2,2048,256]{3,2,0,1:T(8,128)(2,1)}, u32[]{:S(2)}, u32[]{:S(2)}) collective-permute-start(bf16[2,2,2048,256]{3,2,0,1:T(8,128)(2,1)} %copy_bitcast_fusion), channel_id=1, source_target_pairs={{0,1},{1,0},{2,3},{3,2},{4,5},{5,4},{6,7},{7,6},{8,9},{9,8},{10,11... | collective-permute-start | bytes 12582920 | tf_op jit(solution)/shard_map/ppermute | solution.py:68
  16.4 129.2 %collective-permute-start.1 = (bf16[512,2,256]{2,0,1:T(8,128)(2,1)}, bf16[512,2,256]{2,0,1:T(8,128)(2,1)S(1)}, u32[]{:S(2)}, u32[]{:S(2)}) collective-permute-start(bf16[512,2,256]{2,0,1:T(8,128)(2,1)} %copy.35), channel_id=1, source_target_pairs={{0,1},{1,0},{2,3},{3,2},{4,5},{5,4},{6,7},{7,6},{8,9},{9,8},{10,11... | collective-permute-start | bytes 1572872 | tf_op jit(solution)/shard_map/ppermute | solution.py:69
  102.4 6.0 %copy-start.12 = (bf16[512,2,256]{2,1,0:T(2,128)(2,1)S(1)}, bf16[512,2,256]{2,1,0:T(2,128)(2,1)}, u32[]{:S(2)}) copy-start(bf16[512,2,256]{2,1,0:T(2,128)(2,1)} %param.13) | copy-start | bytes 1572868
  112.0 5.1 %collective-permute-start.4 = (f32[4,128,256]{1,2,0:T(8,128)S(1)}, f32[4,128,256]{1,2,0:T(8,128)S(1)}, u32[]{:S(2)}, u32[]{:S(2)}) collective-permute-start(f32[4,128,256]{1,2,0:T(8,128)S(1)} %pad_maximum_fusion.1), channel_id=1, source_target_pairs={{0,1},{1,0},{2,3},{3,2},{4,5},{5,4},{6,7},{7,6},{8,9},{9,8},{10,11... | collective-permute-start | bytes 1572872 | tf_op jit(solution)/shard_map/ppermute | solution.py:29
  118.0 9.3 %collective-permute-start.5 = (f32[4,128,128]{1,2,0:T(8,128)}, f32[4,128,128]{1,2,0:T(8,128)S(1)}, u32[]{:S(2)}, u32[]{:S(2)}) collective-permute-start(f32[4,128,128]{1,2,0:T(8,128)} %get-tuple-element.27), channel_id=1, source_target_pairs={{0,2},{1,3},{2,0},{3,1},{4,6},{5,7},{6,4},{7,5},{8,10},{9,11},{10,... | collective-permute-start | bytes 786440 | tf_op jit(solution)/shard_map/ppermute | solution.py:35
  119.5 13.2 %collective-permute-start.6 = (f32[4,128,128]{1,2,0:T(8,128)}, f32[4,128,128]{1,2,0:T(8,128)}, u32[]{:S(2)}, u32[]{:S(2)}) collective-permute-start(f32[4,128,128]{1,2,0:T(8,128)} %get-tuple-element.26), channel_id=1, source_target_pairs={{0,2},{1,3},{2,0},{3,1},{4,6},{5,7},{6,4},{7,5},{8,10},{9,11},{10,... | collective-permute-start | bytes 786440 | tf_op jit(solution)/shard_map/ppermute | solution.py:34
  136.7 5.4 %copy-start.4 = (f32[8,128,2048]{2,1,0:T(8,128)}, f32[8,128,2048]{2,1,0:T(8,128)S(1)}, u32[]{:S(2)}) copy-start(f32[8,128,2048]{2,1,0:T(8,128)S(1)} %fusion.21) | copy-start | bytes 25165828
  137.2 8.3 %copy-start.10 = (f32[2048,512,1]{1,0,2:T(8,128)S(1)}, f32[2048,512,1]{1,0,2:T(8,128)}, u32[]{:S(2)}) copy-start(f32[2048,512,1]{1,0,2:T(8,128)} %fusion.17) | copy-start | bytes 12582916
  142.1 28.3 %collective-permute-start.7 = (bf16[2,128,2304]{2,1,0:T(8,128)(2,1)}, bf16[2,128,2304]{2,1,0:T(8,128)(2,1)}, u32[]{:S(2)}, u32[]{:S(2)}) collective-permute-start(bf16[2,128,2304]{2,1,0:T(8,128)(2,1)} %get-tuple-element.19), channel_id=1, source_target_pairs={{0,4},{4,0},{8,12},{12,8},{16,20},{20,16},{24,28},{28,24},{1,5},{5... | collective-permute-start | bytes 3538952 | tf_op jit(solution)/shard_map/ppermute | solution.py:128
  142.6 29.2 %collective-permute-start.8 = (bf16[2,128,2304]{2,1,0:T(8,128)(2,1)}, bf16[2,128,2304]{2,1,0:T(8,128)(2,1)}, u32[]{:S(2)}, u32[]{:S(2)}) collective-permute-start(bf16[2,128,2304]{2,1,0:T(8,128)(2,1)} %get-tuple-element.20), channel_id=1, source_target_pairs={{0,8},{4,12},{8,0},{12,4},{16,24},{20,28},{24,16},{28,20},{1,9},{5... | collective-permute-start | bytes 3538952 | tf_op jit(solution)/shard_map/ppermute | solution.py:128
  143.2 53.3 %collective-permute-start.9 = (bf16[2,128,2304]{2,1,0:T(8,128)(2,1)}, bf16[2,128,2304]{2,1,0:T(8,128)(2,1)}, u32[]{:S(2)}, u32[]{:S(2)}) collective-permute-start(bf16[2,128,2304]{2,1,0:T(8,128)(2,1)} %get-tuple-element.21), channel_id=1, source_target_pairs={{0,12},{4,8},{8,4},{12,0},{16,28},{20,24},{24,20},{28,16},{1,13},{... | collective-permute-start | bytes 3538952 | tf_op jit(solution)/shard_map/ppermute | solution.py:128
  150.1 52.6 %collective-permute-start.2 = (bf16[256,2048]{0,1:T(8,128)(2,1)}, bf16[256,2048]{0,1:T(8,128)(2,1)S(1)}, u32[]{:S(2)}, u32[]{:S(2)}) collective-permute-start(bf16[256,2048]{0,1:T(8,128)(2,1)} %get-tuple-element.22), channel_id=1, source_target_pairs={{0,2},{1,3},{2,0},{3,1},{4,6},{5,7},{6,4},{7,5},{8,10},{9,11},{10,... | collective-permute-start | bytes 3145736 | tf_op jit(solution)/shard_map/ppermute | solution.py:82
  151.5 51.2 %collective-permute-start.3 = (bf16[256,2048]{0,1:T(8,128)(2,1)}, bf16[256,2048]{0,1:T(8,128)(2,1)}, u32[]{:S(2)}, u32[]{:S(2)}) collective-permute-start(bf16[256,2048]{0,1:T(8,128)(2,1)} %get-tuple-element.23), channel_id=1, source_target_pairs={{0,2},{1,3},{2,0},{3,1},{4,6},{5,7},{6,4},{7,5},{8,10},{9,11},{10,... | collective-permute-start | bytes 3145736 | tf_op jit(solution)/shard_map/ppermute | solution.py:83
  196.4 6.2 %copy-start.5 = (f32[512,2048]{0,1:T(8,128)S(1)}, f32[512,2048]{0,1:T(8,128)}, u32[]{:S(2)}) copy-start(f32[512,2048]{0,1:T(8,128)} %copy.61) | copy-start | bytes 12582916
  196.4 6.3 %copy-start.9 = (f32[2048,512,1]{1,0,2:T(8,128)S(1)}, f32[2048,512,1]{1,0,2:T(8,128)}, u32[]{:S(2)}) copy-start(f32[2048,512,1]{1,0,2:T(8,128)} %fusion.19) | copy-start | bytes 12582916
  201.1 27.4 %collective-permute-start.10 = (bf16[128,2304]{1,0:T(8,128)(2,1)S(1)}, bf16[128,2304]{1,0:T(8,128)(2,1)}, u32[]{:S(2)}, u32[]{:S(2)}) collective-permute-start(bf16[128,2304]{1,0:T(8,128)(2,1)S(1)} %fusion.49), channel_id=1, source_target_pairs={{0,16},{4,20},{8,24},{12,28},{16,0},{20,4},{24,8},{28,12},{1,17},{... | collective-permute-start | bytes 1769480 | tf_op jit(solution)/shard_map/ppermute | solution.py:133
  230.1 3.8 %copy-start.15 = (f32[128,256]{1,0:T(8,128)S(1)}, f32[128,256]{1,0:T(8,128)}, u32[]{:S(2)}) copy-start(f32[128,256]{1,0:T(8,128)} %param.20) | copy-start | bytes 393220
  231.2 6.9 %copy-start.1 = (bf16[512,2048]{1,0:T(8,128)(2,1)S(1)}, bf16[512,2048]{1,0:T(8,128)(2,1)}, u32[]{:S(2)}) copy-start(bf16[512,2048]{1,0:T(8,128)(2,1)} %param.12) | copy-start | bytes 6291460
  (6 other events, 13.1 us)
Sparse Core Ops, SparseCore 0:
  10.8 82.6 all-gather.2

commit v9 on v8

--- a/solution.py
+++ b/solution.py
@@ -107,8 +107,39 @@
     slot_scale = adapter_alpha_factor / tenant_rank[slot_tenant].astype(jnp.float32)
     b_sc = b_sc * slot_scale[:, None, None, None]
     full = jnp.concatenate([a_sc, b_sc.reshape(TENANTS, rank_width, kv_shard)], axis=2)
-    own = grouped_exchange(full)
+    if full.shape[0] % 4:
+        own = grouped_exchange(full)
+    else:
+        split = full.shape[2] // 2
+        first = group_stage(full[..., :split])
+        later, first = lax.optimization_barrier((full[..., split:], first))
+        second = group_stage(later)
+        own = jnp.concatenate([cross_stage(first), cross_stage(second)], axis=-1)
     return own[:, :feat_shard].T, own[:, feat_shard:]
+
+
+def group_stage(full):
+    n = full.shape[0]
+    member = lax.axis_index("dp") % 4
+    by_member = full.reshape(n // 4, 4, *full.shape[1:])
+    acc = lax.dynamic_index_in_dim(by_member, member, axis=1, keepdims=False)
+    for m in (1, 2, 3):
+        pairs = [(i, (i // 4) * 4 + ((i % 4) ^ m)) for i in range(n)]
+        part = lax.dynamic_index_in_dim(by_member, member ^ m, axis=1, keepdims=False)
+        acc = acc + lax.ppermute(part.astype(jnp.bfloat16), "dp", pairs).astype(jnp.float32)
+    return acc
+
+
+def cross_stage(acc):
+    groups = acc.shape[0]
+    n = groups * 4
+    group = lax.axis_index("dp") // 4
+    total = lax.dynamic_index_in_dim(acc, group, axis=0, keepdims=False)
+    for m in range(1, groups):
+        pairs = [(i, ((i // 4 + m) % groups) * 4 + i % 4) for i in range(n)]
+        part = lax.dynamic_index_in_dim(acc, (group + m) % groups, axis=0, keepdims=False)
+        total = total + lax.ppermute(part.astype(jnp.bfloat16), "dp", pairs).astype(jnp.float32)
+    return total
 
 
 def grouped_exchange(full):

time: 246 us -> 255 us (1.037)
  matrix products: 27.8 us -> 35.7 us
  waiting for transfers between devices: 132 us -> 125 us
  other arithmetic: 18.7 us -> 24.2 us
  starting transfers between devices: 9.69 us -> 14.7 us
    ppermute x4 -> x8, waiting for transfers between devices: 51.1 us -> 35.8 us  [the longest x2 21.9 us: cross_stage(): lax.ppermute(part.astype(jnp.bfloat16), 'dp', pairs).astype(jnp.float32)]
    ppermute x1, waiting for transfers between devices: 0.01 us -> 13.7 us  [frozen_gradient(): lax.ppermute(far_part[half:], 'tensor', row_pairs)]
    slice x0 -> x1, other arithmetic: none -> 6.55 us  [slot_major_grads(): first = group_stage(full[..., :split])]
    ppermute x1, waiting for transfers between devices: 7.27 us -> 1.56 us  [tensor_sum_pair(): second = second + lax.ppermute(second, 'tensor', pairs)]
    unnamed x39 -> x33, local copies, waits for them, and re-layouts: 15.3 us -> 9.82 us
    ppermute x4 -> x8, starting transfers between devices: 5.02 us -> 10 us  [the longest x6 6.98 us: group_stage(): lax.ppermute(part.astype(jnp.bfloat16), 'dp', pairs).astype(jnp.float32)]
    convert_element_type x1 -> x4, local copies, waits for them, and re-layouts: 0.06 us -> 4.66 us  [the longest x2 4.58 us: group_stage(): part.astype(jnp.bfloat16)]
    dot_general x1, matrix products: 2.34 us -> 6.51 us  [slot_major_grads(): jnp.einsum('nsc,nd->scd', back_sel, tokens_in, preferred_element_type=jnp...]
  transfers between devices with their start and end apart: 12 -> 16, of which waited for: 7 -> 9; matrix products, arithmetic and copies ran while one was open for 29% -> 28% of each run, Pallas kernels for 0% -> 0%
where the time goes in v9:
time: 255 us
  waiting for transfers between devices  125 us (49%)
  local copies, waits for them, and re-layouts  40.6 us (16%)
  matrix products  35.7 us (14%)
  other arithmetic  24.2 us (9%)
  starting transfers between devices  14.7 us (6%)
  between operations  14.3 us (6%)
    all_gather x1, waiting for transfers between devices, local(): packed_all = lax.all_gather(packed, 'dp', axis=0, tiled=False)  68.7 us
    ppermute x2, waiting for transfers between devices, cross_stage(): lax.ppermute(part.astype(jnp.bfloat16), 'dp', pairs).astype(jnp.float32)  21.9 us
    ppermute x6, waiting for transfers between devices, group_stage(): lax.ppermute(part.astype(jnp.bfloat16), 'dp', pairs).astype(jnp.float32)  13.9 us
    ppermute x1, waiting for transfers between devices, frozen_gradient(): lax.ppermute(far_part[half:], 'tensor', row_pairs)  13.7 us
    dot_general x2, matrix products, chip_partial(): jnp.einsum('tpk,pdk->td', partner_dy, other, preferred_element_type=jnp.f...  12.5 us
    dot_general x2, matrix products, chip_partial(): jnp.einsum('tpk,pdk->td', grad_out, own, preferred_element_type=jnp.float32)  9.92 us
    unnamed x33, local copies, waits for them, and re-layouts  9.82 us
    gather x2, local copies, waits for them, and re-layouts, local(): picked = jnp.take(packed_all, block_slot, axis=0)  8.91 us
  transfers between devices with their start and end apart: 16, of which 9 were waited for; matrix products, arithmetic and copies ran while one was open for 28% of the time, Pallas kernels for 0%

profile of v9, /device:TPU:0, one launch (start us, length us, event | category | flops | bytes accessed | tf_op | source)
XLA Modules:
  0.0 254.7 jit_solution(3145422844575282795)
XLA Ops:
  10.5 4.5 %copy_bitcast_fusion = bf16[2,2,2048,256]{3,2,0,1:T(8,128)(2,1)} fusion(bf16[2,2,2,2048,256]{4,3,2,1,0:T(8,128)(2,1)} %bitcast.140, s32[]{:T(128)S(6)} %select_n.126), kind=kLoop, calls=%fused_computation.10 | loop fusion | bytes 8388612 | tf_op jit(solution)/shard_map/jit(dynamic_index_in_dim)/squeeze | solution.py:64
  19.7 5.0 %fusion.3 = f32[2048,512,1]{1,0,2:T(8,128)} fusion(bf16[2,2,2,2048,256]{4,3,2,1,0:T(8,128)(2,1)} %bitcast.141, s32[]{:T(128)S(6)} %select_n.128, s32[]{:T(128)S(6)} %select_n.125, bf16[512,2,256]{2,1,0:T(2,128)(2,1)S(1)} %copy-done.10), kind=kOutput, calls=%fused_computation.13 | convolution fusion | flops 1073741824 | bytes 6815752 | tf_op jit(solution)/shard_map/tpk,pdk->td/dot_general | solution.py:74
  24.7 68.7 %all-gather.3.cloned.1.call-done = bf16[18432,128]{1,0:T(8,128)(2,1)} async-done(((bf16[2304,128]{1,0:T(8,128)(2,1)}), bf16[18432,128]{1,0:T(8,128)(2,1)}) %all-gather.3.cloned.1.call-update) | async-done | bytes 4718608 | tf_op jit(solution)/shard_map/all_gather | solution.py:191
  93.4 4.6 %gather_fusion.1 = bf16[4,2304,128]{2,1,0:T(8,128)(2,1)} fusion(bf16[8,2304,128]{2,1,0:T(8,128)(2,1)} %bitcast.145, s32[1024]{0:T(1024)S(1)} %pad_clamp_fusion.1), kind=kCustom, calls=%fused_computation.1 | custom fusion | bytes 4718608 | tf_op jit(solution)/shard_map/jit(_take)/gather | solution.py:195
  98.0 4.3 %copy.46 = bf16[4,2304,128]{1,2,0:T(8,128)(2,1)} copy(bf16[4,2304,128]{2,1,0:T(8,128)(2,1)} %gather_fusion.1) | data formatting | bytes 4718592 | tf_op jit(solution)/shard_map/jit(_take)/gather | solution.py:195
  109.6 2.3 fusion.24
  112.8 4.9 %fusion.5 = f32[2048,512,1]{1,0,2:T(8,128)} fusion(bf16[2,2,2,2048,256]{4,3,2,1,0:T(8,128)(2,1)} %bitcast.142, s32[]{:T(128)S(6)} %select_n.122, s32[]{:T(128)S(6)} %select_n.125, bf16[512,2,256]{2,1,0:T(2,128)(2,1)S(1)} %copy-done.10), kind=kOutput, calls=%fused_computation.15 | convolution fusion | flops 1073741824 | bytes 6815752 | tf_op jit(solution)/shard_map/tpk,pdk->td/dot_general | solution.py:74
  121.0 5.5 %fusion.2 = bf16[512,2048]{0,1:T(8,128)(2,1)} fusion(bf16[512,2,256]{2,0,1:T(8,128)(2,1)S(1)} %collective-permute-done.1, f32[2048,512,1]{1,0,2:T(8,128)} %fusion.3, bf16[2,2,2048,256]{3,2,0,1:T(8,128)(2,1)} %collective-permute-done, s32[]{:T(128)S(6)} %select_n.127), kind=kOutput, calls=%fused_computation.11 | convolution fusion | flops 1075838976 | bytes 8912900 | tf_op jit(solution)/shard_map/tpk,pdk->td/dot_general | solution.py:75
  128.1 5.2 %collective-permute-done.6 = f32[4,128,128]{1,2,0:T(8,128)S(1)} collective-permute-done((f32[4,128,128]{1,2,0:T(8,128)S(1)}, f32[4,128,128]{1,2,0:T(8,128)S(1)}, u32[]{:S(2)}, u32[]{:S(2)}) %collective-permute-start.6) | collective-permute-done | bytes 262176 | tf_op jit(solution)/shard_map/ppermute | solution.py:34
  134.6 6.5 %fusion.7 = f32[8,128,2048]{2,1,0:T(8,128)} fusion(bf16[512,2048]{1,0:T(8,128)(2,1)S(1)} %copy-done, pred[512,8]{0,1:T(8,128)(4,1)S(1)} %iota_compare_fusion, bf16[512,128]{0,1:T(8,128)(2,1)} %copy.53), kind=kOutput, calls=%fused_computation.17 | convolution fusion | flops 2148007936 | bytes 10620928 | tf_op jit(solution)/shard_map/nsc,nd->scd/dot_general | solution.py:100
  141.7 6.6 %fusion.68 = (f32[8,128,1152]{2,1,0:T(8,128)S(1)}, f32[8,128,1152]{2,1,0:T(8,128)}) fusion(f32[8,128,2048]{2,1,0:T(8,128)} %fusion.7, f32[8,128,256]{2,1,0:T(8,128)S(1)} %bitcast.137), kind=kLoop, calls=%fused_computation.112 | loop fusion | flops 1179648 | bytes 23592960 | tf_op jit(solution)/shard_map/slice | solution.py:114
  150.6 2.4 collective-permute-start.9
  156.5 2.8 %fusion.15 = f32[4,128,2048]{2,1,0:T(8,128)} fusion(bf16[4,128,128]{1,2,0:T(8,128)(2,1)S(1)} %get-tuple-element.34, bf16[4,2304,128]{1,2,0:T(8,128)(2,1)S(1)} %copy-done.7), kind=kOutput, calls=%fused_computation.25 | convolution fusion | flops 268435456 | bytes 6422528 | tf_op jit(solution)/shard_map/bnc,bdc->bnd/dot_general | solution.py:221
  159.2 5.4 %copy.71 = f32[512,2048]{0,1:T(8,128)} copy(f32[512,2048]{1,0:T(8,128)} %bitcast.132) | data formatting | bytes 8388608 | tf_op jit(solution)/shard_map/reshape | solution.py:223
  166.6 12.0 %collective-permute-done.9 = bf16[2,128,1152]{2,1,0:T(8,128)(2,1)} collective-permute-done((bf16[2,128,1152]{2,1,0:T(8,128)(2,1)}, bf16[2,128,1152]{2,1,0:T(8,128)(2,1)}, u32[]{:S(2)}, u32[]{:S(2)}) %collective-permute-start.9) | collective-permute-done | bytes 589856 | tf_op jit(solution)/shard_map/ppermute | solution.py:129
  178.6 2.0 fusion.23
  180.6 3.3 %fusion.40 = (bf16[2,128,1152]{2,1,0:T(8,128)(2,1)}, bf16[2,128,1152]{2,1,0:T(8,128)(2,1)}, bf16[2,128,1152]{2,1,0:T(8,128)(2,1)}) fusion(f32[2,4,128,1152]{3,2,1,0:T(8,128)} %bitcast.133, s32[]{:T(128)S(6)} %select_n.139, s32[]{:T(128)S(6)} %select_n.140, s32[]{:T(128)S(6)} %select_n.141), kind=kLoop, calls=%fused_computation.59 | loop fusion | bytes 3538956 | tf_op jit(solution)/shard_map/convert_element_type | solution.py:129
  185.0 2.4 collective-permute-start.13
  187.4 13.7 %collective-permute-done.3 = bf16[256,2048]{0,1:T(8,128)(2,1)} collective-permute-done((bf16[256,2048]{0,1:T(8,128)(2,1)}, bf16[256,2048]{0,1:T(8,128)(2,1)}, u32[]{:S(2)}, u32[]{:S(2)}) %collective-permute-start.3) | collective-permute-done | bytes 1048608 | tf_op jit(solution)/shard_map/ppermute | solution.py:83
  201.2 7.0 %fusion.1 = f32[512,2048]{0,1:T(8,128)} fusion(f32[512,2048]{0,1:T(8,128)S(1)} %copy-done.4, f32[2048,512,1]{1,0,2:T(8,128)} %fusion.5, bf16[512,2,256]{2,0,1:T(8,128)(2,1)S(1)} %collective-permute-done.1, bf16[256,2048]{0,1:T(8,128)(2,1)} %collective-permute-done.3, bf16[256,2048]{0,1:T(8,128)(2,1)} %collective-permute-done.2, ...), kind=kOutput, calls=%fused_computation.8 | convolution fusion | flops 1081081856 | bytes 17301508 | tf_op jit(solution)/shard_map/tpk,pdk->td/dot_general | solution.py:75
  208.2 5.3 %copy.66 = f32[512,2048]{1,0:T(8,128)} copy(f32[512,2048]{0,1:T(8,128)} %fusion.1) | data formatting | bytes 8388608
  218.4 15.7 %collective-permute-done.10 = bf16[128,1152]{1,0:T(8,128)(2,1)S(1)} collective-permute-done((bf16[128,1152]{1,0:T(8,128)(2,1)S(1)}, bf16[128,1152]{1,0:T(8,128)(2,1)S(1)}, u32[]{:S(2)}, u32[]{:S(2)}) %collective-permute-start.10) | collective-permute-done | bytes 294944 | tf_op jit(solution)/shard_map/ppermute | solution.py:141
  234.2 6.2 %collective-permute-done.14 = bf16[128,1152]{1,0:T(8,128)(2,1)S(1)} collective-permute-done((bf16[128,1152]{1,0:T(8,128)(2,1)S(1)}, bf16[128,1152]{1,0:T(8,128)(2,1)S(1)}, u32[]{:S(2)}, u32[]{:S(2)}) %collective-permute-start.14) | collective-permute-done | bytes 294944 | tf_op jit(solution)/shard_map/ppermute | solution.py:141
  244.3 3.5 %fusion.31 = f32[2048,128]{1,0:T(8,128)} fusion(f32[2048,128]{1,0:T(8,128)} %copy.67, f32[2048,128]{1,0:T(8,128)} %param.18, f32[2048,128]{1,0:T(8,128)} %param.17), kind=kLoop, calls=%fused_computation.49 | loop fusion | flops 2883584 | bytes 4194304 | tf_op jit(solution)/shard_map/div | solution.py:22
  (105 shorter events, 40.4 us)
Async XLA Ops:
  7.2 102.5 %copy-start = (bf16[512,2048]{1,0:T(8,128)(2,1)S(1)}, bf16[512,2048]{1,0:T(8,128)(2,1)}, u32[]{:S(2)}) copy-start(bf16[512,2048]{1,0:T(8,128)(2,1)} %param.12) | copy-start | bytes 6291460
  7.2 86.3 %all-gather.3.cloned.1.call-start = ((), (), s32[]{:S(2)}) async-start(), calls=%async_computation | async-start | bytes 5308416 | tf_op jit(solution)/shard_map/all_gather | solution.py:191
  10.5 5.9 %copy-start.14 = (s32[4]{0:T(128)S(1)}, s32[4]{0:T(128)}, u32[]{:S(2)}) copy-start(s32[4]{0:T(128)} %param.21) | copy-start | bytes 52
  10.5 5.9 %copy-start.3 = (s32[8]{0:T(128)S(1)}, s32[8]{0:T(128)}, u32[]{:S(2)}) copy-start(s32[8]{0:T(128)} %param.23) | copy-start | bytes 100
  10.5 6.6 %copy-start.2 = (s32[8]{0:T(128)S(1)}, s32[8]{0:T(128)}, u32[]{:S(2)}) copy-start(s32[8]{0:T(128)} %param.22) | copy-start | bytes 100
  15.1 106.0 %collective-permute-start = (bf16[2,2,2048,256]{3,2,0,1:T(8,128)(2,1)}, bf16[2,2,2048,256]{3,2,0,1:T(8,128)(2,1)}, u32[]{:S(2)}, u32[]{:S(2)}) collective-permute-start(bf16[2,2,2048,256]{3,2,0,1:T(8,128)(2,1)} %copy_bitcast_fusion), channel_id=1, source_target_pairs={{0,1},{1,0},{2,3},{3,2},{4,5},{5,4},{6,7},{7,6},{8,9},{9,8},{10,11... | collective-permute-start | bytes 12582920 | tf_op jit(solution)/shard_map/ppermute | solution.py:68
  16.4 104.6 %collective-permute-start.1 = (bf16[512,2,256]{2,0,1:T(8,128)(2,1)}, bf16[512,2,256]{2,0,1:T(8,128)(2,1)S(1)}, u32[]{:S(2)}, u32[]{:S(2)}) collective-permute-start(bf16[512,2,256]{2,0,1:T(8,128)(2,1)} %copy.41), channel_id=1, source_target_pairs={{0,1},{1,0},{2,3},{3,2},{4,5},{5,4},{6,7},{7,6},{8,9},{9,8},{10,11... | collective-permute-start | bytes 1572872 | tf_op jit(solution)/shard_map/ppermute | solution.py:69
  112.8 4.9 %collective-permute-start.4 = (f32[4,128,256]{1,2,0:T(8,128)}, f32[4,128,256]{1,2,0:T(8,128)}, u32[]{:S(2)}, u32[]{:S(2)}) collective-permute-start(f32[4,128,256]{1,2,0:T(8,128)} %pad_maximum_fusion.3), channel_id=1, source_target_pairs={{0,1},{1,0},{2,3},{3,2},{4,5},{5,4},{6,7},{7,6},{8,9},{9,8},{10,11... | collective-permute-start | bytes 1572872 | tf_op jit(solution)/shard_map/ppermute | solution.py:29
  118.9 9.2 %collective-permute-start.5 = (f32[4,128,128]{1,2,0:T(8,128)S(1)}, f32[4,128,128]{1,2,0:T(8,128)S(1)}, u32[]{:S(2)}, u32[]{:S(2)}) collective-permute-start(f32[4,128,128]{1,2,0:T(8,128)S(1)} %get-tuple-element.36), channel_id=1, source_target_pairs={{0,2},{1,3},{2,0},{3,1},{4,6},{5,7},{6,4},{7,5},{8,10},{9,11},{10,... | collective-permute-start | bytes 786440 | tf_op jit(solution)/shard_map/ppermute | solution.py:35
  120.5 12.9 %collective-permute-start.6 = (f32[4,128,128]{1,2,0:T(8,128)S(1)}, f32[4,128,128]{1,2,0:T(8,128)S(1)}, u32[]{:S(2)}, u32[]{:S(2)}) collective-permute-start(f32[4,128,128]{1,2,0:T(8,128)S(1)} %get-tuple-element.35), channel_id=1, source_target_pairs={{0,2},{1,3},{2,0},{3,1},{4,6},{5,7},{6,4},{7,5},{8,10},{9,11},{10,... | collective-permute-start | bytes 786440 | tf_op jit(solution)/shard_map/ppermute | solution.py:34
  148.2 6.2 %copy-start.5 = (f32[8,128,1152]{2,1,0:T(8,128)}, f32[8,128,1152]{2,1,0:T(8,128)S(1)}, u32[]{:S(2)}) copy-start(f32[8,128,1152]{2,1,0:T(8,128)S(1)} %get-tuple-element.23) | copy-start | bytes 14155780
  149.5 7.0 %copy-start.7 = (bf16[4,2304,128]{1,2,0:T(8,128)(2,1)S(1)}, bf16[4,2304,128]{1,2,0:T(8,128)(2,1)}, u32[]{:S(2)}) copy-start(bf16[4,2304,128]{1,2,0:T(8,128)(2,1)} %copy-done.6) | copy-start | bytes 7077892
  149.5 15.6 %collective-permute-start.7 = (bf16[2,128,1152]{2,1,0:T(8,128)(2,1)}, bf16[2,128,1152]{2,1,0:T(8,128)(2,1)S(1)}, u32[]{:S(2)}, u32[]{:S(2)}) collective-permute-start(bf16[2,128,1152]{2,1,0:T(8,128)(2,1)} %get-tuple-element.28), channel_id=1, source_target_pairs={{0,4},{4,0},{8,12},{12,8},{16,20},{20,16},{24,28},{28,24},{1,5},{5... | collective-permute-start | bytes 1769480 | tf_op jit(solution)/shard_map/ppermute | solution.py:129
  150.0 16.6 %collective-permute-start.8 = (bf16[2,128,1152]{2,1,0:T(8,128)(2,1)}, bf16[2,128,1152]{2,1,0:T(8,128)(2,1)}, u32[]{:S(2)}, u32[]{:S(2)}) collective-permute-start(bf16[2,128,1152]{2,1,0:T(8,128)(2,1)} %get-tuple-element.29), channel_id=1, source_target_pairs={{0,8},{4,12},{8,0},{12,4},{16,24},{20,28},{24,16},{28,20},{1,9},{5... | collective-permute-start | bytes 1769480 | tf_op jit(solution)/shard_map/ppermute | solution.py:129
  150.6 28.0 %collective-permute-start.9 = (bf16[2,128,1152]{2,1,0:T(8,128)(2,1)}, bf16[2,128,1152]{2,1,0:T(8,128)(2,1)}, u32[]{:S(2)}, u32[]{:S(2)}) collective-permute-start(bf16[2,128,1152]{2,1,0:T(8,128)(2,1)} %get-tuple-element.30), channel_id=1, source_target_pairs={{0,12},{4,8},{8,4},{12,0},{16,28},{20,24},{24,20},{28,16},{1,13},{... | collective-permute-start | bytes 1769480 | tf_op jit(solution)/shard_map/ppermute | solution.py:129
  154.4 33.0 %collective-permute-start.2 = (bf16[256,2048]{0,1:T(8,128)(2,1)}, bf16[256,2048]{0,1:T(8,128)(2,1)}, u32[]{:S(2)}, u32[]{:S(2)}) collective-permute-start(bf16[256,2048]{0,1:T(8,128)(2,1)} %get-tuple-element.31), channel_id=1, source_target_pairs={{0,2},{1,3},{2,0},{3,1},{4,6},{5,7},{6,4},{7,5},{8,10},{9,11},{10,... | collective-permute-start | bytes 3145736 | tf_op jit(solution)/shard_map/ppermute | solution.py:82
  155.9 45.3 %collective-permute-start.3 = (bf16[256,2048]{0,1:T(8,128)(2,1)}, bf16[256,2048]{0,1:T(8,128)(2,1)}, u32[]{:S(2)}, u32[]{:S(2)}) collective-permute-start(bf16[256,2048]{0,1:T(8,128)(2,1)} %get-tuple-element.32), channel_id=1, source_target_pairs={{0,2},{1,3},{2,0},{3,1},{4,6},{5,7},{6,4},{7,5},{8,10},{9,11},{10,... | collective-permute-start | bytes 3145736 | tf_op jit(solution)/shard_map/ppermute | solution.py:83
  178.6 22.6 %copy-start.4 = (f32[512,2048]{0,1:T(8,128)S(1)}, f32[512,2048]{0,1:T(8,128)}, u32[]{:S(2)}) copy-start(f32[512,2048]{0,1:T(8,128)} %copy.71) | copy-start | bytes 12582916
  183.9 31.2 %collective-permute-start.11 = (bf16[2,128,1152]{2,1,0:T(8,128)(2,1)}, bf16[2,128,1152]{2,1,0:T(8,128)(2,1)S(1)}, u32[]{:S(2)}, u32[]{:S(2)}) collective-permute-start(bf16[2,128,1152]{2,1,0:T(8,128)(2,1)} %get-tuple-element.25), channel_id=1, source_target_pairs={{0,4},{4,0},{8,12},{12,8},{16,20},{20,16},{24,28},{28,24},{1,5},{5... | collective-permute-start | bytes 1769480 | tf_op jit(solution)/shard_map/ppermute | solution.py:129
  184.5 30.6 %collective-permute-start.12 = (bf16[2,128,1152]{2,1,0:T(8,128)(2,1)}, bf16[2,128,1152]{2,1,0:T(8,128)(2,1)S(1)}, u32[]{:S(2)}, u32[]{:S(2)}) collective-permute-start(bf16[2,128,1152]{2,1,0:T(8,128)(2,1)} %get-tuple-element.26), channel_id=1, source_target_pairs={{0,8},{4,12},{8,0},{12,4},{16,24},{20,28},{24,16},{28,20},{1,9},{5... | collective-permute-start | bytes 1769480 | tf_op jit(solution)/shard_map/ppermute | solution.py:129
  185.0 30.1 %collective-permute-start.13 = (bf16[2,128,1152]{2,1,0:T(8,128)(2,1)}, bf16[2,128,1152]{2,1,0:T(8,128)(2,1)}, u32[]{:S(2)}, u32[]{:S(2)}) collective-permute-start(bf16[2,128,1152]{2,1,0:T(8,128)(2,1)} %get-tuple-element.27), channel_id=1, source_target_pairs={{0,12},{4,8},{8,4},{12,0},{16,28},{20,24},{24,20},{28,16},{1,13},{... | collective-permute-start | bytes 1769480 | tf_op jit(solution)/shard_map/ppermute | solution.py:129
  213.6 20.6 %collective-permute-start.10 = (bf16[128,1152]{1,0:T(8,128)(2,1)S(1)}, bf16[128,1152]{1,0:T(8,128)(2,1)S(1)}, u32[]{:S(2)}, u32[]{:S(2)}) collective-permute-start(bf16[128,1152]{1,0:T(8,128)(2,1)S(1)} %fusion.50), channel_id=1, source_target_pairs={{0,16},{4,20},{8,24},{12,28},{16,0},{20,4},{24,8},{28,12},{1,17},{... | collective-permute-start | bytes 884744 | tf_op jit(solution)/shard_map/ppermute | solution.py:141
  216.9 23.5 %collective-permute-start.14 = (bf16[128,1152]{1,0:T(8,128)(2,1)S(1)}, bf16[128,1152]{1,0:T(8,128)(2,1)S(1)}, u32[]{:S(2)}, u32[]{:S(2)}) collective-permute-start(bf16[128,1152]{1,0:T(8,128)(2,1)S(1)} %fusion.51), channel_id=1, source_target_pairs={{0,16},{4,20},{8,24},{12,28},{16,0},{20,4},{24,8},{28,12},{1,17},{... | collective-permute-start | bytes 884744 | tf_op jit(solution)/shard_map/ppermute | solution.py:141
  241.3 6.5 %copy-start.1 = (bf16[512,2048]{1,0:T(8,128)(2,1)S(1)}, bf16[512,2048]{1,0:T(8,128)(2,1)}, u32[]{:S(2)}) copy-start(bf16[512,2048]{1,0:T(8,128)(2,1)} %param.12) | copy-start | bytes 6291460
  (7 other events, 20.6 us)
Sparse Core Ops, SparseCore 0:
  10.8 82.6 all-gather.2

commit v10 on v8

--- a/solution.py
+++ b/solution.py
@@ -132,6 +132,75 @@
         part = lax.dynamic_index_in_dim(acc, (group + m) % groups, axis=0, keepdims=False)
         total = total + lax.ppermute(part.astype(jnp.bfloat16), "dp", pairs).astype(jnp.float32)
     return total
+
+
+def split_local(
+    tokens_in,
+    grad_out,
+    base_weight,
+    a_master,
+    b_master,
+    a_first,
+    a_second,
+    b_first,
+    b_second,
+    block_tenant,
+    tenant_rank,
+    tenant_slot,
+):
+    tok_rows, feat_shard = tokens_in.shape
+    kv_shard = grad_out.shape[2]
+    rank_width = a_master.shape[1]
+    block_count = tok_rows // TENANT_BLOCK
+    block_slot = tenant_slot[block_tenant]
+    b_all = lax.all_gather(b_master.astype(jnp.bfloat16), "dp", axis=0, tiled=False)
+    a_in, b_all = lax.optimization_barrier((a_master.astype(jnp.bfloat16), b_all))
+    a_all = lax.all_gather(a_in, "dp", axis=0, tiled=False)
+    rank_of_block = tenant_rank[block_tenant].astype(jnp.float32)
+    column_rank = (jnp.arange(rank_width) % PADDED_RANK).astype(jnp.float32)
+    column_rank_mask = (column_rank[None, :] < rank_of_block[:, None]).astype(jnp.float32)
+    adapter_scale_factor = adapter_alpha_factor / rank_of_block
+    dy_blocks = grad_out.reshape(block_count, TENANT_BLOCK, 2, kv_shard)
+    b_blocks = jnp.take(b_all, block_slot, axis=0).reshape(block_count, 2, PADDED_RANK, kv_shard)
+    back_part = jnp.einsum(
+        "bnpk,bprk->bnpr", dy_blocks, b_blocks, preferred_element_type=jnp.float32
+    ).reshape(block_count, TENANT_BLOCK, rank_width)
+    backward_gradient_sum = tensor_sum((back_part,))[0]
+    backward_token_rows = (
+        backward_gradient_sum * (column_rank_mask * adapter_scale_factor[:, None])[:, None, :]
+    ).astype(jnp.bfloat16)
+    token_slot = jnp.repeat(block_slot, TENANT_BLOCK)
+    slot_hot = token_slot[:, None] == jnp.arange(TENANTS)[None, :]
+    back_rows = backward_token_rows.reshape(tok_rows, rank_width)
+    back_sel = jnp.where(slot_hot[:, :, None], back_rows[:, None, :], jnp.zeros((), back_rows.dtype))
+    a_sc = jnp.einsum("nsc,nd->scd", back_sel, tokens_in, preferred_element_type=jnp.float32)
+    a_grad = grouped_exchange(a_sc).T
+    a_blocks = jnp.take(a_all, block_slot, axis=0)
+    x_blocks = tokens_in.reshape(block_count, TENANT_BLOCK, feat_shard)
+    mid_part = jnp.einsum("bnd,bdc->bnc", x_blocks, a_blocks, preferred_element_type=jnp.float32)
+    mid_sum = tensor_sum((mid_part,))[0]
+    middle_rank_rows = (mid_sum * column_rank_mask[:, None, :]).astype(jnp.bfloat16)
+    mid_rows = middle_rank_rows.reshape(tok_rows, 2, PADDED_RANK)
+    mid_sel = jnp.where(
+        slot_hot[:, :, None, None], mid_rows[:, None, :, :], jnp.zeros((), mid_rows.dtype)
+    )
+    b_sc = jnp.einsum("nspr,npk->sprk", mid_sel, grad_out, preferred_element_type=jnp.float32)
+    slot_tenant = jnp.argsort(tenant_slot)
+    slot_scale = adapter_alpha_factor / tenant_rank[slot_tenant].astype(jnp.float32)
+    b_sc = b_sc * slot_scale[:, None, None, None]
+    b_grad = grouped_exchange(b_sc.reshape(TENANTS, rank_width, kv_shard))
+    frozen_gradient_share = frozen_gradient(grad_out, base_weight, feat_shard)
+    adapter_gradient_term = jnp.einsum(
+        "bnc,bdc->bnd", backward_token_rows, a_blocks, preferred_element_type=jnp.float32
+    ).reshape(tok_rows, feat_shard)
+    input_gradient_layer = frozen_gradient_share + adapter_gradient_term
+    return (
+        input_gradient_layer,
+        a_grad,
+        b_grad,
+        adam_step(a_grad, a_first, a_second),
+        adam_step(b_grad, b_first, b_second),
+    )
 
 
 def local(
@@ -267,4 +336,5 @@
         P(("tensor", "dp"), None),
         P(("tensor", "dp"), None),
     )
-    return jax.shard_map(local, mesh=mesh, in_specs=in_specs, out_specs=out_specs, check_vma=False)
+    body = split_local if mesh.shape["dp"] == TENANTS else local
+    return jax.shard_map(body, mesh=mesh, in_specs=in_specs, out_specs=out_specs, check_vma=False)

time: 246 us -> 271 us (1.10)
  blocking collectives: 0 us -> 33 us
  waiting for transfers between devices: 132 us -> 122 us
  other arithmetic: 18.7 us -> 11 us
  starting transfers between devices: 9.69 us -> 17 us
    all_gather x1, waiting for transfers between devices: 68.7 us -> 0.01 us  [split_local(): a_all = lax.all_gather(a_in, 'dp', axis=0, tiled=False)]
    all_gather x0 -> x1, blocking collectives: none -> 33 us  [split_local(): lax.all_gather(b_master.astype(jnp.bfloat16), 'dp', axis=0, tiled=False)]
    ppermute x4 -> x8, waiting for transfers between devices: 51.1 us -> 83.1 us  [grouped_exchange(): lax.ppermute(part.astype(jnp.bfloat16), 'dp', pairs).astype(jnp.float32)]
    ppermute x1, waiting for transfers between devices: 0.01 us -> 22.1 us  [frozen_gradient(): lax.ppermute(far_part[half:], 'tensor', row_pairs)]
    dynamic_slice x0 -> x3, local copies, waits for them, and re-layouts: none -> 7.87 us  [the longest x2 6.1 us: grouped_exchange(): acc = lax.dynamic_index_in_dim(by_member, member, axis=1, keepdims=False)]
    ppermute x4 -> x8, starting transfers between devices: 5.02 us -> 11.2 us  [grouped_exchange(): lax.ppermute(part.astype(jnp.bfloat16), 'dp', pairs).astype(jnp.float32)]
    ppermute x1, waiting for transfers between devices: 0.01 us -> 6.02 us  [frozen_gradient(): lax.ppermute(far_part[:half], 'tensor', row_pairs)]
    gather x5, local copies, waits for them, and re-layouts: 10.9 us -> 6.86 us  [the longest x1 4.37 us: split_local(): a_blocks = jnp.take(a_all, block_slot, axis=0)]
  transfers between devices with their start and end apart: 12 -> 17, of which waited for: 7 -> 8; matrix products, arithmetic and copies ran while one was open for 29% -> 28% of each run, Pallas kernels for 0% -> 0%
where the time goes in v10:
time: 271 us; the launch traced here: 270 us
  waiting for transfers between devices  122 us (45%)
  local copies, waits for them, and re-layouts  43 us (16%)
  blocking collectives  33 us (12%)
  matrix products  30 us (11%)
  starting transfers between devices  17 us (6%)
  between operations  14.4 us (5%)
  other arithmetic  11 us (4%)
    ppermute x8, waiting for transfers between devices, grouped_exchange(): lax.ppermute(part.astype(jnp.bfloat16), 'dp', pairs).astype(jnp.float32)  83.1 us
    all_gather x1, blocking collectives, split_local(): lax.all_gather(b_master.astype(jnp.bfloat16), 'dp', axis=0, tiled=False)  33 us
    ppermute x1, waiting for transfers between devices, frozen_gradient(): lax.ppermute(far_part[half:], 'tensor', row_pairs)  22.1 us
    unnamed x35, local copies, waits for them, and re-layouts  15.6 us
    ppermute x8, starting transfers between devices, grouped_exchange(): lax.ppermute(part.astype(jnp.bfloat16), 'dp', pairs).astype(jnp.float32)  11.2 us
    dot_general x2, matrix products, chip_partial(): jnp.einsum('tpk,pdk->td', partner_dy, other, preferred_element_type=jnp.f...  11.1 us
    ppermute x4, waiting for transfers between devices, tensor_sum(): parts = tuple((p + lax.ppermute(p, 'tensor', pairs) for p in parts))  10.3 us
    dot_general x2, matrix products, chip_partial(): jnp.einsum('tpk,pdk->td', grad_out, own, preferred_element_type=jnp.float32)  10.2 us
  transfers between devices with their start and end apart: 17, of which 8 were waited for; matrix products, arithmetic and copies ran while one was open for 28% of the time, Pallas kernels for 0%

profile of v10, /device:TPU:0, one launch (start us, length us, event | category | flops | bytes accessed | tf_op | source)
XLA Modules:
  0.0 270.0 jit_solution(973967390900934897)
XLA Ops:
  8.3 33.0 %all-gather = bf16[1024,256]{1,0:T(8,128)(2,1)S(1)} all-gather(bf16[128,256]{1,0:T(8,128)(2,1)S(1)} %convert_element_type.128), channel_id=2, replica_groups=mesh['dp'=8,'tensor'=4] {'dp'}, dimensions={0}, use_global_device_ids=true | all-gather | bytes 589824 | tf_op jit(solution)/shard_map/all_gather | solution.py:156
  45.3 4.4 %copy_bitcast_fusion = bf16[2,2,2048,256]{3,2,0,1:T(8,128)(2,1)} fusion(bf16[2,2,2,2048,256]{4,3,2,1,0:T(8,128)(2,1)} %bitcast.129, s32[]{:T(128)S(6)} %select_n.135), kind=kLoop, calls=%fused_computation.10 | loop fusion | bytes 8388612 | tf_op jit(solution)/shard_map/jit(dynamic_index_in_dim)/squeeze | solution.py:64
  54.5 6.1 %collective-permute-done.5 = f32[4,128,128]{2,1,0:T(8,128)S(1)} collective-permute-done((f32[4,128,128]{2,1,0:T(8,128)S(1)}, f32[4,128,128]{2,1,0:T(8,128)S(1)}, u32[]{:S(2)}, u32[]{:S(2)}) %collective-permute-start.5) | collective-permute-done | bytes 262176 | tf_op jit(solution)/shard_map/ppermute | solution.py:45
  60.8 2.3 fusion.9
  63.1 3.3 %copy-done.6 = f32[8,128,2048]{2,1,0:T(8,128)} copy-done((f32[8,128,2048]{2,1,0:T(8,128)}, f32[8,128,2048]{2,1,0:T(8,128)S(1)}, u32[]{:S(2)}) %copy-start.6) | copy-done | bytes 8388632
  78.3 5.1 %fusion.3 = f32[2048,512,1]{1,0,2:T(8,128)} fusion(bf16[2,2,2,2048,256]{4,3,2,1,0:T(8,128)(2,1)} %bitcast.130, s32[]{:T(128)S(6)} %select_n.137, s32[]{:T(128)S(6)} %select_n.134, bf16[512,2,256]{2,1,0:T(2,128)(2,1)} %param.13), kind=kOutput, calls=%fused_computation.12 | convolution fusion | flops 1073741824 | bytes 6815752 | tf_op jit(solution)/shard_map/tpk,pdk->td/dot_general | solution.py:74
  83.5 3.2 %constant_dynamic-slice_fusion.3 = f32[2,1,128,2048]{3,2,1,0:T(8,128)} fusion(f32[2,4,128,2048]{3,2,1,0:T(8,128)} %bitcast.126, s32[]{:T(128)S(6)} %select_n.146), kind=kLoop, calls=%fused_computation.83 | loop fusion | bytes 4194308 | tf_op jit(solution)/shard_map/jit(dynamic_index_in_dim)/dynamic_slice | solution.py:124
  86.7 2.9 %copy.46 = f32[2,1,128,2048]{2,3,0,1:T(8,128)} copy(f32[2,1,128,2048]{3,2,1,0:T(8,128)} %constant_dynamic-slice_fusion.3) | data formatting | bytes 4194304 | tf_op jit(solution)/shard_map/jit(dynamic_index_in_dim)/dynamic_slice | solution.py:124
  89.6 22.9 %collective-permute-done.6 = bf16[2,128,2048]{1,2,0:T(8,128)(2,1)} collective-permute-done((bf16[2,128,2048]{1,2,0:T(8,128)(2,1)}, bf16[2,128,2048]{1,2,0:T(8,128)(2,1)}, u32[]{:S(2)}, u32[]{:S(2)}) %collective-permute-start.6) | collective-permute-done | bytes 1048608 | tf_op jit(solution)/shard_map/ppermute | solution.py:128
  112.5 20.0 %collective-permute-done.7 = bf16[2,128,2048]{1,2,0:T(8,128)(2,1)} collective-permute-done((bf16[2,128,2048]{1,2,0:T(8,128)(2,1)}, bf16[2,128,2048]{1,2,0:T(8,128)(2,1)}, u32[]{:S(2)}, u32[]{:S(2)}) %collective-permute-start.7) | collective-permute-done | bytes 1048608 | tf_op jit(solution)/shard_map/ppermute | solution.py:128
  132.5 22.7 %collective-permute-done.8 = bf16[2,128,2048]{1,2,0:T(8,128)(2,1)S(1)} collective-permute-done((bf16[2,128,2048]{1,2,0:T(8,128)(2,1)}, bf16[2,128,2048]{1,2,0:T(8,128)(2,1)S(1)}, u32[]{:S(2)}, u32[]{:S(2)}) %collective-permute-start.8) | collective-permute-done | bytes 1048608 | tf_op jit(solution)/shard_map/ppermute | solution.py:128
  155.2 2.6 fusion.8
  160.1 5.0 %fusion.5 = f32[2048,512,1]{1,0,2:T(8,128)} fusion(bf16[2,2,2,2048,256]{4,3,2,1,0:T(8,128)(2,1)} %bitcast.131, s32[]{:T(128)S(6)} %select_n.131, s32[]{:T(128)S(6)} %select_n.134, bf16[512,2,256]{2,1,0:T(2,128)(2,1)S(1)} %copy-done.10), kind=kOutput, calls=%fused_computation.14 | convolution fusion | flops 1073741824 | bytes 6815752 | tf_op jit(solution)/shard_map/tpk,pdk->td/dot_general | solution.py:74
  165.1 17.5 %collective-permute-done.9 = bf16[128,2048]{0,1:T(8,128)(2,1)S(1)} collective-permute-done((bf16[128,2048]{0,1:T(8,128)(2,1)S(1)}, bf16[128,2048]{0,1:T(8,128)(2,1)S(1)}, u32[]{:S(2)}, u32[]{:S(2)}) %collective-permute-start.9) | collective-permute-done | bytes 524320 | tf_op jit(solution)/shard_map/ppermute | solution.py:133
  184.6 4.4 %gather_fusion.3 = bf16[4,2048,128]{2,1,0:T(8,128)(2,1)} fusion(bf16[8,2048,128]{2,1,0:T(8,128)(2,1)} %bitcast.134, s32[1024]{0:T(1024)S(1)} %pad_clamp_fusion.1), kind=kCustom, calls=%fused_computation.3 | custom fusion | bytes 4194320 | tf_op jit(solution)/shard_map/jit(_take)/gather | solution.py:178
  189.0 2.7 %convolution_bitcast_fusion = f32[4,128,128]{1,2,0:T(8,128)S(1)} fusion(bf16[4,128,2048]{2,1,0:T(8,128)(2,1)S(1)} %bitcast.123, bf16[4,2048,128]{2,1,0:T(8,128)(2,1)} %gather_fusion.3, pred[4]{0:T(512)(128)(4,1)S(1)} %compare_and_fusion), kind=kOutput, calls=%fused_computation.31 | convolution fusion | flops 269484032 | bytes 4456452 | tf_op jit(solution)/shard_map/bnd,bdc->bnc/dot_general | solution.py:180
  191.9 3.0 %fusion.2 = bf16[512,2048]{0,1:T(8,128)(2,1)S(1)} fusion(bf16[512,2,256]{2,0,1:T(8,128)(2,1)} %collective-permute-done.1, f32[2048,512,1]{1,0,2:T(8,128)S(1)} %copy-done.5, bf16[2,2,2048,256]{3,2,0,1:T(8,128)(2,1)} %collective-permute-done, s32[]{:T(128)S(6)} %select_n.136), kind=kOutput, calls=%fused_computation.11 | convolution fusion | flops 1075838976 | bytes 8912900 | tf_op jit(solution)/shard_map/tpk,pdk->td/dot_general | solution.py:75
  199.9 4.1 %collective-permute-done.11 = f32[4,128,128]{1,2,0:T(8,128)S(1)} collective-permute-done((f32[4,128,128]{1,2,0:T(8,128)S(1)}, f32[4,128,128]{1,2,0:T(8,128)S(1)}, u32[]{:S(2)}, u32[]{:S(2)}) %collective-permute-start.11) | collective-permute-done | bytes 262176 | tf_op jit(solution)/shard_map/ppermute | solution.py:45
  209.2 2.8 %fusion.28 = f32[4,128,2048]{2,1,0:T(8,128)} fusion(bf16[4,128,128]{2,1,0:T(8,128)(2,1)S(1)} %multiply_convert_fusion.1, bf16[4,2048,128]{2,1,0:T(8,128)(2,1)S(1)} %copy-done.4, pred[4]{0:T(512)(128)(4,1)S(1)} %compare_and_fusion), kind=kOutput, calls=%fused_computation.47 | convolution fusion | flops 269484032 | bytes 6422532 | tf_op jit(solution)/shard_map/bnc,bdc->bnd/dot_general | solution.py:193
  212.0 5.4 %copy.59 = f32[512,2048]{0,1:T(8,128)} copy(f32[512,2048]{1,0:T(8,128)} %bitcast.124) | data formatting | bytes 8388608 | tf_op jit(solution)/shard_map/reshape | solution.py:195
  220.6 6.0 %collective-permute-done.2 = bf16[256,2048]{0,1:T(8,128)(2,1)} collective-permute-done((bf16[256,2048]{0,1:T(8,128)(2,1)}, bf16[256,2048]{0,1:T(8,128)(2,1)}, u32[]{:S(2)}, u32[]{:S(2)}) %collective-permute-start.2) | collective-permute-done | bytes 1048608 | tf_op jit(solution)/shard_map/ppermute | solution.py:82
  226.6 22.1 %collective-permute-done.3 = bf16[256,2048]{0,1:T(8,128)(2,1)} collective-permute-done((bf16[256,2048]{0,1:T(8,128)(2,1)}, bf16[256,2048]{0,1:T(8,128)(2,1)}, u32[]{:S(2)}, u32[]{:S(2)}) %collective-permute-start.3) | collective-permute-done | bytes 1048608 | tf_op jit(solution)/shard_map/ppermute | solution.py:83
  248.7 8.2 %fusion.1 = f32[512,2048]{0,1:T(8,128)} fusion(f32[512,2048]{0,1:T(8,128)} %copy.59, f32[2048,512,1]{1,0,2:T(8,128)} %fusion.5, bf16[512,2,256]{2,0,1:T(8,128)(2,1)} %collective-permute-done.1, bf16[256,2048]{0,1:T(8,128)(2,1)} %collective-permute-done.3, bf16[256,2048]{0,1:T(8,128)(2,1)} %collective-permute-done.2, ...), kind=kOutput, calls=%fused_computation.8 | convolution fusion | flops 1081081856 | bytes 17301508 | tf_op jit(solution)/shard_map/tpk,pdk->td/dot_general | solution.py:75
  256.9 5.5 %copy.56 = f32[512,2048]{1,0:T(8,128)} copy(f32[512,2048]{0,1:T(8,128)} %fusion.1) | data formatting | bytes 8388608
  (102 shorter events, 40.2 us)
Async XLA Ops:
  7.2 53.6 %copy-start = (bf16[512,2048]{1,0:T(8,128)(2,1)S(1)}, bf16[512,2048]{1,0:T(8,128)(2,1)}, u32[]{:S(2)}) copy-start(bf16[512,2048]{1,0:T(8,128)(2,1)} %param.12) | copy-start | bytes 6291460
  7.2 36.2 %copy-start.14 = (s32[4]{0:T(128)S(1)}, s32[4]{0:T(128)}, u32[]{:S(2)}) copy-start(s32[4]{0:T(128)} %param.21) | copy-start | bytes 52
  7.2 36.3 %copy-start.3 = (s32[8]{0:T(128)S(1)}, s32[8]{0:T(128)}, u32[]{:S(2)}) copy-start(s32[8]{0:T(128)} %param.23) | copy-start | bytes 100
  7.2 37.5 %copy-start.9 = (bf16[512,2,256]{2,1,0:T(2,128)(2,1)S(1)}, bf16[512,2,256]{2,1,0:T(2,128)(2,1)}, u32[]{:S(2)}) copy-start(bf16[512,2,256]{2,1,0:T(2,128)(2,1)} %param.13) | copy-start | bytes 1572868
  7.2 177.4 %all-gather.4.cloned.1.call-start = ((), (), s32[]{:S(2)}) async-start(), calls=%async_computation | async-start | bytes 4718592 | tf_op jit(solution)/shard_map/all_gather | solution.py:158
  45.2 6.6 %collective-permute-start.4 = (f32[4,128,128]{2,1,0:T(8,128)S(1)}, f32[4,128,128]{2,1,0:T(8,128)S(1)}, u32[]{:S(2)}, u32[]{:S(2)}) collective-permute-start(f32[4,128,128]{2,1,0:T(8,128)S(1)} %copy.43), channel_id=1, source_target_pairs={{0,1},{1,0},{2,3},{3,2},{4,5},{5,4},{6,7},{7,6},{8,9},{9,8},{10,11... | collective-permute-start | bytes 786440 | tf_op jit(solution)/shard_map/ppermute | solution.py:45
  49.7 142.1 %collective-permute-start = (bf16[2,2,2048,256]{3,2,0,1:T(8,128)(2,1)}, bf16[2,2,2048,256]{3,2,0,1:T(8,128)(2,1)}, u32[]{:S(2)}, u32[]{:S(2)}) collective-permute-start(bf16[2,2,2048,256]{3,2,0,1:T(8,128)(2,1)} %copy_bitcast_fusion), channel_id=1, source_target_pairs={{0,1},{1,0},{2,3},{3,2},{4,5},{5,4},{6,7},{7,6},{8,9},{9,8},{10,11... | collective-permute-start | bytes 12582920 | tf_op jit(solution)/shard_map/ppermute | solution.py:68
  51.1 140.8 %collective-permute-start.1 = (bf16[512,2,256]{2,0,1:T(8,128)(2,1)}, bf16[512,2,256]{2,0,1:T(8,128)(2,1)}, u32[]{:S(2)}, u32[]{:S(2)}) collective-permute-start(bf16[512,2,256]{2,0,1:T(8,128)(2,1)} %copy.36), channel_id=1, source_target_pairs={{0,1},{1,0},{2,3},{3,2},{4,5},{5,4},{6,7},{7,6},{8,9},{9,8},{10,11... | collective-permute-start | bytes 1572872 | tf_op jit(solution)/shard_map/ppermute | solution.py:69
  51.9 8.7 %collective-permute-start.5 = (f32[4,128,128]{2,1,0:T(8,128)S(1)}, f32[4,128,128]{2,1,0:T(8,128)S(1)}, u32[]{:S(2)}, u32[]{:S(2)}) collective-permute-start(f32[4,128,128]{2,1,0:T(8,128)S(1)} %add.196), channel_id=1, source_target_pairs={{0,2},{1,3},{2,0},{3,1},{4,6},{5,7},{6,4},{7,5},{8,10},{9,11},{10,... | collective-permute-start | bytes 786440 | tf_op jit(solution)/shard_map/ppermute | solution.py:45
  70.5 42.0 %collective-permute-start.6 = (bf16[2,128,2048]{1,2,0:T(8,128)(2,1)}, bf16[2,128,2048]{1,2,0:T(8,128)(2,1)}, u32[]{:S(2)}, u32[]{:S(2)}) collective-permute-start(bf16[2,128,2048]{1,2,0:T(8,128)(2,1)} %bitcast.135), channel_id=1, source_target_pairs={{0,4},{4,0},{8,12},{12,8},{16,20},{20,16},{24,28},{28,24},{1,5},{5... | collective-permute-start | bytes 3145736 | tf_op jit(solution)/shard_map/ppermute | solution.py:128
  74.5 58.0 %collective-permute-start.7 = (bf16[2,128,2048]{1,2,0:T(8,128)(2,1)}, bf16[2,128,2048]{1,2,0:T(8,128)(2,1)}, u32[]{:S(2)}, u32[]{:S(2)}) collective-permute-start(bf16[2,128,2048]{1,2,0:T(8,128)(2,1)} %bitcast.136), channel_id=1, source_target_pairs={{0,8},{4,12},{8,0},{12,4},{16,24},{20,28},{24,16},{28,20},{1,9},{5... | collective-permute-start | bytes 3145736 | tf_op jit(solution)/shard_map/ppermute | solution.py:128
  75.8 79.4 %collective-permute-start.8 = (bf16[2,128,2048]{1,2,0:T(8,128)(2,1)}, bf16[2,128,2048]{1,2,0:T(8,128)(2,1)S(1)}, u32[]{:S(2)}, u32[]{:S(2)}) collective-permute-start(bf16[2,128,2048]{1,2,0:T(8,128)(2,1)} %bitcast.137), channel_id=1, source_target_pairs={{0,12},{4,8},{8,4},{12,0},{16,28},{20,24},{24,20},{28,16},{1,13},{... | collective-permute-start | bytes 3145736 | tf_op jit(solution)/shard_map/ppermute | solution.py:128
  89.6 70.5 %copy-start.10 = (bf16[512,2,256]{2,1,0:T(2,128)(2,1)S(1)}, bf16[512,2,256]{2,1,0:T(2,128)(2,1)}, u32[]{:S(2)}) copy-start(bf16[512,2,256]{2,1,0:T(2,128)(2,1)} %param.13) | copy-start | bytes 1572868
  157.9 24.7 %collective-permute-start.9 = (bf16[128,2048]{0,1:T(8,128)(2,1)S(1)}, bf16[128,2048]{0,1:T(8,128)(2,1)S(1)}, u32[]{:S(2)}, u32[]{:S(2)}) collective-permute-start(bf16[128,2048]{0,1:T(8,128)(2,1)S(1)} %fusion.29), channel_id=1, source_target_pairs={{0,16},{4,20},{8,24},{12,28},{16,0},{20,4},{24,8},{28,12},{1,17},{... | collective-permute-start | bytes 1572872 | tf_op jit(solution)/shard_map/ppermute | solution.py:133
  160.0 22.6 %copy-start.7 = (f32[2048,128]{1,0:T(8,128)S(1)}, f32[2048,128]{1,0:T(8,128)}, u32[]{:S(2)}) copy-start(f32[2048,128]{1,0:T(8,128)} %param.18) | copy-start | bytes 3145732
  160.0 22.5 %copy-start.8 = (f32[2048,128]{1,0:T(8,128)S(1)}, f32[2048,128]{1,0:T(8,128)}, u32[]{:S(2)}) copy-start(f32[2048,128]{1,0:T(8,128)} %param.17) | copy-start | bytes 3145732
  191.8 3.1 %collective-permute-start.10 = (f32[4,128,128]{1,2,0:T(8,128)S(1)}, f32[4,128,128]{1,2,0:T(8,128)S(1)}, u32[]{:S(2)}, u32[]{:S(2)}) collective-permute-start(f32[4,128,128]{1,2,0:T(8,128)S(1)} %convolution_bitcast_fusion), channel_id=1, source_target_pairs={{0,1},{1,0},{2,3},{3,2},{4,5},{5,4},{6,7},{7,6},{8,9},{9,8},{10,11... | collective-permute-start | bytes 786440 | tf_op jit(solution)/shard_map/ppermute | solution.py:45
  194.9 9.2 %collective-permute-start.11 = (f32[4,128,128]{1,2,0:T(8,128)S(1)}, f32[4,128,128]{1,2,0:T(8,128)S(1)}, u32[]{:S(2)}, u32[]{:S(2)}) collective-permute-start(f32[4,128,128]{1,2,0:T(8,128)S(1)} %add.213), channel_id=1, source_target_pairs={{0,2},{1,3},{2,0},{3,1},{4,6},{5,7},{6,4},{7,5},{8,10},{9,11},{10,... | collective-permute-start | bytes 786440 | tf_op jit(solution)/shard_map/ppermute | solution.py:45
  197.9 28.7 %collective-permute-start.2 = (bf16[256,2048]{0,1:T(8,128)(2,1)}, bf16[256,2048]{0,1:T(8,128)(2,1)}, u32[]{:S(2)}, u32[]{:S(2)}) collective-permute-start(bf16[256,2048]{0,1:T(8,128)(2,1)} %get-tuple-element.28), channel_id=1, source_target_pairs={{0,2},{1,3},{2,0},{3,1},{4,6},{5,7},{6,4},{7,5},{8,10},{9,11},{10,... | collective-permute-start | bytes 3145736 | tf_op jit(solution)/shard_map/ppermute | solution.py:82
  198.4 50.3 %collective-permute-start.3 = (bf16[256,2048]{0,1:T(8,128)(2,1)}, bf16[256,2048]{0,1:T(8,128)(2,1)}, u32[]{:S(2)}, u32[]{:S(2)}) collective-permute-start(bf16[256,2048]{0,1:T(8,128)(2,1)} %get-tuple-element.29), channel_id=1, source_target_pairs={{0,2},{1,3},{2,0},{3,1},{4,6},{5,7},{6,4},{7,5},{8,10},{9,11},{10,... | collective-permute-start | bytes 3145736 | tf_op jit(solution)/shard_map/ppermute | solution.py:83
  205.7 11.8 %collective-permute-start.12 = (bf16[2,128,256]{2,1,0:T(8,128)(2,1)}, bf16[2,128,256]{2,1,0:T(8,128)(2,1)S(1)}, u32[]{:S(2)}, u32[]{:S(2)}) collective-permute-start(bf16[2,128,256]{2,1,0:T(8,128)(2,1)} %get-tuple-element.30), channel_id=1, source_target_pairs={{0,4},{4,0},{8,12},{12,8},{16,20},{20,16},{24,28},{28,24},{1,5},{5... | collective-permute-start | bytes 393224 | tf_op jit(solution)/shard_map/ppermute | solution.py:128
  207.4 10.1 %collective-permute-start.13 = (bf16[2,128,256]{2,1,0:T(8,128)(2,1)}, bf16[2,128,256]{2,1,0:T(8,128)(2,1)}, u32[]{:S(2)}, u32[]{:S(2)}) collective-permute-start(bf16[2,128,256]{2,1,0:T(8,128)(2,1)} %get-tuple-element.32), channel_id=1, source_target_pairs={{0,8},{4,12},{8,0},{12,4},{16,24},{20,28},{24,16},{28,20},{1,9},{5... | collective-permute-start | bytes 393224 | tf_op jit(solution)/shard_map/ppermute | solution.py:128
  207.8 9.7 %collective-permute-start.14 = (bf16[2,128,256]{2,1,0:T(8,128)(2,1)}, bf16[2,128,256]{2,1,0:T(8,128)(2,1)}, u32[]{:S(2)}, u32[]{:S(2)}) collective-permute-start(bf16[2,128,256]{2,1,0:T(8,128)(2,1)} %get-tuple-element.31), channel_id=1, source_target_pairs={{0,12},{4,8},{8,4},{12,0},{16,28},{20,24},{24,20},{28,16},{1,13},{... | collective-permute-start | bytes 393224 | tf_op jit(solution)/shard_map/ppermute | solution.py:128
  218.5 43.8 %collective-permute-start.15 = (bf16[128,256]{1,0:T(8,128)(2,1)S(1)}, bf16[128,256]{1,0:T(8,128)(2,1)S(1)}, u32[]{:S(2)}, u32[]{:S(2)}) collective-permute-start(bf16[128,256]{1,0:T(8,128)(2,1)S(1)} %fusion.50), channel_id=1, source_target_pairs={{0,16},{4,20},{8,24},{12,28},{16,0},{20,4},{24,8},{28,12},{1,17},{... | collective-permute-start | bytes 196616 | tf_op jit(solution)/shard_map/ppermute | solution.py:133
  (8 other events, 43.1 us)
Sparse Core Ops, SparseCore 0:
  43.5 102.3 all-gather.3

commit v11 on v8

--- a/solution.py
+++ b/solution.py
@@ -158,10 +158,12 @@
     b_as_a = b_master.astype(jnp.bfloat16).reshape(b_rows_own * kv_shard // rank_width, rank_width)
     packed = jnp.concatenate([a_master.astype(jnp.bfloat16), b_as_a], axis=0)
     packed_all = lax.all_gather(packed, "dp", axis=0, tiled=False)
+    frozen_gradient_share = frozen_gradient(grad_out, base_weight, feat_shard)
+    frozen_gradient_share, packed_all = lax.optimization_barrier((frozen_gradient_share, packed_all))
     block_slot = tenant_slot[block_tenant]
     slot_major = dp_size == TENANTS
     if slot_major:
-        picked = jnp.take(packed_all, block_slot, axis=0)
+        picked = jnp.take(packed_all, block_slot, axis=0, mode="clip")
         a_blocks = picked[:, :a_rows_own]
         b_blocks = picked[:, a_rows_own:].reshape(block_count, 2, PADDED_RANK, kv_shard)
     else:
@@ -186,7 +188,6 @@
     backward_token_rows = (
         backward_gradient_sum * (column_rank_mask * adapter_scale_factor[:, None])[:, None, :]
     ).astype(jnp.bfloat16)
-    frozen_gradient_share = frozen_gradient(grad_out, base_weight, feat_shard)
     adapter_gradient_term = jnp.einsum(
         "bnc,bdc->bnd", backward_token_rows, a_blocks, preferred_element_type=jnp.float32
     ).reshape(tok_rows, feat_shard)

time: 246 us -> 231 us (0.939)
  local copies, waits for them, and re-layouts: 42.8 us -> 34.2 us
  waiting for transfers between devices: 132 us -> 124 us
  other arithmetic: 18.7 us -> 22.8 us
  matrix products: 27.8 us -> 24.3 us
    all_gather x1, waiting for transfers between devices: 68.7 us -> 10.9 us  [local(): packed_all = lax.all_gather(packed, 'dp', axis=0, tiled=False)]
    ppermute x1, waiting for transfers between devices: 0.01 us -> 22 us  [frozen_gradient(): lax.ppermute(far_part[:half], 'tensor', row_pairs)]
    ppermute x1, waiting for transfers between devices: 0.01 us -> 19.3 us  [frozen_gradient(): lax.ppermute(far_part[half:], 'tensor', row_pairs)]
    add x0 -> x1, other arithmetic: none -> 6.48 us  [local(): input_gradient_layer = frozen_gradient_share + adapter_gradient_term]
    ppermute x4, waiting for transfers between devices: 51.1 us -> 55.7 us  [grouped_exchange(): lax.ppermute(part.astype(jnp.bfloat16), 'dp', pairs).astype(jnp.float32)]
    gather x2 -> x1, local copies, waits for them, and re-layouts: 8.97 us -> 4.69 us  [local(): picked = jnp.take(packed_all, block_slot, axis=0, mode='clip')]
    dot_general x2, matrix products: 10.1 us -> 5.79 us  [chip_partial(): jnp.einsum('tpk,pdk->td', grad_out, own, preferred_element_type=jnp.float32)]
    ppermute x1, waiting for transfers between devices: 7.27 us -> 4.22 us  [tensor_sum_pair(): second = second + lax.ppermute(second, 'tensor', pairs)]
  transfers between devices with their start and end apart: 12 -> 12, of which waited for: 7 -> 11; matrix products, arithmetic and copies ran while one was open for 29% -> 20% of each run, Pallas kernels for 0% -> 0%
where the time goes in v11:
time: 231 us; the launch traced here: 230 us
  waiting for transfers between devices  124 us (54%)
  local copies, waits for them, and re-layouts  34.2 us (15%)
  matrix products  24.3 us (11%)
  other arithmetic  22.8 us (10%)
  between operations  14.3 us (6%)
  starting transfers between devices  10.6 us (5%)
    ppermute x4, waiting for transfers between devices, grouped_exchange(): lax.ppermute(part.astype(jnp.bfloat16), 'dp', pairs).astype(jnp.float32)  55.7 us
    ppermute x1, waiting for transfers between devices, frozen_gradient(): lax.ppermute(far_part[:half], 'tensor', row_pairs)  22 us
    ppermute x1, waiting for transfers between devices, frozen_gradient(): lax.ppermute(far_part[half:], 'tensor', row_pairs)  19.3 us
    unnamed x25, local copies, waits for them, and re-layouts  12.6 us
    all_gather x1, waiting for transfers between devices, local(): packed_all = lax.all_gather(packed, 'dp', axis=0, tiled=False)  10.9 us
    dot_general x2, matrix products, chip_partial(): jnp.einsum('tpk,pdk->td', partner_dy, other, preferred_element_type=jnp.f...  8.52 us
    ppermute x1, waiting for transfers between devices, tensor_sum_pair(): first = first + lax.ppermute(first, 'tensor', pairs)  7.32 us
    add x1, other arithmetic, local(): input_gradient_layer = frozen_gradient_share + adapter_gradient_term  6.48 us
  transfers between devices with their start and end apart: 12, of which 11 were waited for; matrix products, arithmetic and copies ran while one was open for 20% of the time, Pallas kernels for 0%

profile of v11, /device:TPU:0, one launch (start us, length us, event | category | flops | bytes accessed | tf_op | source)
XLA Modules:
  0.0 230.3 jit_solution(11541262085770138524)
XLA Ops:
  10.5 4.5 %copy_bitcast_fusion = bf16[2,2,2048,256]{3,2,0,1:T(8,128)(2,1)} fusion(bf16[2,2,2,2048,256]{4,3,2,1,0:T(8,128)(2,1)} %bitcast.114, s32[]{:T(128)S(6)} %select_n.95), kind=kLoop, calls=%fused_computation.16 | loop fusion | bytes 8388612 | tf_op jit(solution)/shard_map/jit(dynamic_index_in_dim)/squeeze | solution.py:64
  17.4 2.9 %fusion.16 = f32[2048,512,1]{1,0,2:T(8,128)S(1)} fusion(bf16[2,2,2,2048,256]{4,3,2,1,0:T(8,128)(2,1)} %bitcast.115, s32[]{:T(128)S(6)} %select_n.97, s32[]{:T(128)S(6)} %select_n.94, bf16[512,2,256]{2,1,0:T(2,128)(2,1)S(1)} %copy-done.6), kind=kOutput, calls=%fused_computation.32 | convolution fusion | flops 1073741824 | bytes 6815752 | tf_op jit(solution)/shard_map/tpk,pdk->td/dot_general | solution.py:74
  20.3 3.0 %collective-permute-done.1 = bf16[512,2,256]{2,0,1:T(8,128)(2,1)S(1)} collective-permute-done((bf16[512,2,256]{2,0,1:T(8,128)(2,1)}, bf16[512,2,256]{2,0,1:T(8,128)(2,1)S(1)}, u32[]{:S(2)}, u32[]{:S(2)}) %collective-permute-start.1) | collective-permute-done | bytes 524320 | tf_op jit(solution)/shard_map/ppermute | solution.py:69
  23.3 2.9 %fusion.1 = bf16[512,2048]{0,1:T(8,128)(2,1)S(1)} fusion(bf16[512,2,256]{2,0,1:T(8,128)(2,1)S(1)} %collective-permute-done.1, f32[2048,512,1]{1,0,2:T(8,128)S(1)} %fusion.16, bf16[2,2,2048,256]{3,2,0,1:T(8,128)(2,1)} %collective-permute-done, s32[]{:T(128)S(6)} %select_n.96), kind=kOutput, calls=%fused_computation.17 | convolution fusion | flops 1075838976 | bytes 8912900 | tf_op jit(solution)/shard_map/tpk,pdk->td/dot_general | solution.py:75
  27.6 2.9 %collective-permute-start.3 = (bf16[256,2048]{0,1:T(8,128)(2,1)}, bf16[256,2048]{0,1:T(8,128)(2,1)}, u32[]{:S(2)}, u32[]{:S(2)}) collective-permute-start(bf16[256,2048]{0,1:T(8,128)(2,1)} %get-tuple-element.27), channel_id=1, source_target_pairs={{0,2},{1,3},{2,0},{3,1},{4,6},{5,7},{6,4},{7,5},{8,10},{9,11},{10,... | collective-permute-start | bytes 3145736 | tf_op jit(solution)/shard_map/ppermute | solution.py:83
  32.5 2.9 %fusion.18 = f32[2048,512,1]{1,0,2:T(8,128)S(1)} fusion(bf16[2,2,2,2048,256]{4,3,2,1,0:T(8,128)(2,1)} %bitcast.116, s32[]{:T(128)S(6)} %select_n.91, s32[]{:T(128)S(6)} %select_n.94, bf16[512,2,256]{2,1,0:T(2,128)(2,1)S(1)} %copy-done.6), kind=kOutput, calls=%fused_computation.34 | convolution fusion | flops 1073741824 | bytes 6815752 | tf_op jit(solution)/shard_map/tpk,pdk->td/dot_general | solution.py:74
  35.5 19.3 %collective-permute-done.3 = bf16[256,2048]{0,1:T(8,128)(2,1)} collective-permute-done((bf16[256,2048]{0,1:T(8,128)(2,1)}, bf16[256,2048]{0,1:T(8,128)(2,1)}, u32[]{:S(2)}, u32[]{:S(2)}) %collective-permute-start.3) | collective-permute-done | bytes 1048608 | tf_op jit(solution)/shard_map/ppermute | solution.py:83
  54.7 22.0 %collective-permute-done.2 = bf16[256,2048]{0,1:T(8,128)(2,1)} collective-permute-done((bf16[256,2048]{0,1:T(8,128)(2,1)}, bf16[256,2048]{0,1:T(8,128)(2,1)}, u32[]{:S(2)}, u32[]{:S(2)}) %collective-permute-start.2) | collective-permute-done | bytes 1048608 | tf_op jit(solution)/shard_map/ppermute | solution.py:82
  76.7 5.6 %bitcast_add_fusion.1 = f32[512,2048]{0,1:T(8,128)} fusion(f32[2048,512,1]{1,0,2:T(8,128)S(1)} %fusion.18, bf16[512,2,256]{2,0,1:T(8,128)(2,1)S(1)} %collective-permute-done.1, bf16[256,2048]{0,1:T(8,128)(2,1)} %collective-permute-done.3, bf16[256,2048]{0,1:T(8,128)(2,1)} %collective-permute-done.2, bf16[2,2,2048,256]{3,2,0,1:T(8,128)(2,1)} %collective-permute-done, ...), kind=kOutput, calls=%fused_computation.14 | convolution fusion | flops 1080033280 | bytes 13107204 | tf_op jit(solution)/shard_map/tpk,pdk->td/dot_general | solution.py:75
  82.4 10.9 %all-gather.3.cloned.1.call-done = bf16[18432,128]{1,0:T(8,128)(2,1)} async-done(((bf16[2304,128]{1,0:T(8,128)(2,1)}), bf16[18432,128]{1,0:T(8,128)(2,1)}) %all-gather.3.cloned.1.call-update) | async-done | bytes 4718608 | tf_op jit(solution)/shard_map/all_gather | solution.py:160
  93.2 4.7 %gather_fusion.1 = bf16[4,2304,128]{2,1,0:T(8,128)(2,1)} fusion(bf16[8,2304,128]{2,1,0:T(8,128)(2,1)} %bitcast.119, s32[1024]{0:T(1024)S(1)} %pad_clamp_fusion.1), kind=kCustom, calls=%fused_computation.1 | custom fusion | bytes 4718608 | tf_op jit(solution)/shard_map/jit(_take)/gather | solution.py:166
  99.0 2.4 %fusion.36 = f32[4,128,128]{1,2,0:T(8,128)S(1)} fusion(bf16[4,128,2048]{2,1,0:T(8,128)(2,1)S(1)} %bitcast.106, bf16[4,2304,128]{2,1,0:T(8,128)(2,1)} %gather_fusion.1), kind=kOutput, calls=%fused_computation.56 | convolution fusion | flops 268435456 | bytes 4456448 | tf_op jit(solution)/shard_map/bnd,bdc->bnc/dot_general | solution.py:182
  106.7 7.3 %collective-permute-done.6 = f32[4,128,128]{1,2,0:T(8,128)S(1)} collective-permute-done((f32[4,128,128]{1,2,0:T(8,128)}, f32[4,128,128]{1,2,0:T(8,128)S(1)}, u32[]{:S(2)}, u32[]{:S(2)}) %collective-permute-start.6) | collective-permute-done | bytes 262176 | tf_op jit(solution)/shard_map/ppermute | solution.py:34
  114.7 4.2 %collective-permute-done.5 = f32[4,128,128]{1,2,0:T(8,128)} collective-permute-done((f32[4,128,128]{1,2,0:T(8,128)}, f32[4,128,128]{1,2,0:T(8,128)}, u32[]{:S(2)}, u32[]{:S(2)}) %collective-permute-start.5) | collective-permute-done | bytes 262176 | tf_op jit(solution)/shard_map/ppermute | solution.py:35
  130.8 26.6 %collective-permute-done.9 = bf16[2,128,2304]{2,1,0:T(8,128)(2,1)S(1)} collective-permute-done((bf16[2,128,2304]{2,1,0:T(8,128)(2,1)}, bf16[2,128,2304]{2,1,0:T(8,128)(2,1)S(1)}, u32[]{:S(2)}, u32[]{:S(2)}) %collective-permute-start.9) | collective-permute-done | bytes 1179680 | tf_op jit(solution)/shard_map/ppermute | solution.py:128
  157.3 22.7 %collective-permute-done.8 = bf16[2,128,2304]{2,1,0:T(8,128)(2,1)} collective-permute-done((bf16[2,128,2304]{2,1,0:T(8,128)(2,1)}, bf16[2,128,2304]{2,1,0:T(8,128)(2,1)}, u32[]{:S(2)}, u32[]{:S(2)}) %collective-permute-start.8) | collective-permute-done | bytes 1179680 | tf_op jit(solution)/shard_map/ppermute | solution.py:128
  181.0 2.7 %fusion.9 = f32[2,128,2304]{2,1,0:T(8,128)S(1)} fusion(s32[]{:T(128)S(6)} %select_n.104, f32[2,4,128,2048]{3,2,1,0:T(8,128)} %bitcast.108, f32[2,4,128,256]{3,2,1,0:T(8,128)S(1)} %bitcast.111, bf16[2,128,2304]{2,1,0:T(8,128)(2,1)S(1)} %collective-permute-done.9, bf16[2,128,2304]{2,1,0:T(8,128)(2,1)} %collective-permute-done.8, ...), kind=kLoop, calls=%fused_computation.25 | loop fusion | flops 4128768 | bytes 15335428 | tf_op jit(solution)/shard_map/add | solution.py:128
  186.8 4.5 %fusion.30 = f32[4,128,2048]{2,1,0:T(8,128)} fusion(bf16[4,128,128]{1,2,0:T(8,128)(2,1)S(1)} %get-tuple-element.29, bf16[4,2304,128]{2,1,0:T(8,128)(2,1)} %gather_fusion.1), kind=kOutput, calls=%fused_computation.46 | convolution fusion | flops 268435456 | bytes 6422528 | tf_op jit(solution)/shard_map/bnc,bdc->bnd/dot_general | solution.py:191
  191.3 5.4 %copy.60 = f32[512,2048]{0,1:T(8,128)} copy(f32[512,2048]{1,0:T(8,128)} %bitcast.109) | data formatting | bytes 8388608 | tf_op jit(solution)/shard_map/reshape | solution.py:193
  196.7 6.5 %add.154 = f32[512,2048]{0,1:T(8,128)} add(f32[512,2048]{0,1:T(8,128)} %bitcast_add_fusion.1, f32[512,2048]{0,1:T(8,128)} %copy.60) | non-fusion elementwise | flops 1048576 | bytes 12582912 | tf_op jit(solution)/shard_map/add | solution.py:194
  203.2 5.3 %copy.55 = f32[512,2048]{1,0:T(8,128)} copy(f32[512,2048]{0,1:T(8,128)} %add.154) | data formatting | bytes 8388608
  208.5 5.5 %collective-permute-done.10 = bf16[128,2304]{1,0:T(8,128)(2,1)S(1)} collective-permute-done((bf16[128,2304]{1,0:T(8,128)(2,1)S(1)}, bf16[128,2304]{1,0:T(8,128)(2,1)S(1)}, u32[]{:S(2)}, u32[]{:S(2)}) %collective-permute-start.10) | collective-permute-done | bytes 589856 | tf_op jit(solution)/shard_map/ppermute | solution.py:133
  216.5 2.7 %copy.56 = f32[2048,128]{1,0:T(8,128)} copy(f32[2048,128]{0,1:T(8,128)} %slice_bitcast_fusion) | data formatting | bytes 2097152
  220.0 3.5 %fusion.43 = f32[2048,128]{1,0:T(8,128)} fusion(f32[2048,128]{1,0:T(8,128)} %copy.56, f32[2048,128]{1,0:T(8,128)} %param.18, f32[2048,128]{1,0:T(8,128)} %param.17), kind=kLoop, calls=%fused_computation.61 | loop fusion | flops 2883584 | bytes 4194304 | tf_op jit(solution)/shard_map/div | solution.py:22
  (80 shorter events, 35.1 us)
Async XLA Ops:
  7.2 91.8 %copy-start = (bf16[512,2048]{1,0:T(8,128)(2,1)S(1)}, bf16[512,2048]{1,0:T(8,128)(2,1)}, u32[]{:S(2)}) copy-start(bf16[512,2048]{1,0:T(8,128)(2,1)} %param.12) | copy-start | bytes 6291460
  7.2 86.0 %all-gather.3.cloned.1.call-start = ((), (), s32[]{:S(2)}) async-start(), calls=%async_computation | async-start | bytes 5308416 | tf_op jit(solution)/shard_map/all_gather | solution.py:160
  10.5 5.0 %copy-start.6 = (bf16[512,2,256]{2,1,0:T(2,128)(2,1)S(1)}, bf16[512,2,256]{2,1,0:T(2,128)(2,1)}, u32[]{:S(2)}) copy-start(bf16[512,2,256]{2,1,0:T(2,128)(2,1)} %param.13) | copy-start | bytes 1572868
  10.5 5.9 %copy-start.3 = (s32[8]{0:T(128)S(1)}, s32[8]{0:T(128)}, u32[]{:S(2)}) copy-start(s32[8]{0:T(128)} %param.23) | copy-start | bytes 100
  10.5 6.9 %copy-start.10 = (s32[4]{0:T(128)S(1)}, s32[4]{0:T(128)}, u32[]{:S(2)}) copy-start(s32[4]{0:T(128)} %param.21) | copy-start | bytes 52
  15.1 8.2 %collective-permute-start = (bf16[2,2,2048,256]{3,2,0,1:T(8,128)(2,1)}, bf16[2,2,2048,256]{3,2,0,1:T(8,128)(2,1)}, u32[]{:S(2)}, u32[]{:S(2)}) collective-permute-start(bf16[2,2,2048,256]{3,2,0,1:T(8,128)(2,1)} %copy_bitcast_fusion), channel_id=1, source_target_pairs={{0,1},{1,0},{2,3},{3,2},{4,5},{5,4},{6,7},{7,6},{8,9},{9,8},{10,11... | collective-permute-start | bytes 12582920 | tf_op jit(solution)/shard_map/ppermute | solution.py:68
  16.4 6.9 %collective-permute-start.1 = (bf16[512,2,256]{2,0,1:T(8,128)(2,1)}, bf16[512,2,256]{2,0,1:T(8,128)(2,1)S(1)}, u32[]{:S(2)}, u32[]{:S(2)}) collective-permute-start(bf16[512,2,256]{2,0,1:T(8,128)(2,1)} %copy.35), channel_id=1, source_target_pairs={{0,1},{1,0},{2,3},{3,2},{4,5},{5,4},{6,7},{7,6},{8,9},{9,8},{10,11... | collective-permute-start | bytes 1572872 | tf_op jit(solution)/shard_map/ppermute | solution.py:69
  26.2 5.0 %copy-start.2 = (s32[8]{0:T(128)S(1)}, s32[8]{0:T(128)}, u32[]{:S(2)}) copy-start(s32[8]{0:T(128)} %param.22) | copy-start | bytes 100
  27.6 27.1 %collective-permute-start.3 = (bf16[256,2048]{0,1:T(8,128)(2,1)}, bf16[256,2048]{0,1:T(8,128)(2,1)}, u32[]{:S(2)}, u32[]{:S(2)}) collective-permute-start(bf16[256,2048]{0,1:T(8,128)(2,1)} %get-tuple-element.27), channel_id=1, source_target_pairs={{0,2},{1,3},{2,0},{3,1},{4,6},{5,7},{6,4},{7,5},{8,10},{9,11},{10,... | collective-permute-start | bytes 3145736 | tf_op jit(solution)/shard_map/ppermute | solution.py:83
  30.5 46.2 %collective-permute-start.2 = (bf16[256,2048]{0,1:T(8,128)(2,1)}, bf16[256,2048]{0,1:T(8,128)(2,1)}, u32[]{:S(2)}, u32[]{:S(2)}) collective-permute-start(bf16[256,2048]{0,1:T(8,128)(2,1)} %get-tuple-element.26), channel_id=1, source_target_pairs={{0,2},{1,3},{2,0},{3,1},{4,6},{5,7},{6,4},{7,5},{8,10},{9,11},{10,... | collective-permute-start | bytes 3145736 | tf_op jit(solution)/shard_map/ppermute | solution.py:82
  101.8 2.0 collective-permute-start.4
  104.7 9.4 %collective-permute-start.6 = (f32[4,128,128]{1,2,0:T(8,128)}, f32[4,128,128]{1,2,0:T(8,128)S(1)}, u32[]{:S(2)}, u32[]{:S(2)}) collective-permute-start(f32[4,128,128]{1,2,0:T(8,128)} %get-tuple-element.30), channel_id=1, source_target_pairs={{0,2},{1,3},{2,0},{3,1},{4,6},{5,7},{6,4},{7,5},{8,10},{9,11},{10,... | collective-permute-start | bytes 786440 | tf_op jit(solution)/shard_map/ppermute | solution.py:34
  106.1 12.8 %collective-permute-start.5 = (f32[4,128,128]{1,2,0:T(8,128)}, f32[4,128,128]{1,2,0:T(8,128)}, u32[]{:S(2)}, u32[]{:S(2)}) collective-permute-start(f32[4,128,128]{1,2,0:T(8,128)} %get-tuple-element.31), channel_id=1, source_target_pairs={{0,2},{1,3},{2,0},{3,1},{4,6},{5,7},{6,4},{7,5},{8,10},{9,11},{10,... | collective-permute-start | bytes 786440 | tf_op jit(solution)/shard_map/ppermute | solution.py:35
  114.0 0.7 copy-start.7
  123.0 4.3 %copy-start.4 = (f32[8,128,2048]{2,1,0:T(8,128)}, f32[8,128,2048]{2,1,0:T(8,128)S(1)}, u32[]{:S(2)}) copy-start(f32[8,128,2048]{2,1,0:T(8,128)S(1)} %fusion.20) | copy-start | bytes 25165828
  127.3 30.1 %collective-permute-start.9 = (bf16[2,128,2304]{2,1,0:T(8,128)(2,1)}, bf16[2,128,2304]{2,1,0:T(8,128)(2,1)S(1)}, u32[]{:S(2)}, u32[]{:S(2)}) collective-permute-start(bf16[2,128,2304]{2,1,0:T(8,128)(2,1)} %get-tuple-element.25), channel_id=1, source_target_pairs={{0,12},{4,8},{8,4},{12,0},{16,28},{20,24},{24,20},{28,16},{1,13},{... | collective-permute-start | bytes 3538952 | tf_op jit(solution)/shard_map/ppermute | solution.py:128
  127.8 52.3 %collective-permute-start.8 = (bf16[2,128,2304]{2,1,0:T(8,128)(2,1)}, bf16[2,128,2304]{2,1,0:T(8,128)(2,1)}, u32[]{:S(2)}, u32[]{:S(2)}) collective-permute-start(bf16[2,128,2304]{2,1,0:T(8,128)(2,1)} %get-tuple-element.24), channel_id=1, source_target_pairs={{0,8},{4,12},{8,0},{12,4},{16,24},{20,28},{24,16},{28,20},{1,9},{5... | collective-permute-start | bytes 3538952 | tf_op jit(solution)/shard_map/ppermute | solution.py:128
  129.3 51.7 %collective-permute-start.7 = (bf16[2,128,2304]{2,1,0:T(8,128)(2,1)}, bf16[2,128,2304]{2,1,0:T(8,128)(2,1)}, u32[]{:S(2)}, u32[]{:S(2)}) collective-permute-start(bf16[2,128,2304]{2,1,0:T(8,128)(2,1)} %get-tuple-element.23), channel_id=1, source_target_pairs={{0,4},{4,0},{8,12},{12,8},{16,20},{20,16},{24,28},{28,24},{1,5},{5... | collective-permute-start | bytes 3538952 | tf_op jit(solution)/shard_map/ppermute | solution.py:128
  183.7 1.5 copy-start.5
  185.2 28.8 %collective-permute-start.10 = (bf16[128,2304]{1,0:T(8,128)(2,1)S(1)}, bf16[128,2304]{1,0:T(8,128)(2,1)S(1)}, u32[]{:S(2)}, u32[]{:S(2)}) collective-permute-start(bf16[128,2304]{1,0:T(8,128)(2,1)S(1)} %fusion.48), channel_id=1, source_target_pairs={{0,16},{4,20},{8,24},{12,28},{16,0},{20,4},{24,8},{28,12},{1,17},{... | collective-permute-start | bytes 1769480 | tf_op jit(solution)/shard_map/ppermute | solution.py:133
  215.4 3.8 %copy-start.8 = (f32[128,256]{1,0:T(8,128)S(1)}, f32[128,256]{1,0:T(8,128)}, u32[]{:S(2)}) copy-start(f32[128,256]{1,0:T(8,128)} %param.20) | copy-start | bytes 393220
  215.4 3.8 %copy-start.9 = (f32[128,256]{1,0:T(8,128)S(1)}, f32[128,256]{1,0:T(8,128)}, u32[]{:S(2)}) copy-start(f32[128,256]{1,0:T(8,128)} %param.19) | copy-start | bytes 393220
  216.5 6.9 %copy-start.1 = (bf16[512,2048]{1,0:T(8,128)(2,1)S(1)}, bf16[512,2048]{1,0:T(8,128)(2,1)}, u32[]{:S(2)}) copy-start(bf16[512,2048]{1,0:T(8,128)(2,1)} %param.12) | copy-start | bytes 6291460
Sparse Core Ops, SparseCore 0:
  10.6 82.5 all-gather.2

commit v12 on v11

--- a/solution.py
+++ b/solution.py
@@ -106,9 +106,9 @@
     slot_tenant = jnp.argsort(tenant_slot)
     slot_scale = adapter_alpha_factor / tenant_rank[slot_tenant].astype(jnp.float32)
     b_sc = b_sc * slot_scale[:, None, None, None]
-    full = jnp.concatenate([a_sc, b_sc.reshape(TENANTS, rank_width, kv_shard)], axis=2)
-    own = grouped_exchange(full)
-    return own[:, :feat_shard].T, own[:, feat_shard:]
+    a_own = grouped_exchange(a_sc)
+    b_own = grouped_exchange(b_sc.reshape(TENANTS, rank_width, kv_shard))
+    return a_own.T, b_own
 
 
 def grouped_exchange(full):
@@ -183,7 +183,8 @@
     back_part = jnp.einsum(
         "bnpk,bprk->bnpr", dy_blocks, b_blocks, preferred_element_type=jnp.float32
     ).reshape(block_count, TENANT_BLOCK, rank_width)
-    mid_sum, backward_gradient_sum = tensor_sum_pair(mid_part, back_part)
+    backward_gradient_sum = tensor_sum((back_part,))[0]
+    mid_sum = tensor_sum((mid_part,))[0]
     middle_rank_rows = (mid_sum * column_rank_mask[:, None, :]).astype(jnp.bfloat16)
     backward_token_rows = (
         backward_gradient_sum * (column_rank_mask * adapter_scale_factor[:, None])[:, None, :]

time: 231 us -> 219 us (0.948)
  waiting for transfers between devices: 124 us -> 102 us
  local copies, waits for them, and re-layouts: 34.2 us -> 42 us
  starting transfers between devices: 10.6 us -> 15.7 us
    ppermute x4 -> x8, waiting for transfers between devices: 55.7 us -> 40.6 us  [grouped_exchange(): lax.ppermute(part.astype(jnp.bfloat16), 'dp', pairs).astype(jnp.float32)]
    ppermute x3 -> x4, waiting for transfers between devices: 13.3 us -> 6.55 us  [tensor_sum(): parts = tuple((p + lax.ppermute(p, 'tensor', pairs) for p in parts))]
    dynamic_slice x0 -> x3, local copies, waits for them, and re-layouts: none -> 5.6 us  [the longest x2 5.13 us: grouped_exchange(): acc = lax.dynamic_index_in_dim(by_member, member, axis=1, keepdims=False)]
    ppermute x4 -> x8, starting transfers between devices: 5.02 us -> 8.98 us  [grouped_exchange(): lax.ppermute(part.astype(jnp.bfloat16), 'dp', pairs).astype(jnp.float32)]
    unnamed x25 -> x33, local copies, waits for them, and re-layouts: 12.6 us -> 14.5 us
  transfers between devices with their start and end apart: 12 -> 17, of which waited for: 11 -> 6; matrix products, arithmetic and copies ran while one was open for 20% -> 31% of each run, Pallas kernels for 0% -> 0%
where the time goes in v12:
time: 219 us; the launch traced here: 218 us
  waiting for transfers between devices  102 us (47%)
  local copies, waits for them, and re-layouts  42 us (19%)
  matrix products  22.5 us (10%)
  other arithmetic  21.1 us (10%)
  starting transfers between devices  15.7 us (7%)
  between operations  14.4 us (7%)
    ppermute x8, waiting for transfers between devices, grouped_exchange(): lax.ppermute(part.astype(jnp.bfloat16), 'dp', pairs).astype(jnp.float32)  40.6 us
    ppermute x1, waiting for transfers between devices, frozen_gradient(): lax.ppermute(far_part[:half], 'tensor', row_pairs)  22 us
    ppermute x1, waiting for transfers between devices, frozen_gradient(): lax.ppermute(far_part[half:], 'tensor', row_pairs)  20.5 us
    unnamed x33, local copies, waits for them, and re-layouts  14.5 us
    all_gather x1, waiting for transfers between devices, local(): packed_all = lax.all_gather(packed, 'dp', axis=0, tiled=False)  11 us
    ppermute x8, starting transfers between devices, grouped_exchange(): lax.ppermute(part.astype(jnp.bfloat16), 'dp', pairs).astype(jnp.float32)  8.98 us
    dot_general x2, matrix products, chip_partial(): jnp.einsum('tpk,pdk->td', partner_dy, other, preferred_element_type=jnp.f...  8.52 us
    ppermute x4, waiting for transfers between devices, tensor_sum(): parts = tuple((p + lax.ppermute(p, 'tensor', pairs) for p in parts))  6.55 us
  transfers between devices with their start and end apart: 17, of which 6 were waited for; matrix products, arithmetic and copies ran while one was open for 31% of the time, Pallas kernels for 0%

profile of v12, /device:TPU:0, one launch (start us, length us, event | category | flops | bytes accessed | tf_op | source)
XLA Modules:
  0.0 217.9 jit_solution(219566933341102678)
XLA Ops:
  10.5 4.5 %copy_bitcast_fusion = bf16[2,2,2048,256]{3,2,0,1:T(8,128)(2,1)} fusion(bf16[2,2,2,2048,256]{4,3,2,1,0:T(8,128)(2,1)} %bitcast.122, s32[]{:T(128)S(6)} %select_n.108), kind=kLoop, calls=%fused_computation.8 | loop fusion | bytes 8388612 | tf_op jit(solution)/shard_map/jit(dynamic_index_in_dim)/squeeze | solution.py:64
  18.8 2.9 %fusion.2 = f32[2048,512,1]{1,0,2:T(8,128)S(1)} fusion(bf16[2,2,2,2048,256]{4,3,2,1,0:T(8,128)(2,1)} %bitcast.123, s32[]{:T(128)S(6)} %select_n.110, s32[]{:T(128)S(6)} %select_n.107, bf16[512,2,256]{2,1,0:T(2,128)(2,1)S(1)} %copy-done.7), kind=kOutput, calls=%fused_computation.10 | convolution fusion | flops 1073741824 | bytes 6815752 | tf_op jit(solution)/shard_map/tpk,pdk->td/dot_general | solution.py:74
  23.3 2.9 %fusion.1 = bf16[512,2048]{0,1:T(8,128)(2,1)S(1)} fusion(bf16[512,2,256]{2,0,1:T(8,128)(2,1)S(1)} %collective-permute-done.1, f32[2048,512,1]{1,0,2:T(8,128)S(1)} %fusion.2, bf16[2,2,2048,256]{3,2,0,1:T(8,128)(2,1)} %collective-permute-done, s32[]{:T(128)S(6)} %select_n.109), kind=kOutput, calls=%fused_computation.9 | convolution fusion | flops 1075838976 | bytes 8912900 | tf_op jit(solution)/shard_map/tpk,pdk->td/dot_general | solution.py:75
  27.6 2.9 %collective-permute-start.3 = (bf16[256,2048]{0,1:T(8,128)(2,1)}, bf16[256,2048]{0,1:T(8,128)(2,1)}, u32[]{:S(2)}, u32[]{:S(2)}) collective-permute-start(bf16[256,2048]{0,1:T(8,128)(2,1)} %get-tuple-element.29), channel_id=1, source_target_pairs={{0,2},{1,3},{2,0},{3,1},{4,6},{5,7},{6,4},{7,5},{8,10},{9,11},{10,... | collective-permute-start | bytes 3145736 | tf_op jit(solution)/shard_map/ppermute | solution.py:83
  31.4 2.9 %fusion.4 = f32[2048,512,1]{1,0,2:T(8,128)S(1)} fusion(bf16[2,2,2,2048,256]{4,3,2,1,0:T(8,128)(2,1)} %bitcast.124, s32[]{:T(128)S(6)} %select_n.104, s32[]{:T(128)S(6)} %select_n.107, bf16[512,2,256]{2,1,0:T(2,128)(2,1)S(1)} %copy-done.7), kind=kOutput, calls=%fused_computation.12 | convolution fusion | flops 1073741824 | bytes 6815752 | tf_op jit(solution)/shard_map/tpk,pdk->td/dot_general | solution.py:74
  34.3 20.5 %collective-permute-done.3 = bf16[256,2048]{0,1:T(8,128)(2,1)} collective-permute-done((bf16[256,2048]{0,1:T(8,128)(2,1)}, bf16[256,2048]{0,1:T(8,128)(2,1)}, u32[]{:S(2)}, u32[]{:S(2)}) %collective-permute-start.3) | collective-permute-done | bytes 1048608 | tf_op jit(solution)/shard_map/ppermute | solution.py:83
  54.7 22.0 %collective-permute-done.2 = bf16[256,2048]{0,1:T(8,128)(2,1)} collective-permute-done((bf16[256,2048]{0,1:T(8,128)(2,1)}, bf16[256,2048]{0,1:T(8,128)(2,1)}, u32[]{:S(2)}, u32[]{:S(2)}) %collective-permute-start.2) | collective-permute-done | bytes 1048608 | tf_op jit(solution)/shard_map/ppermute | solution.py:82
  76.7 5.6 %bitcast_add_fusion.1 = f32[512,2048]{0,1:T(8,128)} fusion(f32[2048,512,1]{1,0,2:T(8,128)S(1)} %fusion.4, bf16[512,2,256]{2,0,1:T(8,128)(2,1)S(1)} %collective-permute-done.1, bf16[256,2048]{0,1:T(8,128)(2,1)} %collective-permute-done.3, bf16[256,2048]{0,1:T(8,128)(2,1)} %collective-permute-done.2, bf16[2,2,2048,256]{3,2,0,1:T(8,128)(2,1)} %collective-permute-done, ...), kind=kOutput, calls=%fused_computation.6 | convolution fusion | flops 1080033280 | bytes 13107204 | tf_op jit(solution)/shard_map/tpk,pdk->td/dot_general | solution.py:75
  82.4 11.0 %all-gather.3.cloned.1.call-done = bf16[18432,128]{1,0:T(8,128)(2,1)} async-done(((bf16[2304,128]{1,0:T(8,128)(2,1)}), bf16[18432,128]{1,0:T(8,128)(2,1)}) %all-gather.3.cloned.1.call-update) | async-done | bytes 4718608 | tf_op jit(solution)/shard_map/all_gather | solution.py:160
  93.4 4.6 %gather_fusion.1 = bf16[4,2304,128]{2,1,0:T(8,128)(2,1)} fusion(bf16[8,2304,128]{2,1,0:T(8,128)(2,1)} %bitcast.128, s32[1024]{0:T(1024)S(1)} %pad_clamp_fusion.1), kind=kCustom, calls=%fused_computation.1 | custom fusion | bytes 4718608 | tf_op jit(solution)/shard_map/jit(_take)/gather | solution.py:166
  99.6 2.4 %fusion.21 = f32[4,128,128]{1,2,0:T(8,128)S(1)} fusion(bf16[4,128,2048]{2,1,0:T(8,128)(2,1)S(1)} %bitcast.116, bf16[4,2304,128]{2,1,0:T(8,128)(2,1)} %gather_fusion.1), kind=kOutput, calls=%fused_computation.32 | convolution fusion | flops 268435456 | bytes 4456448 | tf_op jit(solution)/shard_map/bnd,bdc->bnc/dot_general | solution.py:182
  105.4 6.5 %collective-permute-done.5 = f32[4,128,128]{2,1,0:T(8,128)S(1)} collective-permute-done((f32[4,128,128]{2,1,0:T(8,128)S(1)}, f32[4,128,128]{2,1,0:T(8,128)S(1)}, u32[]{:S(2)}, u32[]{:S(2)}) %collective-permute-start.5) | collective-permute-done | bytes 262176 | tf_op jit(solution)/shard_map/ppermute | solution.py:45
  112.1 2.3 %fusion.8 = f32[8,128,2048]{2,1,0:T(8,128)S(1)} fusion(bf16[512,2048]{1,0:T(8,128)(2,1)S(1)} %copy-done, pred[512,8]{0,1:T(8,128)(4,1)S(1)} %iota_compare_fusion, bf16[512,128]{0,1:T(8,128)(2,1)S(1)} %copy.45), kind=kOutput, calls=%fused_computation.17 | convolution fusion | flops 2148007936 | bytes 10620928 | tf_op jit(solution)/shard_map/nsc,nd->scd/dot_general | solution.py:100
  114.4 3.3 %copy-done.6 = f32[8,128,2048]{2,1,0:T(8,128)} copy-done((f32[8,128,2048]{2,1,0:T(8,128)}, f32[8,128,2048]{2,1,0:T(8,128)S(1)}, u32[]{:S(2)}) %copy-start.6) | copy-done | bytes 8388632
  130.3 40.6 %collective-permute-done.14 = bf16[2,128,256]{2,1,0:T(8,128)(2,1)S(1)} collective-permute-done((bf16[2,128,256]{2,1,0:T(8,128)(2,1)S(1)}, bf16[2,128,256]{2,1,0:T(8,128)(2,1)S(1)}, u32[]{:S(2)}, u32[]{:S(2)}) %collective-permute-start.14) | collective-permute-done | bytes 131104 | tf_op jit(solution)/shard_map/ppermute | solution.py:128
  171.6 3.2 %constant_dynamic-slice_fusion.3 = f32[2,1,128,2048]{3,2,1,0:T(8,128)} fusion(f32[2,4,128,2048]{3,2,1,0:T(8,128)} %bitcast.119, s32[]{:T(128)S(6)} %select_n.115), kind=kLoop, calls=%fused_computation.81 | loop fusion | bytes 4194308 | tf_op jit(solution)/shard_map/jit(dynamic_index_in_dim)/dynamic_slice | solution.py:124
  174.8 1.9 copy.46
  180.6 2.4 %fusion.7 = f32[2,128,2048]{1,2,0:T(8,128)S(1)} fusion(f32[2,1,128,2048]{2,3,0,1:T(8,128)S(1)} %copy.46, bf16[2,128,2048]{1,2,0:T(8,128)(2,1)} %collective-permute-done.8, bf16[2,128,2048]{1,2,0:T(8,128)(2,1)} %collective-permute-done.7, bf16[2,128,2048]{1,2,0:T(8,128)(2,1)} %collective-permute-done.6), kind=kLoop, calls=%fused_computation.16 | loop fusion | flops 3145728 | bytes 7340032 | tf_op jit(solution)/shard_map/add | solution.py:128
  185.4 2.7 %fusion.18 = f32[4,128,2048]{2,1,0:T(8,128)} fusion(bf16[4,128,128]{2,1,0:T(8,128)(2,1)S(1)} %multiply_convert_fusion.1, bf16[4,2304,128]{2,1,0:T(8,128)(2,1)S(1)} %copy-done.4), kind=kOutput, calls=%fused_computation.27 | convolution fusion | flops 268435456 | bytes 6422528 | tf_op jit(solution)/shard_map/bnc,bdc->bnd/dot_general | solution.py:192
  188.1 5.4 %copy.59 = f32[512,2048]{0,1:T(8,128)} copy(f32[512,2048]{1,0:T(8,128)} %bitcast.117) | data formatting | bytes 8388608 | tf_op jit(solution)/shard_map/reshape | solution.py:194
  193.5 6.5 %add.180 = f32[512,2048]{0,1:T(8,128)} add(f32[512,2048]{0,1:T(8,128)} %bitcast_add_fusion.1, f32[512,2048]{0,1:T(8,128)} %copy.59) | non-fusion elementwise | flops 1048576 | bytes 12582912 | tf_op jit(solution)/shard_map/add | solution.py:195
  200.0 5.4 %copy.56 = f32[512,2048]{1,0:T(8,128)} copy(f32[512,2048]{0,1:T(8,128)} %add.180) | data formatting | bytes 8388608
  205.5 1.8 fusion.48
  207.3 3.7 %fusion.28 = (f32[2048,128]{1,0:T(8,128)}, f32[2048,128]{1,0:T(8,128)}) fusion(f32[2048,128]{1,0:T(8,128)S(1)} %copy-done.9, f32[2048,128]{1,0:T(8,128)} %param.17, bf16[128,2048]{0,1:T(8,128)(2,1)} %collective-permute-done.9, f32[2,128,2048]{1,2,0:T(8,128)} %copy-done.5, s32[]{:T(128)S(6)} %select_n.120), kind=kLoop, calls=%fused_computation.37 | loop fusion | flops 3407872 | bytes 5767172 | tf_op jit(solution)/shard_map/div | solution.py:22
  (101 shorter events, 35.3 us)
Async XLA Ops:
  7.2 92.5 %copy-start = (bf16[512,2048]{1,0:T(8,128)(2,1)S(1)}, bf16[512,2048]{1,0:T(8,128)(2,1)}, u32[]{:S(2)}) copy-start(bf16[512,2048]{1,0:T(8,128)(2,1)} %param.12) | copy-start | bytes 6291460
  7.2 86.2 %all-gather.3.cloned.1.call-start = ((), (), s32[]{:S(2)}) async-start(), calls=%async_computation | async-start | bytes 5308416 | tf_op jit(solution)/shard_map/all_gather | solution.py:160
  10.5 5.9 %copy-start.13 = (s32[4]{0:T(128)S(1)}, s32[4]{0:T(128)}, u32[]{:S(2)}) copy-start(s32[4]{0:T(128)} %param.21) | copy-start | bytes 52
  10.5 5.9 %copy-start.3 = (s32[8]{0:T(128)S(1)}, s32[8]{0:T(128)}, u32[]{:S(2)}) copy-start(s32[8]{0:T(128)} %param.23) | copy-start | bytes 100
  10.5 6.6 %copy-start.2 = (s32[8]{0:T(128)S(1)}, s32[8]{0:T(128)}, u32[]{:S(2)}) copy-start(s32[8]{0:T(128)} %param.22) | copy-start | bytes 100
  15.1 8.2 %collective-permute-start = (bf16[2,2,2048,256]{3,2,0,1:T(8,128)(2,1)}, bf16[2,2,2048,256]{3,2,0,1:T(8,128)(2,1)}, u32[]{:S(2)}, u32[]{:S(2)}) collective-permute-start(bf16[2,2,2048,256]{3,2,0,1:T(8,128)(2,1)} %copy_bitcast_fusion), channel_id=1, source_target_pairs={{0,1},{1,0},{2,3},{3,2},{4,5},{5,4},{6,7},{7,6},{8,9},{9,8},{10,11... | collective-permute-start | bytes 12582920 | tf_op jit(solution)/shard_map/ppermute | solution.py:68
  16.4 6.9 %collective-permute-start.1 = (bf16[512,2,256]{2,0,1:T(8,128)(2,1)}, bf16[512,2,256]{2,0,1:T(8,128)(2,1)S(1)}, u32[]{:S(2)}, u32[]{:S(2)}) collective-permute-start(bf16[512,2,256]{2,0,1:T(8,128)(2,1)} %copy.36), channel_id=1, source_target_pairs={{0,1},{1,0},{2,3},{3,2},{4,5},{5,4},{6,7},{7,6},{8,9},{9,8},{10,11... | collective-permute-start | bytes 1572872 | tf_op jit(solution)/shard_map/ppermute | solution.py:69
  27.6 27.1 %collective-permute-start.3 = (bf16[256,2048]{0,1:T(8,128)(2,1)}, bf16[256,2048]{0,1:T(8,128)(2,1)}, u32[]{:S(2)}, u32[]{:S(2)}) collective-permute-start(bf16[256,2048]{0,1:T(8,128)(2,1)} %get-tuple-element.29), channel_id=1, source_target_pairs={{0,2},{1,3},{2,0},{3,1},{4,6},{5,7},{6,4},{7,5},{8,10},{9,11},{10,... | collective-permute-start | bytes 3145736 | tf_op jit(solution)/shard_map/ppermute | solution.py:83
  30.5 46.2 %collective-permute-start.2 = (bf16[256,2048]{0,1:T(8,128)(2,1)}, bf16[256,2048]{0,1:T(8,128)(2,1)}, u32[]{:S(2)}, u32[]{:S(2)}) collective-permute-start(bf16[256,2048]{0,1:T(8,128)(2,1)} %get-tuple-element.28), channel_id=1, source_target_pairs={{0,2},{1,3},{2,0},{3,1},{4,6},{5,7},{6,4},{7,5},{8,10},{9,11},{10,... | collective-permute-start | bytes 3145736 | tf_op jit(solution)/shard_map/ppermute | solution.py:82
  99.5 3.1 %collective-permute-start.4 = (f32[4,128,128]{2,1,0:T(8,128)S(1)}, f32[4,128,128]{2,1,0:T(8,128)S(1)}, u32[]{:S(2)}, u32[]{:S(2)}) collective-permute-start(f32[4,128,128]{2,1,0:T(8,128)S(1)} %copy.43), channel_id=1, source_target_pairs={{0,1},{1,0},{2,3},{3,2},{4,5},{5,4},{6,7},{7,6},{8,9},{9,8},{10,11... | collective-permute-start | bytes 786440 | tf_op jit(solution)/shard_map/ppermute | solution.py:45
  102.1 2.1 collective-permute-start.10
  102.7 9.2 %collective-permute-start.5 = (f32[4,128,128]{2,1,0:T(8,128)S(1)}, f32[4,128,128]{2,1,0:T(8,128)S(1)}, u32[]{:S(2)}, u32[]{:S(2)}) collective-permute-start(f32[4,128,128]{2,1,0:T(8,128)S(1)} %add.177), channel_id=1, source_target_pairs={{0,2},{1,3},{2,0},{3,1},{4,6},{5,7},{6,4},{7,5},{8,10},{9,11},{10,... | collective-permute-start | bytes 786440 | tf_op jit(solution)/shard_map/ppermute | solution.py:45
  104.3 21.5 %collective-permute-start.11 = (f32[4,128,128]{1,2,0:T(8,128)S(1)}, f32[4,128,128]{1,2,0:T(8,128)}, u32[]{:S(2)}, u32[]{:S(2)}) collective-permute-start(f32[4,128,128]{1,2,0:T(8,128)S(1)} %add.194), channel_id=1, source_target_pairs={{0,2},{1,3},{2,0},{3,1},{4,6},{5,7},{6,4},{7,5},{8,10},{9,11},{10,... | collective-permute-start | bytes 786440 | tf_op jit(solution)/shard_map/ppermute | solution.py:45
  119.7 60.9 %collective-permute-start.8 = (bf16[2,128,2048]{1,2,0:T(8,128)(2,1)}, bf16[2,128,2048]{1,2,0:T(8,128)(2,1)}, u32[]{:S(2)}, u32[]{:S(2)}) collective-permute-start(bf16[2,128,2048]{1,2,0:T(8,128)(2,1)} %bitcast.129), channel_id=1, source_target_pairs={{0,12},{4,8},{8,4},{12,0},{16,28},{20,24},{24,20},{28,16},{1,13},{... | collective-permute-start | bytes 3145736 | tf_op jit(solution)/shard_map/ppermute | solution.py:128
  120.2 6.8 %copy-start.8 = (bf16[512,2,256]{2,1,0:T(2,128)(2,1)S(1)}, bf16[512,2,256]{2,1,0:T(2,128)(2,1)}, u32[]{:S(2)}) copy-start(bf16[512,2,256]{2,1,0:T(2,128)(2,1)} %param.13) | copy-start | bytes 1572868
  121.5 59.1 %collective-permute-start.7 = (bf16[2,128,2048]{1,2,0:T(8,128)(2,1)}, bf16[2,128,2048]{1,2,0:T(8,128)(2,1)}, u32[]{:S(2)}, u32[]{:S(2)}) collective-permute-start(bf16[2,128,2048]{1,2,0:T(8,128)(2,1)} %bitcast.130), channel_id=1, source_target_pairs={{0,8},{4,12},{8,0},{12,4},{16,24},{20,28},{24,16},{28,20},{1,9},{5... | collective-permute-start | bytes 3145736 | tf_op jit(solution)/shard_map/ppermute | solution.py:128
  124.3 56.3 %collective-permute-start.6 = (bf16[2,128,2048]{1,2,0:T(8,128)(2,1)}, bf16[2,128,2048]{1,2,0:T(8,128)(2,1)}, u32[]{:S(2)}, u32[]{:S(2)}) collective-permute-start(bf16[2,128,2048]{1,2,0:T(8,128)(2,1)} %bitcast.107), channel_id=1, source_target_pairs={{0,4},{4,0},{8,12},{12,8},{16,20},{20,16},{24,28},{28,24},{1,5},{5... | collective-permute-start | bytes 3145736 | tf_op jit(solution)/shard_map/ppermute | solution.py:128
  128.3 42.6 %collective-permute-start.14 = (bf16[2,128,256]{2,1,0:T(8,128)(2,1)S(1)}, bf16[2,128,256]{2,1,0:T(8,128)(2,1)S(1)}, u32[]{:S(2)}, u32[]{:S(2)}) collective-permute-start(bf16[2,128,256]{2,1,0:T(8,128)(2,1)S(1)} %get-tuple-element.31), channel_id=1, source_target_pairs={{0,12},{4,8},{8,4},{12,0},{16,28},{20,24},{24,20},{28,16},{1,13},{... | collective-permute-start | bytes 393224 | tf_op jit(solution)/shard_map/ppermute | solution.py:128
  128.8 47.9 %collective-permute-start.13 = (bf16[2,128,256]{2,1,0:T(8,128)(2,1)}, bf16[2,128,256]{2,1,0:T(8,128)(2,1)S(1)}, u32[]{:S(2)}, u32[]{:S(2)}) collective-permute-start(bf16[2,128,256]{2,1,0:T(8,128)(2,1)} %get-tuple-element.32), channel_id=1, source_target_pairs={{0,8},{4,12},{8,0},{12,4},{16,24},{20,28},{24,16},{28,20},{1,9},{5... | collective-permute-start | bytes 393224 | tf_op jit(solution)/shard_map/ppermute | solution.py:128
  170.9 6.5 %collective-permute-start.12 = (bf16[2,128,256]{2,1,0:T(8,128)(2,1)S(1)}, bf16[2,128,256]{2,1,0:T(8,128)(2,1)}, u32[]{:S(2)}, u32[]{:S(2)}) collective-permute-start(bf16[2,128,256]{2,1,0:T(8,128)(2,1)S(1)} %get-tuple-element.30), channel_id=1, source_target_pairs={{0,4},{4,0},{8,12},{12,8},{16,20},{20,16},{24,28},{28,24},{1,5},{5... | collective-permute-start | bytes 393224 | tf_op jit(solution)/shard_map/ppermute | solution.py:128
  179.1 26.4 %collective-permute-start.15 = (bf16[128,256]{1,0:T(8,128)(2,1)}, bf16[128,256]{1,0:T(8,128)(2,1)}, u32[]{:S(2)}, u32[]{:S(2)}) collective-permute-start(bf16[128,256]{1,0:T(8,128)(2,1)} %fusion.52), channel_id=1, source_target_pairs={{0,16},{4,20},{8,24},{12,28},{16,0},{20,4},{24,8},{28,12},{1,17},{... | collective-permute-start | bytes 196616 | tf_op jit(solution)/shard_map/ppermute | solution.py:133
  184.0 23.4 %collective-permute-start.9 = (bf16[128,2048]{0,1:T(8,128)(2,1)}, bf16[128,2048]{0,1:T(8,128)(2,1)}, u32[]{:S(2)}, u32[]{:S(2)}) collective-permute-start(bf16[128,2048]{0,1:T(8,128)(2,1)} %fusion.34), channel_id=1, source_target_pairs={{0,16},{4,20},{8,24},{12,28},{16,0},{20,4},{24,8},{28,12},{1,17},{... | collective-permute-start | bytes 1572872 | tf_op jit(solution)/shard_map/ppermute | solution.py:133
  200.0 7.3 %copy-start.9 = (f32[2048,128]{1,0:T(8,128)S(1)}, f32[2048,128]{1,0:T(8,128)}, u32[]{:S(2)}) copy-start(f32[2048,128]{1,0:T(8,128)} %param.18) | copy-start | bytes 3145732
  205.5 5.6 %copy-start.1 = (bf16[512,2048]{1,0:T(8,128)(2,1)S(1)}, bf16[512,2048]{1,0:T(8,128)(2,1)}, u32[]{:S(2)}) copy-start(bf16[512,2048]{1,0:T(8,128)(2,1)} %param.12) | copy-start | bytes 6291460
  (7 other events, 25.0 us)
Sparse Core Ops, SparseCore 0:
  10.6 82.7 all-gather.2

commit v13 on v9

--- a/solution.py
+++ b/solution.py
@@ -106,16 +106,16 @@
     slot_tenant = jnp.argsort(tenant_slot)
     slot_scale = adapter_alpha_factor / tenant_rank[slot_tenant].astype(jnp.float32)
     b_sc = b_sc * slot_scale[:, None, None, None]
-    full = jnp.concatenate([a_sc, b_sc.reshape(TENANTS, rank_width, kv_shard)], axis=2)
-    if full.shape[0] % 4:
-        own = grouped_exchange(full)
+    b_full = b_sc.reshape(TENANTS, rank_width, kv_shard)
+    if TENANTS % 4:
+        a_own = grouped_exchange(a_sc)
+        b_own = grouped_exchange(b_full)
     else:
-        split = full.shape[2] // 2
-        first = group_stage(full[..., :split])
-        later, first = lax.optimization_barrier((full[..., split:], first))
-        second = group_stage(later)
-        own = jnp.concatenate([cross_stage(first), cross_stage(second)], axis=-1)
-    return own[:, :feat_shard].T, own[:, feat_shard:]
+        a_acc = group_stage(a_sc)
+        b_full, a_acc = lax.optimization_barrier((b_full, a_acc))
+        a_own = cross_stage(a_acc)
+        b_own = grouped_exchange(b_full)
+    return a_own.T, b_own
 
 
 def group_stage(full):
@@ -189,10 +189,12 @@
     b_as_a = b_master.astype(jnp.bfloat16).reshape(b_rows_own * kv_shard // rank_width, rank_width)
     packed = jnp.concatenate([a_master.astype(jnp.bfloat16), b_as_a], axis=0)
     packed_all = lax.all_gather(packed, "dp", axis=0, tiled=False)
+    frozen_gradient_share = frozen_gradient(grad_out, base_weight, feat_shard)
+    frozen_gradient_share, packed_all = lax.optimization_barrier((frozen_gradient_share, packed_all))
     block_slot = tenant_slot[block_tenant]
     slot_major = dp_size == TENANTS
     if slot_major:
-        picked = jnp.take(packed_all, block_slot, axis=0)
+        picked = jnp.take(packed_all, block_slot, axis=0, mode="clip")
         a_blocks = picked[:, :a_rows_own]
         b_blocks = picked[:, a_rows_own:].reshape(block_count, 2, PADDED_RANK, kv_shard)
     else:
@@ -212,12 +214,12 @@
     back_part = jnp.einsum(
         "bnpk,bprk->bnpr", dy_blocks, b_blocks, preferred_element_type=jnp.float32
     ).reshape(block_count, TENANT_BLOCK, rank_width)
-    mid_sum, backward_gradient_sum = tensor_sum_pair(mid_part, back_part)
+    backward_gradient_sum = tensor_sum((back_part,))[0]
+    mid_sum = tensor_sum((mid_part,))[0]
     middle_rank_rows = (mid_sum * column_rank_mask[:, None, :]).astype(jnp.bfloat16)
     backward_token_rows = (
         backward_gradient_sum * (column_rank_mask * adapter_scale_factor[:, None])[:, None, :]
     ).astype(jnp.bfloat16)
-    frozen_gradient_share = frozen_gradient(grad_out, base_weight, feat_shard)
     adapter_gradient_term = jnp.einsum(
         "bnc,bdc->bnd", backward_token_rows, a_blocks, preferred_element_type=jnp.float32
     ).reshape(tok_rows, feat_shard)

time: 255 us -> 215 us (0.84)
  waiting for transfers between devices: 125 us -> 101 us
  matrix products: 35.7 us -> 22.5 us
  other arithmetic: 24.2 us -> 19.9 us
    all_gather x1, waiting for transfers between devices: 68.7 us -> 10.8 us  [local(): packed_all = lax.all_gather(packed, 'dp', axis=0, tiled=False)]
    ppermute x1, waiting for transfers between devices: 0.01 us -> 22 us  [frozen_gradient(): lax.ppermute(far_part[:half], 'tensor', row_pairs)]
    ppermute x2 -> x1, waiting for transfers between devices: 21.9 us -> 0.01 us  [cross_stage(): lax.ppermute(part.astype(jnp.bfloat16), 'dp', pairs).astype(jnp.float32)]
    ppermute x6 -> x3, waiting for transfers between devices: 13.9 us -> 33.9 us  [group_stage(): lax.ppermute(part.astype(jnp.bfloat16), 'dp', pairs).astype(jnp.float32)]
    slice x1 -> x0, other arithmetic: 6.55 us -> none  [slot_major_grads(): first = group_stage(full[..., :split])]
    ppermute x1, waiting for transfers between devices: 13.7 us -> 20.2 us  [frozen_gradient(): lax.ppermute(far_part[half:], 'tensor', row_pairs)]
    dynamic_slice x0 -> x3, local copies, waits for them, and re-layouts: none -> 5.59 us  [the longest x2 5.13 us: group_stage(): acc = lax.dynamic_index_in_dim(by_member, member, axis=1, keepdims=False)]
    add x3 -> x4, other arithmetic: 1.29 us -> 6.62 us  [the longest x1 6.51 us: local(): input_gradient_layer = frozen_gradient_share + adapter_gradient_term]
  transfers between devices with their start and end apart: 16 -> 17, of which waited for: 9 -> 11; matrix products, arithmetic and copies ran while one was open for 28% -> 30% of each run, Pallas kernels for 0% -> 0%
where the time goes in v13:
time: 215 us; the launch traced here: 214 us
  waiting for transfers between devices  101 us (47%)
  local copies, waits for them, and re-layouts  40.4 us (19%)
  matrix products  22.5 us (10%)
  other arithmetic  19.9 us (9%)
  starting transfers between devices  15.4 us (7%)
  between operations  14.3 us (7%)
    ppermute x3, waiting for transfers between devices, group_stage(): lax.ppermute(part.astype(jnp.bfloat16), 'dp', pairs).astype(jnp.float32)  33.9 us
    ppermute x1, waiting for transfers between devices, frozen_gradient(): lax.ppermute(far_part[:half], 'tensor', row_pairs)  22 us
    ppermute x1, waiting for transfers between devices, frozen_gradient(): lax.ppermute(far_part[half:], 'tensor', row_pairs)  20.2 us
    unnamed x31, local copies, waits for them, and re-layouts  13.7 us
    all_gather x1, waiting for transfers between devices, local(): packed_all = lax.all_gather(packed, 'dp', axis=0, tiled=False)  10.8 us
    dot_general x2, matrix products, chip_partial(): jnp.einsum('tpk,pdk->td', partner_dy, other, preferred_element_type=jnp.f...  8.52 us
    add x1, other arithmetic, local(): input_gradient_layer = frozen_gradient_share + adapter_gradient_term  6.51 us
    ppermute x4, waiting for transfers between devices, grouped_exchange(): lax.ppermute(part.astype(jnp.bfloat16), 'dp', pairs).astype(jnp.float32)  6 us
  transfers between devices with their start and end apart: 17, of which 11 were waited for; matrix products, arithmetic and copies ran while one was open for 30% of the time, Pallas kernels for 0%

profile of v13, /device:TPU:0, one launch (start us, length us, event | category | flops | bytes accessed | tf_op | source)
XLA Modules:
  0.0 213.9 jit_solution(13615980936679194900)
XLA Ops:
  10.5 4.5 %copy_bitcast_fusion = bf16[2,2,2048,256]{3,2,0,1:T(8,128)(2,1)} fusion(bf16[2,2,2,2048,256]{4,3,2,1,0:T(8,128)(2,1)} %bitcast.123, s32[]{:T(128)S(6)} %select_n.108), kind=kLoop, calls=%fused_computation.8 | loop fusion | bytes 8388612 | tf_op jit(solution)/shard_map/jit(dynamic_index_in_dim)/squeeze | solution.py:64
  17.8 2.9 %fusion.2 = f32[2048,512,1]{1,0,2:T(8,128)S(1)} fusion(bf16[2,2,2,2048,256]{4,3,2,1,0:T(8,128)(2,1)} %bitcast.124, s32[]{:T(128)S(6)} %select_n.110, s32[]{:T(128)S(6)} %select_n.107, bf16[512,2,256]{2,1,0:T(2,128)(2,1)S(1)} %copy-done.7), kind=kOutput, calls=%fused_computation.10 | convolution fusion | flops 1073741824 | bytes 6815752 | tf_op jit(solution)/shard_map/tpk,pdk->td/dot_general | solution.py:74
  20.7 2.6 %collective-permute-done.1 = bf16[512,2,256]{2,0,1:T(8,128)(2,1)S(1)} collective-permute-done((bf16[512,2,256]{2,0,1:T(8,128)(2,1)}, bf16[512,2,256]{2,0,1:T(8,128)(2,1)S(1)}, u32[]{:S(2)}, u32[]{:S(2)}) %collective-permute-start.1) | collective-permute-done | bytes 524320 | tf_op jit(solution)/shard_map/ppermute | solution.py:69
  23.3 2.9 %fusion.1 = bf16[512,2048]{0,1:T(8,128)(2,1)S(1)} fusion(bf16[512,2,256]{2,0,1:T(8,128)(2,1)S(1)} %collective-permute-done.1, f32[2048,512,1]{1,0,2:T(8,128)S(1)} %fusion.2, bf16[2,2,2048,256]{3,2,0,1:T(8,128)(2,1)} %collective-permute-done, s32[]{:T(128)S(6)} %select_n.109), kind=kOutput, calls=%fused_computation.9 | convolution fusion | flops 1075838976 | bytes 8912900 | tf_op jit(solution)/shard_map/tpk,pdk->td/dot_general | solution.py:75
  27.6 2.9 %collective-permute-start.3 = (bf16[256,2048]{0,1:T(8,128)(2,1)}, bf16[256,2048]{0,1:T(8,128)(2,1)}, u32[]{:S(2)}, u32[]{:S(2)}) collective-permute-start(bf16[256,2048]{0,1:T(8,128)(2,1)} %get-tuple-element.33), channel_id=1, source_target_pairs={{0,2},{1,3},{2,0},{3,1},{4,6},{5,7},{6,4},{7,5},{8,10},{9,11},{10,... | collective-permute-start | bytes 3145736 | tf_op jit(solution)/shard_map/ppermute | solution.py:83
  31.6 2.9 %fusion.4 = f32[2048,512,1]{1,0,2:T(8,128)S(1)} fusion(bf16[2,2,2,2048,256]{4,3,2,1,0:T(8,128)(2,1)} %bitcast.125, s32[]{:T(128)S(6)} %select_n.104, s32[]{:T(128)S(6)} %select_n.107, bf16[512,2,256]{2,1,0:T(2,128)(2,1)S(1)} %copy-done.7), kind=kOutput, calls=%fused_computation.12 | convolution fusion | flops 1073741824 | bytes 6815752 | tf_op jit(solution)/shard_map/tpk,pdk->td/dot_general | solution.py:74
  34.5 20.2 %collective-permute-done.3 = bf16[256,2048]{0,1:T(8,128)(2,1)} collective-permute-done((bf16[256,2048]{0,1:T(8,128)(2,1)}, bf16[256,2048]{0,1:T(8,128)(2,1)}, u32[]{:S(2)}, u32[]{:S(2)}) %collective-permute-start.3) | collective-permute-done | bytes 1048608 | tf_op jit(solution)/shard_map/ppermute | solution.py:83
  54.7 22.0 %collective-permute-done.2 = bf16[256,2048]{0,1:T(8,128)(2,1)} collective-permute-done((bf16[256,2048]{0,1:T(8,128)(2,1)}, bf16[256,2048]{0,1:T(8,128)(2,1)}, u32[]{:S(2)}, u32[]{:S(2)}) %collective-permute-start.2) | collective-permute-done | bytes 1048608 | tf_op jit(solution)/shard_map/ppermute | solution.py:82
  76.7 5.6 %bitcast_add_fusion.1 = f32[512,2048]{0,1:T(8,128)} fusion(f32[2048,512,1]{1,0,2:T(8,128)S(1)} %fusion.4, bf16[512,2,256]{2,0,1:T(8,128)(2,1)S(1)} %collective-permute-done.1, bf16[256,2048]{0,1:T(8,128)(2,1)} %collective-permute-done.3, bf16[256,2048]{0,1:T(8,128)(2,1)} %collective-permute-done.2, bf16[2,2,2048,256]{3,2,0,1:T(8,128)(2,1)} %collective-permute-done, ...), kind=kOutput, calls=%fused_computation.6 | convolution fusion | flops 1080033280 | bytes 13107204 | tf_op jit(solution)/shard_map/tpk,pdk->td/dot_general | solution.py:75
  82.3 10.8 %all-gather.3.cloned.1.call-done = bf16[18432,128]{1,0:T(8,128)(2,1)} async-done(((bf16[2304,128]{1,0:T(8,128)(2,1)}), bf16[18432,128]{1,0:T(8,128)(2,1)}) %all-gather.3.cloned.1.call-update) | async-done | bytes 4718608 | tf_op jit(solution)/shard_map/all_gather | solution.py:191
  93.2 4.6 %gather_fusion.1 = bf16[4,2304,128]{2,1,0:T(8,128)(2,1)} fusion(bf16[8,2304,128]{2,1,0:T(8,128)(2,1)} %bitcast.129, s32[1024]{0:T(1024)S(1)} %pad_clamp_fusion.1), kind=kCustom, calls=%fused_computation.1 | custom fusion | bytes 4718608 | tf_op jit(solution)/shard_map/jit(_take)/gather | solution.py:197
  99.4 2.4 %fusion.21 = f32[4,128,128]{1,2,0:T(8,128)S(1)} fusion(bf16[4,128,2048]{2,1,0:T(8,128)(2,1)S(1)} %bitcast.117, bf16[4,2304,128]{2,1,0:T(8,128)(2,1)} %gather_fusion.1), kind=kOutput, calls=%fused_computation.32 | convolution fusion | flops 268435456 | bytes 4456448 | tf_op jit(solution)/shard_map/bnd,bdc->bnc/dot_general | solution.py:213
  105.8 5.9 %collective-permute-done.5 = f32[4,128,128]{2,1,0:T(8,128)S(1)} collective-permute-done((f32[4,128,128]{2,1,0:T(8,128)S(1)}, f32[4,128,128]{2,1,0:T(8,128)S(1)}, u32[]{:S(2)}, u32[]{:S(2)}) %collective-permute-start.5) | collective-permute-done | bytes 262176 | tf_op jit(solution)/shard_map/ppermute | solution.py:45
  111.9 2.3 %fusion.8 = f32[8,128,2048]{2,1,0:T(8,128)S(1)} fusion(bf16[512,2048]{1,0:T(8,128)(2,1)S(1)} %copy-done, pred[512,8]{0,1:T(8,128)(4,1)S(1)} %iota_compare_fusion, bf16[512,128]{0,1:T(8,128)(2,1)S(1)} %copy.49), kind=kOutput, calls=%fused_computation.17 | convolution fusion | flops 2148007936 | bytes 10620928 | tf_op jit(solution)/shard_map/nsc,nd->scd/dot_general | solution.py:100
  114.2 3.3 %copy-done.6 = f32[8,128,2048]{2,1,0:T(8,128)} copy-done((f32[8,128,2048]{2,1,0:T(8,128)}, f32[8,128,2048]{2,1,0:T(8,128)S(1)}, u32[]{:S(2)}) %copy-start.6) | copy-done | bytes 8388632
  127.5 3.2 %constant_dynamic-slice_fusion.3 = f32[2,1,128,2048]{3,2,1,0:T(8,128)} fusion(f32[2,4,128,2048]{3,2,1,0:T(8,128)} %bitcast.120, s32[]{:T(128)S(6)} %select_n.117), kind=kLoop, calls=%fused_computation.81 | loop fusion | bytes 4194308 | tf_op jit(solution)/shard_map/jit(dynamic_index_in_dim)/dynamic_slice | solution.py:125
  132.6 14.2 %collective-permute-done.10 = bf16[2,128,2048]{1,2,0:T(8,128)(2,1)} collective-permute-done((bf16[2,128,2048]{1,2,0:T(8,128)(2,1)}, bf16[2,128,2048]{1,2,0:T(8,128)(2,1)}, u32[]{:S(2)}, u32[]{:S(2)}) %collective-permute-start.10) | collective-permute-done | bytes 1048608 | tf_op jit(solution)/shard_map/ppermute | solution.py:129
  146.8 18.8 %collective-permute-done.9 = bf16[2,128,2048]{1,2,0:T(8,128)(2,1)} collective-permute-done((bf16[2,128,2048]{1,2,0:T(8,128)(2,1)}, bf16[2,128,2048]{1,2,0:T(8,128)(2,1)}, u32[]{:S(2)}, u32[]{:S(2)}) %collective-permute-start.9) | collective-permute-done | bytes 1048608 | tf_op jit(solution)/shard_map/ppermute | solution.py:129
  176.1 2.9 %collective-permute-done.13 = bf16[2,128,256]{2,1,0:T(8,128)(2,1)S(1)} collective-permute-done((bf16[2,128,256]{2,1,0:T(8,128)(2,1)S(1)}, bf16[2,128,256]{2,1,0:T(8,128)(2,1)S(1)}, u32[]{:S(2)}, u32[]{:S(2)}) %collective-permute-start.13) | collective-permute-done | bytes 131104 | tf_op jit(solution)/shard_map/ppermute | solution.py:159
  179.7 2.7 %fusion.18 = f32[4,128,2048]{2,1,0:T(8,128)} fusion(bf16[4,128,128]{2,1,0:T(8,128)(2,1)S(1)} %multiply_convert_fusion.1, bf16[4,2304,128]{2,1,0:T(8,128)(2,1)S(1)} %copy-done.4), kind=kOutput, calls=%fused_computation.27 | convolution fusion | flops 268435456 | bytes 6422528 | tf_op jit(solution)/shard_map/bnc,bdc->bnd/dot_general | solution.py:223
  182.4 5.5 %copy.59 = f32[512,2048]{0,1:T(8,128)} copy(f32[512,2048]{1,0:T(8,128)} %bitcast.118) | data formatting | bytes 8388608 | tf_op jit(solution)/shard_map/reshape | solution.py:225
  187.9 6.5 %add.180 = f32[512,2048]{0,1:T(8,128)} add(f32[512,2048]{0,1:T(8,128)} %bitcast_add_fusion.1, f32[512,2048]{0,1:T(8,128)} %copy.59) | non-fusion elementwise | flops 1048576 | bytes 12582912 | tf_op jit(solution)/shard_map/add | solution.py:226
  194.4 5.4 %copy.56 = f32[512,2048]{1,0:T(8,128)} copy(f32[512,2048]{0,1:T(8,128)} %add.180) | data formatting | bytes 8388608
  203.3 3.7 %fusion.28 = (f32[2048,128]{1,0:T(8,128)}, f32[2048,128]{1,0:T(8,128)}) fusion(f32[2048,128]{1,0:T(8,128)S(1)} %copy-done.9, f32[2048,128]{1,0:T(8,128)} %param.17, bf16[128,2048]{0,1:T(8,128)(2,1)} %collective-permute-done.11, f32[2,128,2048]{1,2,0:T(8,128)} %copy-done.5, s32[]{:T(128)S(6)} %select_n.122), kind=kLoop, calls=%fused_computation.37 | loop fusion | flops 3407872 | bytes 5767172 | tf_op jit(solution)/shard_map/div | solution.py:22
  (99 shorter events, 40.8 us)
Async XLA Ops:
  7.2 92.3 %copy-start = (bf16[512,2048]{1,0:T(8,128)(2,1)S(1)}, bf16[512,2048]{1,0:T(8,128)(2,1)}, u32[]{:S(2)}) copy-start(bf16[512,2048]{1,0:T(8,128)(2,1)} %param.12) | copy-start | bytes 6291460
  7.2 86.0 %all-gather.3.cloned.1.call-start = ((), (), s32[]{:S(2)}) async-start(), calls=%async_computation | async-start | bytes 5308416 | tf_op jit(solution)/shard_map/all_gather | solution.py:191
  10.5 6.6 %copy-start.2 = (s32[8]{0:T(128)S(1)}, s32[8]{0:T(128)}, u32[]{:S(2)}) copy-start(s32[8]{0:T(128)} %param.22) | copy-start | bytes 100
  15.1 8.2 %collective-permute-start = (bf16[2,2,2048,256]{3,2,0,1:T(8,128)(2,1)}, bf16[2,2,2048,256]{3,2,0,1:T(8,128)(2,1)}, u32[]{:S(2)}, u32[]{:S(2)}) collective-permute-start(bf16[2,2,2048,256]{3,2,0,1:T(8,128)(2,1)} %copy_bitcast_fusion), channel_id=1, source_target_pairs={{0,1},{1,0},{2,3},{3,2},{4,5},{5,4},{6,7},{7,6},{8,9},{9,8},{10,11... | collective-permute-start | bytes 12582920 | tf_op jit(solution)/shard_map/ppermute | solution.py:68
  16.4 6.9 %collective-permute-start.1 = (bf16[512,2,256]{2,0,1:T(8,128)(2,1)}, bf16[512,2,256]{2,0,1:T(8,128)(2,1)S(1)}, u32[]{:S(2)}, u32[]{:S(2)}) collective-permute-start(bf16[512,2,256]{2,0,1:T(8,128)(2,1)} %copy.36), channel_id=1, source_target_pairs={{0,1},{1,0},{2,3},{3,2},{4,5},{5,4},{6,7},{7,6},{8,9},{9,8},{10,11... | collective-permute-start | bytes 1572872 | tf_op jit(solution)/shard_map/ppermute | solution.py:69
  27.6 27.1 %collective-permute-start.3 = (bf16[256,2048]{0,1:T(8,128)(2,1)}, bf16[256,2048]{0,1:T(8,128)(2,1)}, u32[]{:S(2)}, u32[]{:S(2)}) collective-permute-start(bf16[256,2048]{0,1:T(8,128)(2,1)} %get-tuple-element.33), channel_id=1, source_target_pairs={{0,2},{1,3},{2,0},{3,1},{4,6},{5,7},{6,4},{7,5},{8,10},{9,11},{10,... | collective-permute-start | bytes 3145736 | tf_op jit(solution)/shard_map/ppermute | solution.py:83
  30.5 46.2 %collective-permute-start.2 = (bf16[256,2048]{0,1:T(8,128)(2,1)}, bf16[256,2048]{0,1:T(8,128)(2,1)}, u32[]{:S(2)}, u32[]{:S(2)}) collective-permute-start(bf16[256,2048]{0,1:T(8,128)(2,1)} %get-tuple-element.32), channel_id=1, source_target_pairs={{0,2},{1,3},{2,0},{3,1},{4,6},{5,7},{6,4},{7,5},{8,10},{9,11},{10,... | collective-permute-start | bytes 3145736 | tf_op jit(solution)/shard_map/ppermute | solution.py:82
  99.4 3.1 %collective-permute-start.4 = (f32[4,128,128]{2,1,0:T(8,128)S(1)}, f32[4,128,128]{2,1,0:T(8,128)S(1)}, u32[]{:S(2)}, u32[]{:S(2)}) collective-permute-start(f32[4,128,128]{2,1,0:T(8,128)S(1)} %copy.43), channel_id=1, source_target_pairs={{0,1},{1,0},{2,3},{3,2},{4,5},{5,4},{6,7},{7,6},{8,9},{9,8},{10,11... | collective-permute-start | bytes 786440 | tf_op jit(solution)/shard_map/ppermute | solution.py:45
  101.9 3.3 %collective-permute-start.6 = (f32[4,128,128]{1,2,0:T(8,128)S(1)}, f32[4,128,128]{1,2,0:T(8,128)S(1)}, u32[]{:S(2)}, u32[]{:S(2)}) collective-permute-start(f32[4,128,128]{1,2,0:T(8,128)S(1)} %fusion.21), channel_id=1, source_target_pairs={{0,1},{1,0},{2,3},{3,2},{4,5},{5,4},{6,7},{7,6},{8,9},{9,8},{10,11... | collective-permute-start | bytes 786440 | tf_op jit(solution)/shard_map/ppermute | solution.py:45
  102.5 9.2 %collective-permute-start.5 = (f32[4,128,128]{2,1,0:T(8,128)S(1)}, f32[4,128,128]{2,1,0:T(8,128)S(1)}, u32[]{:S(2)}, u32[]{:S(2)}) collective-permute-start(f32[4,128,128]{2,1,0:T(8,128)S(1)} %add.177), channel_id=1, source_target_pairs={{0,2},{1,3},{2,0},{3,1},{4,6},{5,7},{6,4},{7,5},{8,10},{9,11},{10,... | collective-permute-start | bytes 786440 | tf_op jit(solution)/shard_map/ppermute | solution.py:45
  105.2 20.4 %collective-permute-start.7 = (f32[4,128,128]{1,2,0:T(8,128)S(1)}, f32[4,128,128]{1,2,0:T(8,128)}, u32[]{:S(2)}, u32[]{:S(2)}) collective-permute-start(f32[4,128,128]{1,2,0:T(8,128)S(1)} %add.181), channel_id=1, source_target_pairs={{0,2},{1,3},{2,0},{3,1},{4,6},{5,7},{6,4},{7,5},{8,10},{9,11},{10,... | collective-permute-start | bytes 786440 | tf_op jit(solution)/shard_map/ppermute | solution.py:45
  119.5 27.4 %collective-permute-start.10 = (bf16[2,128,2048]{1,2,0:T(8,128)(2,1)}, bf16[2,128,2048]{1,2,0:T(8,128)(2,1)}, u32[]{:S(2)}, u32[]{:S(2)}) collective-permute-start(bf16[2,128,2048]{1,2,0:T(8,128)(2,1)} %bitcast.130), channel_id=1, source_target_pairs={{0,12},{4,8},{8,4},{12,0},{16,28},{20,24},{24,20},{28,16},{1,13},{... | collective-permute-start | bytes 3145736 | tf_op jit(solution)/shard_map/ppermute | solution.py:129
  120.0 6.9 %copy-start.8 = (bf16[512,2,256]{2,1,0:T(2,128)(2,1)S(1)}, bf16[512,2,256]{2,1,0:T(2,128)(2,1)}, u32[]{:S(2)}) copy-start(bf16[512,2,256]{2,1,0:T(2,128)(2,1)} %param.13) | copy-start | bytes 1572868
  121.3 44.3 %collective-permute-start.9 = (bf16[2,128,2048]{1,2,0:T(8,128)(2,1)}, bf16[2,128,2048]{1,2,0:T(8,128)(2,1)}, u32[]{:S(2)}, u32[]{:S(2)}) collective-permute-start(bf16[2,128,2048]{1,2,0:T(8,128)(2,1)} %bitcast.131), channel_id=1, source_target_pairs={{0,8},{4,12},{8,0},{12,4},{16,24},{20,28},{24,16},{28,20},{1,9},{5... | collective-permute-start | bytes 3145736 | tf_op jit(solution)/shard_map/ppermute | solution.py:129
  124.1 42.4 %collective-permute-start.8 = (bf16[2,128,2048]{1,2,0:T(8,128)(2,1)}, bf16[2,128,2048]{1,2,0:T(8,128)(2,1)}, u32[]{:S(2)}, u32[]{:S(2)}) collective-permute-start(bf16[2,128,2048]{1,2,0:T(8,128)(2,1)} %bitcast.108), channel_id=1, source_target_pairs={{0,4},{4,0},{8,12},{12,8},{16,20},{20,16},{24,28},{28,24},{1,5},{5... | collective-permute-start | bytes 3145736 | tf_op jit(solution)/shard_map/ppermute | solution.py:129
  168.7 13.7 %copy-start.5 = (f32[2,128,2048]{1,2,0:T(8,128)}, f32[2,128,2048]{1,2,0:T(8,128)S(1)}, u32[]{:S(2)}) copy-start(f32[2,128,2048]{1,2,0:T(8,128)S(1)} %fusion.7) | copy-start | bytes 6291460
  168.7 11.0 %copy-start.4 = (bf16[4,2304,128]{2,1,0:T(8,128)(2,1)S(1)}, bf16[4,2304,128]{2,1,0:T(8,128)(2,1)}, u32[]{:S(2)}) copy-start(bf16[4,2304,128]{2,1,0:T(8,128)(2,1)} %gather_fusion.1) | copy-start | bytes 7077892
  168.8 7.3 %collective-permute-start.14 = (bf16[2,128,256]{2,1,0:T(8,128)(2,1)S(1)}, bf16[2,128,256]{2,1,0:T(8,128)(2,1)S(1)}, u32[]{:S(2)}, u32[]{:S(2)}) collective-permute-start(bf16[2,128,256]{2,1,0:T(8,128)(2,1)S(1)} %get-tuple-element.35), channel_id=1, source_target_pairs={{0,12},{4,8},{8,4},{12,0},{16,28},{20,24},{24,20},{28,16},{1,13},{... | collective-permute-start | bytes 393224 | tf_op jit(solution)/shard_map/ppermute | solution.py:159
  169.5 9.6 %collective-permute-start.13 = (bf16[2,128,256]{2,1,0:T(8,128)(2,1)S(1)}, bf16[2,128,256]{2,1,0:T(8,128)(2,1)S(1)}, u32[]{:S(2)}, u32[]{:S(2)}) collective-permute-start(bf16[2,128,256]{2,1,0:T(8,128)(2,1)S(1)} %get-tuple-element.36), channel_id=1, source_target_pairs={{0,8},{4,12},{8,0},{12,4},{16,24},{20,28},{24,16},{28,20},{1,9},{5... | collective-permute-start | bytes 393224 | tf_op jit(solution)/shard_map/ppermute | solution.py:159
  170.9 8.1 %collective-permute-start.12 = (bf16[2,128,256]{2,1,0:T(8,128)(2,1)S(1)}, bf16[2,128,256]{2,1,0:T(8,128)(2,1)S(1)}, u32[]{:S(2)}, u32[]{:S(2)}) collective-permute-start(bf16[2,128,256]{2,1,0:T(8,128)(2,1)S(1)} %get-tuple-element.34), channel_id=1, source_target_pairs={{0,4},{4,0},{8,12},{12,8},{16,20},{20,16},{24,28},{28,24},{1,5},{5... | collective-permute-start | bytes 393224 | tf_op jit(solution)/shard_map/ppermute | solution.py:159
  173.2 30.1 %collective-permute-start.11 = (bf16[128,2048]{0,1:T(8,128)(2,1)}, bf16[128,2048]{0,1:T(8,128)(2,1)}, u32[]{:S(2)}, u32[]{:S(2)}) collective-permute-start(bf16[128,2048]{0,1:T(8,128)(2,1)} %fusion.34), channel_id=1, source_target_pairs={{0,16},{4,20},{8,24},{12,28},{16,0},{20,4},{24,8},{28,12},{1,17},{... | collective-permute-start | bytes 1572872 | tf_op jit(solution)/shard_map/ppermute | solution.py:141
  179.1 22.4 %collective-permute-start.15 = (bf16[128,256]{1,0:T(8,128)(2,1)S(1)}, bf16[128,256]{1,0:T(8,128)(2,1)}, u32[]{:S(2)}, u32[]{:S(2)}) collective-permute-start(bf16[128,256]{1,0:T(8,128)(2,1)S(1)} %fusion.52), channel_id=1, source_target_pairs={{0,16},{4,20},{8,24},{12,28},{16,0},{20,4},{24,8},{28,12},{1,17},{... | collective-permute-start | bytes 196616 | tf_op jit(solution)/shard_map/ppermute | solution.py:164
  194.4 7.1 %copy-start.10 = (f32[128,256]{1,0:T(8,128)S(1)}, f32[128,256]{1,0:T(8,128)}, u32[]{:S(2)}) copy-start(f32[128,256]{1,0:T(8,128)} %param.20) | copy-start | bytes 393220
  194.4 8.9 %copy-start.9 = (f32[2048,128]{1,0:T(8,128)S(1)}, f32[2048,128]{1,0:T(8,128)}, u32[]{:S(2)}) copy-start(f32[2048,128]{1,0:T(8,128)} %param.18) | copy-start | bytes 3145732
  (6 other events, 31.9 us)
Sparse Core Ops, SparseCore 0:
  10.6 82.5 all-gather.2

commit v14 on v13

--- a/solution.py
+++ b/solution.py
@@ -88,7 +88,8 @@
 
 
 def slot_major_grads(
-    tokens_in, grad_out, middle_rank_rows, backward_token_rows, block_slot, tenant_rank, tenant_slot
+    tokens_in, grad_out, middle_rank_rows, backward_token_rows, block_slot, tenant_rank, tenant_slot,
+    layer_gradient,
 ):
     tok_rows, feat_shard = tokens_in.shape
     kv_shard = grad_out.shape[2]
@@ -112,10 +113,10 @@
         b_own = grouped_exchange(b_full)
     else:
         a_acc = group_stage(a_sc)
-        b_full, a_acc = lax.optimization_barrier((b_full, a_acc))
+        b_full, a_acc, layer_gradient = lax.optimization_barrier((b_full, a_acc, layer_gradient))
         a_own = cross_stage(a_acc)
         b_own = grouped_exchange(b_full)
-    return a_own.T, b_own
+    return a_own.T, b_own, layer_gradient
 
 
 def group_stage(full):
@@ -225,9 +226,9 @@
     ).reshape(tok_rows, feat_shard)
     input_gradient_layer = frozen_gradient_share + adapter_gradient_term
     if slot_major:
-        a_grad, b_grad = slot_major_grads(
+        a_grad, b_grad, input_gradient_layer = slot_major_grads(
             tokens_in, grad_out, middle_rank_rows, backward_token_rows, block_slot,
-            tenant_rank, tenant_slot,
+            tenant_rank, tenant_slot, input_gradient_layer,
         )
     else:
         a_terms = jnp.einsum(

time: 215 us -> 215 us (level)
    ppermute x3, waiting for transfers between devices: 33.9 us -> 17.6 us  [group_stage(): lax.ppermute(part.astype(jnp.bfloat16), 'dp', pairs).astype(jnp.float32)]
    ppermute x4, waiting for transfers between devices: 6 us -> 21.1 us  [grouped_exchange(): lax.ppermute(part.astype(jnp.bfloat16), 'dp', pairs).astype(jnp.float32)]
    ppermute x1, starting transfers between devices: 0.03 us -> 2.86 us  [frozen_gradient(): lax.ppermute(far_part[:half], 'tensor', row_pairs)]
    ppermute x1, starting transfers between devices: 2.86 us -> 0.03 us  [frozen_gradient(): lax.ppermute(far_part[half:], 'tensor', row_pairs)]
    unnamed x31 -> x29, local copies, waits for them, and re-layouts: 13.7 us -> 15.4 us
  transfers between devices with their start and end apart: 17 -> 17, of which waited for: 11 -> 9; matrix products, arithmetic and copies ran while one was open for 30% -> 30% of each run, Pallas kernels for 0% -> 0%
where the time goes in v14:
time: 215 us; the launch traced here: 214 us
  waiting for transfers between devices  100 us (47%)
  local copies, waits for them, and re-layouts  41.4 us (19%)
  matrix products  24.1 us (11%)
  other arithmetic  18.6 us (9%)
  starting transfers between devices  15.3 us (7%)
  between operations  14.4 us (7%)
    ppermute x1, waiting for transfers between devices, frozen_gradient(): lax.ppermute(far_part[half:], 'tensor', row_pairs)  22 us
    ppermute x4, waiting for transfers between devices, grouped_exchange(): lax.ppermute(part.astype(jnp.bfloat16), 'dp', pairs).astype(jnp.float32)  21.1 us
    ppermute x1, waiting for transfers between devices, frozen_gradient(): lax.ppermute(far_part[:half], 'tensor', row_pairs)  20.5 us
    ppermute x3, waiting for transfers between devices, group_stage(): lax.ppermute(part.astype(jnp.bfloat16), 'dp', pairs).astype(jnp.float32)  17.6 us
    unnamed x29, local copies, waits for them, and re-layouts  15.4 us
    all_gather x1, waiting for transfers between devices, local(): packed_all = lax.all_gather(packed, 'dp', axis=0, tiled=False)  11 us
    dot_general x2, matrix products, chip_partial(): jnp.einsum('tpk,pdk->td', partner_dy, other, preferred_element_type=jnp.f...  8.52 us
    ppermute x4, waiting for transfers between devices, tensor_sum(): parts = tuple((p + lax.ppermute(p, 'tensor', pairs) for p in parts))  6.53 us
  transfers between devices with their start and end apart: 17, of which 9 were waited for; matrix products, arithmetic and copies ran while one was open for 30% of the time, Pallas kernels for 0%

profile of v14, /device:TPU:0, one launch (start us, length us, event | category | flops | bytes accessed | tf_op | source)
XLA Modules:
  0.0 214.1 jit_solution(11700305190976513378)
XLA Ops:
  10.5 4.5 %copy_bitcast_fusion = bf16[2,2,2048,256]{3,2,0,1:T(8,128)(2,1)} fusion(bf16[2,2,2,2048,256]{4,3,2,1,0:T(8,128)(2,1)} %bitcast.123, s32[]{:T(128)S(6)} %select_n.109), kind=kLoop, calls=%fused_computation.8 | loop fusion | bytes 8388612 | tf_op jit(solution)/shard_map/jit(dynamic_index_in_dim)/squeeze | solution.py:64
  18.8 2.9 %fusion.2 = f32[2048,512,1]{1,0,2:T(8,128)S(1)} fusion(bf16[2,2,2,2048,256]{4,3,2,1,0:T(8,128)(2,1)} %bitcast.124, s32[]{:T(128)S(6)} %select_n.111, s32[]{:T(128)S(6)} %select_n.108, bf16[512,2,256]{2,1,0:T(2,128)(2,1)S(1)} %copy-done.7), kind=kOutput, calls=%fused_computation.10 | convolution fusion | flops 1073741824 | bytes 6815752 | tf_op jit(solution)/shard_map/tpk,pdk->td/dot_general | solution.py:74
  23.3 2.9 %fusion.1 = bf16[512,2048]{0,1:T(8,128)(2,1)S(1)} fusion(bf16[512,2,256]{2,0,1:T(8,128)(2,1)S(1)} %collective-permute-done.1, f32[2048,512,1]{1,0,2:T(8,128)S(1)} %fusion.2, bf16[2,2,2048,256]{3,2,0,1:T(8,128)(2,1)} %collective-permute-done, s32[]{:T(128)S(6)} %select_n.110), kind=kOutput, calls=%fused_computation.9 | convolution fusion | flops 1075838976 | bytes 8912900 | tf_op jit(solution)/shard_map/tpk,pdk->td/dot_general | solution.py:75
  27.6 2.9 %collective-permute-start.2 = (bf16[256,2048]{0,1:T(8,128)(2,1)}, bf16[256,2048]{0,1:T(8,128)(2,1)}, u32[]{:S(2)}, u32[]{:S(2)}) collective-permute-start(bf16[256,2048]{0,1:T(8,128)(2,1)} %get-tuple-element.34), channel_id=1, source_target_pairs={{0,2},{1,3},{2,0},{3,1},{4,6},{5,7},{6,4},{7,5},{8,10},{9,11},{10,... | collective-permute-start | bytes 3145736 | tf_op jit(solution)/shard_map/ppermute | solution.py:82
  31.4 2.9 %fusion.4 = f32[2048,512,1]{1,0,2:T(8,128)S(1)} fusion(bf16[2,2,2,2048,256]{4,3,2,1,0:T(8,128)(2,1)} %bitcast.125, s32[]{:T(128)S(6)} %select_n.105, s32[]{:T(128)S(6)} %select_n.108, bf16[512,2,256]{2,1,0:T(2,128)(2,1)S(1)} %copy-done.7), kind=kOutput, calls=%fused_computation.12 | convolution fusion | flops 1073741824 | bytes 6815752 | tf_op jit(solution)/shard_map/tpk,pdk->td/dot_general | solution.py:74
  34.3 20.5 %collective-permute-done.2 = bf16[256,2048]{0,1:T(8,128)(2,1)} collective-permute-done((bf16[256,2048]{0,1:T(8,128)(2,1)}, bf16[256,2048]{0,1:T(8,128)(2,1)}, u32[]{:S(2)}, u32[]{:S(2)}) %collective-permute-start.2) | collective-permute-done | bytes 1048608 | tf_op jit(solution)/shard_map/ppermute | solution.py:82
  54.7 22.0 %collective-permute-done.3 = bf16[256,2048]{0,1:T(8,128)(2,1)} collective-permute-done((bf16[256,2048]{0,1:T(8,128)(2,1)}, bf16[256,2048]{0,1:T(8,128)(2,1)}, u32[]{:S(2)}, u32[]{:S(2)}) %collective-permute-start.3) | collective-permute-done | bytes 1048608 | tf_op jit(solution)/shard_map/ppermute | solution.py:83
  76.7 5.6 %bitcast_add_fusion.1 = f32[512,2048]{0,1:T(8,128)} fusion(f32[2048,512,1]{1,0,2:T(8,128)S(1)} %fusion.4, bf16[512,2,256]{2,0,1:T(8,128)(2,1)S(1)} %collective-permute-done.1, bf16[256,2048]{0,1:T(8,128)(2,1)} %collective-permute-done.3, bf16[256,2048]{0,1:T(8,128)(2,1)} %collective-permute-done.2, bf16[2,2,2048,256]{3,2,0,1:T(8,128)(2,1)} %collective-permute-done, ...), kind=kOutput, calls=%fused_computation.6 | convolution fusion | flops 1080033280 | bytes 13107204 | tf_op jit(solution)/shard_map/tpk,pdk->td/dot_general | solution.py:75
  82.4 11.0 %all-gather.3.cloned.1.call-done = bf16[18432,128]{1,0:T(8,128)(2,1)} async-done(((bf16[2304,128]{1,0:T(8,128)(2,1)}), bf16[18432,128]{1,0:T(8,128)(2,1)}) %all-gather.3.cloned.1.call-update) | async-done | bytes 4718608 | tf_op jit(solution)/shard_map/all_gather | solution.py:192
  93.4 4.7 %gather_fusion.1 = bf16[4,2304,128]{2,1,0:T(8,128)(2,1)} fusion(bf16[8,2304,128]{2,1,0:T(8,128)(2,1)} %bitcast.129, s32[1024]{0:T(1024)S(1)} %pad_clamp_fusion.1), kind=kCustom, calls=%fused_computation.1 | custom fusion | bytes 4718608 | tf_op jit(solution)/shard_map/jit(_take)/gather | solution.py:198
  99.7 2.4 %fusion.21 = f32[4,128,128]{1,2,0:T(8,128)S(1)} fusion(bf16[4,128,2048]{2,1,0:T(8,128)(2,1)S(1)} %bitcast.117, bf16[4,2304,128]{2,1,0:T(8,128)(2,1)} %gather_fusion.1), kind=kOutput, calls=%fused_computation.32 | convolution fusion | flops 268435456 | bytes 4456448 | tf_op jit(solution)/shard_map/bnd,bdc->bnc/dot_general | solution.py:214
  105.4 6.5 %collective-permute-done.7 = f32[4,128,128]{2,1,0:T(8,128)S(1)} collective-permute-done((f32[4,128,128]{2,1,0:T(8,128)S(1)}, f32[4,128,128]{2,1,0:T(8,128)S(1)}, u32[]{:S(2)}, u32[]{:S(2)}) %collective-permute-start.7) | collective-permute-done | bytes 262176 | tf_op jit(solution)/shard_map/ppermute | solution.py:45
  112.1 2.3 %fusion.8 = f32[8,128,2048]{2,1,0:T(8,128)S(1)} fusion(bf16[512,2048]{1,0:T(8,128)(2,1)S(1)} %copy-done, pred[512,8]{0,1:T(8,128)(4,1)S(1)} %iota_compare_fusion, bf16[512,128]{0,1:T(8,128)(2,1)S(1)} %copy.48), kind=kOutput, calls=%fused_computation.17 | convolution fusion | flops 2148007936 | bytes 10620928 | tf_op jit(solution)/shard_map/nsc,nd->scd/dot_general | solution.py:101
  114.4 3.3 %copy-done.6 = f32[8,128,2048]{2,1,0:T(8,128)} copy-done((f32[8,128,2048]{2,1,0:T(8,128)}, f32[8,128,2048]{2,1,0:T(8,128)S(1)}, u32[]{:S(2)}) %copy-start.6) | copy-done | bytes 8388632
  125.8 4.2 %fusion.18 = f32[4,128,2048]{2,1,0:T(8,128)} fusion(bf16[4,128,128]{2,1,0:T(8,128)(2,1)S(1)} %multiply_convert_fusion, bf16[4,2304,128]{2,1,0:T(8,128)(2,1)} %gather_fusion.1), kind=kOutput, calls=%fused_computation.27 | convolution fusion | flops 268435456 | bytes 6422528 | tf_op jit(solution)/shard_map/bnc,bdc->bnd/dot_general | solution.py:224
  130.0 5.4 %copy.62 = f32[512,2048]{0,1:T(8,128)} copy(f32[512,2048]{1,0:T(8,128)} %bitcast.118) | data formatting | bytes 8388608 | tf_op jit(solution)/shard_map/reshape | solution.py:226
  135.4 3.1 %constant_dynamic-slice_fusion.3 = f32[2,1,128,2048]{3,2,1,0:T(8,128)} fusion(f32[2,4,128,2048]{3,2,1,0:T(8,128)} %bitcast.120, s32[]{:T(128)S(6)} %select_n.117), kind=kLoop, calls=%fused_computation.81 | loop fusion | bytes 4194308 | tf_op jit(solution)/shard_map/jit(dynamic_index_in_dim)/dynamic_slice | solution.py:126
  144.0 5.2 %add.191 = f32[512,2048]{0,1:T(8,128)} add(f32[512,2048]{0,1:T(8,128)S(1)} %copy-done.4, f32[512,2048]{0,1:T(8,128)} %copy.62) | non-fusion elementwise | flops 1048576 | bytes 12582912 | tf_op jit(solution)/shard_map/add | solution.py:227
  149.1 17.5 %collective-permute-done.8 = bf16[2,128,2048]{1,2,0:T(8,128)(2,1)} collective-permute-done((bf16[2,128,2048]{1,2,0:T(8,128)(2,1)}, bf16[2,128,2048]{1,2,0:T(8,128)(2,1)}, u32[]{:S(2)}, u32[]{:S(2)}) %collective-permute-start.8) | collective-permute-done | bytes 1048608 | tf_op jit(solution)/shard_map/ppermute | solution.py:130
  170.2 2.4 %collective-permute-start.14 = (bf16[2,128,256]{2,1,0:T(8,128)(2,1)S(1)}, bf16[2,128,256]{2,1,0:T(8,128)(2,1)S(1)}, u32[]{:S(2)}, u32[]{:S(2)}) collective-permute-start(bf16[2,128,256]{2,1,0:T(8,128)(2,1)S(1)} %get-tuple-element.37), channel_id=1, source_target_pairs={{0,12},{4,8},{8,4},{12,0},{16,28},{20,24},{24,20},{28,16},{1,13},{... | collective-permute-start | bytes 393224 | tf_op jit(solution)/shard_map/ppermute | solution.py:160
  176.1 5.6 %collective-permute-done.14 = bf16[2,128,256]{2,1,0:T(8,128)(2,1)S(1)} collective-permute-done((bf16[2,128,256]{2,1,0:T(8,128)(2,1)S(1)}, bf16[2,128,256]{2,1,0:T(8,128)(2,1)S(1)}, u32[]{:S(2)}, u32[]{:S(2)}) %collective-permute-start.14) | collective-permute-done | bytes 131104 | tf_op jit(solution)/shard_map/ppermute | solution.py:160
  181.9 5.4 %copy.57 = f32[512,2048]{1,0:T(8,128)} copy(f32[512,2048]{0,1:T(8,128)} %add.191) | data formatting | bytes 8388608
  187.3 14.4 %collective-permute-done.15 = bf16[128,256]{1,0:T(8,128)(2,1)} collective-permute-done((bf16[128,256]{1,0:T(8,128)(2,1)S(1)}, bf16[128,256]{1,0:T(8,128)(2,1)}, u32[]{:S(2)}, u32[]{:S(2)}) %collective-permute-start.15) | collective-permute-done | bytes 65568 | tf_op jit(solution)/shard_map/ppermute | solution.py:165
  203.5 3.7 %fusion.28 = (f32[2048,128]{1,0:T(8,128)}, f32[2048,128]{1,0:T(8,128)}) fusion(f32[2048,128]{1,0:T(8,128)S(1)} %copy-done.9, f32[2048,128]{1,0:T(8,128)} %param.17, bf16[128,2048]{0,1:T(8,128)(2,1)} %collective-permute-done.11, f32[2,128,2048]{1,2,0:T(8,128)} %copy-done.5, s32[]{:T(128)S(6)} %select_n.122), kind=kLoop, calls=%fused_computation.37 | loop fusion | flops 3407872 | bytes 5767172 | tf_op jit(solution)/shard_map/div | solution.py:22
  (97 shorter events, 38.4 us)
Async XLA Ops:
  7.2 92.5 %copy-start = (bf16[512,2048]{1,0:T(8,128)(2,1)S(1)}, bf16[512,2048]{1,0:T(8,128)(2,1)}, u32[]{:S(2)}) copy-start(bf16[512,2048]{1,0:T(8,128)(2,1)} %param.12) | copy-start | bytes 6291460
  7.2 86.2 %all-gather.3.cloned.1.call-start = ((), (), s32[]{:S(2)}) async-start(), calls=%async_computation | async-start | bytes 5308416 | tf_op jit(solution)/shard_map/all_gather | solution.py:192
  10.5 5.9 %copy-start.11 = (s32[4]{0:T(128)S(1)}, s32[4]{0:T(128)}, u32[]{:S(2)}) copy-start(s32[4]{0:T(128)} %param.21) | copy-start | bytes 52
  10.5 5.9 %copy-start.3 = (s32[8]{0:T(128)S(1)}, s32[8]{0:T(128)}, u32[]{:S(2)}) copy-start(s32[8]{0:T(128)} %param.23) | copy-start | bytes 100
  10.5 6.6 %copy-start.2 = (s32[8]{0:T(128)S(1)}, s32[8]{0:T(128)}, u32[]{:S(2)}) copy-start(s32[8]{0:T(128)} %param.22) | copy-start | bytes 100
  15.1 8.2 %collective-permute-start = (bf16[2,2,2048,256]{3,2,0,1:T(8,128)(2,1)}, bf16[2,2,2048,256]{3,2,0,1:T(8,128)(2,1)}, u32[]{:S(2)}, u32[]{:S(2)}) collective-permute-start(bf16[2,2,2048,256]{3,2,0,1:T(8,128)(2,1)} %copy_bitcast_fusion), channel_id=1, source_target_pairs={{0,1},{1,0},{2,3},{3,2},{4,5},{5,4},{6,7},{7,6},{8,9},{9,8},{10,11... | collective-permute-start | bytes 12582920 | tf_op jit(solution)/shard_map/ppermute | solution.py:68
  16.4 6.9 %collective-permute-start.1 = (bf16[512,2,256]{2,0,1:T(8,128)(2,1)}, bf16[512,2,256]{2,0,1:T(8,128)(2,1)S(1)}, u32[]{:S(2)}, u32[]{:S(2)}) collective-permute-start(bf16[512,2,256]{2,0,1:T(8,128)(2,1)} %copy.36), channel_id=1, source_target_pairs={{0,1},{1,0},{2,3},{3,2},{4,5},{5,4},{6,7},{7,6},{8,9},{9,8},{10,11... | collective-permute-start | bytes 1572872 | tf_op jit(solution)/shard_map/ppermute | solution.py:69
  27.6 27.1 %collective-permute-start.2 = (bf16[256,2048]{0,1:T(8,128)(2,1)}, bf16[256,2048]{0,1:T(8,128)(2,1)}, u32[]{:S(2)}, u32[]{:S(2)}) collective-permute-start(bf16[256,2048]{0,1:T(8,128)(2,1)} %get-tuple-element.34), channel_id=1, source_target_pairs={{0,2},{1,3},{2,0},{3,1},{4,6},{5,7},{6,4},{7,5},{8,10},{9,11},{10,... | collective-permute-start | bytes 3145736 | tf_op jit(solution)/shard_map/ppermute | solution.py:82
  30.5 46.2 %collective-permute-start.3 = (bf16[256,2048]{0,1:T(8,128)(2,1)}, bf16[256,2048]{0,1:T(8,128)(2,1)}, u32[]{:S(2)}, u32[]{:S(2)}) collective-permute-start(bf16[256,2048]{0,1:T(8,128)(2,1)} %get-tuple-element.35), channel_id=1, source_target_pairs={{0,2},{1,3},{2,0},{3,1},{4,6},{5,7},{6,4},{7,5},{8,10},{9,11},{10,... | collective-permute-start | bytes 3145736 | tf_op jit(solution)/shard_map/ppermute | solution.py:83
  99.6 3.1 %collective-permute-start.6 = (f32[4,128,128]{2,1,0:T(8,128)S(1)}, f32[4,128,128]{2,1,0:T(8,128)S(1)}, u32[]{:S(2)}, u32[]{:S(2)}) collective-permute-start(f32[4,128,128]{2,1,0:T(8,128)S(1)} %copy.47), channel_id=1, source_target_pairs={{0,1},{1,0},{2,3},{3,2},{4,5},{5,4},{6,7},{7,6},{8,9},{9,8},{10,11... | collective-permute-start | bytes 786440 | tf_op jit(solution)/shard_map/ppermute | solution.py:45
  102.1 2.2 %collective-permute-start.4 = (f32[4,128,128]{1,2,0:T(8,128)S(1)}, f32[4,128,128]{1,2,0:T(8,128)S(1)}, u32[]{:S(2)}, u32[]{:S(2)}) collective-permute-start(f32[4,128,128]{1,2,0:T(8,128)S(1)} %fusion.21), channel_id=1, source_target_pairs={{0,1},{1,0},{2,3},{3,2},{4,5},{5,4},{6,7},{7,6},{8,9},{9,8},{10,11... | collective-permute-start | bytes 786440 | tf_op jit(solution)/shard_map/ppermute | solution.py:45
  102.7 9.2 %collective-permute-start.7 = (f32[4,128,128]{2,1,0:T(8,128)S(1)}, f32[4,128,128]{2,1,0:T(8,128)S(1)}, u32[]{:S(2)}, u32[]{:S(2)}) collective-permute-start(f32[4,128,128]{2,1,0:T(8,128)S(1)} %add.181), channel_id=1, source_target_pairs={{0,2},{1,3},{2,0},{3,1},{4,6},{5,7},{6,4},{7,5},{8,10},{9,11},{10,... | collective-permute-start | bytes 786440 | tf_op jit(solution)/shard_map/ppermute | solution.py:45
  104.3 36.2 %collective-permute-start.5 = (f32[4,128,128]{1,2,0:T(8,128)S(1)}, f32[4,128,128]{1,2,0:T(8,128)}, u32[]{:S(2)}, u32[]{:S(2)}) collective-permute-start(f32[4,128,128]{1,2,0:T(8,128)S(1)} %add.177), channel_id=1, source_target_pairs={{0,2},{1,3},{2,0},{3,1},{4,6},{5,7},{6,4},{7,5},{8,10},{9,11},{10,... | collective-permute-start | bytes 786440 | tf_op jit(solution)/shard_map/ppermute | solution.py:45
  119.7 29.5 %collective-permute-start.10 = (bf16[2,128,2048]{1,2,0:T(8,128)(2,1)}, bf16[2,128,2048]{1,2,0:T(8,128)(2,1)}, u32[]{:S(2)}, u32[]{:S(2)}) collective-permute-start(bf16[2,128,2048]{1,2,0:T(8,128)(2,1)} %bitcast.130), channel_id=1, source_target_pairs={{0,12},{4,8},{8,4},{12,0},{16,28},{20,24},{24,20},{28,16},{1,13},{... | collective-permute-start | bytes 3145736 | tf_op jit(solution)/shard_map/ppermute | solution.py:130
  121.5 45.2 %collective-permute-start.8 = (bf16[2,128,2048]{1,2,0:T(8,128)(2,1)}, bf16[2,128,2048]{1,2,0:T(8,128)(2,1)}, u32[]{:S(2)}, u32[]{:S(2)}) collective-permute-start(bf16[2,128,2048]{1,2,0:T(8,128)(2,1)} %bitcast.108), channel_id=1, source_target_pairs={{0,4},{4,0},{8,12},{12,8},{16,20},{20,16},{24,28},{28,24},{1,5},{5... | collective-permute-start | bytes 3145736 | tf_op jit(solution)/shard_map/ppermute | solution.py:130
  124.3 42.4 %collective-permute-start.9 = (bf16[2,128,2048]{1,2,0:T(8,128)(2,1)}, bf16[2,128,2048]{1,2,0:T(8,128)(2,1)}, u32[]{:S(2)}, u32[]{:S(2)}) collective-permute-start(bf16[2,128,2048]{1,2,0:T(8,128)(2,1)} %bitcast.107), channel_id=1, source_target_pairs={{0,8},{4,12},{8,0},{12,4},{16,24},{20,28},{24,16},{28,20},{1,9},{5... | collective-permute-start | bytes 3145736 | tf_op jit(solution)/shard_map/ppermute | solution.py:130
  169.0 5.9 %collective-permute-start.12 = (bf16[2,128,256]{2,1,0:T(8,128)(2,1)S(1)}, bf16[2,128,256]{2,1,0:T(8,128)(2,1)S(1)}, u32[]{:S(2)}, u32[]{:S(2)}) collective-permute-start(bf16[2,128,256]{2,1,0:T(8,128)(2,1)S(1)} %get-tuple-element.36), channel_id=1, source_target_pairs={{0,4},{4,0},{8,12},{12,8},{16,20},{20,16},{24,28},{28,24},{1,5},{5... | collective-permute-start | bytes 393224 | tf_op jit(solution)/shard_map/ppermute | solution.py:160
  169.7 6.4 %collective-permute-start.13 = (bf16[2,128,256]{2,1,0:T(8,128)(2,1)S(1)}, bf16[2,128,256]{2,1,0:T(8,128)(2,1)S(1)}, u32[]{:S(2)}, u32[]{:S(2)}) collective-permute-start(bf16[2,128,256]{2,1,0:T(8,128)(2,1)S(1)} %get-tuple-element.38), channel_id=1, source_target_pairs={{0,8},{4,12},{8,0},{12,4},{16,24},{20,28},{24,16},{28,20},{1,9},{5... | collective-permute-start | bytes 393224 | tf_op jit(solution)/shard_map/ppermute | solution.py:160
  170.2 11.4 %collective-permute-start.14 = (bf16[2,128,256]{2,1,0:T(8,128)(2,1)S(1)}, bf16[2,128,256]{2,1,0:T(8,128)(2,1)S(1)}, u32[]{:S(2)}, u32[]{:S(2)}) collective-permute-start(bf16[2,128,256]{2,1,0:T(8,128)(2,1)S(1)} %get-tuple-element.37), channel_id=1, source_target_pairs={{0,12},{4,8},{8,4},{12,0},{16,28},{20,24},{24,20},{28,16},{1,13},{... | collective-permute-start | bytes 393224 | tf_op jit(solution)/shard_map/ppermute | solution.py:160
  173.4 30.1 %collective-permute-start.11 = (bf16[128,2048]{0,1:T(8,128)(2,1)}, bf16[128,2048]{0,1:T(8,128)(2,1)}, u32[]{:S(2)}, u32[]{:S(2)}) collective-permute-start(bf16[128,2048]{0,1:T(8,128)(2,1)} %fusion.34), channel_id=1, source_target_pairs={{0,16},{4,20},{8,24},{12,28},{16,0},{20,4},{24,8},{28,12},{1,17},{... | collective-permute-start | bytes 1572872 | tf_op jit(solution)/shard_map/ppermute | solution.py:142
  181.8 19.9 %collective-permute-start.15 = (bf16[128,256]{1,0:T(8,128)(2,1)S(1)}, bf16[128,256]{1,0:T(8,128)(2,1)}, u32[]{:S(2)}, u32[]{:S(2)}) collective-permute-start(bf16[128,256]{1,0:T(8,128)(2,1)S(1)} %fusion.52), channel_id=1, source_target_pairs={{0,16},{4,20},{8,24},{12,28},{16,0},{20,4},{24,8},{28,12},{1,17},{... | collective-permute-start | bytes 196616 | tf_op jit(solution)/shard_map/ppermute | solution.py:165
  181.9 19.8 %copy-start.10 = (f32[128,256]{1,0:T(8,128)S(1)}, f32[128,256]{1,0:T(8,128)}, u32[]{:S(2)}) copy-start(f32[128,256]{1,0:T(8,128)} %param.20) | copy-start | bytes 393220
  181.9 21.7 %copy-start.9 = (f32[2048,128]{1,0:T(8,128)S(1)}, f32[2048,128]{1,0:T(8,128)}, u32[]{:S(2)}) copy-start(f32[2048,128]{1,0:T(8,128)} %param.18) | copy-start | bytes 3145732
  201.7 5.6 %copy-start.1 = (bf16[512,2048]{1,0:T(8,128)(2,1)S(1)}, bf16[512,2048]{1,0:T(8,128)(2,1)}, u32[]{:S(2)}) copy-start(bf16[512,2048]{1,0:T(8,128)(2,1)} %param.12) | copy-start | bytes 6291460
  (5 other events, 17.4 us)
Sparse Core Ops, SparseCore 0:
  10.6 82.7 all-gather.2

commit v15 on v14

--- a/solution.py
+++ b/solution.py
@@ -113,9 +113,9 @@
         b_own = grouped_exchange(b_full)
     else:
         a_acc = group_stage(a_sc)
-        b_full, a_acc, layer_gradient = lax.optimization_barrier((b_full, a_acc, layer_gradient))
+        b_own = grouped_exchange(b_full)
+        b_own, a_acc, layer_gradient = lax.optimization_barrier((b_own, a_acc, layer_gradient))
         a_own = cross_stage(a_acc)
-        b_own = grouped_exchange(b_full)
     return a_own.T, b_own, layer_gradient
 
 

time: 215 us -> 239 us (1.11)
  waiting for transfers between devices: 100 us -> 121 us
  other arithmetic: 18.6 us -> 23 us
    ppermute x4, waiting for transfers between devices: 21.1 us -> 42.6 us  [grouped_exchange(): lax.ppermute(part.astype(jnp.bfloat16), 'dp', pairs).astype(jnp.float32)]
    ppermute x3, waiting for transfers between devices: 17.6 us -> 0.01 us  [group_stage(): lax.ppermute(part.astype(jnp.bfloat16), 'dp', pairs).astype(jnp.float32)]
    ppermute x1, waiting for transfers between devices: 0.01 us -> 16.1 us  [cross_stage(): lax.ppermute(part.astype(jnp.bfloat16), 'dp', pairs).astype(jnp.float32)]
    unnamed x29 -> x35, local copies, waits for them, and re-layouts: 15.4 us -> 13.1 us
  transfers between devices with their start and end apart: 17 -> 17, of which waited for: 9 -> 9; matrix products, arithmetic and copies ran while one was open for 30% -> 27% of each run, Pallas kernels for 0% -> 0%
where the time goes in v15:
time: 239 us; the launch traced here: 238 us
  waiting for transfers between devices  121 us (51%)
  local copies, waits for them, and re-layouts  40.7 us (17%)
  matrix products  24.1 us (10%)
  other arithmetic  23 us (10%)
  starting transfers between devices  15.2 us (6%)
  between operations  14.4 us (6%)
    ppermute x4, waiting for transfers between devices, grouped_exchange(): lax.ppermute(part.astype(jnp.bfloat16), 'dp', pairs).astype(jnp.float32)  42.6 us
    ppermute x1, waiting for transfers between devices, frozen_gradient(): lax.ppermute(far_part[half:], 'tensor', row_pairs)  22 us
    ppermute x1, waiting for transfers between devices, frozen_gradient(): lax.ppermute(far_part[:half], 'tensor', row_pairs)  19.6 us
    ppermute x1, waiting for transfers between devices, cross_stage(): lax.ppermute(part.astype(jnp.bfloat16), 'dp', pairs).astype(jnp.float32)  16.1 us
    unnamed x35, local copies, waits for them, and re-layouts  13.1 us
    all_gather x1, waiting for transfers between devices, local(): packed_all = lax.all_gather(packed, 'dp', axis=0, tiled=False)  10.8 us
    dot_general x2, matrix products, chip_partial(): jnp.einsum('tpk,pdk->td', partner_dy, other, preferred_element_type=jnp.f...  8.52 us
    ppermute x4, waiting for transfers between devices, tensor_sum(): parts = tuple((p + lax.ppermute(p, 'tensor', pairs) for p in parts))  7.34 us
  transfers between devices with their start and end apart: 17, of which 9 were waited for; matrix products, arithmetic and copies ran while one was open for 27% of the time, Pallas kernels for 0%

profile of v15, /device:TPU:0, one launch (start us, length us, event | category | flops | bytes accessed | tf_op | source)
XLA Modules:
  0.0 238.5 jit_solution(11104868836258581882)
XLA Ops:
  10.5 4.5 %copy_bitcast_fusion = bf16[2,2,2048,256]{3,2,0,1:T(8,128)(2,1)} fusion(bf16[2,2,2,2048,256]{4,3,2,1,0:T(8,128)(2,1)} %bitcast.121, s32[]{:T(128)S(6)} %select_n.109), kind=kLoop, calls=%fused_computation.8 | loop fusion | bytes 8388612 | tf_op jit(solution)/shard_map/jit(dynamic_index_in_dim)/squeeze | solution.py:64
  17.8 2.9 %fusion.2 = f32[2048,512,1]{1,0,2:T(8,128)S(1)} fusion(bf16[2,2,2,2048,256]{4,3,2,1,0:T(8,128)(2,1)} %bitcast.122, s32[]{:T(128)S(6)} %select_n.111, s32[]{:T(128)S(6)} %select_n.108, bf16[512,2,256]{2,1,0:T(2,128)(2,1)S(1)} %copy-done.7), kind=kOutput, calls=%fused_computation.10 | convolution fusion | flops 1073741824 | bytes 6815752 | tf_op jit(solution)/shard_map/tpk,pdk->td/dot_general | solution.py:74
  20.7 2.5 %collective-permute-done.1 = bf16[512,2,256]{2,0,1:T(8,128)(2,1)S(1)} collective-permute-done((bf16[512,2,256]{2,0,1:T(8,128)(2,1)}, bf16[512,2,256]{2,0,1:T(8,128)(2,1)S(1)}, u32[]{:S(2)}, u32[]{:S(2)}) %collective-permute-start.1) | collective-permute-done | bytes 524320 | tf_op jit(solution)/shard_map/ppermute | solution.py:69
  23.3 2.9 %fusion.1 = bf16[512,2048]{0,1:T(8,128)(2,1)S(1)} fusion(bf16[512,2,256]{2,0,1:T(8,128)(2,1)S(1)} %collective-permute-done.1, f32[2048,512,1]{1,0,2:T(8,128)S(1)} %fusion.2, bf16[2,2,2048,256]{3,2,0,1:T(8,128)(2,1)} %collective-permute-done, s32[]{:T(128)S(6)} %select_n.110), kind=kOutput, calls=%fused_computation.9 | convolution fusion | flops 1075838976 | bytes 8912900 | tf_op jit(solution)/shard_map/tpk,pdk->td/dot_general | solution.py:75
  27.6 2.9 %collective-permute-start.2 = (bf16[256,2048]{0,1:T(8,128)(2,1)}, bf16[256,2048]{0,1:T(8,128)(2,1)}, u32[]{:S(2)}, u32[]{:S(2)}) collective-permute-start(bf16[256,2048]{0,1:T(8,128)(2,1)} %get-tuple-element.32), channel_id=1, source_target_pairs={{0,2},{1,3},{2,0},{3,1},{4,6},{5,7},{6,4},{7,5},{8,10},{9,11},{10,... | collective-permute-start | bytes 3145736 | tf_op jit(solution)/shard_map/ppermute | solution.py:82
  32.2 2.9 %fusion.4 = f32[2048,512,1]{1,0,2:T(8,128)S(1)} fusion(bf16[2,2,2,2048,256]{4,3,2,1,0:T(8,128)(2,1)} %bitcast.123, s32[]{:T(128)S(6)} %select_n.105, s32[]{:T(128)S(6)} %select_n.108, bf16[512,2,256]{2,1,0:T(2,128)(2,1)S(1)} %copy-done.7), kind=kOutput, calls=%fused_computation.12 | convolution fusion | flops 1073741824 | bytes 6815752 | tf_op jit(solution)/shard_map/tpk,pdk->td/dot_general | solution.py:74
  35.1 19.6 %collective-permute-done.2 = bf16[256,2048]{0,1:T(8,128)(2,1)} collective-permute-done((bf16[256,2048]{0,1:T(8,128)(2,1)}, bf16[256,2048]{0,1:T(8,128)(2,1)}, u32[]{:S(2)}, u32[]{:S(2)}) %collective-permute-start.2) | collective-permute-done | bytes 1048608 | tf_op jit(solution)/shard_map/ppermute | solution.py:82
  54.7 22.0 %collective-permute-done.3 = bf16[256,2048]{0,1:T(8,128)(2,1)} collective-permute-done((bf16[256,2048]{0,1:T(8,128)(2,1)}, bf16[256,2048]{0,1:T(8,128)(2,1)}, u32[]{:S(2)}, u32[]{:S(2)}) %collective-permute-start.3) | collective-permute-done | bytes 1048608 | tf_op jit(solution)/shard_map/ppermute | solution.py:83
  76.7 5.6 %bitcast_add_fusion.1 = f32[512,2048]{0,1:T(8,128)} fusion(f32[2048,512,1]{1,0,2:T(8,128)S(1)} %fusion.4, bf16[512,2,256]{2,0,1:T(8,128)(2,1)S(1)} %collective-permute-done.1, bf16[256,2048]{0,1:T(8,128)(2,1)} %collective-permute-done.3, bf16[256,2048]{0,1:T(8,128)(2,1)} %collective-permute-done.2, bf16[2,2,2048,256]{3,2,0,1:T(8,128)(2,1)} %collective-permute-done, ...), kind=kOutput, calls=%fused_computation.6 | convolution fusion | flops 1080033280 | bytes 13107204 | tf_op jit(solution)/shard_map/tpk,pdk->td/dot_general | solution.py:75
  82.4 10.8 %all-gather.3.cloned.1.call-done = bf16[18432,128]{1,0:T(8,128)(2,1)} async-done(((bf16[2304,128]{1,0:T(8,128)(2,1)}), bf16[18432,128]{1,0:T(8,128)(2,1)}) %all-gather.3.cloned.1.call-update) | async-done | bytes 4718608 | tf_op jit(solution)/shard_map/all_gather | solution.py:192
  93.2 4.6 %gather_fusion.1 = bf16[4,2304,128]{2,1,0:T(8,128)(2,1)} fusion(bf16[8,2304,128]{2,1,0:T(8,128)(2,1)} %bitcast.127, s32[1024]{0:T(1024)S(1)} %pad_clamp_fusion.1), kind=kCustom, calls=%fused_computation.1 | custom fusion | bytes 4718608 | tf_op jit(solution)/shard_map/jit(_take)/gather | solution.py:198
  99.4 2.4 %fusion.21 = f32[4,128,128]{1,2,0:T(8,128)S(1)} fusion(bf16[4,128,2048]{2,1,0:T(8,128)(2,1)S(1)} %bitcast.115, bf16[4,2304,128]{2,1,0:T(8,128)(2,1)} %gather_fusion.1), kind=kOutput, calls=%fused_computation.32 | convolution fusion | flops 268435456 | bytes 4456448 | tf_op jit(solution)/shard_map/bnd,bdc->bnc/dot_general | solution.py:214
  107.9 3.9 %collective-permute-done.11 = f32[4,128,128]{2,1,0:T(8,128)} collective-permute-done((f32[4,128,128]{2,1,0:T(8,128)S(1)}, f32[4,128,128]{2,1,0:T(8,128)}, u32[]{:S(2)}, u32[]{:S(2)}) %collective-permute-start.11) | collective-permute-done | bytes 262176 | tf_op jit(solution)/shard_map/ppermute | solution.py:45
  112.9 3.5 %collective-permute-done.5 = f32[4,128,128]{1,2,0:T(8,128)S(1)} collective-permute-done((f32[4,128,128]{1,2,0:T(8,128)S(1)}, f32[4,128,128]{1,2,0:T(8,128)S(1)}, u32[]{:S(2)}, u32[]{:S(2)}) %collective-permute-start.5) | collective-permute-done | bytes 262176 | tf_op jit(solution)/shard_map/ppermute | solution.py:45
  116.7 2.3 fusion.8
  128.4 2.4 %collective-permute-start.14 = (bf16[2,128,2048]{1,2,0:T(8,128)(2,1)}, bf16[2,128,2048]{1,2,0:T(8,128)(2,1)}, u32[]{:S(2)}, u32[]{:S(2)}) collective-permute-start(bf16[2,128,2048]{1,2,0:T(8,128)(2,1)} %bitcast.105), channel_id=1, source_target_pairs={{0,12},{4,8},{8,4},{12,0},{16,28},{20,24},{24,20},{28,16},{1,13},{... | collective-permute-start | bytes 3145736 | tf_op jit(solution)/shard_map/ppermute | solution.py:130
  132.9 4.3 %fusion.18 = f32[4,128,2048]{2,1,0:T(8,128)} fusion(bf16[4,128,128]{2,1,0:T(8,128)(2,1)S(1)} %multiply_convert_fusion, bf16[4,2304,128]{2,1,0:T(8,128)(2,1)} %gather_fusion.1), kind=kOutput, calls=%fused_computation.27 | convolution fusion | flops 268435456 | bytes 6422528 | tf_op jit(solution)/shard_map/bnc,bdc->bnd/dot_general | solution.py:224
  137.2 40.3 %collective-permute-done.7 = bf16[2,128,256]{2,1,0:T(8,128)(2,1)S(1)} collective-permute-done((bf16[2,128,256]{2,1,0:T(8,128)(2,1)}, bf16[2,128,256]{2,1,0:T(8,128)(2,1)S(1)}, u32[]{:S(2)}, u32[]{:S(2)}) %collective-permute-start.7) | collective-permute-done | bytes 131104 | tf_op jit(solution)/shard_map/ppermute | solution.py:160
  182.3 3.1 %constant_dynamic-slice_fusion.3 = f32[2,1,128,2048]{3,2,1,0:T(8,128)} fusion(f32[2,4,128,2048]{3,2,1,0:T(8,128)} %bitcast.118, s32[]{:T(128)S(6)} %select_n.116), kind=kLoop, calls=%fused_computation.81 | loop fusion | bytes 4194308 | tf_op jit(solution)/shard_map/jit(dynamic_index_in_dim)/dynamic_slice | solution.py:126
  185.5 5.3 %copy.62 = f32[512,2048]{0,1:T(8,128)} copy(f32[512,2048]{1,0:T(8,128)} %bitcast.116) | data formatting | bytes 8388608 | tf_op jit(solution)/shard_map/reshape | solution.py:226
  192.7 6.4 %add.199 = f32[512,2048]{0,1:T(8,128)} add(f32[512,2048]{0,1:T(8,128)} %bitcast_add_fusion.1, f32[512,2048]{0,1:T(8,128)} %copy.62) | non-fusion elementwise | flops 1048576 | bytes 12582912 | tf_op jit(solution)/shard_map/add | solution.py:227
  205.7 5.3 %copy.57 = f32[512,2048]{1,0:T(8,128)} copy(f32[512,2048]{0,1:T(8,128)} %add.199) | data formatting | bytes 8388608
  211.8 16.1 %collective-permute-done.15 = bf16[128,2048]{0,1:T(8,128)(2,1)} collective-permute-done((bf16[128,2048]{0,1:T(8,128)(2,1)}, bf16[128,2048]{0,1:T(8,128)(2,1)}, u32[]{:S(2)}, u32[]{:S(2)}) %collective-permute-start.15) | collective-permute-done | bytes 524320 | tf_op jit(solution)/shard_map/ppermute | solution.py:142
  227.9 3.7 %fusion.28 = (f32[2048,128]{1,0:T(8,128)}, f32[2048,128]{1,0:T(8,128)}) fusion(f32[2048,128]{1,0:T(8,128)S(1)} %copy-done.8, f32[2048,128]{1,0:T(8,128)} %param.17, bf16[128,2048]{0,1:T(8,128)(2,1)} %collective-permute-done.15, f32[2,128,2048]{1,2,0:T(8,128)} %copy-done.4, s32[]{:T(128)S(6)} %select_n.121), kind=kLoop, calls=%fused_computation.37 | loop fusion | flops 3407872 | bytes 5767172 | tf_op jit(solution)/shard_map/div | solution.py:22
  (104 shorter events, 43.7 us)
Async XLA Ops:
  7.2 92.2 %copy-start = (bf16[512,2048]{1,0:T(8,128)(2,1)S(1)}, bf16[512,2048]{1,0:T(8,128)(2,1)}, u32[]{:S(2)}) copy-start(bf16[512,2048]{1,0:T(8,128)(2,1)} %param.12) | copy-start | bytes 6291460
  7.2 86.0 %all-gather.3.cloned.1.call-start = ((), (), s32[]{:S(2)}) async-start(), calls=%async_computation | async-start | bytes 5308416 | tf_op jit(solution)/shard_map/all_gather | solution.py:192
  15.1 8.2 %collective-permute-start = (bf16[2,2,2048,256]{3,2,0,1:T(8,128)(2,1)}, bf16[2,2,2048,256]{3,2,0,1:T(8,128)(2,1)}, u32[]{:S(2)}, u32[]{:S(2)}) collective-permute-start(bf16[2,2,2048,256]{3,2,0,1:T(8,128)(2,1)} %copy_bitcast_fusion), channel_id=1, source_target_pairs={{0,1},{1,0},{2,3},{3,2},{4,5},{5,4},{6,7},{7,6},{8,9},{9,8},{10,11... | collective-permute-start | bytes 12582920 | tf_op jit(solution)/shard_map/ppermute | solution.py:68
  16.4 6.9 %collective-permute-start.1 = (bf16[512,2,256]{2,0,1:T(8,128)(2,1)}, bf16[512,2,256]{2,0,1:T(8,128)(2,1)S(1)}, u32[]{:S(2)}, u32[]{:S(2)}) collective-permute-start(bf16[512,2,256]{2,0,1:T(8,128)(2,1)} %copy.36), channel_id=1, source_target_pairs={{0,1},{1,0},{2,3},{3,2},{4,5},{5,4},{6,7},{7,6},{8,9},{9,8},{10,11... | collective-permute-start | bytes 1572872 | tf_op jit(solution)/shard_map/ppermute | solution.py:69
  27.6 27.1 %collective-permute-start.2 = (bf16[256,2048]{0,1:T(8,128)(2,1)}, bf16[256,2048]{0,1:T(8,128)(2,1)}, u32[]{:S(2)}, u32[]{:S(2)}) collective-permute-start(bf16[256,2048]{0,1:T(8,128)(2,1)} %get-tuple-element.32), channel_id=1, source_target_pairs={{0,2},{1,3},{2,0},{3,1},{4,6},{5,7},{6,4},{7,5},{8,10},{9,11},{10,... | collective-permute-start | bytes 3145736 | tf_op jit(solution)/shard_map/ppermute | solution.py:82
  30.5 46.2 %collective-permute-start.3 = (bf16[256,2048]{0,1:T(8,128)(2,1)}, bf16[256,2048]{0,1:T(8,128)(2,1)}, u32[]{:S(2)}, u32[]{:S(2)}) collective-permute-start(bf16[256,2048]{0,1:T(8,128)(2,1)} %get-tuple-element.33), channel_id=1, source_target_pairs={{0,2},{1,3},{2,0},{3,1},{4,6},{5,7},{6,4},{7,5},{8,10},{9,11},{10,... | collective-permute-start | bytes 3145736 | tf_op jit(solution)/shard_map/ppermute | solution.py:83
  99.3 3.1 %collective-permute-start.10 = (f32[4,128,128]{2,1,0:T(8,128)S(1)}, f32[4,128,128]{2,1,0:T(8,128)S(1)}, u32[]{:S(2)}, u32[]{:S(2)}) collective-permute-start(f32[4,128,128]{2,1,0:T(8,128)S(1)} %copy.49), channel_id=1, source_target_pairs={{0,1},{1,0},{2,3},{3,2},{4,5},{5,4},{6,7},{7,6},{8,9},{9,8},{10,11... | collective-permute-start | bytes 786440 | tf_op jit(solution)/shard_map/ppermute | solution.py:45
  101.8 14.9 %copy-start.12 = (pred[512,8]{0,1:T(8,128)(4,1)S(1)}, pred[512,8]{0,1:T(8,128)(4,1)}, u32[]{:S(2)}) copy-start(pred[512,8]{0,1:T(8,128)(4,1)} %iota_compare_fusion) | copy-start | bytes 12292
  101.8 3.3 %collective-permute-start.4 = (f32[4,128,128]{1,2,0:T(8,128)S(1)}, f32[4,128,128]{1,2,0:T(8,128)}, u32[]{:S(2)}, u32[]{:S(2)}) collective-permute-start(f32[4,128,128]{1,2,0:T(8,128)S(1)} %fusion.21), channel_id=1, source_target_pairs={{0,1},{1,0},{2,3},{3,2},{4,5},{5,4},{6,7},{7,6},{8,9},{9,8},{10,11... | collective-permute-start | bytes 786440 | tf_op jit(solution)/shard_map/ppermute | solution.py:45
  102.4 9.3 %collective-permute-start.11 = (f32[4,128,128]{2,1,0:T(8,128)S(1)}, f32[4,128,128]{2,1,0:T(8,128)}, u32[]{:S(2)}, u32[]{:S(2)}) collective-permute-start(f32[4,128,128]{2,1,0:T(8,128)S(1)} %add.194), channel_id=1, source_target_pairs={{0,2},{1,3},{2,0},{3,1},{4,6},{5,7},{6,4},{7,5},{8,10},{9,11},{10,... | collective-permute-start | bytes 786440 | tf_op jit(solution)/shard_map/ppermute | solution.py:45
  106.1 10.2 %collective-permute-start.5 = (f32[4,128,128]{1,2,0:T(8,128)S(1)}, f32[4,128,128]{1,2,0:T(8,128)S(1)}, u32[]{:S(2)}, u32[]{:S(2)}) collective-permute-start(f32[4,128,128]{1,2,0:T(8,128)S(1)} %add.177), channel_id=1, source_target_pairs={{0,2},{1,3},{2,0},{3,1},{4,6},{5,7},{6,4},{7,5},{8,10},{9,11},{10,... | collective-permute-start | bytes 786440 | tf_op jit(solution)/shard_map/ppermute | solution.py:45
  120.9 10.5 %collective-permute-start.6 = (bf16[2,128,256]{2,1,0:T(8,128)(2,1)}, bf16[2,128,256]{2,1,0:T(8,128)(2,1)S(1)}, u32[]{:S(2)}, u32[]{:S(2)}) collective-permute-start(bf16[2,128,256]{2,1,0:T(8,128)(2,1)} %get-tuple-element.34), channel_id=1, source_target_pairs={{0,4},{4,0},{8,12},{12,8},{16,20},{20,16},{24,28},{28,24},{1,5},{5... | collective-permute-start | bytes 393224 | tf_op jit(solution)/shard_map/ppermute | solution.py:160
  124.8 75.3 %collective-permute-start.12 = (bf16[2,128,2048]{1,2,0:T(8,128)(2,1)}, bf16[2,128,2048]{1,2,0:T(8,128)(2,1)S(1)}, u32[]{:S(2)}, u32[]{:S(2)}) collective-permute-start(bf16[2,128,2048]{1,2,0:T(8,128)(2,1)} %bitcast.128), channel_id=1, source_target_pairs={{0,4},{4,0},{8,12},{12,8},{16,20},{20,16},{24,28},{28,24},{1,5},{5... | collective-permute-start | bytes 3145736 | tf_op jit(solution)/shard_map/ppermute | solution.py:130
  126.6 73.4 %collective-permute-start.13 = (bf16[2,128,2048]{1,2,0:T(8,128)(2,1)}, bf16[2,128,2048]{1,2,0:T(8,128)(2,1)}, u32[]{:S(2)}, u32[]{:S(2)}) collective-permute-start(bf16[2,128,2048]{1,2,0:T(8,128)(2,1)} %bitcast.129), channel_id=1, source_target_pairs={{0,8},{4,12},{8,0},{12,4},{16,24},{20,28},{24,16},{28,20},{1,9},{5... | collective-permute-start | bytes 3145736 | tf_op jit(solution)/shard_map/ppermute | solution.py:130
  128.4 71.6 %collective-permute-start.14 = (bf16[2,128,2048]{1,2,0:T(8,128)(2,1)}, bf16[2,128,2048]{1,2,0:T(8,128)(2,1)}, u32[]{:S(2)}, u32[]{:S(2)}) collective-permute-start(bf16[2,128,2048]{1,2,0:T(8,128)(2,1)} %bitcast.105), channel_id=1, source_target_pairs={{0,12},{4,8},{8,4},{12,0},{16,28},{20,24},{24,20},{28,16},{1,13},{... | collective-permute-start | bytes 3145736 | tf_op jit(solution)/shard_map/ppermute | solution.py:130
  130.8 46.6 %collective-permute-start.7 = (bf16[2,128,256]{2,1,0:T(8,128)(2,1)}, bf16[2,128,256]{2,1,0:T(8,128)(2,1)S(1)}, u32[]{:S(2)}, u32[]{:S(2)}) collective-permute-start(bf16[2,128,256]{2,1,0:T(8,128)(2,1)} %get-tuple-element.36), channel_id=1, source_target_pairs={{0,8},{4,12},{8,0},{12,4},{16,24},{20,28},{24,16},{28,20},{1,9},{5... | collective-permute-start | bytes 393224 | tf_op jit(solution)/shard_map/ppermute | solution.py:160
  131.4 48.4 %collective-permute-start.8 = (bf16[2,128,256]{2,1,0:T(8,128)(2,1)}, bf16[2,128,256]{2,1,0:T(8,128)(2,1)S(1)}, u32[]{:S(2)}, u32[]{:S(2)}) collective-permute-start(bf16[2,128,256]{2,1,0:T(8,128)(2,1)} %get-tuple-element.35), channel_id=1, source_target_pairs={{0,12},{4,8},{8,4},{12,0},{16,28},{20,24},{24,20},{28,16},{1,13},{... | collective-permute-start | bytes 393224 | tf_op jit(solution)/shard_map/ppermute | solution.py:160
  180.8 18.3 %collective-permute-start.9 = (bf16[128,256]{1,0:T(8,128)(2,1)S(1)}, bf16[128,256]{1,0:T(8,128)(2,1)}, u32[]{:S(2)}, u32[]{:S(2)}) collective-permute-start(bf16[128,256]{1,0:T(8,128)(2,1)S(1)} %fusion.52), channel_id=1, source_target_pairs={{0,16},{4,20},{8,24},{12,28},{16,0},{20,4},{24,8},{28,12},{1,17},{... | collective-permute-start | bytes 196616 | tf_op jit(solution)/shard_map/ppermute | solution.py:165
  200.0 11.0 %copy-start.9 = (f32[128,256]{1,0:T(8,128)}, f32[128,256]{1,0:T(8,128)S(1)}, u32[]{:S(2)}) copy-start(f32[128,256]{1,0:T(8,128)S(1)} %bitcast_add_fusion.6) | copy-start | bytes 393220
  204.2 6.8 %copy-start.10 = (f32[128,256]{1,0:T(8,128)S(1)}, f32[128,256]{1,0:T(8,128)}, u32[]{:S(2)}) copy-start(f32[128,256]{1,0:T(8,128)} %param.20) | copy-start | bytes 393220
  204.2 6.8 %copy-start.11 = (f32[128,256]{1,0:T(8,128)S(1)}, f32[128,256]{1,0:T(8,128)}, u32[]{:S(2)}) copy-start(f32[128,256]{1,0:T(8,128)} %param.19) | copy-start | bytes 393220
  204.2 23.7 %copy-start.8 = (f32[2048,128]{1,0:T(8,128)S(1)}, f32[2048,128]{1,0:T(8,128)}, u32[]{:S(2)}) copy-start(f32[2048,128]{1,0:T(8,128)} %param.18) | copy-start | bytes 3145732
  204.3 23.7 %collective-permute-start.15 = (bf16[128,2048]{0,1:T(8,128)(2,1)}, bf16[128,2048]{0,1:T(8,128)(2,1)}, u32[]{:S(2)}, u32[]{:S(2)}) collective-permute-start(bf16[128,2048]{0,1:T(8,128)(2,1)} %fusion.34), channel_id=1, source_target_pairs={{0,16},{4,20},{8,24},{12,28},{16,0},{20,4},{24,8},{28,12},{1,17},{... | collective-permute-start | bytes 1572872 | tf_op jit(solution)/shard_map/ppermute | solution.py:142
  211.1 20.6 %copy-start.1 = (bf16[512,2048]{1,0:T(8,128)(2,1)S(1)}, bf16[512,2048]{1,0:T(8,128)(2,1)}, u32[]{:S(2)}) copy-start(bf16[512,2048]{1,0:T(8,128)(2,1)} %param.12) | copy-start | bytes 6291460
  (8 other events, 32.7 us)
Sparse Core Ops, SparseCore 0:
  10.6 82.5 all-gather.2

commit v16 on v13

--- a/solution.py
+++ b/solution.py
@@ -194,9 +194,9 @@
     block_slot = tenant_slot[block_tenant]
     slot_major = dp_size == TENANTS
     if slot_major:
-        picked = jnp.take(packed_all, block_slot, axis=0, mode="clip")
-        a_blocks = picked[:, :a_rows_own]
-        b_blocks = picked[:, a_rows_own:].reshape(block_count, 2, PADDED_RANK, kv_shard)
+        b_blocks = jnp.take(packed_all[:, a_rows_own:], block_slot, axis=0, mode="clip").reshape(
+            block_count, 2, PADDED_RANK, kv_shard
+        )
     else:
         a_all = packed_all[:, :a_rows_own].reshape(TENANTS, feat_shard, rank_width)
         b_all = packed_all[:, a_rows_own:].reshape(dp_size, b_rows_own, kv_shard).reshape(
@@ -210,10 +210,13 @@
     adapter_scale_factor = adapter_alpha_factor / rank_of_block
     x_blocks = tokens_in.reshape(block_count, TENANT_BLOCK, feat_shard)
     dy_blocks = grad_out.reshape(block_count, TENANT_BLOCK, 2, kv_shard)
-    mid_part = jnp.einsum("bnd,bdc->bnc", x_blocks, a_blocks, preferred_element_type=jnp.float32)
     back_part = jnp.einsum(
         "bnpk,bprk->bnpr", dy_blocks, b_blocks, preferred_element_type=jnp.float32
     ).reshape(block_count, TENANT_BLOCK, rank_width)
+    if slot_major:
+        late_all, _ = lax.optimization_barrier((packed_all, back_part))
+        a_blocks = jnp.take(late_all, block_slot, axis=0, mode="clip")[:, :a_rows_own]
+    mid_part = jnp.einsum("bnd,bdc->bnc", x_blocks, a_blocks, preferred_element_type=jnp.float32)
     backward_gradient_sum = tensor_sum((back_part,))[0]
     mid_sum = tensor_sum((mid_part,))[0]
     middle_rank_rows = (mid_sum * column_rank_mask[:, None, :]).astype(jnp.bfloat16)

time: 215 us -> 215 us (level)
    gather x1 -> x2, local copies, waits for them, and re-layouts: 4.65 us -> 5.25 us  [the longest x1 4.65 us: local(): jnp.take(late_all, block_slot, axis=0, mode='clip')[:, :a_rows_own]]
  transfers between devices with their start and end apart: 17 -> 17, of which waited for: 11 -> 11; matrix products, arithmetic and copies ran while one was open for 30% -> 32% of each run, Pallas kernels for 0% -> 0%
where the time goes in v16:
time: 215 us
  waiting for transfers between devices  101 us (47%)
  local copies, waits for them, and re-layouts  41.1 us (19%)
  matrix products  22.5 us (10%)
  other arithmetic  19.9 us (9%)
  starting transfers between devices  15.4 us (7%)
  between operations  14.3 us (7%)
    ppermute x3, waiting for transfers between devices, group_stage(): lax.ppermute(part.astype(jnp.bfloat16), 'dp', pairs).astype(jnp.float32)  33.9 us
    ppermute x1, waiting for transfers between devices, frozen_gradient(): lax.ppermute(far_part[:half], 'tensor', row_pairs)  22 us
    ppermute x1, waiting for transfers between devices, frozen_gradient(): lax.ppermute(far_part[half:], 'tensor', row_pairs)  20.2 us
    unnamed x31, local copies, waits for them, and re-layouts  13.7 us
    all_gather x1, waiting for transfers between devices, local(): packed_all = lax.all_gather(packed, 'dp', axis=0, tiled=False)  10.8 us
    dot_general x2, matrix products, chip_partial(): jnp.einsum('tpk,pdk->td', partner_dy, other, preferred_element_type=jnp.f...  8.52 us
    add x1, other arithmetic, local(): input_gradient_layer = frozen_gradient_share + adapter_gradient_term  6.51 us
    ppermute x4, waiting for transfers between devices, grouped_exchange(): lax.ppermute(part.astype(jnp.bfloat16), 'dp', pairs).astype(jnp.float32)  5.95 us
  transfers between devices with their start and end apart: 17, of which 11 were waited for; matrix products, arithmetic and copies ran while one was open for 32% of the time, Pallas kernels for 0%

profile of v16, /device:TPU:0, one launch (start us, length us, event | category | flops | bytes accessed | tf_op | source)
XLA Modules:
  0.0 214.6 jit_solution(11603572168039076040)
XLA Ops:
  10.5 4.5 %copy_bitcast_fusion = bf16[2,2,2048,256]{3,2,0,1:T(8,128)(2,1)} fusion(bf16[2,2,2,2048,256]{4,3,2,1,0:T(8,128)(2,1)} %bitcast.123, s32[]{:T(128)S(6)} %select_n.108), kind=kLoop, calls=%fused_computation.9 | loop fusion | bytes 8388612 | tf_op jit(solution)/shard_map/jit(dynamic_index_in_dim)/squeeze | solution.py:64
  17.8 2.9 %fusion.2 = f32[2048,512,1]{1,0,2:T(8,128)S(1)} fusion(bf16[2,2,2,2048,256]{4,3,2,1,0:T(8,128)(2,1)} %bitcast.124, s32[]{:T(128)S(6)} %select_n.110, s32[]{:T(128)S(6)} %select_n.107, bf16[512,2,256]{2,1,0:T(2,128)(2,1)S(1)} %copy-done.7), kind=kOutput, calls=%fused_computation.11 | convolution fusion | flops 1073741824 | bytes 6815752 | tf_op jit(solution)/shard_map/tpk,pdk->td/dot_general | solution.py:74
  20.7 2.6 %collective-permute-done.1 = bf16[512,2,256]{2,0,1:T(8,128)(2,1)S(1)} collective-permute-done((bf16[512,2,256]{2,0,1:T(8,128)(2,1)}, bf16[512,2,256]{2,0,1:T(8,128)(2,1)S(1)}, u32[]{:S(2)}, u32[]{:S(2)}) %collective-permute-start.1) | collective-permute-done | bytes 524320 | tf_op jit(solution)/shard_map/ppermute | solution.py:69
  23.3 2.9 %fusion.1 = bf16[512,2048]{0,1:T(8,128)(2,1)S(1)} fusion(bf16[512,2,256]{2,0,1:T(8,128)(2,1)S(1)} %collective-permute-done.1, f32[2048,512,1]{1,0,2:T(8,128)S(1)} %fusion.2, bf16[2,2,2048,256]{3,2,0,1:T(8,128)(2,1)} %collective-permute-done, s32[]{:T(128)S(6)} %select_n.109), kind=kOutput, calls=%fused_computation.10 | convolution fusion | flops 1075838976 | bytes 8912900 | tf_op jit(solution)/shard_map/tpk,pdk->td/dot_general | solution.py:75
  27.6 2.9 %collective-permute-start.3 = (bf16[256,2048]{0,1:T(8,128)(2,1)}, bf16[256,2048]{0,1:T(8,128)(2,1)}, u32[]{:S(2)}, u32[]{:S(2)}) collective-permute-start(bf16[256,2048]{0,1:T(8,128)(2,1)} %get-tuple-element.35), channel_id=1, source_target_pairs={{0,2},{1,3},{2,0},{3,1},{4,6},{5,7},{6,4},{7,5},{8,10},{9,11},{10,... | collective-permute-start | bytes 3145736 | tf_op jit(solution)/shard_map/ppermute | solution.py:83
  31.6 2.9 %fusion.4 = f32[2048,512,1]{1,0,2:T(8,128)S(1)} fusion(bf16[2,2,2,2048,256]{4,3,2,1,0:T(8,128)(2,1)} %bitcast.125, s32[]{:T(128)S(6)} %select_n.104, s32[]{:T(128)S(6)} %select_n.107, bf16[512,2,256]{2,1,0:T(2,128)(2,1)S(1)} %copy-done.7), kind=kOutput, calls=%fused_computation.13 | convolution fusion | flops 1073741824 | bytes 6815752 | tf_op jit(solution)/shard_map/tpk,pdk->td/dot_general | solution.py:74
  34.5 20.2 %collective-permute-done.3 = bf16[256,2048]{0,1:T(8,128)(2,1)} collective-permute-done((bf16[256,2048]{0,1:T(8,128)(2,1)}, bf16[256,2048]{0,1:T(8,128)(2,1)}, u32[]{:S(2)}, u32[]{:S(2)}) %collective-permute-start.3) | collective-permute-done | bytes 1048608 | tf_op jit(solution)/shard_map/ppermute | solution.py:83
  54.7 22.0 %collective-permute-done.2 = bf16[256,2048]{0,1:T(8,128)(2,1)} collective-permute-done((bf16[256,2048]{0,1:T(8,128)(2,1)}, bf16[256,2048]{0,1:T(8,128)(2,1)}, u32[]{:S(2)}, u32[]{:S(2)}) %collective-permute-start.2) | collective-permute-done | bytes 1048608 | tf_op jit(solution)/shard_map/ppermute | solution.py:82
  76.7 5.6 %bitcast_add_fusion.1 = f32[512,2048]{0,1:T(8,128)} fusion(f32[2048,512,1]{1,0,2:T(8,128)S(1)} %fusion.4, bf16[512,2,256]{2,0,1:T(8,128)(2,1)S(1)} %collective-permute-done.1, bf16[256,2048]{0,1:T(8,128)(2,1)} %collective-permute-done.3, bf16[256,2048]{0,1:T(8,128)(2,1)} %collective-permute-done.2, bf16[2,2,2048,256]{3,2,0,1:T(8,128)(2,1)} %collective-permute-done, ...), kind=kOutput, calls=%fused_computation.7 | convolution fusion | flops 1080033280 | bytes 13107204 | tf_op jit(solution)/shard_map/tpk,pdk->td/dot_general | solution.py:75
  82.3 10.8 %all-gather.3.cloned.1.call-done = bf16[18432,128]{1,0:T(8,128)(2,1)} async-done(((bf16[2304,128]{1,0:T(8,128)(2,1)}), bf16[18432,128]{1,0:T(8,128)(2,1)}) %all-gather.3.cloned.1.call-update) | async-done | bytes 4718608 | tf_op jit(solution)/shard_map/all_gather | solution.py:191
  95.5 4.6 %gather_fusion.3 = bf16[4,2304,128]{2,1,0:T(8,128)(2,1)} fusion(bf16[8,2304,128]{2,1,0:T(8,128)(2,1)} %bitcast.129, s32[1024]{0:T(1024)S(1)} %pad_clamp_fusion.1), kind=kCustom, calls=%fused_computation.3 | custom fusion | bytes 4718608 | tf_op jit(solution)/shard_map/jit(_take)/gather | solution.py:218
  100.2 2.4 %fusion.21 = f32[4,128,128]{1,2,0:T(8,128)S(1)} fusion(bf16[4,128,2048]{2,1,0:T(8,128)(2,1)S(1)} %bitcast.117, bf16[4,2304,128]{2,1,0:T(8,128)(2,1)} %gather_fusion.3), kind=kOutput, calls=%fused_computation.33 | convolution fusion | flops 268435456 | bytes 4456448 | tf_op jit(solution)/shard_map/bnd,bdc->bnc/dot_general | solution.py:219
  106.6 5.9 %collective-permute-done.5 = f32[4,128,128]{2,1,0:T(8,128)S(1)} collective-permute-done((f32[4,128,128]{2,1,0:T(8,128)S(1)}, f32[4,128,128]{2,1,0:T(8,128)S(1)}, u32[]{:S(2)}, u32[]{:S(2)}) %collective-permute-start.5) | collective-permute-done | bytes 262176 | tf_op jit(solution)/shard_map/ppermute | solution.py:45
  112.6 2.3 %fusion.8 = f32[8,128,2048]{2,1,0:T(8,128)S(1)} fusion(bf16[512,2048]{1,0:T(8,128)(2,1)S(1)} %copy-done, pred[512,8]{0,1:T(8,128)(4,1)S(1)} %iota_compare_fusion, bf16[512,128]{0,1:T(8,128)(2,1)S(1)} %copy.49), kind=kOutput, calls=%fused_computation.18 | convolution fusion | flops 2148007936 | bytes 10620928 | tf_op jit(solution)/shard_map/nsc,nd->scd/dot_general | solution.py:100
  114.9 3.3 %copy-done.6 = f32[8,128,2048]{2,1,0:T(8,128)} copy-done((f32[8,128,2048]{2,1,0:T(8,128)}, f32[8,128,2048]{2,1,0:T(8,128)S(1)}, u32[]{:S(2)}) %copy-start.6) | copy-done | bytes 8388632
  128.2 3.2 %constant_dynamic-slice_fusion.3 = f32[2,1,128,2048]{3,2,1,0:T(8,128)} fusion(f32[2,4,128,2048]{3,2,1,0:T(8,128)} %bitcast.120, s32[]{:T(128)S(6)} %select_n.117), kind=kLoop, calls=%fused_computation.82 | loop fusion | bytes 4194308 | tf_op jit(solution)/shard_map/jit(dynamic_index_in_dim)/dynamic_slice | solution.py:125
  133.3 14.2 %collective-permute-done.10 = bf16[2,128,2048]{1,2,0:T(8,128)(2,1)} collective-permute-done((bf16[2,128,2048]{1,2,0:T(8,128)(2,1)}, bf16[2,128,2048]{1,2,0:T(8,128)(2,1)}, u32[]{:S(2)}, u32[]{:S(2)}) %collective-permute-start.10) | collective-permute-done | bytes 1048608 | tf_op jit(solution)/shard_map/ppermute | solution.py:129
  147.5 18.8 %collective-permute-done.9 = bf16[2,128,2048]{1,2,0:T(8,128)(2,1)} collective-permute-done((bf16[2,128,2048]{1,2,0:T(8,128)(2,1)}, bf16[2,128,2048]{1,2,0:T(8,128)(2,1)}, u32[]{:S(2)}, u32[]{:S(2)}) %collective-permute-start.9) | collective-permute-done | bytes 1048608 | tf_op jit(solution)/shard_map/ppermute | solution.py:129
  176.9 2.8 %collective-permute-done.13 = bf16[2,128,256]{2,1,0:T(8,128)(2,1)S(1)} collective-permute-done((bf16[2,128,256]{2,1,0:T(8,128)(2,1)S(1)}, bf16[2,128,256]{2,1,0:T(8,128)(2,1)S(1)}, u32[]{:S(2)}, u32[]{:S(2)}) %collective-permute-start.13) | collective-permute-done | bytes 131104 | tf_op jit(solution)/shard_map/ppermute | solution.py:159
  180.5 2.7 %fusion.18 = f32[4,128,2048]{2,1,0:T(8,128)} fusion(bf16[4,128,128]{2,1,0:T(8,128)(2,1)S(1)} %multiply_convert_fusion.1, bf16[4,2304,128]{2,1,0:T(8,128)(2,1)S(1)} %copy-done.4), kind=kOutput, calls=%fused_computation.28 | convolution fusion | flops 268435456 | bytes 6422528 | tf_op jit(solution)/shard_map/bnc,bdc->bnd/dot_general | solution.py:226
  183.1 5.5 %copy.59 = f32[512,2048]{0,1:T(8,128)} copy(f32[512,2048]{1,0:T(8,128)} %bitcast.118) | data formatting | bytes 8388608 | tf_op jit(solution)/shard_map/reshape | solution.py:228
  188.6 6.5 %add.180 = f32[512,2048]{0,1:T(8,128)} add(f32[512,2048]{0,1:T(8,128)} %bitcast_add_fusion.1, f32[512,2048]{0,1:T(8,128)} %copy.59) | non-fusion elementwise | flops 1048576 | bytes 12582912 | tf_op jit(solution)/shard_map/add | solution.py:229
  195.1 5.4 %copy.56 = f32[512,2048]{1,0:T(8,128)} copy(f32[512,2048]{0,1:T(8,128)} %add.180) | data formatting | bytes 8388608
  204.0 3.7 %fusion.28 = (f32[2048,128]{1,0:T(8,128)}, f32[2048,128]{1,0:T(8,128)}) fusion(f32[2048,128]{1,0:T(8,128)S(1)} %copy-done.9, f32[2048,128]{1,0:T(8,128)} %param.17, bf16[128,2048]{0,1:T(8,128)(2,1)} %collective-permute-done.11, f32[2,128,2048]{1,2,0:T(8,128)} %copy-done.5, s32[]{:T(128)S(6)} %select_n.122), kind=kLoop, calls=%fused_computation.38 | loop fusion | flops 3407872 | bytes 5767172 | tf_op jit(solution)/shard_map/div | solution.py:22
  (100 shorter events, 41.5 us)
Async XLA Ops:
  7.2 93.0 %copy-start = (bf16[512,2048]{1,0:T(8,128)(2,1)S(1)}, bf16[512,2048]{1,0:T(8,128)(2,1)}, u32[]{:S(2)}) copy-start(bf16[512,2048]{1,0:T(8,128)(2,1)} %param.12) | copy-start | bytes 6291460
  7.2 86.0 %all-gather.3.cloned.1.call-start = ((), (), s32[]{:S(2)}) async-start(), calls=%async_computation | async-start | bytes 5308416 | tf_op jit(solution)/shard_map/all_gather | solution.py:191
  10.5 6.6 %copy-start.2 = (s32[8]{0:T(128)S(1)}, s32[8]{0:T(128)}, u32[]{:S(2)}) copy-start(s32[8]{0:T(128)} %param.22) | copy-start | bytes 100
  15.1 8.2 %collective-permute-start = (bf16[2,2,2048,256]{3,2,0,1:T(8,128)(2,1)}, bf16[2,2,2048,256]{3,2,0,1:T(8,128)(2,1)}, u32[]{:S(2)}, u32[]{:S(2)}) collective-permute-start(bf16[2,2,2048,256]{3,2,0,1:T(8,128)(2,1)} %copy_bitcast_fusion), channel_id=1, source_target_pairs={{0,1},{1,0},{2,3},{3,2},{4,5},{5,4},{6,7},{7,6},{8,9},{9,8},{10,11... | collective-permute-start | bytes 12582920 | tf_op jit(solution)/shard_map/ppermute | solution.py:68
  16.4 6.9 %collective-permute-start.1 = (bf16[512,2,256]{2,0,1:T(8,128)(2,1)}, bf16[512,2,256]{2,0,1:T(8,128)(2,1)S(1)}, u32[]{:S(2)}, u32[]{:S(2)}) collective-permute-start(bf16[512,2,256]{2,0,1:T(8,128)(2,1)} %copy.36), channel_id=1, source_target_pairs={{0,1},{1,0},{2,3},{3,2},{4,5},{5,4},{6,7},{7,6},{8,9},{9,8},{10,11... | collective-permute-start | bytes 1572872 | tf_op jit(solution)/shard_map/ppermute | solution.py:69
  27.6 27.1 %collective-permute-start.3 = (bf16[256,2048]{0,1:T(8,128)(2,1)}, bf16[256,2048]{0,1:T(8,128)(2,1)}, u32[]{:S(2)}, u32[]{:S(2)}) collective-permute-start(bf16[256,2048]{0,1:T(8,128)(2,1)} %get-tuple-element.35), channel_id=1, source_target_pairs={{0,2},{1,3},{2,0},{3,1},{4,6},{5,7},{6,4},{7,5},{8,10},{9,11},{10,... | collective-permute-start | bytes 3145736 | tf_op jit(solution)/shard_map/ppermute | solution.py:83
  30.5 46.2 %collective-permute-start.2 = (bf16[256,2048]{0,1:T(8,128)(2,1)}, bf16[256,2048]{0,1:T(8,128)(2,1)}, u32[]{:S(2)}, u32[]{:S(2)}) collective-permute-start(bf16[256,2048]{0,1:T(8,128)(2,1)} %get-tuple-element.34), channel_id=1, source_target_pairs={{0,2},{1,3},{2,0},{3,1},{4,6},{5,7},{6,4},{7,5},{8,10},{9,11},{10,... | collective-permute-start | bytes 3145736 | tf_op jit(solution)/shard_map/ppermute | solution.py:82
  95.4 7.7 %collective-permute-start.4 = (f32[4,128,128]{2,1,0:T(8,128)S(1)}, f32[4,128,128]{2,1,0:T(8,128)S(1)}, u32[]{:S(2)}, u32[]{:S(2)}) collective-permute-start(f32[4,128,128]{2,1,0:T(8,128)S(1)} %copy.43), channel_id=1, source_target_pairs={{0,1},{1,0},{2,3},{3,2},{4,5},{5,4},{6,7},{7,6},{8,9},{9,8},{10,11... | collective-permute-start | bytes 786440 | tf_op jit(solution)/shard_map/ppermute | solution.py:45
  102.6 3.3 %collective-permute-start.6 = (f32[4,128,128]{1,2,0:T(8,128)S(1)}, f32[4,128,128]{1,2,0:T(8,128)S(1)}, u32[]{:S(2)}, u32[]{:S(2)}) collective-permute-start(f32[4,128,128]{1,2,0:T(8,128)S(1)} %fusion.21), channel_id=1, source_target_pairs={{0,1},{1,0},{2,3},{3,2},{4,5},{5,4},{6,7},{7,6},{8,9},{9,8},{10,11... | collective-permute-start | bytes 786440 | tf_op jit(solution)/shard_map/ppermute | solution.py:45
  103.2 9.2 %collective-permute-start.5 = (f32[4,128,128]{2,1,0:T(8,128)S(1)}, f32[4,128,128]{2,1,0:T(8,128)S(1)}, u32[]{:S(2)}, u32[]{:S(2)}) collective-permute-start(f32[4,128,128]{2,1,0:T(8,128)S(1)} %add.177), channel_id=1, source_target_pairs={{0,2},{1,3},{2,0},{3,1},{4,6},{5,7},{6,4},{7,5},{8,10},{9,11},{10,... | collective-permute-start | bytes 786440 | tf_op jit(solution)/shard_map/ppermute | solution.py:45
  106.0 20.4 %collective-permute-start.7 = (f32[4,128,128]{1,2,0:T(8,128)S(1)}, f32[4,128,128]{1,2,0:T(8,128)}, u32[]{:S(2)}, u32[]{:S(2)}) collective-permute-start(f32[4,128,128]{1,2,0:T(8,128)S(1)} %add.181), channel_id=1, source_target_pairs={{0,2},{1,3},{2,0},{3,1},{4,6},{5,7},{6,4},{7,5},{8,10},{9,11},{10,... | collective-permute-start | bytes 786440 | tf_op jit(solution)/shard_map/ppermute | solution.py:45
  120.2 27.4 %collective-permute-start.10 = (bf16[2,128,2048]{1,2,0:T(8,128)(2,1)}, bf16[2,128,2048]{1,2,0:T(8,128)(2,1)}, u32[]{:S(2)}, u32[]{:S(2)}) collective-permute-start(bf16[2,128,2048]{1,2,0:T(8,128)(2,1)} %bitcast.131), channel_id=1, source_target_pairs={{0,12},{4,8},{8,4},{12,0},{16,28},{20,24},{24,20},{28,16},{1,13},{... | collective-permute-start | bytes 3145736 | tf_op jit(solution)/shard_map/ppermute | solution.py:129
  120.7 6.9 %copy-start.8 = (bf16[512,2,256]{2,1,0:T(2,128)(2,1)S(1)}, bf16[512,2,256]{2,1,0:T(2,128)(2,1)}, u32[]{:S(2)}) copy-start(bf16[512,2,256]{2,1,0:T(2,128)(2,1)} %param.13) | copy-start | bytes 1572868
  122.0 44.3 %collective-permute-start.9 = (bf16[2,128,2048]{1,2,0:T(8,128)(2,1)}, bf16[2,128,2048]{1,2,0:T(8,128)(2,1)}, u32[]{:S(2)}, u32[]{:S(2)}) collective-permute-start(bf16[2,128,2048]{1,2,0:T(8,128)(2,1)} %bitcast.132), channel_id=1, source_target_pairs={{0,8},{4,12},{8,0},{12,4},{16,24},{20,28},{24,16},{28,20},{1,9},{5... | collective-permute-start | bytes 3145736 | tf_op jit(solution)/shard_map/ppermute | solution.py:129
  124.8 42.4 %collective-permute-start.8 = (bf16[2,128,2048]{1,2,0:T(8,128)(2,1)}, bf16[2,128,2048]{1,2,0:T(8,128)(2,1)}, u32[]{:S(2)}, u32[]{:S(2)}) collective-permute-start(bf16[2,128,2048]{1,2,0:T(8,128)(2,1)} %bitcast.108), channel_id=1, source_target_pairs={{0,4},{4,0},{8,12},{12,8},{16,20},{20,16},{24,28},{28,24},{1,5},{5... | collective-permute-start | bytes 3145736 | tf_op jit(solution)/shard_map/ppermute | solution.py:129
  169.4 13.7 %copy-start.5 = (f32[2,128,2048]{1,2,0:T(8,128)}, f32[2,128,2048]{1,2,0:T(8,128)S(1)}, u32[]{:S(2)}) copy-start(f32[2,128,2048]{1,2,0:T(8,128)S(1)} %fusion.7) | copy-start | bytes 6291460
  169.5 11.0 %copy-start.4 = (bf16[4,2304,128]{2,1,0:T(8,128)(2,1)S(1)}, bf16[4,2304,128]{2,1,0:T(8,128)(2,1)}, u32[]{:S(2)}) copy-start(bf16[4,2304,128]{2,1,0:T(8,128)(2,1)} %gather_fusion.3) | copy-start | bytes 7077892
  169.5 7.3 %collective-permute-start.14 = (bf16[2,128,256]{2,1,0:T(8,128)(2,1)S(1)}, bf16[2,128,256]{2,1,0:T(8,128)(2,1)S(1)}, u32[]{:S(2)}, u32[]{:S(2)}) collective-permute-start(bf16[2,128,256]{2,1,0:T(8,128)(2,1)S(1)} %get-tuple-element.37), channel_id=1, source_target_pairs={{0,12},{4,8},{8,4},{12,0},{16,28},{20,24},{24,20},{28,16},{1,13},{... | collective-permute-start | bytes 393224 | tf_op jit(solution)/shard_map/ppermute | solution.py:159
  170.2 9.5 %collective-permute-start.13 = (bf16[2,128,256]{2,1,0:T(8,128)(2,1)S(1)}, bf16[2,128,256]{2,1,0:T(8,128)(2,1)S(1)}, u32[]{:S(2)}, u32[]{:S(2)}) collective-permute-start(bf16[2,128,256]{2,1,0:T(8,128)(2,1)S(1)} %get-tuple-element.38), channel_id=1, source_target_pairs={{0,8},{4,12},{8,0},{12,4},{16,24},{20,28},{24,16},{28,20},{1,9},{5... | collective-permute-start | bytes 393224 | tf_op jit(solution)/shard_map/ppermute | solution.py:159
  171.7 8.0 %collective-permute-start.12 = (bf16[2,128,256]{2,1,0:T(8,128)(2,1)S(1)}, bf16[2,128,256]{2,1,0:T(8,128)(2,1)S(1)}, u32[]{:S(2)}, u32[]{:S(2)}) collective-permute-start(bf16[2,128,256]{2,1,0:T(8,128)(2,1)S(1)} %get-tuple-element.36), channel_id=1, source_target_pairs={{0,4},{4,0},{8,12},{12,8},{16,20},{20,16},{24,28},{28,24},{1,5},{5... | collective-permute-start | bytes 393224 | tf_op jit(solution)/shard_map/ppermute | solution.py:159
  173.9 30.1 %collective-permute-start.11 = (bf16[128,2048]{0,1:T(8,128)(2,1)}, bf16[128,2048]{0,1:T(8,128)(2,1)}, u32[]{:S(2)}, u32[]{:S(2)}) collective-permute-start(bf16[128,2048]{0,1:T(8,128)(2,1)} %fusion.34), channel_id=1, source_target_pairs={{0,16},{4,20},{8,24},{12,28},{16,0},{20,4},{24,8},{28,12},{1,17},{... | collective-permute-start | bytes 1572872 | tf_op jit(solution)/shard_map/ppermute | solution.py:141
  179.8 22.4 %collective-permute-start.15 = (bf16[128,256]{1,0:T(8,128)(2,1)S(1)}, bf16[128,256]{1,0:T(8,128)(2,1)}, u32[]{:S(2)}, u32[]{:S(2)}) collective-permute-start(bf16[128,256]{1,0:T(8,128)(2,1)S(1)} %fusion.52), channel_id=1, source_target_pairs={{0,16},{4,20},{8,24},{12,28},{16,0},{20,4},{24,8},{28,12},{1,17},{... | collective-permute-start | bytes 196616 | tf_op jit(solution)/shard_map/ppermute | solution.py:164
  195.1 7.1 %copy-start.10 = (f32[128,256]{1,0:T(8,128)S(1)}, f32[128,256]{1,0:T(8,128)}, u32[]{:S(2)}) copy-start(f32[128,256]{1,0:T(8,128)} %param.20) | copy-start | bytes 393220
  195.1 8.9 %copy-start.9 = (f32[2048,128]{1,0:T(8,128)S(1)}, f32[2048,128]{1,0:T(8,128)}, u32[]{:S(2)}) copy-start(f32[2048,128]{1,0:T(8,128)} %param.18) | copy-start | bytes 3145732
  (6 other events, 31.9 us)
Sparse Core Ops, SparseCore 0:
  10.6 82.5 all-gather.2

commit v17 on v13

--- a/solution.py
+++ b/solution.py
@@ -111,10 +111,11 @@
         a_own = grouped_exchange(a_sc)
         b_own = grouped_exchange(b_full)
     else:
-        a_acc = group_stage(a_sc)
-        b_full, a_acc = lax.optimization_barrier((b_full, a_acc))
-        a_own = cross_stage(a_acc)
-        b_own = grouped_exchange(b_full)
+        feat_cols = a_sc.shape[-1]
+        both = jnp.concatenate([group_stage(a_sc), group_stage(b_full)], axis=-1)
+        own = cross_stage(both)
+        a_own = own[:, :feat_cols]
+        b_own = own[:, feat_cols:]
     return a_own.T, b_own
 
 

time: 215 us -> 222 us (1.033)
  waiting for transfers between devices: 101 us -> 110 us
  local copies, waits for them, and re-layouts: 40.4 us -> 34.8 us
  other arithmetic: 19.9 us -> 22.7 us
  matrix products: 22.5 us -> 25 us
    ppermute x3 -> x6, waiting for transfers between devices: 33.9 us -> 48.2 us  [group_stage(): lax.ppermute(part.astype(jnp.bfloat16), 'dp', pairs).astype(jnp.float32)]
    ppermute x4 -> x0, waiting for transfers between devices: 6 us -> none  [grouped_exchange(): lax.ppermute(part.astype(jnp.bfloat16), 'dp', pairs).astype(jnp.float32)]
    dynamic_slice x3 -> x0, local copies, waits for them, and re-layouts: 5.59 us -> none  [the longest x2 5.13 us: group_stage(): acc = lax.dynamic_index_in_dim(by_member, member, axis=1, keepdims=False)]
    ppermute x4 -> x0, starting transfers between devices: 4.17 us -> none  [grouped_exchange(): lax.ppermute(part.astype(jnp.bfloat16), 'dp', pairs).astype(jnp.float32)]
    ppermute x3 -> x6, starting transfers between devices: 3.49 us -> 6.12 us  [group_stage(): lax.ppermute(part.astype(jnp.bfloat16), 'dp', pairs).astype(jnp.float32)]
    unnamed x31 -> x21, local copies, waits for them, and re-layouts: 13.7 us -> 12.2 us
  transfers between devices with their start and end apart: 17 -> 16, of which waited for: 11 -> 8; matrix products, arithmetic and copies ran while one was open for 30% -> 26% of each run, Pallas kernels for 0% -> 0%
where the time goes in v17:
time: 222 us
  waiting for transfers between devices  110 us (50%)
  local copies, waits for them, and re-layouts  34.8 us (16%)
  matrix products  25 us (11%)
  other arithmetic  22.7 us (10%)
  starting transfers between devices  14.6 us (7%)
  between operations  14.3 us (6%)
    ppermute x6, waiting for transfers between devices, group_stage(): lax.ppermute(part.astype(jnp.bfloat16), 'dp', pairs).astype(jnp.float32)  48.2 us
    ppermute x1, waiting for transfers between devices, frozen_gradient(): lax.ppermute(far_part[:half], 'tensor', row_pairs)  22 us
    ppermute x1, waiting for transfers between devices, frozen_gradient(): lax.ppermute(far_part[half:], 'tensor', row_pairs)  20.5 us
    unnamed x21, local copies, waits for them, and re-layouts  12.2 us
    all_gather x1, waiting for transfers between devices, local(): packed_all = lax.all_gather(packed, 'dp', axis=0, tiled=False)  11 us
    dot_general x2, matrix products, chip_partial(): jnp.einsum('tpk,pdk->td', partner_dy, other, preferred_element_type=jnp.f...  8.52 us
    add x1, other arithmetic, local(): input_gradient_layer = frozen_gradient_share + adapter_gradient_term  6.48 us
    ppermute x6, starting transfers between devices, group_stage(): lax.ppermute(part.astype(jnp.bfloat16), 'dp', pairs).astype(jnp.float32)  6.12 us
  transfers between devices with their start and end apart: 16, of which 8 were waited for; matrix products, arithmetic and copies ran while one was open for 26% of the time, Pallas kernels for 0%

profile of v17, /device:TPU:0, one launch (start us, length us, event | category | flops | bytes accessed | tf_op | source)
XLA Modules:
  0.0 221.6 jit_solution(16249716081456527586)
XLA Ops:
  10.5 4.5 %copy_bitcast_fusion = bf16[2,2,2048,256]{3,2,0,1:T(8,128)(2,1)} fusion(bf16[2,2,2,2048,256]{4,3,2,1,0:T(8,128)(2,1)} %bitcast.124, s32[]{:T(128)S(6)} %select_n.102), kind=kLoop, calls=%fused_computation.8 | loop fusion | bytes 8388612 | tf_op jit(solution)/shard_map/jit(dynamic_index_in_dim)/squeeze | solution.py:64
  18.8 2.9 %fusion.2 = f32[2048,512,1]{1,0,2:T(8,128)S(1)} fusion(bf16[2,2,2,2048,256]{4,3,2,1,0:T(8,128)(2,1)} %bitcast.125, s32[]{:T(128)S(6)} %select_n.104, s32[]{:T(128)S(6)} %select_n.101, bf16[512,2,256]{2,1,0:T(2,128)(2,1)S(1)} %copy-done.5), kind=kOutput, calls=%fused_computation.17 | convolution fusion | flops 1073741824 | bytes 6815752 | tf_op jit(solution)/shard_map/tpk,pdk->td/dot_general | solution.py:74
  23.3 2.9 %fusion.1 = bf16[512,2048]{0,1:T(8,128)(2,1)S(1)} fusion(bf16[512,2,256]{2,0,1:T(8,128)(2,1)S(1)} %collective-permute-done.1, f32[2048,512,1]{1,0,2:T(8,128)S(1)} %fusion.2, bf16[2,2,2048,256]{3,2,0,1:T(8,128)(2,1)} %collective-permute-done, s32[]{:T(128)S(6)} %select_n.103), kind=kOutput, calls=%fused_computation.11 | convolution fusion | flops 1075838976 | bytes 8912900 | tf_op jit(solution)/shard_map/tpk,pdk->td/dot_general | solution.py:75
  27.6 2.9 %collective-permute-start.3 = (bf16[256,2048]{0,1:T(8,128)(2,1)}, bf16[256,2048]{0,1:T(8,128)(2,1)}, u32[]{:S(2)}, u32[]{:S(2)}) collective-permute-start(bf16[256,2048]{0,1:T(8,128)(2,1)} %get-tuple-element.27), channel_id=1, source_target_pairs={{0,2},{1,3},{2,0},{3,1},{4,6},{5,7},{6,4},{7,5},{8,10},{9,11},{10,... | collective-permute-start | bytes 3145736 | tf_op jit(solution)/shard_map/ppermute | solution.py:83
  31.4 2.9 %fusion.4 = f32[2048,512,1]{1,0,2:T(8,128)S(1)} fusion(bf16[2,2,2,2048,256]{4,3,2,1,0:T(8,128)(2,1)} %bitcast.126, s32[]{:T(128)S(6)} %select_n.98, s32[]{:T(128)S(6)} %select_n.101, bf16[512,2,256]{2,1,0:T(2,128)(2,1)S(1)} %copy-done.5), kind=kOutput, calls=%fused_computation.19 | convolution fusion | flops 1073741824 | bytes 6815752 | tf_op jit(solution)/shard_map/tpk,pdk->td/dot_general | solution.py:74
  34.3 20.5 %collective-permute-done.3 = bf16[256,2048]{0,1:T(8,128)(2,1)} collective-permute-done((bf16[256,2048]{0,1:T(8,128)(2,1)}, bf16[256,2048]{0,1:T(8,128)(2,1)}, u32[]{:S(2)}, u32[]{:S(2)}) %collective-permute-start.3) | collective-permute-done | bytes 1048608 | tf_op jit(solution)/shard_map/ppermute | solution.py:83
  54.7 22.0 %collective-permute-done.2 = bf16[256,2048]{0,1:T(8,128)(2,1)} collective-permute-done((bf16[256,2048]{0,1:T(8,128)(2,1)}, bf16[256,2048]{0,1:T(8,128)(2,1)}, u32[]{:S(2)}, u32[]{:S(2)}) %collective-permute-start.2) | collective-permute-done | bytes 1048608 | tf_op jit(solution)/shard_map/ppermute | solution.py:82
  76.7 5.6 %bitcast_add_fusion.1 = f32[512,2048]{0,1:T(8,128)} fusion(f32[2048,512,1]{1,0,2:T(8,128)S(1)} %fusion.4, bf16[512,2,256]{2,0,1:T(8,128)(2,1)S(1)} %collective-permute-done.1, bf16[256,2048]{0,1:T(8,128)(2,1)} %collective-permute-done.3, bf16[256,2048]{0,1:T(8,128)(2,1)} %collective-permute-done.2, bf16[2,2,2048,256]{3,2,0,1:T(8,128)(2,1)} %collective-permute-done, ...), kind=kOutput, calls=%fused_computation.6 | convolution fusion | flops 1080033280 | bytes 13107204 | tf_op jit(solution)/shard_map/tpk,pdk->td/dot_general | solution.py:75
  82.4 11.0 %all-gather.3.cloned.1.call-done = bf16[18432,128]{1,0:T(8,128)(2,1)} async-done(((bf16[2304,128]{1,0:T(8,128)(2,1)}), bf16[18432,128]{1,0:T(8,128)(2,1)}) %all-gather.3.cloned.1.call-update) | async-done | bytes 4718608 | tf_op jit(solution)/shard_map/all_gather | solution.py:192
  93.4 4.7 %gather_fusion.1 = bf16[4,2304,128]{2,1,0:T(8,128)(2,1)} fusion(bf16[8,2304,128]{2,1,0:T(8,128)(2,1)} %bitcast.130, s32[1024]{0:T(1024)S(1)} %pad_clamp_fusion.1), kind=kCustom, calls=%fused_computation.1 | custom fusion | bytes 4718608 | tf_op jit(solution)/shard_map/jit(_take)/gather | solution.py:198
  99.7 3.2 %fusion.26 = f32[4,128,128]{1,2,0:T(8,128)} fusion(bf16[4,128,2048]{2,1,0:T(8,128)(2,1)S(1)} %bitcast.118, bf16[4,2304,128]{2,1,0:T(8,128)(2,1)} %gather_fusion.1), kind=kOutput, calls=%fused_computation.44 | convolution fusion | flops 268435456 | bytes 4456448 | tf_op jit(solution)/shard_map/bnd,bdc->bnc/dot_general | solution.py:214
  107.4 5.3 %collective-permute-done.5 = f32[4,128,128]{2,1,0:T(8,128)} collective-permute-done((f32[4,128,128]{2,1,0:T(8,128)S(1)}, f32[4,128,128]{2,1,0:T(8,128)}, u32[]{:S(2)}, u32[]{:S(2)}) %collective-permute-start.5) | collective-permute-done | bytes 262176 | tf_op jit(solution)/shard_map/ppermute | solution.py:45
  113.8 2.3 %fusion.8 = f32[8,128,2048]{2,1,0:T(8,128)S(1)} fusion(bf16[512,2048]{1,0:T(8,128)(2,1)S(1)} %copy-done, pred[512,8]{0,1:T(8,128)(4,1)S(1)} %iota_compare_fusion, bf16[512,128]{0,1:T(8,128)(2,1)S(1)} %copy.48), kind=kOutput, calls=%fused_computation.24 | convolution fusion | flops 2148007936 | bytes 10620928 | tf_op jit(solution)/shard_map/nsc,nd->scd/dot_general | solution.py:100
  116.2 3.2 %copy-done.4 = f32[8,128,2048]{2,1,0:T(8,128)} copy-done((f32[8,128,2048]{2,1,0:T(8,128)}, f32[8,128,2048]{2,1,0:T(8,128)S(1)}, u32[]{:S(2)}) %copy-start.4) | copy-done | bytes 8388632
  119.4 1.8 fusion.34
  128.7 43.8 %collective-permute-done.13 = bf16[2,128,256]{2,1,0:T(8,128)(2,1)S(1)} collective-permute-done((bf16[2,128,256]{2,1,0:T(8,128)(2,1)S(1)}, bf16[2,128,256]{2,1,0:T(8,128)(2,1)S(1)}, u32[]{:S(2)}, u32[]{:S(2)}) %collective-permute-start.13) | collective-permute-done | bytes 131104 | tf_op jit(solution)/shard_map/ppermute | solution.py:130
  173.0 4.4 %collective-permute-done.11 = bf16[2,128,256]{2,1,0:T(8,128)(2,1)S(1)} collective-permute-done((bf16[2,128,256]{2,1,0:T(8,128)(2,1)S(1)}, bf16[2,128,256]{2,1,0:T(8,128)(2,1)S(1)}, u32[]{:S(2)}, u32[]{:S(2)}) %collective-permute-start.11) | collective-permute-done | bytes 131104 | tf_op jit(solution)/shard_map/ppermute | solution.py:130
  177.5 3.2 %fusion.7 = f32[2,128,2048]{2,1,0:T(8,128)S(1)} fusion(bf16[2,128,2048]{2,1,0:T(8,128)(2,1)} %collective-permute-done.8, bf16[2,128,2048]{2,1,0:T(8,128)(2,1)} %collective-permute-done.7, bf16[2,128,2048]{2,1,0:T(8,128)(2,1)} %collective-permute-done.6, f32[2,4,128,2048]{3,2,1,0:T(8,128)} %bitcast.121, s32[]{:T(128)S(6)} %select_n.109), kind=kLoop, calls=%fused_computation.23 | loop fusion | flops 3145728 | bytes 7340036 | tf_op jit(solution)/shard_map/add | solution.py:130
  182.3 4.4 %fusion.18 = f32[4,128,2048]{2,1,0:T(8,128)} fusion(bf16[4,128,128]{2,1,0:T(8,128)(2,1)S(1)} %multiply_convert_fusion.1, bf16[4,2304,128]{2,1,0:T(8,128)(2,1)} %gather_fusion.1), kind=kOutput, calls=%fused_computation.34 | convolution fusion | flops 268435456 | bytes 6422528 | tf_op jit(solution)/shard_map/bnc,bdc->bnd/dot_general | solution.py:224
  186.8 5.4 %copy.65 = f32[512,2048]{0,1:T(8,128)} copy(f32[512,2048]{1,0:T(8,128)} %bitcast.119) | data formatting | bytes 8388608 | tf_op jit(solution)/shard_map/reshape | solution.py:226
  192.2 6.5 %add.172 = f32[512,2048]{0,1:T(8,128)} add(f32[512,2048]{0,1:T(8,128)} %bitcast_add_fusion.1, f32[512,2048]{0,1:T(8,128)} %copy.65) | non-fusion elementwise | flops 1048576 | bytes 12582912 | tf_op jit(solution)/shard_map/add | solution.py:227
  198.7 5.3 %copy.61 = f32[512,2048]{1,0:T(8,128)} copy(f32[512,2048]{0,1:T(8,128)} %add.172) | data formatting | bytes 8388608
  207.8 2.7 %copy.62 = f32[2048,128]{1,0:T(8,128)} copy(f32[2048,128]{0,1:T(8,128)} %slice_bitcast_fusion) | data formatting | bytes 2097152
  211.3 3.5 %fusion.33 = f32[2048,128]{1,0:T(8,128)} fusion(f32[2048,128]{1,0:T(8,128)} %copy.62, f32[2048,128]{1,0:T(8,128)} %param.18, f32[2048,128]{1,0:T(8,128)} %param.17), kind=kLoop, calls=%fused_computation.49 | loop fusion | flops 2883584 | bytes 4194304 | tf_op jit(solution)/shard_map/div | solution.py:22
  (86 shorter events, 32.3 us)
Async XLA Ops:
  7.2 92.5 %copy-start = (bf16[512,2048]{1,0:T(8,128)(2,1)S(1)}, bf16[512,2048]{1,0:T(8,128)(2,1)}, u32[]{:S(2)}) copy-start(bf16[512,2048]{1,0:T(8,128)(2,1)} %param.12) | copy-start | bytes 6291460
  7.2 86.2 %all-gather.3.cloned.1.call-start = ((), (), s32[]{:S(2)}) async-start(), calls=%async_computation | async-start | bytes 5308416 | tf_op jit(solution)/shard_map/all_gather | solution.py:192
  10.5 5.0 %copy-start.5 = (bf16[512,2,256]{2,1,0:T(2,128)(2,1)S(1)}, bf16[512,2,256]{2,1,0:T(2,128)(2,1)}, u32[]{:S(2)}) copy-start(bf16[512,2,256]{2,1,0:T(2,128)(2,1)} %param.13) | copy-start | bytes 1572868
  10.5 5.9 %copy-start.8 = (s32[4]{0:T(128)S(1)}, s32[4]{0:T(128)}, u32[]{:S(2)}) copy-start(s32[4]{0:T(128)} %param.21) | copy-start | bytes 52
  10.5 5.9 %copy-start.3 = (s32[8]{0:T(128)S(1)}, s32[8]{0:T(128)}, u32[]{:S(2)}) copy-start(s32[8]{0:T(128)} %param.23) | copy-start | bytes 100
  10.5 6.6 %copy-start.2 = (s32[8]{0:T(128)S(1)}, s32[8]{0:T(128)}, u32[]{:S(2)}) copy-start(s32[8]{0:T(128)} %param.22) | copy-start | bytes 100
  15.1 8.2 %collective-permute-start = (bf16[2,2,2048,256]{3,2,0,1:T(8,128)(2,1)}, bf16[2,2,2048,256]{3,2,0,1:T(8,128)(2,1)}, u32[]{:S(2)}, u32[]{:S(2)}) collective-permute-start(bf16[2,2,2048,256]{3,2,0,1:T(8,128)(2,1)} %copy_bitcast_fusion), channel_id=1, source_target_pairs={{0,1},{1,0},{2,3},{3,2},{4,5},{5,4},{6,7},{7,6},{8,9},{9,8},{10,11... | collective-permute-start | bytes 12582920 | tf_op jit(solution)/shard_map/ppermute | solution.py:68
  16.4 6.9 %collective-permute-start.1 = (bf16[512,2,256]{2,0,1:T(8,128)(2,1)}, bf16[512,2,256]{2,0,1:T(8,128)(2,1)S(1)}, u32[]{:S(2)}, u32[]{:S(2)}) collective-permute-start(bf16[512,2,256]{2,0,1:T(8,128)(2,1)} %copy.39), channel_id=1, source_target_pairs={{0,1},{1,0},{2,3},{3,2},{4,5},{5,4},{6,7},{7,6},{8,9},{9,8},{10,11... | collective-permute-start | bytes 1572872 | tf_op jit(solution)/shard_map/ppermute | solution.py:69
  27.6 27.1 %collective-permute-start.3 = (bf16[256,2048]{0,1:T(8,128)(2,1)}, bf16[256,2048]{0,1:T(8,128)(2,1)}, u32[]{:S(2)}, u32[]{:S(2)}) collective-permute-start(bf16[256,2048]{0,1:T(8,128)(2,1)} %get-tuple-element.27), channel_id=1, source_target_pairs={{0,2},{1,3},{2,0},{3,1},{4,6},{5,7},{6,4},{7,5},{8,10},{9,11},{10,... | collective-permute-start | bytes 3145736 | tf_op jit(solution)/shard_map/ppermute | solution.py:83
  30.5 46.2 %collective-permute-start.2 = (bf16[256,2048]{0,1:T(8,128)(2,1)}, bf16[256,2048]{0,1:T(8,128)(2,1)}, u32[]{:S(2)}, u32[]{:S(2)}) collective-permute-start(bf16[256,2048]{0,1:T(8,128)(2,1)} %get-tuple-element.26), channel_id=1, source_target_pairs={{0,2},{1,3},{2,0},{3,1},{4,6},{5,7},{6,4},{7,5},{8,10},{9,11},{10,... | collective-permute-start | bytes 3145736 | tf_op jit(solution)/shard_map/ppermute | solution.py:82
  99.6 3.7 %collective-permute-start.4 = (f32[4,128,128]{2,1,0:T(8,128)S(1)}, f32[4,128,128]{2,1,0:T(8,128)S(1)}, u32[]{:S(2)}, u32[]{:S(2)}) collective-permute-start(f32[4,128,128]{2,1,0:T(8,128)S(1)} %copy.46), channel_id=1, source_target_pairs={{0,1},{1,0},{2,3},{3,2},{4,5},{5,4},{6,7},{7,6},{8,9},{9,8},{10,11... | collective-permute-start | bytes 786440 | tf_op jit(solution)/shard_map/ppermute | solution.py:45
  102.8 2.1 collective-permute-start.9
  103.4 9.3 %collective-permute-start.5 = (f32[4,128,128]{2,1,0:T(8,128)S(1)}, f32[4,128,128]{2,1,0:T(8,128)}, u32[]{:S(2)}, u32[]{:S(2)}) collective-permute-start(f32[4,128,128]{2,1,0:T(8,128)S(1)} %add.169), channel_id=1, source_target_pairs={{0,2},{1,3},{2,0},{3,1},{4,6},{5,7},{6,4},{7,5},{8,10},{9,11},{10,... | collective-permute-start | bytes 786440 | tf_op jit(solution)/shard_map/ppermute | solution.py:45
  106.0 18.7 %collective-permute-start.10 = (f32[4,128,128]{1,2,0:T(8,128)S(1)}, f32[4,128,128]{1,2,0:T(8,128)}, u32[]{:S(2)}, u32[]{:S(2)}) collective-permute-start(f32[4,128,128]{1,2,0:T(8,128)S(1)} %add.181), channel_id=1, source_target_pairs={{0,2},{1,3},{2,0},{3,1},{4,6},{5,7},{6,4},{7,5},{8,10},{9,11},{10,... | collective-permute-start | bytes 786440 | tf_op jit(solution)/shard_map/ppermute | solution.py:45
  121.2 56.3 %collective-permute-start.8 = (bf16[2,128,2048]{2,1,0:T(8,128)(2,1)}, bf16[2,128,2048]{2,1,0:T(8,128)(2,1)}, u32[]{:S(2)}, u32[]{:S(2)}) collective-permute-start(bf16[2,128,2048]{2,1,0:T(8,128)(2,1)} %get-tuple-element.25), channel_id=1, source_target_pairs={{0,12},{4,8},{8,4},{12,0},{16,28},{20,24},{24,20},{28,16},{1,13},{... | collective-permute-start | bytes 3145736 | tf_op jit(solution)/shard_map/ppermute | solution.py:130
  121.7 55.8 %collective-permute-start.7 = (bf16[2,128,2048]{2,1,0:T(8,128)(2,1)}, bf16[2,128,2048]{2,1,0:T(8,128)(2,1)}, u32[]{:S(2)}, u32[]{:S(2)}) collective-permute-start(bf16[2,128,2048]{2,1,0:T(8,128)(2,1)} %get-tuple-element.24), channel_id=1, source_target_pairs={{0,8},{4,12},{8,0},{12,4},{16,24},{20,28},{24,16},{28,20},{1,9},{5... | collective-permute-start | bytes 3145736 | tf_op jit(solution)/shard_map/ppermute | solution.py:130
  123.2 54.3 %collective-permute-start.6 = (bf16[2,128,2048]{2,1,0:T(8,128)(2,1)}, bf16[2,128,2048]{2,1,0:T(8,128)(2,1)}, u32[]{:S(2)}, u32[]{:S(2)}) collective-permute-start(bf16[2,128,2048]{2,1,0:T(8,128)(2,1)} %get-tuple-element.23), channel_id=1, source_target_pairs={{0,4},{4,0},{8,12},{12,8},{16,20},{20,16},{24,28},{28,24},{1,5},{5... | collective-permute-start | bytes 3145736 | tf_op jit(solution)/shard_map/ppermute | solution.py:130
  126.6 45.9 %collective-permute-start.13 = (bf16[2,128,256]{2,1,0:T(8,128)(2,1)S(1)}, bf16[2,128,256]{2,1,0:T(8,128)(2,1)S(1)}, u32[]{:S(2)}, u32[]{:S(2)}) collective-permute-start(bf16[2,128,256]{2,1,0:T(8,128)(2,1)S(1)} %get-tuple-element.29), channel_id=1, source_target_pairs={{0,12},{4,8},{8,4},{12,0},{16,28},{20,24},{24,20},{28,16},{1,13},{... | collective-permute-start | bytes 393224 | tf_op jit(solution)/shard_map/ppermute | solution.py:130
  127.2 45.9 %collective-permute-start.12 = (bf16[2,128,256]{2,1,0:T(8,128)(2,1)S(1)}, bf16[2,128,256]{2,1,0:T(8,128)(2,1)S(1)}, u32[]{:S(2)}, u32[]{:S(2)}) collective-permute-start(bf16[2,128,256]{2,1,0:T(8,128)(2,1)S(1)} %get-tuple-element.30), channel_id=1, source_target_pairs={{0,8},{4,12},{8,0},{12,4},{16,24},{20,28},{24,16},{28,20},{1,9},{5... | collective-permute-start | bytes 393224 | tf_op jit(solution)/shard_map/ppermute | solution.py:130
  172.5 5.0 %collective-permute-start.11 = (bf16[2,128,256]{2,1,0:T(8,128)(2,1)S(1)}, bf16[2,128,256]{2,1,0:T(8,128)(2,1)S(1)}, u32[]{:S(2)}, u32[]{:S(2)}) collective-permute-start(bf16[2,128,256]{2,1,0:T(8,128)(2,1)S(1)} %get-tuple-element.28), channel_id=1, source_target_pairs={{0,4},{4,0},{8,12},{12,8},{16,20},{20,16},{24,28},{28,24},{1,5},{5... | collective-permute-start | bytes 393224 | tf_op jit(solution)/shard_map/ppermute | solution.py:130
  180.8 24.7 %collective-permute-start.14 = (bf16[128,2304]{1,0:T(8,128)(2,1)S(1)}, bf16[128,2304]{1,0:T(8,128)(2,1)}, u32[]{:S(2)}, u32[]{:S(2)}) collective-permute-start(bf16[128,2304]{1,0:T(8,128)(2,1)S(1)} %fusion.41), channel_id=1, source_target_pairs={{0,16},{4,20},{8,24},{12,28},{16,0},{20,4},{24,8},{28,12},{1,17},{... | collective-permute-start | bytes 1769480 | tf_op jit(solution)/shard_map/ppermute | solution.py:142
  206.7 3.8 %copy-start.6 = (f32[128,256]{1,0:T(8,128)S(1)}, f32[128,256]{1,0:T(8,128)}, u32[]{:S(2)}) copy-start(f32[128,256]{1,0:T(8,128)} %param.20) | copy-start | bytes 393220
  206.7 3.8 %copy-start.7 = (f32[128,256]{1,0:T(8,128)S(1)}, f32[128,256]{1,0:T(8,128)}, u32[]{:S(2)}) copy-start(f32[128,256]{1,0:T(8,128)} %param.19) | copy-start | bytes 393220
  207.8 6.9 %copy-start.1 = (bf16[512,2048]{1,0:T(8,128)(2,1)S(1)}, bf16[512,2048]{1,0:T(8,128)(2,1)}, u32[]{:S(2)}) copy-start(bf16[512,2048]{1,0:T(8,128)(2,1)} %param.12) | copy-start | bytes 6291460
  (1 other events, 3.3 us)
Sparse Core Ops, SparseCore 0:
  10.6 82.7 all-gather.2

commit v18 on v13

--- a/solution.py
+++ b/solution.py
@@ -112,9 +112,10 @@
         b_own = grouped_exchange(b_full)
     else:
         a_acc = group_stage(a_sc)
-        b_full, a_acc = lax.optimization_barrier((b_full, a_acc))
+        b_acc = group_stage(b_full)
+        b_acc, a_acc = lax.optimization_barrier((b_acc, a_acc))
         a_own = cross_stage(a_acc)
-        b_own = grouped_exchange(b_full)
+        b_own = cross_stage(b_acc)
     return a_own.T, b_own
 
 

time: 215 us -> 219 us (1.019)
  waiting for transfers between devices: 101 us -> 104 us
    ppermute x3 -> x6, waiting for transfers between devices: 33.9 us -> 40.6 us  [group_stage(): lax.ppermute(part.astype(jnp.bfloat16), 'dp', pairs).astype(jnp.float32)]
    ppermute x4 -> x0, waiting for transfers between devices: 6 us -> none  [grouped_exchange(): lax.ppermute(part.astype(jnp.bfloat16), 'dp', pairs).astype(jnp.float32)]
    ppermute x4 -> x0, starting transfers between devices: 4.17 us -> none  [grouped_exchange(): lax.ppermute(part.astype(jnp.bfloat16), 'dp', pairs).astype(jnp.float32)]
    ppermute x3 -> x6, starting transfers between devices: 3.49 us -> 6.06 us  [group_stage(): lax.ppermute(part.astype(jnp.bfloat16), 'dp', pairs).astype(jnp.float32)]
    unnamed x31 -> x33, local copies, waits for them, and re-layouts: 13.7 us -> 14.5 us
  transfers between devices with their start and end apart: 17 -> 17, of which waited for: 11 -> 7; matrix products, arithmetic and copies ran while one was open for 30% -> 29% of each run, Pallas kernels for 0% -> 0%
where the time goes in v18:
time: 219 us
  waiting for transfers between devices  104 us (47%)
  local copies, waits for them, and re-layouts  41.3 us (19%)
  matrix products  22.5 us (10%)
  other arithmetic  21.1 us (10%)
  starting transfers between devices  15.7 us (7%)
  between operations  14.4 us (7%)
    ppermute x6, waiting for transfers between devices, group_stage(): lax.ppermute(part.astype(jnp.bfloat16), 'dp', pairs).astype(jnp.float32)  40.6 us
    ppermute x1, waiting for transfers between devices, frozen_gradient(): lax.ppermute(far_part[:half], 'tensor', row_pairs)  22 us
    ppermute x1, waiting for transfers between devices, frozen_gradient(): lax.ppermute(far_part[half:], 'tensor', row_pairs)  20.5 us
    unnamed x33, local copies, waits for them, and re-layouts  14.5 us
    all_gather x1, waiting for transfers between devices, local(): packed_all = lax.all_gather(packed, 'dp', axis=0, tiled=False)  11 us
    dot_general x2, matrix products, chip_partial(): jnp.einsum('tpk,pdk->td', partner_dy, other, preferred_element_type=jnp.f...  8.52 us
    ppermute x4, waiting for transfers between devices, tensor_sum(): parts = tuple((p + lax.ppermute(p, 'tensor', pairs) for p in parts))  6.55 us
    add x1, other arithmetic, local(): input_gradient_layer = frozen_gradient_share + adapter_gradient_term  6.5 us
  transfers between devices with their start and end apart: 17, of which 7 were waited for; matrix products, arithmetic and copies ran while one was open for 29% of the time, Pallas kernels for 0%

profile of v18, /device:TPU:0, one launch (start us, length us, event | category | flops | bytes accessed | tf_op | source)
XLA Modules:
  0.0 218.9 jit_solution(18139480841152812193)
XLA Ops:
  10.5 4.5 %copy_bitcast_fusion = bf16[2,2,2048,256]{3,2,0,1:T(8,128)(2,1)} fusion(bf16[2,2,2,2048,256]{4,3,2,1,0:T(8,128)(2,1)} %bitcast.122, s32[]{:T(128)S(6)} %select_n.108), kind=kLoop, calls=%fused_computation.8 | loop fusion | bytes 8388612 | tf_op jit(solution)/shard_map/jit(dynamic_index_in_dim)/squeeze | solution.py:64
  18.8 2.9 %fusion.2 = f32[2048,512,1]{1,0,2:T(8,128)S(1)} fusion(bf16[2,2,2,2048,256]{4,3,2,1,0:T(8,128)(2,1)} %bitcast.123, s32[]{:T(128)S(6)} %select_n.110, s32[]{:T(128)S(6)} %select_n.107, bf16[512,2,256]{2,1,0:T(2,128)(2,1)S(1)} %copy-done.7), kind=kOutput, calls=%fused_computation.10 | convolution fusion | flops 1073741824 | bytes 6815752 | tf_op jit(solution)/shard_map/tpk,pdk->td/dot_general | solution.py:74
  23.3 2.9 %fusion.1 = bf16[512,2048]{0,1:T(8,128)(2,1)S(1)} fusion(bf16[512,2,256]{2,0,1:T(8,128)(2,1)S(1)} %collective-permute-done.1, f32[2048,512,1]{1,0,2:T(8,128)S(1)} %fusion.2, bf16[2,2,2048,256]{3,2,0,1:T(8,128)(2,1)} %collective-permute-done, s32[]{:T(128)S(6)} %select_n.109), kind=kOutput, calls=%fused_computation.9 | convolution fusion | flops 1075838976 | bytes 8912900 | tf_op jit(solution)/shard_map/tpk,pdk->td/dot_general | solution.py:75
  27.6 2.9 %collective-permute-start.3 = (bf16[256,2048]{0,1:T(8,128)(2,1)}, bf16[256,2048]{0,1:T(8,128)(2,1)}, u32[]{:S(2)}, u32[]{:S(2)}) collective-permute-start(bf16[256,2048]{0,1:T(8,128)(2,1)} %get-tuple-element.33), channel_id=1, source_target_pairs={{0,2},{1,3},{2,0},{3,1},{4,6},{5,7},{6,4},{7,5},{8,10},{9,11},{10,... | collective-permute-start | bytes 3145736 | tf_op jit(solution)/shard_map/ppermute | solution.py:83
  31.4 2.9 %fusion.4 = f32[2048,512,1]{1,0,2:T(8,128)S(1)} fusion(bf16[2,2,2,2048,256]{4,3,2,1,0:T(8,128)(2,1)} %bitcast.124, s32[]{:T(128)S(6)} %select_n.104, s32[]{:T(128)S(6)} %select_n.107, bf16[512,2,256]{2,1,0:T(2,128)(2,1)S(1)} %copy-done.7), kind=kOutput, calls=%fused_computation.12 | convolution fusion | flops 1073741824 | bytes 6815752 | tf_op jit(solution)/shard_map/tpk,pdk->td/dot_general | solution.py:74
  34.3 20.5 %collective-permute-done.3 = bf16[256,2048]{0,1:T(8,128)(2,1)} collective-permute-done((bf16[256,2048]{0,1:T(8,128)(2,1)}, bf16[256,2048]{0,1:T(8,128)(2,1)}, u32[]{:S(2)}, u32[]{:S(2)}) %collective-permute-start.3) | collective-permute-done | bytes 1048608 | tf_op jit(solution)/shard_map/ppermute | solution.py:83
  54.7 22.0 %collective-permute-done.2 = bf16[256,2048]{0,1:T(8,128)(2,1)} collective-permute-done((bf16[256,2048]{0,1:T(8,128)(2,1)}, bf16[256,2048]{0,1:T(8,128)(2,1)}, u32[]{:S(2)}, u32[]{:S(2)}) %collective-permute-start.2) | collective-permute-done | bytes 1048608 | tf_op jit(solution)/shard_map/ppermute | solution.py:82
  76.7 5.6 %bitcast_add_fusion.1 = f32[512,2048]{0,1:T(8,128)} fusion(f32[2048,512,1]{1,0,2:T(8,128)S(1)} %fusion.4, bf16[512,2,256]{2,0,1:T(8,128)(2,1)S(1)} %collective-permute-done.1, bf16[256,2048]{0,1:T(8,128)(2,1)} %collective-permute-done.3, bf16[256,2048]{0,1:T(8,128)(2,1)} %collective-permute-done.2, bf16[2,2,2048,256]{3,2,0,1:T(8,128)(2,1)} %collective-permute-done, ...), kind=kOutput, calls=%fused_computation.6 | convolution fusion | flops 1080033280 | bytes 13107204 | tf_op jit(solution)/shard_map/tpk,pdk->td/dot_general | solution.py:75
  82.4 11.0 %all-gather.3.cloned.1.call-done = bf16[18432,128]{1,0:T(8,128)(2,1)} async-done(((bf16[2304,128]{1,0:T(8,128)(2,1)}), bf16[18432,128]{1,0:T(8,128)(2,1)}) %all-gather.3.cloned.1.call-update) | async-done | bytes 4718608 | tf_op jit(solution)/shard_map/all_gather | solution.py:192
  93.4 4.6 %gather_fusion.1 = bf16[4,2304,128]{2,1,0:T(8,128)(2,1)} fusion(bf16[8,2304,128]{2,1,0:T(8,128)(2,1)} %bitcast.128, s32[1024]{0:T(1024)S(1)} %pad_clamp_fusion.1), kind=kCustom, calls=%fused_computation.1 | custom fusion | bytes 4718608 | tf_op jit(solution)/shard_map/jit(_take)/gather | solution.py:198
  99.6 2.4 %fusion.21 = f32[4,128,128]{1,2,0:T(8,128)S(1)} fusion(bf16[4,128,2048]{2,1,0:T(8,128)(2,1)S(1)} %bitcast.116, bf16[4,2304,128]{2,1,0:T(8,128)(2,1)} %gather_fusion.1), kind=kOutput, calls=%fused_computation.32 | convolution fusion | flops 268435456 | bytes 4456448 | tf_op jit(solution)/shard_map/bnd,bdc->bnc/dot_general | solution.py:214
  105.4 6.5 %collective-permute-done.5 = f32[4,128,128]{2,1,0:T(8,128)S(1)} collective-permute-done((f32[4,128,128]{2,1,0:T(8,128)S(1)}, f32[4,128,128]{2,1,0:T(8,128)S(1)}, u32[]{:S(2)}, u32[]{:S(2)}) %collective-permute-start.5) | collective-permute-done | bytes 262176 | tf_op jit(solution)/shard_map/ppermute | solution.py:45
  112.1 2.3 %fusion.8 = f32[8,128,2048]{2,1,0:T(8,128)S(1)} fusion(bf16[512,2048]{1,0:T(8,128)(2,1)S(1)} %copy-done, pred[512,8]{0,1:T(8,128)(4,1)S(1)} %iota_compare_fusion, bf16[512,128]{0,1:T(8,128)(2,1)S(1)} %copy.51), kind=kOutput, calls=%fused_computation.17 | convolution fusion | flops 2148007936 | bytes 10620928 | tf_op jit(solution)/shard_map/nsc,nd->scd/dot_general | solution.py:100
  114.4 3.3 %copy-done.6 = f32[8,128,2048]{2,1,0:T(8,128)} copy-done((f32[8,128,2048]{2,1,0:T(8,128)}, f32[8,128,2048]{2,1,0:T(8,128)S(1)}, u32[]{:S(2)}) %copy-start.6) | copy-done | bytes 8388632
  130.3 40.6 %collective-permute-done.10 = bf16[2,128,256]{2,1,0:T(8,128)(2,1)S(1)} collective-permute-done((bf16[2,128,256]{2,1,0:T(8,128)(2,1)S(1)}, bf16[2,128,256]{2,1,0:T(8,128)(2,1)S(1)}, u32[]{:S(2)}, u32[]{:S(2)}) %collective-permute-start.10) | collective-permute-done | bytes 131104 | tf_op jit(solution)/shard_map/ppermute | solution.py:130
  171.6 3.2 %constant_dynamic-slice_fusion.3 = f32[2,1,128,2048]{3,2,1,0:T(8,128)} fusion(f32[2,4,128,2048]{3,2,1,0:T(8,128)} %bitcast.119, s32[]{:T(128)S(6)} %select_n.116), kind=kLoop, calls=%fused_computation.81 | loop fusion | bytes 4194308 | tf_op jit(solution)/shard_map/jit(dynamic_index_in_dim)/dynamic_slice | solution.py:126
  174.8 1.9 copy.52
  178.5 2.4 %fusion.7 = f32[2,128,2048]{1,2,0:T(8,128)S(1)} fusion(f32[2,1,128,2048]{2,3,0,1:T(8,128)S(1)} %copy.52, bf16[2,128,2048]{1,2,0:T(8,128)(2,1)} %collective-permute-done.13, bf16[2,128,2048]{1,2,0:T(8,128)(2,1)} %collective-permute-done.12, bf16[2,128,2048]{1,2,0:T(8,128)(2,1)} %collective-permute-done.11), kind=kLoop, calls=%fused_computation.16 | loop fusion | flops 3145728 | bytes 7340032 | tf_op jit(solution)/shard_map/add | solution.py:130
  184.9 2.7 %fusion.18 = f32[4,128,2048]{2,1,0:T(8,128)} fusion(bf16[4,128,128]{2,1,0:T(8,128)(2,1)S(1)} %multiply_convert_fusion.1, bf16[4,2304,128]{2,1,0:T(8,128)(2,1)S(1)} %copy-done.4), kind=kOutput, calls=%fused_computation.27 | convolution fusion | flops 268435456 | bytes 6422528 | tf_op jit(solution)/shard_map/bnc,bdc->bnd/dot_general | solution.py:224
  187.5 5.4 %copy.59 = f32[512,2048]{0,1:T(8,128)} copy(f32[512,2048]{1,0:T(8,128)} %bitcast.117) | data formatting | bytes 8388608 | tf_op jit(solution)/shard_map/reshape | solution.py:226
  193.0 6.5 %add.180 = f32[512,2048]{0,1:T(8,128)} add(f32[512,2048]{0,1:T(8,128)} %bitcast_add_fusion.1, f32[512,2048]{0,1:T(8,128)} %copy.59) | non-fusion elementwise | flops 1048576 | bytes 12582912 | tf_op jit(solution)/shard_map/add | solution.py:227
  199.5 5.4 %copy.56 = f32[512,2048]{1,0:T(8,128)} copy(f32[512,2048]{0,1:T(8,128)} %add.180) | data formatting | bytes 8388608
  206.5 1.8 fusion.48
  208.3 3.7 %fusion.28 = (f32[2048,128]{1,0:T(8,128)}, f32[2048,128]{1,0:T(8,128)}) fusion(f32[2048,128]{1,0:T(8,128)S(1)} %copy-done.9, f32[2048,128]{1,0:T(8,128)} %param.17, bf16[128,2048]{0,1:T(8,128)(2,1)} %collective-permute-done.14, f32[2,128,2048]{1,2,0:T(8,128)} %copy-done.5, s32[]{:T(128)S(6)} %select_n.122), kind=kLoop, calls=%fused_computation.37 | loop fusion | flops 3407872 | bytes 5767172 | tf_op jit(solution)/shard_map/div | solution.py:22
  (101 shorter events, 36.3 us)
Async XLA Ops:
  7.2 92.5 %copy-start = (bf16[512,2048]{1,0:T(8,128)(2,1)S(1)}, bf16[512,2048]{1,0:T(8,128)(2,1)}, u32[]{:S(2)}) copy-start(bf16[512,2048]{1,0:T(8,128)(2,1)} %param.12) | copy-start | bytes 6291460
  7.2 86.2 %all-gather.3.cloned.1.call-start = ((), (), s32[]{:S(2)}) async-start(), calls=%async_computation | async-start | bytes 5308416 | tf_op jit(solution)/shard_map/all_gather | solution.py:192
  10.5 6.6 %copy-start.2 = (s32[8]{0:T(128)S(1)}, s32[8]{0:T(128)}, u32[]{:S(2)}) copy-start(s32[8]{0:T(128)} %param.22) | copy-start | bytes 100
  15.1 8.2 %collective-permute-start = (bf16[2,2,2048,256]{3,2,0,1:T(8,128)(2,1)}, bf16[2,2,2048,256]{3,2,0,1:T(8,128)(2,1)}, u32[]{:S(2)}, u32[]{:S(2)}) collective-permute-start(bf16[2,2,2048,256]{3,2,0,1:T(8,128)(2,1)} %copy_bitcast_fusion), channel_id=1, source_target_pairs={{0,1},{1,0},{2,3},{3,2},{4,5},{5,4},{6,7},{7,6},{8,9},{9,8},{10,11... | collective-permute-start | bytes 12582920 | tf_op jit(solution)/shard_map/ppermute | solution.py:68
  16.4 6.9 %collective-permute-start.1 = (bf16[512,2,256]{2,0,1:T(8,128)(2,1)}, bf16[512,2,256]{2,0,1:T(8,128)(2,1)S(1)}, u32[]{:S(2)}, u32[]{:S(2)}) collective-permute-start(bf16[512,2,256]{2,0,1:T(8,128)(2,1)} %copy.36), channel_id=1, source_target_pairs={{0,1},{1,0},{2,3},{3,2},{4,5},{5,4},{6,7},{7,6},{8,9},{9,8},{10,11... | collective-permute-start | bytes 1572872 | tf_op jit(solution)/shard_map/ppermute | solution.py:69
  27.6 27.1 %collective-permute-start.3 = (bf16[256,2048]{0,1:T(8,128)(2,1)}, bf16[256,2048]{0,1:T(8,128)(2,1)}, u32[]{:S(2)}, u32[]{:S(2)}) collective-permute-start(bf16[256,2048]{0,1:T(8,128)(2,1)} %get-tuple-element.33), channel_id=1, source_target_pairs={{0,2},{1,3},{2,0},{3,1},{4,6},{5,7},{6,4},{7,5},{8,10},{9,11},{10,... | collective-permute-start | bytes 3145736 | tf_op jit(solution)/shard_map/ppermute | solution.py:83
  30.5 46.2 %collective-permute-start.2 = (bf16[256,2048]{0,1:T(8,128)(2,1)}, bf16[256,2048]{0,1:T(8,128)(2,1)}, u32[]{:S(2)}, u32[]{:S(2)}) collective-permute-start(bf16[256,2048]{0,1:T(8,128)(2,1)} %get-tuple-element.32), channel_id=1, source_target_pairs={{0,2},{1,3},{2,0},{3,1},{4,6},{5,7},{6,4},{7,5},{8,10},{9,11},{10,... | collective-permute-start | bytes 3145736 | tf_op jit(solution)/shard_map/ppermute | solution.py:82
  99.5 3.1 %collective-permute-start.4 = (f32[4,128,128]{2,1,0:T(8,128)S(1)}, f32[4,128,128]{2,1,0:T(8,128)S(1)}, u32[]{:S(2)}, u32[]{:S(2)}) collective-permute-start(f32[4,128,128]{2,1,0:T(8,128)S(1)} %copy.43), channel_id=1, source_target_pairs={{0,1},{1,0},{2,3},{3,2},{4,5},{5,4},{6,7},{7,6},{8,9},{9,8},{10,11... | collective-permute-start | bytes 786440 | tf_op jit(solution)/shard_map/ppermute | solution.py:45
  102.1 2.1 collective-permute-start.6
  102.7 9.2 %collective-permute-start.5 = (f32[4,128,128]{2,1,0:T(8,128)S(1)}, f32[4,128,128]{2,1,0:T(8,128)S(1)}, u32[]{:S(2)}, u32[]{:S(2)}) collective-permute-start(f32[4,128,128]{2,1,0:T(8,128)S(1)} %add.177), channel_id=1, source_target_pairs={{0,2},{1,3},{2,0},{3,1},{4,6},{5,7},{6,4},{7,5},{8,10},{9,11},{10,... | collective-permute-start | bytes 786440 | tf_op jit(solution)/shard_map/ppermute | solution.py:45
  104.3 21.5 %collective-permute-start.7 = (f32[4,128,128]{1,2,0:T(8,128)S(1)}, f32[4,128,128]{1,2,0:T(8,128)}, u32[]{:S(2)}, u32[]{:S(2)}) collective-permute-start(f32[4,128,128]{1,2,0:T(8,128)S(1)} %add.181), channel_id=1, source_target_pairs={{0,2},{1,3},{2,0},{3,1},{4,6},{5,7},{6,4},{7,5},{8,10},{9,11},{10,... | collective-permute-start | bytes 786440 | tf_op jit(solution)/shard_map/ppermute | solution.py:45
  119.7 58.8 %collective-permute-start.13 = (bf16[2,128,2048]{1,2,0:T(8,128)(2,1)}, bf16[2,128,2048]{1,2,0:T(8,128)(2,1)}, u32[]{:S(2)}, u32[]{:S(2)}) collective-permute-start(bf16[2,128,2048]{1,2,0:T(8,128)(2,1)} %bitcast.129), channel_id=1, source_target_pairs={{0,12},{4,8},{8,4},{12,0},{16,28},{20,24},{24,20},{28,16},{1,13},{... | collective-permute-start | bytes 3145736 | tf_op jit(solution)/shard_map/ppermute | solution.py:130
  120.2 6.8 %copy-start.8 = (bf16[512,2,256]{2,1,0:T(2,128)(2,1)S(1)}, bf16[512,2,256]{2,1,0:T(2,128)(2,1)}, u32[]{:S(2)}) copy-start(bf16[512,2,256]{2,1,0:T(2,128)(2,1)} %param.13) | copy-start | bytes 1572868
  121.5 57.0 %collective-permute-start.12 = (bf16[2,128,2048]{1,2,0:T(8,128)(2,1)}, bf16[2,128,2048]{1,2,0:T(8,128)(2,1)}, u32[]{:S(2)}, u32[]{:S(2)}) collective-permute-start(bf16[2,128,2048]{1,2,0:T(8,128)(2,1)} %bitcast.130), channel_id=1, source_target_pairs={{0,8},{4,12},{8,0},{12,4},{16,24},{20,28},{24,16},{28,20},{1,9},{5... | collective-permute-start | bytes 3145736 | tf_op jit(solution)/shard_map/ppermute | solution.py:130
  124.3 54.2 %collective-permute-start.11 = (bf16[2,128,2048]{1,2,0:T(8,128)(2,1)}, bf16[2,128,2048]{1,2,0:T(8,128)(2,1)}, u32[]{:S(2)}, u32[]{:S(2)}) collective-permute-start(bf16[2,128,2048]{1,2,0:T(8,128)(2,1)} %bitcast.107), channel_id=1, source_target_pairs={{0,4},{4,0},{8,12},{12,8},{16,20},{20,16},{24,28},{28,24},{1,5},{5... | collective-permute-start | bytes 3145736 | tf_op jit(solution)/shard_map/ppermute | solution.py:130
  128.3 42.6 %collective-permute-start.10 = (bf16[2,128,256]{2,1,0:T(8,128)(2,1)S(1)}, bf16[2,128,256]{2,1,0:T(8,128)(2,1)S(1)}, u32[]{:S(2)}, u32[]{:S(2)}) collective-permute-start(bf16[2,128,256]{2,1,0:T(8,128)(2,1)S(1)} %get-tuple-element.35), channel_id=1, source_target_pairs={{0,12},{4,8},{8,4},{12,0},{16,28},{20,24},{24,20},{28,16},{1,13},{... | collective-permute-start | bytes 393224 | tf_op jit(solution)/shard_map/ppermute | solution.py:130
  128.8 47.9 %collective-permute-start.9 = (bf16[2,128,256]{2,1,0:T(8,128)(2,1)}, bf16[2,128,256]{2,1,0:T(8,128)(2,1)S(1)}, u32[]{:S(2)}, u32[]{:S(2)}) collective-permute-start(bf16[2,128,256]{2,1,0:T(8,128)(2,1)} %get-tuple-element.36), channel_id=1, source_target_pairs={{0,8},{4,12},{8,0},{12,4},{16,24},{20,28},{24,16},{28,20},{1,9},{5... | collective-permute-start | bytes 393224 | tf_op jit(solution)/shard_map/ppermute | solution.py:130
  170.9 6.5 %collective-permute-start.8 = (bf16[2,128,256]{2,1,0:T(8,128)(2,1)S(1)}, bf16[2,128,256]{2,1,0:T(8,128)(2,1)}, u32[]{:S(2)}, u32[]{:S(2)}) collective-permute-start(bf16[2,128,256]{2,1,0:T(8,128)(2,1)S(1)} %get-tuple-element.34), channel_id=1, source_target_pairs={{0,4},{4,0},{8,12},{12,8},{16,20},{20,16},{24,28},{28,24},{1,5},{5... | collective-permute-start | bytes 393224 | tf_op jit(solution)/shard_map/ppermute | solution.py:130
  178.5 6.4 %copy-start.4 = (bf16[4,2304,128]{2,1,0:T(8,128)(2,1)S(1)}, bf16[4,2304,128]{2,1,0:T(8,128)(2,1)}, u32[]{:S(2)}) copy-start(bf16[4,2304,128]{2,1,0:T(8,128)(2,1)} %gather_fusion.1) | copy-start | bytes 7077892
  180.9 6.6 %copy-start.5 = (f32[2,128,2048]{1,2,0:T(8,128)}, f32[2,128,2048]{1,2,0:T(8,128)S(1)}, u32[]{:S(2)}) copy-start(f32[2,128,2048]{1,2,0:T(8,128)S(1)} %fusion.7) | copy-start | bytes 6291460
  181.9 26.4 %collective-permute-start.14 = (bf16[128,2048]{0,1:T(8,128)(2,1)}, bf16[128,2048]{0,1:T(8,128)(2,1)}, u32[]{:S(2)}, u32[]{:S(2)}) collective-permute-start(bf16[128,2048]{0,1:T(8,128)(2,1)} %fusion.34), channel_id=1, source_target_pairs={{0,16},{4,20},{8,24},{12,28},{16,0},{20,4},{24,8},{28,12},{1,17},{... | collective-permute-start | bytes 1572872 | tf_op jit(solution)/shard_map/ppermute | solution.py:142
  183.3 23.1 %collective-permute-start.15 = (bf16[128,256]{1,0:T(8,128)(2,1)S(1)}, bf16[128,256]{1,0:T(8,128)(2,1)}, u32[]{:S(2)}, u32[]{:S(2)}) collective-permute-start(bf16[128,256]{1,0:T(8,128)(2,1)S(1)} %fusion.52), channel_id=1, source_target_pairs={{0,16},{4,20},{8,24},{12,28},{16,0},{20,4},{24,8},{28,12},{1,17},{... | collective-permute-start | bytes 196616 | tf_op jit(solution)/shard_map/ppermute | solution.py:142
  199.5 7.0 %copy-start.10 = (f32[128,256]{1,0:T(8,128)S(1)}, f32[128,256]{1,0:T(8,128)}, u32[]{:S(2)}) copy-start(f32[128,256]{1,0:T(8,128)} %param.20) | copy-start | bytes 393220
  199.5 8.8 %copy-start.9 = (f32[2048,128]{1,0:T(8,128)S(1)}, f32[2048,128]{1,0:T(8,128)}, u32[]{:S(2)}) copy-start(f32[2048,128]{1,0:T(8,128)} %param.18) | copy-start | bytes 3145732
  (7 other events, 27.1 us)
Sparse Core Ops, SparseCore 0:
  10.6 82.7 all-gather.2
